TPU v7x, 256 devices: a whole 4x4x8 slice. The times are simulated.
256 devices in a mesh: gx: 8 (over x, core), gy: 8 (over z), gz: 4 (over y).
Axes of the slice: x: 4, y: 4, z: 8, core: 2. Of those that a mesh axis runs over, the one named last changes fastest.
Arguments:
- orbitals: float32 [32, 64, 128, 512], P(None, 'gx', 'gy', 'gz'), may hold values from -12 to 12
- potential: float32 [64, 128, 512], P('gx', 'gy', 'gz'), may hold values from -1 to 1
Outputs:
- filtered_basis: float32 [32, 64, 128, 512], P(None, 'gx', 'gy', 'gz')
- r_factor: float32 [32, 32], replicated
All inputs are finite; a program needn't handle non-finite values.
Results may differ from a plain program's by a relative error of at most 0.00013.
Values sent between devices are 32-bit elements; how exact they have to be, the bound alone decides.
No kernel may reach another device: no remote copies, remote signals or barrier semaphores. Data moves between devices by JAX's collectives and lax.ppermute only.
A program may use at most 128 MiB of HBM per device.

v0:
```python
import jax
import jax.numpy as jnp
from jax import lax
from jax.sharding import PartitionSpec as P

TAPS = (-1.0 / 12.0, 4.0 / 3.0, -2.5, 4.0 / 3.0, -1.0 / 12.0)


def padded_2(x, sides, width):
    for axis, dim in sides:
        devices, length = (lax.axis_size(axis), x.shape[dim])
        up = [(i, (i + 1) % devices) for i in range(devices)]
        down = [(j, i) for i, j in up]
        last = lax.slice_in_dim(x, length - width, length, axis=dim)
        leading = lax.slice_in_dim(x, 0, width, axis=dim)
        before = lax.ppermute(last, axis, up)
        after = lax.ppermute(leading, axis, down)
        x = jnp.concatenate([before, x, after], axis=dim)
    return x


def window(padded, shift_x, shift_y, shift_z):
    sizes = padded.shape
    return padded[
        :,
        2 + shift_x : sizes[1] - 2 + shift_x,
        2 + shift_y : sizes[2] - 2 + shift_y,
        2 + shift_z : sizes[3] - 2 + shift_z,
    ]


def laplacian(padded):
    summed = 3.0 * TAPS[2] * window(padded, 0, 0, 0)
    for offset, weight in ((-2, TAPS[0]), (-1, TAPS[1]), (1, TAPS[3]), (2, TAPS[4])):
        summed = summed + weight * window(padded, offset, 0, 0)
        summed = summed + weight * window(padded, 0, offset, 0)
        summed = summed + weight * window(padded, 0, 0, offset)
    return summed


def hamiltonian(padded, potential_core):
    return -0.5 * laplacian(padded) + potential_core * window(padded, 0, 0, 0)


def with_rims(field):
    return padded_2(field, (("gx", 1), ("gy", 2), ("gz", 3)), 2)


def per_device(orbitals, potential):
    potential_cube = potential[None]
    first = (hamiltonian(with_rims(orbitals), potential_cube) - 5.5 * orbitals) / 3.5
    second = 2.0 * (hamiltonian(with_rims(first), potential_cube) - 5.5 * first) / 3.5 - orbitals
    norb_count = orbitals.shape[0]
    filtered = second.reshape(norb_count, -1)
    all_cells = filtered.shape[1] * lax.axis_size("gx") * lax.axis_size("gy") * lax.axis_size("gz")
    correlation = jnp.dot(filtered, filtered.T, precision=lax.Precision.HIGHEST) / all_cells
    lower = jnp.linalg.cholesky(lax.psum(correlation, ("gx", "gy", "gz")))
    basis = jax.scipy.linalg.solve_triangular(lower, filtered, lower=True)
    return (basis.reshape(orbitals.shape), lower.T)


def solution(mesh):
    in_specs = (P(None, "gx", "gy", "gz"), P("gx", "gy", "gz"))
    out_specs = (P(None, "gx", "gy", "gz"), P())
    return jax.shard_map(
        per_device, mesh=mesh, in_specs=in_specs, out_specs=out_specs, check_vma=False
    )
```

profile of v0, /device:TPU:1, one launch (start us, length us, event | category | flops | bytes accessed | tf_op | source)
XLA Modules:
  0.0 230.9 jit_solution(3430019254784717829)
XLA Ops:
  0.6 1.3 fusion.59
  2.2 2.6 %collective-permute-start = (f32[32,2,16,128]{3,0,2,1:T(8,128)S(1)}, f32[32,2,16,128]{3,0,2,1:T(8,128)S(1)}, u32[]{:S(2)}, u32[]{:S(2)}) collective-permute-start(f32[32,2,16,128]{3,0,2,1:T(8,128)S(1)} %copy.80), channel_id=1, source_target_pairs={{0,32},{32,64},{64,96},{96,128},{128,160},{160,192},{192,224},{224... | collective-permute-start | bytes 1572872 | tf_op jit(solution)/shard_map/ppermute | solution.py:16
  5.1 0.6 collective-permute-start.1
  5.8 5.2 %collective-permute-done = f32[32,2,16,128]{3,0,2,1:T(8,128)S(1)} collective-permute-done((f32[32,2,16,128]{3,0,2,1:T(8,128)S(1)}, f32[32,2,16,128]{3,0,2,1:T(8,128)S(1)}, u32[]{:S(2)}, u32[]{:S(2)}) %collective-permute-start) | collective-permute-done | bytes 524320 | tf_op jit(solution)/shard_map/ppermute | solution.py:16
  11.1 1.4 constant_dynamic-update-slice_fusion
  12.5 1.6 collective-permute-done.1
  14.2 1.4 collective-permute-start.2
  15.6 4.0 %collective-permute-start.3 = (f32[32,12,2,128]{3,0,2,1:T(8,128)S(1)}, f32[32,12,2,128]{3,0,2,1:T(8,128)S(1)}, u32[]{:S(2)}, u32[]{:S(2)}) collective-permute-start(f32[32,12,2,128]{3,0,2,1:T(8,128)S(1)} %get-tuple-element.21), channel_id=1, source_target_pairs={{4,0},{8,4},{12,8},{16,12},{20,16},{24,20},{28,24},{0,28},{5,1},{9... | collective-permute-start | bytes 1179656 | tf_op jit(solution)/shard_map/ppermute | solution.py:17
  19.7 8.1 %collective-permute-done.2 = f32[32,12,2,128]{3,0,2,1:T(8,128)S(1)} collective-permute-done((f32[32,12,2,128]{3,0,2,1:T(8,128)S(1)}, f32[32,12,2,128]{3,0,2,1:T(8,128)S(1)}, u32[]{:S(2)}, u32[]{:S(2)}) %collective-permute-start.2) | collective-permute-done | bytes 393248 | tf_op jit(solution)/shard_map/ppermute | solution.py:16
  27.8 0.4 pad_maximum_fusion
  28.2 4.7 %fusion.56 = (f32[32,12,20,2]{3,0,2,1:T(8,128)}, f32[32,12,20,2]{3,0,2,1:T(8,128)}) fusion(f32[32,12,20,128]{3,0,2,1:T(8,128)S(1)} %pad_maximum_fusion), kind=kLoop, calls=%fused_computation.120 | loop fusion | bytes 245760 | tf_op jit(solution)/shard_map/slice | solution.py:14
  32.9 3.4 %copy.47 = f32[32,12,20,2]{0,2,3,1:T(8,128)S(1)} copy(f32[32,12,20,2]{3,0,2,1:T(8,128)} %get-tuple-element.14) | data formatting | bytes 122880 | tf_op jit(solution)/shard_map/slice | solution.py:14
  36.3 1.4 collective-permute-start.4
  37.6 3.4 %copy.50 = f32[32,12,20,2]{0,2,3,1:T(8,128)S(1)} copy(f32[32,12,20,2]{3,0,2,1:T(8,128)} %get-tuple-element.15) | data formatting | bytes 122880 | tf_op jit(solution)/shard_map/slice | solution.py:15
  41.0 1.7 collective-permute-start.5
  42.7 1.6 collective-permute-done.4
  44.3 2.9 %copy.48 = f32[32,12,20,2]{3,0,2,1:T(8,128)} copy(f32[32,12,20,2]{0,2,3,1:T(8,128)S(1)} %collective-permute-done.4) | data formatting | bytes 122880 | tf_op jit(solution)/shard_map/ppermute | solution.py:16
  47.2 0.4 collective-permute-done.5
  47.7 2.9 %copy.51 = f32[32,12,20,2]{3,0,2,1:T(8,128)} copy(f32[32,12,20,2]{0,2,3,1:T(8,128)S(1)} %collective-permute-done.5) | data formatting | bytes 122880 | tf_op jit(solution)/shard_map/ppermute | solution.py:17
  50.5 17.0 %broadcast_multiply_fusion = (f32[32,8,16,128]{3,0,2,1:T(8,128)S(1)}, f32[32,8,16,128]{3,0,2,1:T(8,128)}) fusion(f32[8,16,128]{2,1,0:T(8,128)S(1)} %copy-done.5, f32[32,12,20,2]{3,0,2,1:T(8,128)} %copy.51, f32[32,12,2,128]{3,0,2,1:T(8,128)S(1)} %collective-permute-done.3, f32[32,12,16,128]{3,0,2,1:T(8,128)} %copy-done.1, ...), kind=kLoop, calls=%fused_computation.97 | loop fusion | flops 24641536 | bytes 18800640 | tf_op jit(solution)/shard_map/div | solution.py:51
  67.6 5.3 %collective-permute-start.6 = (f32[32,2,16,128]{3,0,2,1:T(8,128)S(1)}, f32[32,2,16,128]{3,0,2,1:T(8,128)S(1)}, u32[]{:S(2)}, u32[]{:S(2)}) collective-permute-start(f32[32,2,16,128]{3,0,2,1:T(8,128)S(1)} %get-tuple-element.22), channel_id=1, source_target_pairs={{0,32},{32,64},{64,96},{96,128},{128,160},{160,192},{192,224},{224... | collective-permute-start | bytes 1572872 | tf_op jit(solution)/shard_map/ppermute | solution.py:16
  72.9 6.1 %collective-permute-done.6 = f32[32,2,16,128]{3,0,2,1:T(8,128)S(1)} collective-permute-done((f32[32,2,16,128]{3,0,2,1:T(8,128)S(1)}, f32[32,2,16,128]{3,0,2,1:T(8,128)S(1)}, u32[]{:S(2)}, u32[]{:S(2)}) %collective-permute-start.6) | collective-permute-done | bytes 524320 | tf_op jit(solution)/shard_map/ppermute | solution.py:16
  79.1 2.5 %collective-permute-done.7 = f32[32,2,16,128]{3,0,2,1:T(8,128)S(1)} collective-permute-done((f32[32,2,16,128]{3,0,2,1:T(8,128)S(1)}, f32[32,2,16,128]{3,0,2,1:T(8,128)S(1)}, u32[]{:S(2)}, u32[]{:S(2)}) %collective-permute-start.7) | collective-permute-done | bytes 524320 | tf_op jit(solution)/shard_map/ppermute | solution.py:17
  81.7 2.7 %collective-permute-start.9 = (f32[32,12,2,128]{3,0,2,1:T(8,128)S(1)}, f32[32,12,2,128]{3,0,2,1:T(8,128)S(1)}, u32[]{:S(2)}, u32[]{:S(2)}) collective-permute-start(f32[32,12,2,128]{3,0,2,1:T(8,128)S(1)} %get-tuple-element.19), channel_id=1, source_target_pairs={{4,0},{8,4},{12,8},{16,12},{20,16},{24,20},{28,24},{0,28},{5,1},{9... | collective-permute-start | bytes 1179656 | tf_op jit(solution)/shard_map/ppermute | solution.py:17
  84.4 0.6 broadcast_multiply_fusion.1
  85.0 8.1 %collective-permute-done.8 = f32[32,12,2,128]{3,0,2,1:T(8,128)S(1)} collective-permute-done((f32[32,12,2,128]{3,0,2,1:T(8,128)S(1)}, f32[32,12,2,128]{3,0,2,1:T(8,128)S(1)}, u32[]{:S(2)}, u32[]{:S(2)}) %collective-permute-start.8) | collective-permute-done | bytes 393248 | tf_op jit(solution)/shard_map/ppermute | solution.py:16
  93.1 0.4 pad_maximum_fusion.1
  93.5 0.4 copy-done.4
  94.0 4.7 %fusion.55 = (f32[32,12,20,2]{3,0,2,1:T(8,128)}, f32[32,12,20,2]{3,0,2,1:T(8,128)}) fusion(f32[32,12,20,128]{3,0,2,1:T(8,128)S(1)} %pad_maximum_fusion.1), kind=kLoop, calls=%fused_computation.119 | loop fusion | bytes 245760 | tf_op jit(solution)/shard_map/slice | solution.py:14
  98.6 4.0 %copy.54 = f32[32,12,20,2]{0,2,3,1:T(8,128)} copy(f32[32,12,20,2]{3,0,2,1:T(8,128)} %get-tuple-element.12) | data formatting | bytes 122880 | tf_op jit(solution)/shard_map/slice | solution.py:14
  102.7 4.0 %copy.56 = f32[32,12,20,2]{0,2,3,1:T(8,128)} copy(f32[32,12,20,2]{3,0,2,1:T(8,128)} %get-tuple-element.13) | data formatting | bytes 122880 | tf_op jit(solution)/shard_map/slice | solution.py:15
  106.7 2.7 %collective-permute-start.11 = (f32[32,12,20,2]{0,2,3,1:T(8,128)}, f32[32,12,20,2]{0,2,3,1:T(8,128)}, u32[]{:S(2)}, u32[]{:S(2)}) collective-permute-start(f32[32,12,20,2]{0,2,3,1:T(8,128)} %copy.56), channel_id=1, source_target_pairs={{1,0},{2,1},{3,2},{0,3},{5,4},{6,5},{7,6},{4,7},{9,8},{10,9},{11,1... | collective-permute-start | bytes 184328 | tf_op jit(solution)/shard_map/ppermute | solution.py:17
  109.4 4.3 %maximum_maximum_fusion = (f32[32,12,18,128]{3,0,2,1:T(8,128)}, f32[32,12,18,128]{3,0,2,1:T(8,128)}) fusion(f32[32,2,16,128]{3,0,2,1:T(8,128)S(1)} %collective-permute-done.7, f32[32,8,16,128]{3,0,2,1:T(8,128)S(1)} %get-tuple-element.10, f32[32,2,16,128]{3,0,2,1:T(8,128)S(1)} %collective-permute-done.6, f32[32,12,2,128]{3,0,2,1:T(8,128)S(1)} %collective-permute-done.8, ...), kind=kLoop, calls=%fused_computation.6 | loop fusion | flops 5308416 | bytes 11010048 | tf_op jit(solution)/shard_map/concatenate | solution.py:18
  113.7 5.4 %collective-permute-done.10 = f32[32,12,20,2]{0,2,3,1:T(8,128)} collective-permute-done((f32[32,12,20,2]{0,2,3,1:T(8,128)}, f32[32,12,20,2]{0,2,3,1:T(8,128)}, u32[]{:S(2)}, u32[]{:S(2)}) %collective-permute-start.10) | collective-permute-done | bytes 61472 | tf_op jit(solution)/shard_map/ppermute | solution.py:16
  119.1 3.7 %copy.55 = f32[32,12,20,2]{3,0,2,1:T(8,128)} copy(f32[32,12,20,2]{0,2,3,1:T(8,128)} %collective-permute-done.10) | data formatting | bytes 122880 | tf_op jit(solution)/shard_map/ppermute | solution.py:16
  122.9 3.8 %copy.57 = f32[32,12,20,2]{3,0,2,1:T(8,128)} copy(f32[32,12,20,2]{0,2,3,1:T(8,128)} %collective-permute-done.11) | data formatting | bytes 122880 | tf_op jit(solution)/shard_map/ppermute | solution.py:17
  126.6 9.9 %fusion.12 = f32[32,8,16,128]{3,0,2,1:T(8,128)S(1)} fusion(f32[32,8,16,128]{3,0,2,1:T(8,128)S(1)} %get-tuple-element.10, f32[32,2,16,128]{3,0,2,1:T(8,128)S(1)} %collective-permute-done.7, f32[32,2,16,128]{3,0,2,1:T(8,128)S(1)} %collective-permute-done.6, f32[32,12,20,2]{3,0,2,1:T(8,128)} %copy.57, f32[32,12,2,128]{3,0,2,1:T(8,128)} %copy-done.4, ...), kind=kLoop, calls=%fused_computation.24 | loop fusion | flops 29360128 | bytes 18800640 | tf_op jit(solution)/shard_map/sub | solution.py:52
  136.5 1.8 fusion.50
  138.3 1.2 copy.61
  139.5 76.7 %psum.7 = f32[32,32]{0,1:T(8,128)S(1)} all-reduce(f32[32,32]{0,1:T(8,128)S(1)} %fusion.50), channel_id=1, replica_groups=mesh['gx'=8,'gy'=8,'gz'=4] {'gx','gy','gz'}, use_global_device_ids=true, to_apply=%region_0.0 | all-reduce | flops 1024 | bytes 8192 | tf_op jit(solution)/shard_map/psum | solution.py:57
  216.2 1.2 copy.83
  217.9 2.9 %cholesky.16 = f32[32,32]{1,0:T(8,128)S(1)} custom-call(f32[32,32]{1,0:T(8,128)S(1)} %fusion.52), custom_call_target="Cholesky" | custom-call | tf_op jit(solution)/shard_map/jit(cholesky)/cholesky | solution.py:57
  220.9 0.6 compare_reduce_fusion
  221.5 0.7 fusion.53
  222.2 0.7 copy.65
  222.8 2.4 %custom-call.7 = f32[1,32,32]{1,2,0:T(8,128)S(1)} custom-call(f32[1,32,32]{2,1,0:T(8,128)S(1)} %get-tuple-element.34), custom_call_target="InvertDiagBlocksLowerTriangular" | custom-call | tf_op jit(solution)/shard_map/jit(_solve_triangular)/triangular_solve | solution.py:58
  225.3 3.0 %fusion.48 = f32[32,8,16,128]{3,0,2,1:T(8,128)S(1)} fusion(f32[8,16,128,32]{2,1,0,3:T(8,128)S(1)} %bitcast.32, f32[1,32,32]{1,2,0:T(8,128)S(1)} %custom-call.7), kind=kOutput, calls=%fused_computation.93 | convolution fusion | flops 201326592 | bytes 4198400 | tf_op jit(solution)/shard_map/jit(_solve_triangular)/triangular_solve | solution.py:58
  228.3 2.5 %copy.64 = f32[32,8,16,128]{3,2,1,0:T(8,128)} copy(f32[32,8,16,128]{3,0,2,1:T(8,128)S(1)} %fusion.48) | data formatting | bytes 4194304
  (30 shorter events, 1.6 us)
Async XLA Ops:
  1.9 9.2 %copy-start = (f32[32,8,16,128]{3,2,1,0:T(8,128)S(1)}, f32[32,8,16,128]{3,2,1,0:T(8,128)}, u32[]{:S(2)}) copy-start(f32[32,8,16,128]{3,2,1,0:T(8,128)} %param.2) | copy-start | bytes 6291460
  2.2 8.7 %collective-permute-start = (f32[32,2,16,128]{3,0,2,1:T(8,128)S(1)}, f32[32,2,16,128]{3,0,2,1:T(8,128)S(1)}, u32[]{:S(2)}, u32[]{:S(2)}) collective-permute-start(f32[32,2,16,128]{3,0,2,1:T(8,128)S(1)} %copy.80), channel_id=1, source_target_pairs={{0,32},{32,64},{64,96},{96,128},{128,160},{160,192},{192,224},{224... | collective-permute-start | bytes 1572872 | tf_op jit(solution)/shard_map/ppermute | solution.py:16
  5.1 8.9 %collective-permute-start.1 = (f32[32,2,16,128]{3,0,2,1:T(8,128)S(1)}, f32[32,2,16,128]{3,0,2,1:T(8,128)S(1)}, u32[]{:S(2)}, u32[]{:S(2)}) collective-permute-start(f32[32,2,16,128]{3,0,2,1:T(8,128)S(1)} %copy.81), channel_id=1, source_target_pairs={{32,0},{64,32},{96,64},{128,96},{160,128},{192,160},{224,192},{0,2... | collective-permute-start | bytes 1572872 | tf_op jit(solution)/shard_map/ppermute | solution.py:17
  12.5 15.3 %copy-start.3 = (f32[32,10,16,128]{3,0,2,1:T(8,128)}, f32[32,10,16,128]{3,0,2,1:T(8,128)S(1)}, u32[]{:S(2)}) copy-start(f32[32,10,16,128]{3,0,2,1:T(8,128)S(1)} %get-tuple-element.24) | copy-start | bytes 7864324
  14.1 13.6 %copy-start.2 = (f32[32,10,16,128]{3,0,2,1:T(8,128)}, f32[32,10,16,128]{3,0,2,1:T(8,128)S(1)}, u32[]{:S(2)}) copy-start(f32[32,10,16,128]{3,0,2,1:T(8,128)S(1)} %get-tuple-element.31) | copy-start | bytes 7864324
  14.2 13.6 %copy-start.1 = (f32[32,12,16,128]{3,0,2,1:T(8,128)}, f32[32,12,16,128]{3,0,2,1:T(8,128)S(1)}, u32[]{:S(2)}) copy-start(f32[32,12,16,128]{3,0,2,1:T(8,128)S(1)} %get-tuple-element.32) | copy-start | bytes 9437188
  14.2 13.5 %collective-permute-start.2 = (f32[32,12,2,128]{3,0,2,1:T(8,128)S(1)}, f32[32,12,2,128]{3,0,2,1:T(8,128)S(1)}, u32[]{:S(2)}, u32[]{:S(2)}) collective-permute-start(f32[32,12,2,128]{3,0,2,1:T(8,128)S(1)} %get-tuple-element.20), channel_id=1, source_target_pairs={{0,4},{4,8},{8,12},{12,16},{16,20},{20,24},{24,28},{28,0},{1,5},{5... | collective-permute-start | bytes 1179656 | tf_op jit(solution)/shard_map/ppermute | solution.py:16
  15.6 12.1 %collective-permute-start.3 = (f32[32,12,2,128]{3,0,2,1:T(8,128)S(1)}, f32[32,12,2,128]{3,0,2,1:T(8,128)S(1)}, u32[]{:S(2)}, u32[]{:S(2)}) collective-permute-start(f32[32,12,2,128]{3,0,2,1:T(8,128)S(1)} %get-tuple-element.21), channel_id=1, source_target_pairs={{4,0},{8,4},{12,8},{16,12},{20,16},{24,20},{28,24},{0,28},{5,1},{9... | collective-permute-start | bytes 1179656 | tf_op jit(solution)/shard_map/ppermute | solution.py:17
  36.3 8.1 %collective-permute-start.4 = (f32[32,12,20,2]{0,2,3,1:T(8,128)S(1)}, f32[32,12,20,2]{0,2,3,1:T(8,128)S(1)}, u32[]{:S(2)}, u32[]{:S(2)}) collective-permute-start(f32[32,12,20,2]{0,2,3,1:T(8,128)S(1)} %copy.47), channel_id=1, source_target_pairs={{0,1},{1,2},{2,3},{3,0},{4,5},{5,6},{6,7},{7,4},{8,9},{9,10},{10,1... | collective-permute-start | bytes 184328 | tf_op jit(solution)/shard_map/ppermute | solution.py:16
  41.0 6.7 %collective-permute-start.5 = (f32[32,12,20,2]{0,2,3,1:T(8,128)S(1)}, f32[32,12,20,2]{0,2,3,1:T(8,128)S(1)}, u32[]{:S(2)}, u32[]{:S(2)}) collective-permute-start(f32[32,12,20,2]{0,2,3,1:T(8,128)S(1)} %copy.50), channel_id=1, source_target_pairs={{1,0},{2,1},{3,2},{0,3},{5,4},{6,5},{7,6},{4,7},{9,8},{10,9},{11,1... | collective-permute-start | bytes 184328 | tf_op jit(solution)/shard_map/ppermute | solution.py:17
  47.2 3.3 %copy-start.5 = (f32[8,16,128]{2,1,0:T(8,128)S(1)}, f32[8,16,128]{2,1,0:T(8,128)}, u32[]{:S(2)}) copy-start(f32[8,16,128]{2,1,0:T(8,128)} %param.3) | copy-start | bytes 196612
  67.6 16.8 %copy-start.6 = (f32[8,16,128]{2,1,0:T(8,128)S(1)}, f32[8,16,128]{2,1,0:T(8,128)}, u32[]{:S(2)}) copy-start(f32[8,16,128]{2,1,0:T(8,128)} %param.3) | copy-start | bytes 196612
  67.6 11.5 %collective-permute-start.6 = (f32[32,2,16,128]{3,0,2,1:T(8,128)S(1)}, f32[32,2,16,128]{3,0,2,1:T(8,128)S(1)}, u32[]{:S(2)}, u32[]{:S(2)}) collective-permute-start(f32[32,2,16,128]{3,0,2,1:T(8,128)S(1)} %get-tuple-element.22), channel_id=1, source_target_pairs={{0,32},{32,64},{64,96},{96,128},{128,160},{160,192},{192,224},{224... | collective-permute-start | bytes 1572872 | tf_op jit(solution)/shard_map/ppermute | solution.py:16
  72.9 8.6 %collective-permute-start.7 = (f32[32,2,16,128]{3,0,2,1:T(8,128)S(1)}, f32[32,2,16,128]{3,0,2,1:T(8,128)S(1)}, u32[]{:S(2)}, u32[]{:S(2)}) collective-permute-start(f32[32,2,16,128]{3,0,2,1:T(8,128)S(1)} %get-tuple-element.23), channel_id=1, source_target_pairs={{32,0},{64,32},{96,64},{128,96},{160,128},{192,160},{224,192},{0,2... | collective-permute-start | bytes 1572872 | tf_op jit(solution)/shard_map/ppermute | solution.py:17
  81.6 11.5 %collective-permute-start.8 = (f32[32,12,2,128]{3,0,2,1:T(8,128)S(1)}, f32[32,12,2,128]{3,0,2,1:T(8,128)S(1)}, u32[]{:S(2)}, u32[]{:S(2)}) collective-permute-start(f32[32,12,2,128]{3,0,2,1:T(8,128)S(1)} %get-tuple-element.18), channel_id=1, source_target_pairs={{0,4},{4,8},{8,12},{12,16},{16,20},{20,24},{24,28},{28,0},{1,5},{5... | collective-permute-start | bytes 1179656 | tf_op jit(solution)/shard_map/ppermute | solution.py:16
  81.7 11.4 %collective-permute-start.9 = (f32[32,12,2,128]{3,0,2,1:T(8,128)S(1)}, f32[32,12,2,128]{3,0,2,1:T(8,128)S(1)}, u32[]{:S(2)}, u32[]{:S(2)}) collective-permute-start(f32[32,12,2,128]{3,0,2,1:T(8,128)S(1)} %get-tuple-element.19), channel_id=1, source_target_pairs={{4,0},{8,4},{12,8},{16,12},{20,16},{24,20},{28,24},{0,28},{5,1},{9... | collective-permute-start | bytes 1179656 | tf_op jit(solution)/shard_map/ppermute | solution.py:17
  93.1 0.9 copy-start.4
  106.7 16.2 %collective-permute-start.11 = (f32[32,12,20,2]{0,2,3,1:T(8,128)}, f32[32,12,20,2]{0,2,3,1:T(8,128)}, u32[]{:S(2)}, u32[]{:S(2)}) collective-permute-start(f32[32,12,20,2]{0,2,3,1:T(8,128)} %copy.56), channel_id=1, source_target_pairs={{1,0},{2,1},{3,2},{0,3},{5,4},{6,5},{7,6},{4,7},{9,8},{10,9},{11,1... | collective-permute-start | bytes 184328 | tf_op jit(solution)/shard_map/ppermute | solution.py:17
  109.4 9.8 %collective-permute-start.10 = (f32[32,12,20,2]{0,2,3,1:T(8,128)}, f32[32,12,20,2]{0,2,3,1:T(8,128)}, u32[]{:S(2)}, u32[]{:S(2)}) collective-permute-start(f32[32,12,20,2]{0,2,3,1:T(8,128)} %copy.54), channel_id=1, source_target_pairs={{0,1},{1,2},{2,3},{3,0},{4,5},{5,6},{6,7},{7,4},{8,9},{9,10},{10,1... | collective-permute-start | bytes 184328 | tf_op jit(solution)/shard_map/ppermute | solution.py:16
where the time goes:
time: 231 us
  blocking collectives  76.7 us (33%)
  local copies, waits for them, and re-layouts  47.5 us (21%)
  other arithmetic  39.4 us (17%)
  waiting for transfers between devices  39.1 us (17%)
  starting transfers between devices  22.5 us (10%)
  matrix products  4.81 us (2%)
    psum x1, blocking collectives, per_device(): lower = jnp.linalg.cholesky(lax.psum(correlation, ('gx', 'gy', 'gz')))  76.7 us
    ppermute x6, waiting for transfers between devices, padded_2(): before = lax.ppermute(last, axis, up)  34.6 us
    div x1, other arithmetic, per_device(): (hamiltonian(with_rims(orbitals), potential_cube) - 5.5 * orbitals) / 3.5  17 us
    slice x6, local copies, waits for them, and re-layouts, padded_2(): last = lax.slice_in_dim(x, length - width, length, axis=dim)  16.9 us
    ppermute x6, starting transfers between devices, padded_2(): after = lax.ppermute(leading, axis, down)  11.7 us
    ppermute x6, starting transfers between devices, padded_2(): before = lax.ppermute(last, axis, up)  10.8 us
    sub x1, other arithmetic, per_device(): 2.0 * (hamiltonian(with_rims(first), potential_cube) - 5.5 * first) / 3.5  9.89 us
    slice x3, local copies, waits for them, and re-layouts, padded_2(): leading = lax.slice_in_dim(x, 0, width, axis=dim)  8.68 us
  transfers between devices with their start and end apart: 12, of which 9 were waited for; matrix products, arithmetic and copies ran while one was open for 7% of the time, Pallas kernels for 0%

commit v1 on v0

v1 whole, which is shorter than its diff:
```python
import jax
import jax.numpy as jnp
from jax import lax
from jax.sharding import PartitionSpec as P

TAPS = (-1.0 / 12.0, 4.0 / 3.0, -2.5, 4.0 / 3.0, -1.0 / 12.0)
AXES = ("gx", "gy", "gz")


def shift_pairs(n, step):
    return [(i, (i + step) % n) for i in range(n)]


def halos(f):
    out = {}
    for axis, dim in (("gx", 1), ("gy", 2), ("gz", 3)):
        n, length = lax.axis_size(axis), f.shape[dim]
        last = lax.slice_in_dim(f, length - 2, length, axis=dim)
        first = lax.slice_in_dim(f, 0, 2, axis=dim)
        if dim == 3:
            shape = last.shape
            pack = lambda a: jnp.transpose(a, (0, 3, 1, 2)).reshape(shape[0] * 2, -1)
            unpack = lambda a: jnp.transpose(a.reshape(shape[0], 2, shape[1], shape[2]), (0, 2, 3, 1))
            before = unpack(lax.ppermute(pack(last), axis, shift_pairs(n, 1)))
            after = unpack(lax.ppermute(pack(first), axis, shift_pairs(n, -1)))
        else:
            before = lax.ppermute(last, axis, shift_pairs(n, 1))
            after = lax.ppermute(first, axis, shift_pairs(n, -1))
        out[dim] = (before, after)
    return out


def laplacian(f, rims):
    summed = 3.0 * TAPS[2] * f
    for dim in (1, 2, 3):
        before, after = rims[dim]
        ext = jnp.concatenate([before, f, after], axis=dim)
        length = f.shape[dim]
        for offset, weight in ((-2, TAPS[0]), (-1, TAPS[1]), (1, TAPS[3]), (2, TAPS[4])):
            summed = summed + weight * lax.slice_in_dim(ext, 2 + offset, 2 + offset + length, axis=dim)
    return summed


def hamiltonian(f, potential_cube):
    return -0.5 * laplacian(f, halos(f)) + potential_cube * f


def butterfly_sum(c):
    for axis in ("gz", "gy", "gx"):
        n = lax.axis_size(axis)
        d = 1
        while d < n:
            c = c + lax.ppermute(c, axis, [(i, i ^ d) for i in range(n)])
            d *= 2
    return c


def per_device(orbitals, potential):
    potential_cube = potential[None]
    first = (hamiltonian(orbitals, potential_cube) - 5.5 * orbitals) / 3.5
    second = 2.0 * (hamiltonian(first, potential_cube) - 5.5 * first) / 3.5 - orbitals
    norb_count = orbitals.shape[0]
    filtered = second.reshape(norb_count, -1)
    all_cells = filtered.shape[1] * lax.axis_size("gx") * lax.axis_size("gy") * lax.axis_size("gz")
    correlation = jnp.dot(filtered, filtered.T, precision=lax.Precision.HIGHEST) / all_cells
    lower = jnp.linalg.cholesky(butterfly_sum(correlation))
    eye = jnp.eye(norb_count, dtype=lower.dtype)
    inverse = jax.scipy.linalg.solve_triangular(lower, eye, lower=True)
    basis = jnp.dot(inverse, filtered, precision=lax.Precision.HIGHEST)
    return (basis.reshape(orbitals.shape), lower.T)


def solution(mesh):
    in_specs = (P(None, "gx", "gy", "gz"), P("gx", "gy", "gz"))
    out_specs = (P(None, "gx", "gy", "gz"), P())
    return jax.shard_map(
        per_device, mesh=mesh, in_specs=in_specs, out_specs=out_specs, check_vma=False
    )
```

time: 231 us -> 145 us (0.63)
  blocking collectives: 76.7 us -> 0 us
  waiting for transfers between devices: 39.1 us -> 19.4 us
  starting transfers between devices: 22.5 us -> 34.9 us
  other arithmetic: 39.4 us -> 32.4 us
  local copies, waits for them, and re-layouts: 47.5 us -> 50.9 us
    psum x1 -> x0, blocking collectives: 76.7 us -> none  [per_device(): lower = jnp.linalg.cholesky(lax.psum(correlation, ('gx', 'gy', 'gz')))]
    transpose x0 -> x10, local copies, waits for them, and re-layouts: none -> 29.7 us  [the longest x6 18.1 us: halos(): pack = lambda a: jnp.transpose(a, (0, 3, 1, 2)).reshape(shape[0] * 2, -1)]
    slice x9 -> x6, local copies, waits for them, and re-layouts: 25.5 us -> 5.4 us  [the longest x5 4.67 us: halos(): last = lax.slice_in_dim(f, length - 2, length, axis=dim)]
    ppermute x12 -> x20, waiting for transfers between devices: 39.1 us -> 19.4 us  [the longest x8 19.4 us: butterfly_sum(): c = c + lax.ppermute(c, axis, [(i, i ^ d) for i in range(n)])]
    ppermute x12 -> x20, starting transfers between devices: 22.5 us -> 34.9 us  [the longest x8 15.7 us: butterfly_sum(): c = c + lax.ppermute(c, axis, [(i, i ^ d) for i in range(n)])]
    ppermute x4 -> x3, local copies, waits for them, and re-layouts: 13.2 us -> 3.26 us  [the longest x2 2.17 us: halos(): before = lax.ppermute(last, axis, shift_pairs(n, 1))]
    div x2, other arithmetic: 17 us -> 8.27 us  [the longest x1 8.26 us: per_device(): first = (hamiltonian(orbitals, potential_cube) - 5.5 * orbitals) / 3.5]
    sub x1, other arithmetic: 9.89 us -> 17.4 us  [per_device(): 2.0 * (hamiltonian(first, potential_cube) - 5.5 * first) / 3.5 - orbitals]
  transfers between devices with their start and end apart: 12 -> 20, of which waited for: 9 -> 8; matrix products, arithmetic and copies ran while one was open for 7% -> 29% of each run, Pallas kernels for 0% -> 0%
where the time goes in v1:
time: 145 us
  local copies, waits for them, and re-layouts  50.9 us (35%)
  starting transfers between devices  34.9 us (24%)
  other arithmetic  32.4 us (22%)
  waiting for transfers between devices  19.4 us (13%)
  matrix products  6.07 us (4%)
    ppermute x8, waiting for transfers between devices, butterfly_sum(): c = c + lax.ppermute(c, axis, [(i, i ^ d) for i in range(n)])  19.4 us
    transpose x6, local copies, waits for them, and re-layouts, halos(): pack = lambda a: jnp.transpose(a, (0, 3, 1, 2)).reshape(shape[0] * 2, -1)  18.1 us
    sub x1, other arithmetic, per_device(): 2.0 * (hamiltonian(first, potential_cube) - 5.5 * first) / 3.5 - orbitals  17.4 us
    ppermute x8, starting transfers between devices, butterfly_sum(): c = c + lax.ppermute(c, axis, [(i, i ^ d) for i in range(n)])  15.7 us
    transpose x4, local copies, waits for them, and re-layouts, halos(): jnp.transpose(a.reshape(shape[0], 2, shape[1], shape[2]), (0, 2, 3, 1))  11.6 us
    unnamed x17, local copies, waits for them, and re-layouts  8.43 us
    div x1, other arithmetic, per_device(): first = (hamiltonian(orbitals, potential_cube) - 5.5 * orbitals) / 3.5  8.26 us
    ppermute x4, starting transfers between devices, halos(): after = lax.ppermute(first, axis, shift_pairs(n, -1))  7.38 us
  transfers between devices with their start and end apart: 20, of which 8 were waited for; matrix products, arithmetic and copies ran while one was open for 29% of the time, Pallas kernels for 0%

profile of v1, /device:TPU:1, one launch (start us, length us, event | category | flops | bytes accessed | tf_op | source)
XLA Modules:
  0.0 144.5 jit_solution(3569436757873750518)
XLA Ops:
  0.6 2.4 %fusion.73 = (f32[32,2,16,128]{3,2,1,0:T(8,128)}, f32[32,2,16,128]{3,2,1,0:T(8,128)}) fusion(f32[32,8,16,128]{3,2,1,0:T(8,128)} %param.2), kind=kLoop, calls=%fused_computation.123 | loop fusion | bytes 2097152 | tf_op jit(solution)/shard_map/slice | solution.py:18
  3.1 2.6 %collective-permute-start = (f32[32,2,16,128]{3,2,1,0:T(8,128)}, f32[32,2,16,128]{3,2,1,0:T(8,128)}, u32[]{:S(2)}, u32[]{:S(2)}) collective-permute-start(f32[32,2,16,128]{3,2,1,0:T(8,128)} %get-tuple-element.23), channel_id=1, source_target_pairs={{0,32},{32,64},{64,96},{96,128},{128,160},{160,192},{192,224},{224... | collective-permute-start | bytes 1572872 | tf_op jit(solution)/shard_map/ppermute | solution.py:27
  6.5 1.1 collective-permute-start.2
  7.6 2.8 %slice_bitcast_fusion.3 = (f32[32,2,8,16]{1,3,2,0:T(8,128)}, f32[32,2,8,16]{1,3,2,0:T(8,128)}) fusion(f32[32,8,16,128]{3,2,1,0:T(8,128)S(1)} %copy-done), kind=kLoop, calls=%fused_computation.99 | loop fusion | bytes 131072 | tf_op jit(solution)/shard_map/transpose | solution.py:22
  10.3 3.1 %copy.92 = f32[32,2,8,16]{3,2,1,0:T(8,128)S(1)} copy(f32[32,2,8,16]{1,3,2,0:T(8,128)} %get-tuple-element.27) | data formatting | bytes 65536 | tf_op jit(solution)/shard_map/transpose | solution.py:22
  13.6 1.4 collective-permute-start.4
  15.0 3.1 %copy.94 = f32[32,2,8,16]{3,2,1,0:T(8,128)S(1)} copy(f32[32,2,8,16]{1,3,2,0:T(8,128)} %get-tuple-element.28) | data formatting | bytes 65536 | tf_op jit(solution)/shard_map/transpose | solution.py:22
  18.3 1.5 %collective-permute-start.5 = (f32[64,128]{1,0:T(8,128)S(1)}, f32[64,128]{1,0:T(8,128)S(1)}, u32[]{:S(2)}, u32[]{:S(2)}) collective-permute-start(f32[64,128]{1,0:T(8,128)S(1)} %reshape.46), channel_id=1, source_target_pairs={{0,3},{1,0},{2,1},{3,2},{4,7},{5,4},{6,5},{7,6},{8,11},{9,8},{10,9... | collective-permute-start | bytes 98312 | tf_op jit(solution)/shard_map/ppermute | solution.py:25
  20.6 4.0 %collective-permute-start.3 = (f32[32,8,2,128]{3,1,2,0:T(8,128)}, f32[32,8,2,128]{3,1,2,0:T(8,128)S(1)}, u32[]{:S(2)}, u32[]{:S(2)}) collective-permute-start(f32[32,8,2,128]{3,1,2,0:T(8,128)} %copy.115), channel_id=1, source_target_pairs={{0,28},{4,0},{8,4},{12,8},{16,12},{20,16},{24,20},{28,24},{1,29},{... | collective-permute-start | bytes 786440 | tf_op jit(solution)/shard_map/ppermute | solution.py:28
  24.6 2.9 %copy.93 = f32[32,8,16,2]{3,2,1,0:T(8,128)} copy(f32[32,8,16,2]{2,1,3,0:T(8,128)S(1)} %bitcast.55) | data formatting | bytes 65536 | tf_op jit(solution)/shard_map/transpose | solution.py:23
  27.7 2.9 %copy.95 = f32[32,8,16,2]{3,2,1,0:T(8,128)} copy(f32[32,8,16,2]{2,1,3,0:T(8,128)S(1)} %bitcast.56) | data formatting | bytes 65536 | tf_op jit(solution)/shard_map/transpose | solution.py:23
  30.6 1.1 copy.89
  31.7 1.1 constant_dynamic-update-slice_fusion.1
  33.6 1.2 copy-done.2
  34.8 8.3 %broadcast_multiply_fusion = (f32[32,8,16,128]{3,2,1,0:T(8,128)S(1)}, f32[32,8,16,128]{3,2,1,0:T(8,128)}) fusion(f32[32,8,16,128]{3,2,1,0:T(8,128)S(1)} %copy-done, f32[8,16,128]{2,1,0:T(8,128)S(1)} %copy-done.3, f32[32,8,16,2]{3,2,1,0:T(8,128)} %copy.95, f32[32,8,16,2]{3,2,1,0:T(8,128)} %copy.93, f32[32,8,18,128]{3,2,1,0:T(8,128)S(1)} %copy_dynamic-update-slice_fusion, ...), kind=kLoop, calls=%fused_computation.103 | loop fusion | flops 19398656 | bytes 19267584 | tf_op jit(solution)/shard_map/div | solution.py:60
  43.1 1.1 fusion.71
  44.4 2.5 %collective-permute-start.6 = (f32[32,2,16,128]{3,2,1,0:T(8,128)}, f32[32,2,16,128]{3,2,1,0:T(8,128)S(1)}, u32[]{:S(2)}, u32[]{:S(2)}) collective-permute-start(f32[32,2,16,128]{3,2,1,0:T(8,128)} %get-tuple-element.14), channel_id=1, source_target_pairs={{0,32},{32,64},{64,96},{96,128},{128,160},{160,192},{192,224},{224... | collective-permute-start | bytes 1572872 | tf_op jit(solution)/shard_map/ppermute | solution.py:27
  47.1 0.7 copy.96
  47.8 0.7 copy.98
  48.5 2.7 %collective-permute-start.9 = (f32[32,8,2,128]{3,1,2,0:T(8,128)}, f32[32,8,2,128]{3,1,2,0:T(8,128)}, u32[]{:S(2)}, u32[]{:S(2)}) collective-permute-start(f32[32,8,2,128]{3,1,2,0:T(8,128)} %copy.98), channel_id=1, source_target_pairs={{0,28},{4,0},{8,4},{12,8},{16,12},{20,16},{24,20},{28,24},{1,29},{... | collective-permute-start | bytes 786440 | tf_op jit(solution)/shard_map/ppermute | solution.py:28
  51.2 2.8 %slice_bitcast_fusion.1 = (f32[32,2,8,16]{1,3,2,0:T(8,128)}, f32[32,2,8,16]{1,3,2,0:T(8,128)}) fusion(f32[32,8,16,128]{3,2,1,0:T(8,128)S(1)} %get-tuple-element.12), kind=kLoop, calls=%fused_computation.68 | loop fusion | bytes 131072 | tf_op jit(solution)/shard_map/transpose | solution.py:22
  54.0 3.1 %copy.100 = f32[32,2,8,16]{3,2,1,0:T(8,128)S(1)} copy(f32[32,2,8,16]{1,3,2,0:T(8,128)} %get-tuple-element.18) | data formatting | bytes 65536 | tf_op jit(solution)/shard_map/transpose | solution.py:22
  57.5 3.1 %copy.102 = f32[32,2,8,16]{3,2,1,0:T(8,128)S(1)} copy(f32[32,2,8,16]{1,3,2,0:T(8,128)} %get-tuple-element.19) | data formatting | bytes 65536 | tf_op jit(solution)/shard_map/transpose | solution.py:22
  60.6 0.8 reshape.50
  62.0 2.6 %collective-permute-start.11 = (f32[64,128]{1,0:T(8,128)}, f32[64,128]{1,0:T(8,128)}, u32[]{:S(2)}, u32[]{:S(2)}) collective-permute-start(f32[64,128]{1,0:T(8,128)} %reshape.50), channel_id=1, source_target_pairs={{0,3},{1,0},{2,1},{3,2},{4,7},{5,4},{6,5},{7,6},{8,11},{9,8},{10,9... | collective-permute-start | bytes 98312 | tf_op jit(solution)/shard_map/ppermute | solution.py:25
  64.6 0.9 reshape.49
  65.5 2.9 %copy.101 = f32[32,8,16,2]{3,2,1,0:T(8,128)} copy(f32[32,8,16,2]{2,1,3,0:T(8,128)S(1)} %bitcast.57) | data formatting | bytes 65536 | tf_op jit(solution)/shard_map/transpose | solution.py:23
  68.4 0.9 reshape.51
  69.3 2.9 %copy.103 = f32[32,8,16,2]{3,2,1,0:T(8,128)} copy(f32[32,8,16,2]{2,1,3,0:T(8,128)S(1)} %bitcast.58) | data formatting | bytes 65536 | tf_op jit(solution)/shard_map/transpose | solution.py:23
  72.2 1.1 copy.97
  73.3 1.1 copy.99
  74.4 17.4 %multiply_subtract_fusion = f32[32,8,16,128]{3,2,1,0:T(8,128)S(1)} fusion(f32[32,8,16,128]{3,2,1,0:T(8,128)S(1)} %copy-done, f32[32,8,16,128]{3,2,1,0:T(8,128)} %get-tuple-element.13, f32[32,8,16,2]{3,2,1,0:T(8,128)} %copy.103, f32[32,8,16,128]{3,2,1,0:T(8,128)} %copy-done.1, f32[32,8,16,2]{3,2,1,0:T(8,128)} %copy.101, f32[32,8,2,128]{3,2,1,0:T(2,128)S(1)} %copy.99, ...), kind=kLoop, calls=%fused_computation.97 | loop fusion | flops 23068672 | bytes 10092544 | tf_op jit(solution)/shard_map/sub | solution.py:61
  91.7 2.8 %fusion.64 = f32[32,32]{0,1:T(8,128)S(1)} fusion(f32[32,8,16,128]{3,2,1,0:T(8,128)S(1)} %multiply_subtract_fusion), kind=kOutput, calls=%fused_computation.102 | convolution fusion | flops 201327616 | bytes 2101248 | tf_op jit(solution)/shard_map/dot_general | solution.py:65
  94.7 2.6 %collective-permute-done.12 = f32[32,32]{0,1:T(8,128)S(1)} collective-permute-done((f32[32,32]{0,1:T(8,128)S(1)}, f32[32,32]{0,1:T(8,128)S(1)}, u32[]{:S(2)}, u32[]{:S(2)}) %collective-permute-start.12) | collective-permute-done | bytes 4128 | tf_op jit(solution)/shard_map/ppermute | solution.py:53
  97.8 3.6 %collective-permute-done.13 = f32[32,32]{0,1:T(8,128)S(1)} collective-permute-done((f32[32,32]{0,1:T(8,128)S(1)}, f32[32,32]{0,1:T(8,128)S(1)}, u32[]{:S(2)}, u32[]{:S(2)}) %collective-permute-start.13) | collective-permute-done | bytes 4128 | tf_op jit(solution)/shard_map/ppermute | solution.py:53
  101.4 2.6 %collective-permute-done.14 = f32[32,32]{0,1:T(8,128)S(1)} collective-permute-done((f32[32,32]{0,1:T(8,128)S(1)}, f32[32,32]{0,1:T(8,128)S(1)}, u32[]{:S(2)}, u32[]{:S(2)}) %collective-permute-start.14) | collective-permute-done | bytes 4128 | tf_op jit(solution)/shard_map/ppermute | solution.py:53
  104.7 2.8 %collective-permute-done.15 = f32[32,32]{0,1:T(8,128)S(1)} collective-permute-done((f32[32,32]{0,1:T(8,128)S(1)}, f32[32,32]{0,1:T(8,128)S(1)}, u32[]{:S(2)}, u32[]{:S(2)}) %collective-permute-start.15) | collective-permute-done | bytes 4128 | tf_op jit(solution)/shard_map/ppermute | solution.py:53
  107.5 4.3 %collective-permute-start.16 = (f32[32,32]{0,1:T(8,128)S(1)}, f32[32,32]{0,1:T(8,128)S(1)}, u32[]{:S(2)}, u32[]{:S(2)}) collective-permute-start(f32[32,32]{0,1:T(8,128)S(1)} %add.143), channel_id=1, source_target_pairs={{0,16},{4,20},{8,24},{12,28},{16,0},{20,4},{24,8},{28,12},{1,17},{... | collective-permute-start | bytes 12296 | tf_op jit(solution)/shard_map/ppermute | solution.py:53
  111.7 2.2 %collective-permute-done.16 = f32[32,32]{0,1:T(8,128)S(1)} collective-permute-done((f32[32,32]{0,1:T(8,128)S(1)}, f32[32,32]{0,1:T(8,128)S(1)}, u32[]{:S(2)}, u32[]{:S(2)}) %collective-permute-start.16) | collective-permute-done | bytes 4128 | tf_op jit(solution)/shard_map/ppermute | solution.py:53
  114.0 9.8 %collective-permute-start.17 = (f32[32,32]{0,1:T(8,128)S(1)}, f32[32,32]{0,1:T(8,128)S(1)}, u32[]{:S(2)}, u32[]{:S(2)}) collective-permute-start(f32[32,32]{0,1:T(8,128)S(1)} %add.144), channel_id=1, source_target_pairs={{0,32},{32,0},{64,96},{96,64},{128,160},{160,128},{192,224},{224,1... | collective-permute-start | bytes 12296 | tf_op jit(solution)/shard_map/ppermute | solution.py:53
  123.8 0.8 collective-permute-done.17
  124.6 2.6 %collective-permute-done.18 = f32[32,32]{0,1:T(8,128)S(1)} collective-permute-done((f32[32,32]{0,1:T(8,128)S(1)}, f32[32,32]{0,1:T(8,128)S(1)}, u32[]{:S(2)}, u32[]{:S(2)}) %collective-permute-start.18) | collective-permute-done | bytes 4128 | tf_op jit(solution)/shard_map/ppermute | solution.py:53
  127.5 1.2 copy.128
  129.1 2.2 %collective-permute-done.19 = f32[32,32]{0,1:T(8,128)S(1)} collective-permute-done((f32[32,32]{0,1:T(8,128)S(1)}, f32[32,32]{0,1:T(8,128)S(1)}, u32[]{:S(2)}, u32[]{:S(2)}) %collective-permute-start.19) | collective-permute-done | bytes 4128 | tf_op jit(solution)/shard_map/ppermute | solution.py:53
  131.4 2.9 %cholesky.17 = f32[32,32]{1,0:T(8,128)S(1)} custom-call(f32[32,32]{1,0:T(8,128)S(1)} %fusion.68), custom_call_target="Cholesky" | custom-call | tf_op jit(solution)/shard_map/jit(cholesky)/cholesky | solution.py:66
  135.6 2.4 %custom-call.7 = f32[1,32,32]{1,2,0:T(8,128)S(1)} custom-call(f32[1,32,32]{2,1,0:T(8,128)S(1)} %get-tuple-element.30), custom_call_target="InvertDiagBlocksLowerTriangular" | custom-call | tf_op jit(solution)/shard_map/jit(_solve_triangular)/triangular_solve | solution.py:68
  138.3 3.0 %fusion.57 = f32[32,8,16,128]{3,0,2,1:T(8,128)S(1)} fusion(f32[32,32,1,1]{1,0,3,2:T(8,128)S(1)} %convolution_bitcast_fusion, f32[8,16,128,32]{2,1,0,3:T(8,128)S(1)} %bitcast.54), kind=kOutput, calls=%fused_computation.93 | convolution fusion | flops 201326592 | bytes 4198400 | tf_op jit(solution)/shard_map/dot_general | solution.py:69
  141.3 2.5 %copy.109 = f32[32,8,16,128]{3,2,1,0:T(8,128)} copy(f32[32,8,16,128]{3,0,2,1:T(8,128)S(1)} %fusion.57) | data formatting | bytes 4194304
  (60 shorter events, 8.5 us)
Async XLA Ops:
  0.6 5.6 %copy-start = (f32[32,8,16,128]{3,2,1,0:T(8,128)S(1)}, f32[32,8,16,128]{3,2,1,0:T(8,128)}, u32[]{:S(2)}) copy-start(f32[32,8,16,128]{3,2,1,0:T(8,128)} %param.2) | copy-start | bytes 6291460
  3.1 28.6 %collective-permute-start = (f32[32,2,16,128]{3,2,1,0:T(8,128)}, f32[32,2,16,128]{3,2,1,0:T(8,128)}, u32[]{:S(2)}, u32[]{:S(2)}) collective-permute-start(f32[32,2,16,128]{3,2,1,0:T(8,128)} %get-tuple-element.23), channel_id=1, source_target_pairs={{0,32},{32,64},{64,96},{96,128},{128,160},{160,192},{192,224},{224... | collective-permute-start | bytes 1572872 | tf_op jit(solution)/shard_map/ppermute | solution.py:27
  5.6 27.7 %collective-permute-start.1 = (f32[32,2,16,128]{3,2,1,0:T(8,128)}, f32[32,2,16,128]{3,2,1,0:T(8,128)S(1)}, u32[]{:S(2)}, u32[]{:S(2)}) collective-permute-start(f32[32,2,16,128]{3,2,1,0:T(8,128)} %get-tuple-element.24), channel_id=1, source_target_pairs={{0,224},{32,0},{64,32},{96,64},{128,96},{160,128},{192,160},{224,1... | collective-permute-start | bytes 1572872 | tf_op jit(solution)/shard_map/ppermute | solution.py:28
  6.5 24.1 %collective-permute-start.2 = (f32[32,8,2,128]{3,1,2,0:T(8,128)S(1)}, f32[32,8,2,128]{3,1,2,0:T(8,128)}, u32[]{:S(2)}, u32[]{:S(2)}) collective-permute-start(f32[32,8,2,128]{3,1,2,0:T(8,128)S(1)} %copy.114), channel_id=1, source_target_pairs={{0,4},{4,8},{8,12},{12,16},{16,20},{20,24},{24,28},{28,0},{1,5},{5... | collective-permute-start | bytes 786440 | tf_op jit(solution)/shard_map/ppermute | solution.py:27
  13.6 6.9 %collective-permute-start.4 = (f32[64,128]{1,0:T(8,128)S(1)}, f32[64,128]{1,0:T(8,128)S(1)}, u32[]{:S(2)}, u32[]{:S(2)}) collective-permute-start(f32[64,128]{1,0:T(8,128)S(1)} %reshape.44), channel_id=1, source_target_pairs={{0,1},{1,2},{2,3},{3,0},{4,5},{5,6},{6,7},{7,4},{8,9},{9,10},{10,1... | collective-permute-start | bytes 98312 | tf_op jit(solution)/shard_map/ppermute | solution.py:24
  18.3 9.2 %collective-permute-start.5 = (f32[64,128]{1,0:T(8,128)S(1)}, f32[64,128]{1,0:T(8,128)S(1)}, u32[]{:S(2)}, u32[]{:S(2)}) collective-permute-start(f32[64,128]{1,0:T(8,128)S(1)} %reshape.46), channel_id=1, source_target_pairs={{0,3},{1,0},{2,1},{3,2},{4,7},{5,4},{6,5},{7,6},{8,11},{9,8},{10,9... | collective-permute-start | bytes 98312 | tf_op jit(solution)/shard_map/ppermute | solution.py:25
  20.6 12.8 %collective-permute-start.3 = (f32[32,8,2,128]{3,1,2,0:T(8,128)}, f32[32,8,2,128]{3,1,2,0:T(8,128)S(1)}, u32[]{:S(2)}, u32[]{:S(2)}) collective-permute-start(f32[32,8,2,128]{3,1,2,0:T(8,128)} %copy.115), channel_id=1, source_target_pairs={{0,28},{4,0},{8,4},{12,8},{16,12},{20,16},{24,20},{28,24},{1,29},{... | collective-permute-start | bytes 786440 | tf_op jit(solution)/shard_map/ppermute | solution.py:28
  32.8 2.0 %copy-start.3 = (f32[8,16,128]{2,1,0:T(8,128)S(1)}, f32[8,16,128]{2,1,0:T(8,128)}, u32[]{:S(2)}) copy-start(f32[8,16,128]{2,1,0:T(8,128)} %param.3) | copy-start | bytes 196612
  33.3 1.5 %copy-start.2 = (f32[32,10,16,128]{3,2,1,0:T(8,128)}, f32[32,10,16,128]{3,2,1,0:T(8,128)S(1)}, u32[]{:S(2)}) copy-start(f32[32,10,16,128]{3,2,1,0:T(8,128)S(1)} %get-tuple-element.20) | copy-start | bytes 7864324
  43.1 8.1 %copy-start.1 = (f32[32,8,16,128]{3,2,1,0:T(8,128)}, f32[32,8,16,128]{3,2,1,0:T(8,128)S(1)}, u32[]{:S(2)}) copy-start(f32[32,8,16,128]{3,2,1,0:T(8,128)S(1)} %get-tuple-element.12) | copy-start | bytes 6291460
  44.4 29.9 %collective-permute-start.6 = (f32[32,2,16,128]{3,2,1,0:T(8,128)}, f32[32,2,16,128]{3,2,1,0:T(8,128)S(1)}, u32[]{:S(2)}, u32[]{:S(2)}) collective-permute-start(f32[32,2,16,128]{3,2,1,0:T(8,128)} %get-tuple-element.14), channel_id=1, source_target_pairs={{0,32},{32,64},{64,96},{96,128},{128,160},{160,192},{192,224},{224... | collective-permute-start | bytes 1572872 | tf_op jit(solution)/shard_map/ppermute | solution.py:27
  46.9 27.4 %collective-permute-start.7 = (f32[32,2,16,128]{3,2,1,0:T(8,128)}, f32[32,2,16,128]{3,2,1,0:T(8,128)S(1)}, u32[]{:S(2)}, u32[]{:S(2)}) collective-permute-start(f32[32,2,16,128]{3,2,1,0:T(8,128)} %get-tuple-element.15), channel_id=1, source_target_pairs={{0,224},{32,0},{64,32},{96,64},{128,96},{160,128},{192,160},{224,1... | collective-permute-start | bytes 1572872 | tf_op jit(solution)/shard_map/ppermute | solution.py:28
  47.8 24.4 %collective-permute-start.8 = (f32[32,8,2,128]{3,1,2,0:T(8,128)}, f32[32,8,2,128]{3,1,2,0:T(8,128)}, u32[]{:S(2)}, u32[]{:S(2)}) collective-permute-start(f32[32,8,2,128]{3,1,2,0:T(8,128)} %copy.96), channel_id=1, source_target_pairs={{0,4},{4,8},{8,12},{12,16},{16,20},{20,24},{24,28},{28,0},{1,5},{5... | collective-permute-start | bytes 786440 | tf_op jit(solution)/shard_map/ppermute | solution.py:27
  48.5 24.7 %collective-permute-start.9 = (f32[32,8,2,128]{3,1,2,0:T(8,128)}, f32[32,8,2,128]{3,1,2,0:T(8,128)}, u32[]{:S(2)}, u32[]{:S(2)}) collective-permute-start(f32[32,8,2,128]{3,1,2,0:T(8,128)} %copy.98), channel_id=1, source_target_pairs={{0,28},{4,0},{8,4},{12,8},{16,12},{20,16},{24,20},{28,24},{1,29},{... | collective-permute-start | bytes 786440 | tf_op jit(solution)/shard_map/ppermute | solution.py:28
  57.3 4.1 %collective-permute-start.10 = (f32[64,128]{1,0:T(8,128)S(1)}, f32[64,128]{1,0:T(8,128)S(1)}, u32[]{:S(2)}, u32[]{:S(2)}) collective-permute-start(f32[64,128]{1,0:T(8,128)S(1)} %reshape.48), channel_id=1, source_target_pairs={{0,1},{1,2},{2,3},{3,0},{4,5},{5,6},{6,7},{7,4},{8,9},{9,10},{10,1... | collective-permute-start | bytes 98312 | tf_op jit(solution)/shard_map/ppermute | solution.py:24
  61.4 0.6 copy-start.4
  62.0 6.4 %collective-permute-start.11 = (f32[64,128]{1,0:T(8,128)}, f32[64,128]{1,0:T(8,128)}, u32[]{:S(2)}, u32[]{:S(2)}) collective-permute-start(f32[64,128]{1,0:T(8,128)} %reshape.50), channel_id=1, source_target_pairs={{0,3},{1,0},{2,1},{3,2},{4,7},{5,4},{6,5},{7,6},{8,11},{9,8},{10,9... | collective-permute-start | bytes 98312 | tf_op jit(solution)/shard_map/ppermute | solution.py:25
  94.6 2.7 %collective-permute-start.12 = (f32[32,32]{0,1:T(8,128)S(1)}, f32[32,32]{0,1:T(8,128)S(1)}, u32[]{:S(2)}, u32[]{:S(2)}) collective-permute-start(f32[32,32]{0,1:T(8,128)S(1)} %fusion.64), channel_id=1, source_target_pairs={{0,1},{1,0},{2,3},{3,2},{4,5},{5,4},{6,7},{7,6},{8,9},{9,8},{10,11... | collective-permute-start | bytes 12296 | tf_op jit(solution)/shard_map/ppermute | solution.py:53
  97.3 4.1 %collective-permute-start.13 = (f32[32,32]{0,1:T(8,128)S(1)}, f32[32,32]{0,1:T(8,128)S(1)}, u32[]{:S(2)}, u32[]{:S(2)}) collective-permute-start(f32[32,32]{0,1:T(8,128)S(1)} %add.140), channel_id=1, source_target_pairs={{0,2},{1,3},{2,0},{3,1},{4,6},{5,7},{6,4},{7,5},{8,10},{9,11},{10,... | collective-permute-start | bytes 12296 | tf_op jit(solution)/shard_map/ppermute | solution.py:53
  101.4 2.6 %collective-permute-start.14 = (f32[32,32]{0,1:T(8,128)S(1)}, f32[32,32]{0,1:T(8,128)S(1)}, u32[]{:S(2)}, u32[]{:S(2)}) collective-permute-start(f32[32,32]{0,1:T(8,128)S(1)} %add.141), channel_id=1, source_target_pairs={{0,4},{4,0},{8,12},{12,8},{16,20},{20,16},{24,28},{28,24},{1,5},{5... | collective-permute-start | bytes 12296 | tf_op jit(solution)/shard_map/ppermute | solution.py:53
  104.0 3.5 %collective-permute-start.15 = (f32[32,32]{0,1:T(8,128)S(1)}, f32[32,32]{0,1:T(8,128)S(1)}, u32[]{:S(2)}, u32[]{:S(2)}) collective-permute-start(f32[32,32]{0,1:T(8,128)S(1)} %add.142), channel_id=1, source_target_pairs={{0,8},{4,12},{8,0},{12,4},{16,24},{20,28},{24,16},{28,20},{1,9},{5... | collective-permute-start | bytes 12296 | tf_op jit(solution)/shard_map/ppermute | solution.py:53
  107.5 6.5 %collective-permute-start.16 = (f32[32,32]{0,1:T(8,128)S(1)}, f32[32,32]{0,1:T(8,128)S(1)}, u32[]{:S(2)}, u32[]{:S(2)}) collective-permute-start(f32[32,32]{0,1:T(8,128)S(1)} %add.143), channel_id=1, source_target_pairs={{0,16},{4,20},{8,24},{12,28},{16,0},{20,4},{24,8},{28,12},{1,17},{... | collective-permute-start | bytes 12296 | tf_op jit(solution)/shard_map/ppermute | solution.py:53
  114.0 10.6 %collective-permute-start.17 = (f32[32,32]{0,1:T(8,128)S(1)}, f32[32,32]{0,1:T(8,128)S(1)}, u32[]{:S(2)}, u32[]{:S(2)}) collective-permute-start(f32[32,32]{0,1:T(8,128)S(1)} %add.144), channel_id=1, source_target_pairs={{0,32},{32,0},{64,96},{96,64},{128,160},{160,128},{192,224},{224,1... | collective-permute-start | bytes 12296 | tf_op jit(solution)/shard_map/ppermute | solution.py:53
  124.6 2.6 %collective-permute-start.18 = (f32[32,32]{0,1:T(8,128)S(1)}, f32[32,32]{0,1:T(8,128)S(1)}, u32[]{:S(2)}, u32[]{:S(2)}) collective-permute-start(f32[32,32]{0,1:T(8,128)S(1)} %add.145), channel_id=1, source_target_pairs={{0,64},{32,96},{64,0},{96,32},{128,192},{160,224},{192,128},{224,1... | collective-permute-start | bytes 12296 | tf_op jit(solution)/shard_map/ppermute | solution.py:53
  127.2 4.1 %collective-permute-start.19 = (f32[32,32]{0,1:T(8,128)S(1)}, f32[32,32]{0,1:T(8,128)S(1)}, u32[]{:S(2)}, u32[]{:S(2)}) collective-permute-start(f32[32,32]{0,1:T(8,128)S(1)} %add.146), channel_id=1, source_target_pairs={{0,128},{32,160},{64,192},{96,224},{128,0},{160,32},{192,64},{224,... | collective-permute-start | bytes 12296 | tf_op jit(solution)/shard_map/ppermute | solution.py:53

commit v2 on v1

v2 whole, which is shorter than its diff:
```python
import functools

import jax
import jax.numpy as jnp
from jax import lax
from jax.experimental import pallas as pl
from jax.experimental.pallas import tpu as pltpu
from jax.sharding import PartitionSpec as P

TAPS = (-1.0 / 12.0, 4.0 / 3.0, -2.5, 4.0 / 3.0, -1.0 / 12.0)
BLOCK = 4
INTERPRET = False
HI = lax.Precision.HIGHEST


def shift_pairs(n, step):
    return [(i, (i + step) % n) for i in range(n)]


def face_selector(rows, lanes):
    r = lax.broadcasted_iota(jnp.int32, (rows, lanes), 0)
    l = lax.broadcasted_iota(jnp.int32, (rows, lanes), 1)
    pick = ((r < 2) & (l == r)) | ((r >= 2) & (r < 4) & (l == r + lanes - 4))
    return jnp.where(pick, 1.0, 0.0).astype(jnp.float32)


def placer(rows, lanes, low_side):
    r = lax.broadcasted_iota(jnp.int32, (rows, lanes), 0)
    l = lax.broadcasted_iota(jnp.int32, (rows, lanes), 1)
    if low_side:
        pick = ((r == 2) & (l == 0)) | ((r == 3) & (l == 1))
    else:
        pick = ((r == 0) & (l == lanes - 2)) | ((r == 1) & (l == lanes - 1))
    return jnp.where(pick, 1.0, 0.0).astype(jnp.float32)


def faces_of(plane, selector):
    return lax.dot_general(selector, plane, (((1,), (1,)), ((), ())), precision=HI,
                           preferred_element_type=jnp.float32)


def stage_kernel(*refs, last):
    if last:
        (f_ref, xlo_ref, xhi_ref, ylo_ref, yhi_ref, zlo_ref, zhi_ref, pot_ref, orb_ref,
         out_ref) = refs
    else:
        (f_ref, xlo_ref, xhi_ref, ylo_ref, yhi_ref, zlo_ref, zhi_ref, pot_ref,
         out_ref, face_ref) = refs
    nb, cx, cy, cz = f_ref.shape
    rows = cx * cy
    frows = zlo_ref.shape[1]
    t_lo = placer(frows, cz, True)
    t_hi = placer(frows, cz, False)
    sel = face_selector(frows, cz)
    lane = lax.broadcasted_iota(jnp.int32, (rows, cz), 1)
    yid = lax.broadcasted_iota(jnp.int32, (cx, cy, cz), 1)
    pot = pot_ref[...]
    tn = (((0,), (0,)), ((), ()))
    for b in range(nb):
        f3 = f_ref[b]
        summed = 3.0 * TAPS[2] * f3
        ext = jnp.concatenate([xlo_ref[b], f3, xhi_ref[b]], axis=0)
        for offset, weight in ((-2, TAPS[0]), (-1, TAPS[1]), (1, TAPS[3]), (2, TAPS[4])):
            summed = summed + weight * ext[2 + offset: 2 + offset + cx]
        ylo = ylo_ref[b]
        yhi = yhi_ref[b]
        ym2 = jnp.where(yid == 0, ylo[:, 0:1, :], jnp.where(yid == 1, ylo[:, 1:2, :], pltpu.roll(f3, 2, 1)))
        ym1 = jnp.where(yid == 0, ylo[:, 1:2, :], pltpu.roll(f3, 1, 1))
        yp1 = jnp.where(yid == cy - 1, yhi[:, 0:1, :], pltpu.roll(f3, cy - 1, 1))
        yp2 = jnp.where(yid == cy - 2, yhi[:, 0:1, :], jnp.where(yid == cy - 1, yhi[:, 1:2, :], pltpu.roll(f3, cy - 2, 1)))
        for shifted, weight in ((ym2, TAPS[0]), (ym1, TAPS[1]), (yp1, TAPS[3]), (yp2, TAPS[4])):
            summed = summed + weight * shifted
        f2 = f3.reshape(rows, cz)
        zl = lax.dot_general(zlo_ref[b], t_lo, tn, precision=HI, preferred_element_type=jnp.float32)
        zh = lax.dot_general(zhi_ref[b], t_hi, tn, precision=HI, preferred_element_type=jnp.float32)
        zm2 = jnp.where(lane < 2, zl, pltpu.roll(f2, 2, 1))
        zm1 = jnp.where(lane < 1, pltpu.roll(zl, cz - 1, 1), pltpu.roll(f2, 1, 1))
        zp1 = jnp.where(lane >= cz - 1, pltpu.roll(zh, 1, 1), pltpu.roll(f2, cz - 1, 1))
        zp2 = jnp.where(lane >= cz - 2, zh, pltpu.roll(f2, cz - 2, 1))
        summed = summed.reshape(rows, cz)
        for shifted, weight in ((zm2, TAPS[0]), (zm1, TAPS[1]), (zp1, TAPS[3]), (zp2, TAPS[4])):
            summed = summed + weight * shifted
        pot2 = pot.reshape(rows, cz)
        h = -0.5 * summed + pot2 * f2
        if last:
            res = 2.0 * (h - 5.5 * f2) / 3.5 - orb_ref[b].reshape(rows, cz)
        else:
            res = (h - 5.5 * f2) / 3.5
            face_ref[b] = faces_of(res, sel)
        out_ref[b] = res.reshape(cx, cy, cz)


def z_face_kernel(f_ref, face_ref):
    nb, cx, cy, cz = f_ref.shape
    sel = face_selector(face_ref.shape[1], cz)
    for b in range(nb):
        face_ref[b] = faces_of(f_ref[b].reshape(cx * cy, cz), sel)


def z_faces(f):
    norb, cx, cy, cz = f.shape
    blk = pl.BlockSpec((BLOCK, cx, cy, cz), lambda i: (i, 0, 0, 0))
    fblk = pl.BlockSpec((BLOCK, 8, cx * cy), lambda i: (i, 0, 0))
    return pl.pallas_call(
        z_face_kernel, grid=(norb // BLOCK,), in_specs=[blk], out_specs=fblk,
        out_shape=jax.ShapeDtypeStruct((norb, 8, cx * cy), jnp.float32), interpret=INTERPRET,
    )(f)


def exchange(f, zface):
    out = []
    for axis, dim in (("gx", 1), ("gy", 2)):
        n, length = lax.axis_size(axis), f.shape[dim]
        last = lax.slice_in_dim(f, length - 2, length, axis=dim)
        first = lax.slice_in_dim(f, 0, 2, axis=dim)
        out.append(lax.ppermute(last, axis, shift_pairs(n, 1)))
        out.append(lax.ppermute(first, axis, shift_pairs(n, -1)))
    n = lax.axis_size("gz")
    out.append(lax.ppermute(zface, "gz", shift_pairs(n, 1)))
    out.append(lax.ppermute(zface, "gz", shift_pairs(n, -1)))
    return out


def stage(f, rims, potential, orbitals=None):
    norb, cx, cy, cz = f.shape
    last = orbitals is not None
    blk = pl.BlockSpec((BLOCK, cx, cy, cz), lambda i: (i, 0, 0, 0))
    xblk = pl.BlockSpec((BLOCK, 2, cy, cz), lambda i: (i, 0, 0, 0))
    yblk = pl.BlockSpec((BLOCK, cx, 2, cz), lambda i: (i, 0, 0, 0))
    fblk = pl.BlockSpec((BLOCK, 8, cx * cy), lambda i: (i, 0, 0))
    pblk = pl.BlockSpec((cx, cy, cz), lambda i: (0, 0, 0))
    in_specs = [blk, xblk, xblk, yblk, yblk, fblk, fblk, pblk]
    args = [f, *rims, potential]
    if last:
        in_specs.append(blk)
        args.append(orbitals)
        out_specs = blk
        out_shape = jax.ShapeDtypeStruct(f.shape, jnp.float32)
    else:
        out_specs = (blk, fblk)
        out_shape = (jax.ShapeDtypeStruct(f.shape, jnp.float32),
                     jax.ShapeDtypeStruct((norb, 8, cx * cy), jnp.float32))
    return pl.pallas_call(
        functools.partial(stage_kernel, last=last), grid=(norb // BLOCK,), in_specs=in_specs,
        out_specs=out_specs, out_shape=out_shape, interpret=INTERPRET,
        compiler_params=pltpu.CompilerParams(dimension_semantics=("arbitrary",)),
    )(*args)


def butterfly_sum(c):
    for axis in ("gz", "gy", "gx"):
        n = lax.axis_size(axis)
        d = 1
        while d < n:
            c = c + lax.ppermute(c, axis, [(i, i ^ d) for i in range(n)])
            d *= 2
    return c


def per_device(orbitals, potential):
    first, first_z = stage(orbitals, exchange(orbitals, z_faces(orbitals)), potential)
    second = stage(first, exchange(first, first_z), potential, orbitals)
    norb_count = orbitals.shape[0]
    filtered = second.reshape(norb_count, -1)
    all_cells = filtered.shape[1] * lax.axis_size("gx") * lax.axis_size("gy") * lax.axis_size("gz")
    correlation = jnp.dot(filtered, filtered.T, precision=HI) / all_cells
    lower = jnp.linalg.cholesky(butterfly_sum(correlation))
    eye = jnp.eye(norb_count, dtype=lower.dtype)
    inverse = jax.scipy.linalg.solve_triangular(lower, eye, lower=True)
    basis = jnp.dot(inverse, filtered, precision=HI)
    return (basis.reshape(orbitals.shape), lower.T)


def solution(mesh):
    in_specs = (P(None, "gx", "gy", "gz"), P("gx", "gy", "gz"))
    out_specs = (P(None, "gx", "gy", "gz"), P())
    return jax.shard_map(
        per_device, mesh=mesh, in_specs=in_specs, out_specs=out_specs, check_vma=False
    )
```

time: 145 us -> 127 us (0.88)
  local copies, waits for them, and re-layouts: 50.9 us -> 11.5 us
  Pallas kernels: 0 us -> 32.9 us
  other arithmetic: 32.4 us -> 6.72 us
  waiting for transfers between devices: 19.4 us -> 33.5 us
  starting transfers between devices: 34.9 us -> 30.8 us
  matrix products: 6.07 us -> 9.57 us
    pallas_call x0 -> x3, Pallas kernels: none -> 32.9 us  [the longest x2 25.5 us: stage(): pl.pallas_call(functools.partial(stage_kernel, last=last), grid=(norb //...]
    transpose x10 -> x0, local copies, waits for them, and re-layouts: 29.7 us -> none  [the longest x6 18.1 us: halos(): pack = lambda a: jnp.transpose(a, (0, 3, 1, 2)).reshape(shape[0] * 2, -1)]
    sub x1 -> x0, other arithmetic: 17.4 us -> none  [per_device(): 2.0 * (hamiltonian(first, potential_cube) - 5.5 * first) / 3.5 - orbitals]
    ppermute x12, waiting for transfers between devices: 0.03 us -> 13.3 us  [the longest x2 9.34 us: exchange(): out.append(lax.ppermute(zface, 'gz', shift_pairs(n, 1)))]
    div x1 -> x0, other arithmetic: 8.26 us -> none  [per_device(): first = (hamiltonian(orbitals, potential_cube) - 5.5 * orbitals) / 3.5]
    dot_general x2, matrix products: 5.85 us -> 9.35 us  [the longest x1 6.34 us: per_device(): correlation = jnp.dot(filtered, filtered.T, precision=HI) / all_cells]
    ppermute x3 -> x0, local copies, waits for them, and re-layouts: 3.26 us -> none  [the longest x2 2.17 us: halos(): before = lax.ppermute(last, axis, shift_pairs(n, 1))]
    reshape x8 -> x0, local copies, waits for them, and re-layouts: 3.22 us -> none  [the longest x4 2 us: halos(): a.reshape(shape[0], 2, shape[1], shape[2])]
  transfers between devices with their start and end apart: 20 -> 20, of which waited for: 8 -> 12; matrix products, arithmetic and copies ran while one was open for 29% -> 4% of each run, Pallas kernels for 0% -> 0%
where the time goes in v2:
time: 127 us; the launch traced here: 126 us
  waiting for transfers between devices  33.5 us (26%)
  Pallas kernels  32.9 us (26%)
  starting transfers between devices  30.8 us (24%)
  local copies, waits for them, and re-layouts  11.5 us (9%)
  matrix products  9.57 us (8%)
  other arithmetic  6.72 us (5%)
    pallas_call x2, Pallas kernels, stage(): pl.pallas_call(functools.partial(stage_kernel, last=last), grid=(norb //...  25.5 us
    ppermute x8, waiting for transfers between devices, butterfly_sum(): c = c + lax.ppermute(c, axis, [(i, i ^ d) for i in range(n)])  20.2 us
    ppermute x8, starting transfers between devices, butterfly_sum(): c = c + lax.ppermute(c, axis, [(i, i ^ d) for i in range(n)])  12.7 us
    ppermute x2, waiting for transfers between devices, exchange(): out.append(lax.ppermute(zface, 'gz', shift_pairs(n, 1)))  9.34 us
    ppermute x4, starting transfers between devices, exchange(): out.append(lax.ppermute(first, axis, shift_pairs(n, -1)))  8.93 us
    unnamed x36, local copies, waits for them, and re-layouts  8.15 us
    pallas_call x1, Pallas kernels, z_faces(): pl.pallas_call(z_face_kernel, grid=(norb // BLOCK,), in_specs=[blk], out_...  7.32 us
    dot_general x1, matrix products, per_device(): correlation = jnp.dot(filtered, filtered.T, precision=HI) / all_cells  6.34 us
  transfers between devices with their start and end apart: 20, of which 12 were waited for; matrix products, arithmetic and copies ran while one was open for 4% of the time, Pallas kernels for 0%

profile of v2, /device:TPU:1, one launch (start us, length us, event | category | flops | bytes accessed | tf_op | source)
XLA Modules:
  0.0 125.8 jit_solution(8659836538589405645)
XLA Ops:
  0.6 7.3 %shard_map.41 = f32[32,8,128]{2,1,0:T(8,128)} custom-call(f32[32,8,16,128]{3,2,1,0:T(8,128)} %refs_8_.1), custom_call_target="tpu_custom_call" | custom-call | tf_op jit(solution)/shard_map/pallas_call | solution.py:104
  8.0 3.6 %collective-permute-start.5 = (f32[32,8,128]{2,1,0:T(8,128)}, f32[32,8,128]{2,1,0:T(8,128)S(1)}, u32[]{:S(2)}, u32[]{:S(2)}) collective-permute-start(f32[32,8,128]{2,1,0:T(8,128)} %shard_map.41), channel_id=1, source_target_pairs={{0,3},{1,0},{2,1},{3,2},{4,7},{5,4},{6,5},{7,6},{8,11},{9,8},{10,9... | collective-permute-start | bytes 393224 | tf_op jit(solution)/shard_map/ppermute | solution.py:120
  11.6 1.0 collective-permute-start.1
  12.6 1.1 collective-permute-start
  13.7 0.2 fusion.15
  13.9 5.7 %collective-permute-start.3 = (f32[32,8,2,128]{3,2,1,0:T(2,128)S(1)}, f32[32,8,2,128]{3,2,1,0:T(2,128)S(1)}, u32[]{:S(2)}, u32[]{:S(2)}) collective-permute-start(f32[32,8,2,128]{3,2,1,0:T(2,128)S(1)} %get-tuple-element.14), channel_id=1, source_target_pairs={{0,28},{4,0},{8,4},{12,8},{16,12},{20,16},{24,20},{28,24},{1,29},{... | collective-permute-start | bytes 786440 | tf_op jit(solution)/shard_map/ppermute | solution.py:117
  19.6 5.0 %collective-permute-done.4.refs_5_ = f32[32,8,128]{2,1,0:T(8,128)S(1)} collective-permute-done((f32[32,8,128]{2,1,0:T(8,128)S(1)}, f32[32,8,128]{2,1,0:T(8,128)S(1)}, u32[]{:S(2)}, u32[]{:S(2)}) %collective-permute-start.4) | collective-permute-done | bytes 131104 | tf_op jit(solution)/shard_map/ppermute | solution.py:119
  24.7 2.9 %collective-permute-done.2.refs_3_ = f32[32,8,2,128]{3,2,1,0:T(2,128)S(1)} collective-permute-done((f32[32,8,2,128]{3,2,1,0:T(2,128)S(1)}, f32[32,8,2,128]{3,2,1,0:T(2,128)S(1)}, u32[]{:S(2)}, u32[]{:S(2)}) %collective-permute-start.2) | collective-permute-done | bytes 262176 | tf_op jit(solution)/shard_map/ppermute | solution.py:116
  27.6 0.7 copy-done.9
  28.2 0.2 copy-done.2
  28.4 0.8 copy-done.4
  29.2 15.5 %shard_map.42 = (f32[32,8,16,128]{3,2,1,0:T(8,128)}, f32[32,8,128]{2,1,0:T(8,128)}) custom-call(f32[32,8,16,128]{3,2,1,0:T(8,128)} %refs_8_.1, f32[32,2,16,128]{3,2,1,0:T(8,128)} %copy-done.4, f32[32,2,16,128]{3,2,1,0:T(8,128)} %copy-done.2, f32[32,8,2,128]{3,2,1,0:T(2,128)} %copy-done.9, f32[32,8,2,128]{3,2,1,0:T(2,128)} %copy-done.8, ...), custom_call_target="tpu_custom_call" | custom-call | tf_op jit(solution)/shard_map/pallas_call | solution.py:143
  44.7 0.5 collective-permute-start.11
  45.3 1.3 %fusion.14 = (f32[32,2,16,128]{3,2,1,0:T(8,128)S(1)}, f32[32,2,16,128]{3,2,1,0:T(8,128)S(1)}) fusion(f32[32,8,16,128]{3,2,1,0:T(8,128)} %get-tuple-element.4.refs_0_), kind=kLoop, calls=%fused_computation.19 | loop fusion | bytes 2097152 | tf_op jit(solution)/shard_map/slice | solution.py:115
  46.5 2.2 %collective-permute-start.7 = (f32[32,2,16,128]{3,2,1,0:T(8,128)S(1)}, f32[32,2,16,128]{3,2,1,0:T(8,128)S(1)}, u32[]{:S(2)}, u32[]{:S(2)}) collective-permute-start(f32[32,2,16,128]{3,2,1,0:T(8,128)S(1)} %get-tuple-element.12), channel_id=1, source_target_pairs={{0,224},{32,0},{64,32},{96,64},{128,96},{160,128},{192,160},{224,1... | collective-permute-start | bytes 1572872 | tf_op jit(solution)/shard_map/ppermute | solution.py:117
  48.8 1.1 collective-permute-start.6
  49.9 1.8 %fusion.13 = (f32[32,8,2,128]{3,2,1,0:T(2,128)S(1)}, f32[32,8,2,128]{3,2,1,0:T(2,128)S(1)}) fusion(f32[32,8,16,128]{3,2,1,0:T(8,128)} %get-tuple-element.4.refs_0_), kind=kLoop, calls=%fused_computation.18 | loop fusion | bytes 1048576 | tf_op jit(solution)/shard_map/slice | solution.py:115
  51.7 1.5 %collective-permute-start.8 = (f32[32,8,2,128]{3,2,1,0:T(2,128)S(1)}, f32[32,8,2,128]{3,2,1,0:T(2,128)S(1)}, u32[]{:S(2)}, u32[]{:S(2)}) collective-permute-start(f32[32,8,2,128]{3,2,1,0:T(2,128)S(1)} %get-tuple-element.11), channel_id=1, source_target_pairs={{0,4},{4,8},{8,12},{12,16},{16,20},{20,24},{24,28},{28,0},{1,5},{5... | collective-permute-start | bytes 786440 | tf_op jit(solution)/shard_map/ppermute | solution.py:116
  53.2 1.3 collective-permute-start.10
  54.5 4.3 %collective-permute-done.10.refs_5_ = f32[32,8,128]{2,1,0:T(8,128)S(1)} collective-permute-done((f32[32,8,128]{2,1,0:T(8,128)S(1)}, f32[32,8,128]{2,1,0:T(8,128)S(1)}, u32[]{:S(2)}, u32[]{:S(2)}) %collective-permute-start.10) | collective-permute-done | bytes 131104 | tf_op jit(solution)/shard_map/ppermute | solution.py:119
  58.8 1.1 collective-permute-done.8.refs_3_
  59.9 0.7 copy-done.7
  60.6 0.2 copy-done.3
  60.8 0.8 copy-done.5
  61.6 10.1 %shard_map.43 = f32[32,8,16,128]{3,2,1,0:T(8,128)} custom-call(f32[32,8,16,128]{3,2,1,0:T(8,128)} %get-tuple-element.4.refs_0_, f32[32,2,16,128]{3,2,1,0:T(8,128)} %copy-done.5, f32[32,2,16,128]{3,2,1,0:T(8,128)} %copy-done.3, f32[32,8,2,128]{3,2,1,0:T(2,128)} %copy-done.7, f32[32,8,2,128]{3,2,1,0:T(2,128)} %copy-done.6, f32[32,8,128]{2,1,0:T(8,128)} %copy-done.11, ...), custom_call_target="tpu_custom_call" | custom-call | tf_op jit(solution)/shard_map/pallas_call | solution.py:143
  71.6 6.3 %fusion.7 = f32[32,32]{0,1:T(8,128)S(1)} fusion(f32[32,8,16,128]{3,2,1,0:T(8,128)} %shard_map.43), kind=kOutput, calls=%fused_computation.7 | convolution fusion | flops 201327616 | bytes 2101248 | tf_op jit(solution)/shard_map/dot_general | solution.py:166
  78.0 0.6 collective-permute-start.12
  78.6 2.0 %collective-permute-done.12 = f32[32,32]{0,1:T(8,128)S(1)} collective-permute-done((f32[32,32]{0,1:T(8,128)S(1)}, f32[32,32]{0,1:T(8,128)S(1)}, u32[]{:S(2)}, u32[]{:S(2)}) %collective-permute-start.12) | collective-permute-done | bytes 4128 | tf_op jit(solution)/shard_map/ppermute | solution.py:155
  80.7 4.1 %collective-permute-done.13 = f32[32,32]{0,1:T(8,128)S(1)} collective-permute-done((f32[32,32]{0,1:T(8,128)S(1)}, f32[32,32]{0,1:T(8,128)S(1)}, u32[]{:S(2)}, u32[]{:S(2)}) %collective-permute-start.13) | collective-permute-done | bytes 4128 | tf_op jit(solution)/shard_map/ppermute | solution.py:155
  84.8 2.9 %collective-permute-done.14 = f32[32,32]{0,1:T(8,128)S(1)} collective-permute-done((f32[32,32]{0,1:T(8,128)S(1)}, f32[32,32]{0,1:T(8,128)S(1)}, u32[]{:S(2)}, u32[]{:S(2)}) %collective-permute-start.14) | collective-permute-done | bytes 4128 | tf_op jit(solution)/shard_map/ppermute | solution.py:155
  87.7 3.5 %collective-permute-done.15 = f32[32,32]{0,1:T(8,128)S(1)} collective-permute-done((f32[32,32]{0,1:T(8,128)S(1)}, f32[32,32]{0,1:T(8,128)S(1)}, u32[]{:S(2)}, u32[]{:S(2)}) %collective-permute-start.15) | collective-permute-done | bytes 4128 | tf_op jit(solution)/shard_map/ppermute | solution.py:155
  91.1 1.1 collective-permute-start.16
  92.3 5.4 %collective-permute-done.16 = f32[32,32]{0,1:T(8,128)S(1)} collective-permute-done((f32[32,32]{0,1:T(8,128)S(1)}, f32[32,32]{0,1:T(8,128)S(1)}, u32[]{:S(2)}, u32[]{:S(2)}) %collective-permute-start.16) | collective-permute-done | bytes 4128 | tf_op jit(solution)/shard_map/ppermute | solution.py:155
  97.7 7.3 %collective-permute-start.17 = (f32[32,32]{0,1:T(8,128)S(1)}, f32[32,32]{0,1:T(8,128)S(1)}, u32[]{:S(2)}, u32[]{:S(2)}) collective-permute-start(f32[32,32]{0,1:T(8,128)S(1)} %add.40), channel_id=1, source_target_pairs={{0,32},{32,0},{64,96},{96,64},{128,160},{160,128},{192,224},{224,1... | collective-permute-start | bytes 12296 | tf_op jit(solution)/shard_map/ppermute | solution.py:155
  105.0 0.8 collective-permute-done.17
  105.9 1.2 collective-permute-start.18
  107.1 1.4 %collective-permute-done.18 = f32[32,32]{0,1:T(8,128)S(1)} collective-permute-done((f32[32,32]{0,1:T(8,128)S(1)}, f32[32,32]{0,1:T(8,128)S(1)}, u32[]{:S(2)}, u32[]{:S(2)}) %collective-permute-start.18) | collective-permute-done | bytes 4128 | tf_op jit(solution)/shard_map/ppermute | solution.py:155
  108.5 2.4 %collective-permute-start.19 = (f32[32,32]{0,1:T(8,128)S(1)}, f32[32,32]{0,1:T(8,128)S(1)}, u32[]{:S(2)}, u32[]{:S(2)}) collective-permute-start(f32[32,32]{0,1:T(8,128)S(1)} %add.42), channel_id=1, source_target_pairs={{0,128},{32,160},{64,192},{96,224},{128,0},{160,32},{192,64},{224,... | collective-permute-start | bytes 12296 | tf_op jit(solution)/shard_map/ppermute | solution.py:155
  110.8 1.2 copy.31
  112.1 0.4 copy.21
  112.6 2.9 %cholesky.17 = f32[32,32]{1,0:T(8,128)S(1)} custom-call(f32[32,32]{1,0:T(8,128)S(1)} %fusion.11), custom_call_target="Cholesky" | custom-call | tf_op jit(solution)/shard_map/jit(cholesky)/cholesky | solution.py:167
  115.6 0.6 compare_reduce_fusion
  116.2 0.7 fusion.12
  116.9 0.7 copy.16
  117.6 2.4 %custom-call.7 = f32[1,32,32]{1,2,0:T(8,128)S(1)} custom-call(f32[1,32,32]{2,1,0:T(8,128)S(1)} %get-tuple-element.19), custom_call_target="InvertDiagBlocksLowerTriangular" | custom-call | tf_op jit(solution)/shard_map/jit(_solve_triangular)/triangular_solve | solution.py:169
  120.0 0.2 convolution_bitcast_fusion
  120.2 3.0 %fusion = f32[32,8,16,128]{3,0,2,1:T(8,128)S(1)} fusion(f32[32,32,1,1]{1,0,3,2:T(8,128)S(1)} %convolution_bitcast_fusion, f32[8,16,128,32]{2,1,0,3:T(8,128)S(1)} %bitcast.34), kind=kOutput, calls=%fused_computation.1 | convolution fusion | flops 201326592 | bytes 4198400 | tf_op jit(solution)/shard_map/dot_general | solution.py:170
  123.3 2.5 %copy.15 = f32[32,8,16,128]{3,2,1,0:T(8,128)} copy(f32[32,8,16,128]{3,0,2,1:T(8,128)S(1)} %fusion) | data formatting | bytes 4194304
  (53 shorter events, 0.6 us)
Async XLA Ops:
  0.6 10.9 %copy-start = (f32[32,8,16,128]{3,2,1,0:T(8,128)S(1)}, f32[32,8,16,128]{3,2,1,0:T(8,128)}, u32[]{:S(2)}) copy-start(f32[32,8,16,128]{3,2,1,0:T(8,128)} %refs_8_.1) | copy-start | bytes 6291460
  8.0 11.6 %copy-start.13 = (f32[32,8,128]{2,1,0:T(8,128)S(1)}, f32[32,8,128]{2,1,0:T(8,128)}, u32[]{:S(2)}) copy-start(f32[32,8,128]{2,1,0:T(8,128)} %shard_map.41) | copy-start | bytes 393220
  8.0 11.6 %collective-permute-start.5 = (f32[32,8,128]{2,1,0:T(8,128)}, f32[32,8,128]{2,1,0:T(8,128)S(1)}, u32[]{:S(2)}, u32[]{:S(2)}) collective-permute-start(f32[32,8,128]{2,1,0:T(8,128)} %shard_map.41), channel_id=1, source_target_pairs={{0,3},{1,0},{2,1},{3,2},{4,7},{5,4},{6,5},{7,6},{8,11},{9,8},{10,9... | collective-permute-start | bytes 393224 | tf_op jit(solution)/shard_map/ppermute | solution.py:120
  11.6 15.9 %collective-permute-start.1 = (f32[32,2,16,128]{3,2,1,0:T(8,128)S(1)}, f32[32,2,16,128]{3,2,1,0:T(8,128)S(1)}, u32[]{:S(2)}, u32[]{:S(2)}) collective-permute-start(f32[32,2,16,128]{3,2,1,0:T(8,128)S(1)} %get-tuple-element.16), channel_id=1, source_target_pairs={{0,224},{32,0},{64,32},{96,64},{128,96},{160,128},{192,160},{224,1... | collective-permute-start | bytes 1572872 | tf_op jit(solution)/shard_map/ppermute | solution.py:117
  12.6 15.0 %collective-permute-start = (f32[32,2,16,128]{3,2,1,0:T(8,128)S(1)}, f32[32,2,16,128]{3,2,1,0:T(8,128)S(1)}, u32[]{:S(2)}, u32[]{:S(2)}) collective-permute-start(f32[32,2,16,128]{3,2,1,0:T(8,128)S(1)} %get-tuple-element.17), channel_id=1, source_target_pairs={{0,32},{32,64},{64,96},{96,128},{128,160},{160,192},{192,224},{224... | collective-permute-start | bytes 1572872 | tf_op jit(solution)/shard_map/ppermute | solution.py:116
  13.9 10.8 %collective-permute-start.3 = (f32[32,8,2,128]{3,2,1,0:T(2,128)S(1)}, f32[32,8,2,128]{3,2,1,0:T(2,128)S(1)}, u32[]{:S(2)}, u32[]{:S(2)}) collective-permute-start(f32[32,8,2,128]{3,2,1,0:T(2,128)S(1)} %get-tuple-element.14), channel_id=1, source_target_pairs={{0,28},{4,0},{8,4},{12,8},{16,12},{20,16},{24,20},{28,24},{1,29},{... | collective-permute-start | bytes 786440 | tf_op jit(solution)/shard_map/ppermute | solution.py:117
  19.5 8.0 %collective-permute-start.2 = (f32[32,8,2,128]{3,2,1,0:T(2,128)S(1)}, f32[32,8,2,128]{3,2,1,0:T(2,128)S(1)}, u32[]{:S(2)}, u32[]{:S(2)}) collective-permute-start(f32[32,8,2,128]{3,2,1,0:T(2,128)S(1)} %get-tuple-element.15), channel_id=1, source_target_pairs={{0,4},{4,8},{8,12},{12,16},{16,20},{20,24},{24,28},{28,0},{1,5},{5... | collective-permute-start | bytes 786440 | tf_op jit(solution)/shard_map/ppermute | solution.py:116
  19.5 8.0 %copy-start.12 = (f32[32,8,128]{2,1,0:T(8,128)}, f32[32,8,128]{2,1,0:T(8,128)S(1)}, u32[]{:S(2)}) copy-start(f32[32,8,128]{2,1,0:T(8,128)S(1)} %collective-permute-done.5.refs_6_) | copy-start | bytes 393220
  19.6 5.1 %collective-permute-start.4 = (f32[32,8,128]{2,1,0:T(8,128)S(1)}, f32[32,8,128]{2,1,0:T(8,128)S(1)}, u32[]{:S(2)}, u32[]{:S(2)}) collective-permute-start(f32[32,8,128]{2,1,0:T(8,128)S(1)} %copy-done.13), channel_id=1, source_target_pairs={{0,1},{1,2},{2,3},{3,0},{4,5},{5,6},{6,7},{7,4},{8,9},{9,10},{10,1... | collective-permute-start | bytes 393224 | tf_op jit(solution)/shard_map/ppermute | solution.py:119
  24.7 2.9 %copy-start.14 = (f32[32,8,128]{2,1,0:T(8,128)}, f32[32,8,128]{2,1,0:T(8,128)S(1)}, u32[]{:S(2)}) copy-start(f32[32,8,128]{2,1,0:T(8,128)S(1)} %collective-permute-done.4.refs_5_) | copy-start | bytes 393220
  24.7 2.9 %copy-start.8 = (f32[32,8,2,128]{3,2,1,0:T(2,128)}, f32[32,8,2,128]{3,2,1,0:T(2,128)S(1)}, u32[]{:S(2)}) copy-start(f32[32,8,2,128]{3,2,1,0:T(2,128)S(1)} %collective-permute-done.3.refs_4_) | copy-start | bytes 786436
  27.5 0.7 copy-start.9
  27.5 0.9 copy-start.2
  28.4 0.8 copy-start.4
  44.7 8.5 %copy-start.15 = (f32[32,8,128]{2,1,0:T(8,128)S(1)}, f32[32,8,128]{2,1,0:T(8,128)}, u32[]{:S(2)}) copy-start(f32[32,8,128]{2,1,0:T(8,128)} %get-tuple-element.5) | copy-start | bytes 393220
  44.7 8.5 %collective-permute-start.11 = (f32[32,8,128]{2,1,0:T(8,128)}, f32[32,8,128]{2,1,0:T(8,128)S(1)}, u32[]{:S(2)}, u32[]{:S(2)}) collective-permute-start(f32[32,8,128]{2,1,0:T(8,128)} %get-tuple-element.5), channel_id=1, source_target_pairs={{0,3},{1,0},{2,1},{3,2},{4,7},{5,4},{6,5},{7,6},{8,11},{9,8},{10,9... | collective-permute-start | bytes 393224 | tf_op jit(solution)/shard_map/ppermute | solution.py:120
  46.5 13.3 %collective-permute-start.7 = (f32[32,2,16,128]{3,2,1,0:T(8,128)S(1)}, f32[32,2,16,128]{3,2,1,0:T(8,128)S(1)}, u32[]{:S(2)}, u32[]{:S(2)}) collective-permute-start(f32[32,2,16,128]{3,2,1,0:T(8,128)S(1)} %get-tuple-element.12), channel_id=1, source_target_pairs={{0,224},{32,0},{64,32},{96,64},{128,96},{160,128},{192,160},{224,1... | collective-permute-start | bytes 1572872 | tf_op jit(solution)/shard_map/ppermute | solution.py:117
  48.8 11.1 %collective-permute-start.6 = (f32[32,2,16,128]{3,2,1,0:T(8,128)S(1)}, f32[32,2,16,128]{3,2,1,0:T(8,128)S(1)}, u32[]{:S(2)}, u32[]{:S(2)}) collective-permute-start(f32[32,2,16,128]{3,2,1,0:T(8,128)S(1)} %get-tuple-element.13), channel_id=1, source_target_pairs={{0,32},{32,64},{64,96},{96,128},{128,160},{160,192},{192,224},{224... | collective-permute-start | bytes 1572872 | tf_op jit(solution)/shard_map/ppermute | solution.py:116
  51.7 7.1 %collective-permute-start.9 = (f32[32,8,2,128]{3,2,1,0:T(2,128)S(1)}, f32[32,8,2,128]{3,2,1,0:T(2,128)S(1)}, u32[]{:S(2)}, u32[]{:S(2)}) collective-permute-start(f32[32,8,2,128]{3,2,1,0:T(2,128)S(1)} %get-tuple-element.10), channel_id=1, source_target_pairs={{0,28},{4,0},{8,4},{12,8},{16,12},{20,16},{24,20},{28,24},{1,29},{... | collective-permute-start | bytes 786440 | tf_op jit(solution)/shard_map/ppermute | solution.py:117
  51.7 8.1 %collective-permute-start.8 = (f32[32,8,2,128]{3,2,1,0:T(2,128)S(1)}, f32[32,8,2,128]{3,2,1,0:T(2,128)S(1)}, u32[]{:S(2)}, u32[]{:S(2)}) collective-permute-start(f32[32,8,2,128]{3,2,1,0:T(2,128)S(1)} %get-tuple-element.11), channel_id=1, source_target_pairs={{0,4},{4,8},{8,12},{12,16},{16,20},{20,24},{24,28},{28,0},{1,5},{5... | collective-permute-start | bytes 786440 | tf_op jit(solution)/shard_map/ppermute | solution.py:116
  53.2 6.7 %copy-start.10 = (f32[32,8,128]{2,1,0:T(8,128)}, f32[32,8,128]{2,1,0:T(8,128)S(1)}, u32[]{:S(2)}) copy-start(f32[32,8,128]{2,1,0:T(8,128)S(1)} %collective-permute-done.11.refs_6_) | copy-start | bytes 393220
  53.2 5.6 %collective-permute-start.10 = (f32[32,8,128]{2,1,0:T(8,128)S(1)}, f32[32,8,128]{2,1,0:T(8,128)S(1)}, u32[]{:S(2)}, u32[]{:S(2)}) collective-permute-start(f32[32,8,128]{2,1,0:T(8,128)S(1)} %copy-done.15), channel_id=1, source_target_pairs={{0,1},{1,2},{2,3},{3,0},{4,5},{5,6},{6,7},{7,4},{8,9},{9,10},{10,1... | collective-permute-start | bytes 393224 | tf_op jit(solution)/shard_map/ppermute | solution.py:119
  58.8 1.1 copy-start.11
  58.8 1.1 copy-start.6
  59.9 0.7 copy-start.7
  59.9 0.9 copy-start.3
  60.8 0.8 copy-start.5
  71.6 39.2 %copy-start.1 = (f32[32,8,16,128]{3,2,1,0:T(8,128)S(1)}, f32[32,8,16,128]{3,2,1,0:T(8,128)}, u32[]{:S(2)}) copy-start(f32[32,8,16,128]{3,2,1,0:T(8,128)} %shard_map.43) | copy-start | bytes 6291460
  78.0 2.7 %collective-permute-start.12 = (f32[32,32]{0,1:T(8,128)S(1)}, f32[32,32]{0,1:T(8,128)S(1)}, u32[]{:S(2)}, u32[]{:S(2)}) collective-permute-start(f32[32,32]{0,1:T(8,128)S(1)} %fusion.7), channel_id=1, source_target_pairs={{0,1},{1,0},{2,3},{3,2},{4,5},{5,4},{6,7},{7,6},{8,9},{9,8},{10,11... | collective-permute-start | bytes 12296 | tf_op jit(solution)/shard_map/ppermute | solution.py:155
  80.7 4.1 %collective-permute-start.13 = (f32[32,32]{0,1:T(8,128)S(1)}, f32[32,32]{0,1:T(8,128)S(1)}, u32[]{:S(2)}, u32[]{:S(2)}) collective-permute-start(f32[32,32]{0,1:T(8,128)S(1)} %add.36), channel_id=1, source_target_pairs={{0,2},{1,3},{2,0},{3,1},{4,6},{5,7},{6,4},{7,5},{8,10},{9,11},{10,... | collective-permute-start | bytes 12296 | tf_op jit(solution)/shard_map/ppermute | solution.py:155
  84.8 2.9 %collective-permute-start.14 = (f32[32,32]{0,1:T(8,128)S(1)}, f32[32,32]{0,1:T(8,128)S(1)}, u32[]{:S(2)}, u32[]{:S(2)}) collective-permute-start(f32[32,32]{0,1:T(8,128)S(1)} %add.37), channel_id=1, source_target_pairs={{0,4},{4,0},{8,12},{12,8},{16,20},{20,16},{24,28},{28,24},{1,5},{5... | collective-permute-start | bytes 12296 | tf_op jit(solution)/shard_map/ppermute | solution.py:155
  87.6 3.5 %collective-permute-start.15 = (f32[32,32]{0,1:T(8,128)S(1)}, f32[32,32]{0,1:T(8,128)S(1)}, u32[]{:S(2)}, u32[]{:S(2)}) collective-permute-start(f32[32,32]{0,1:T(8,128)S(1)} %add.38), channel_id=1, source_target_pairs={{0,8},{4,12},{8,0},{12,4},{16,24},{20,28},{24,16},{28,20},{1,9},{5... | collective-permute-start | bytes 12296 | tf_op jit(solution)/shard_map/ppermute | solution.py:155
  91.1 6.5 %collective-permute-start.16 = (f32[32,32]{0,1:T(8,128)S(1)}, f32[32,32]{0,1:T(8,128)S(1)}, u32[]{:S(2)}, u32[]{:S(2)}) collective-permute-start(f32[32,32]{0,1:T(8,128)S(1)} %add.39), channel_id=1, source_target_pairs={{0,16},{4,20},{8,24},{12,28},{16,0},{20,4},{24,8},{28,12},{1,17},{... | collective-permute-start | bytes 12296 | tf_op jit(solution)/shard_map/ppermute | solution.py:155
  97.7 8.2 %collective-permute-start.17 = (f32[32,32]{0,1:T(8,128)S(1)}, f32[32,32]{0,1:T(8,128)S(1)}, u32[]{:S(2)}, u32[]{:S(2)}) collective-permute-start(f32[32,32]{0,1:T(8,128)S(1)} %add.40), channel_id=1, source_target_pairs={{0,32},{32,0},{64,96},{96,64},{128,160},{160,128},{192,224},{224,1... | collective-permute-start | bytes 12296 | tf_op jit(solution)/shard_map/ppermute | solution.py:155
  105.9 2.6 %collective-permute-start.18 = (f32[32,32]{0,1:T(8,128)S(1)}, f32[32,32]{0,1:T(8,128)S(1)}, u32[]{:S(2)}, u32[]{:S(2)}) collective-permute-start(f32[32,32]{0,1:T(8,128)S(1)} %add.41), channel_id=1, source_target_pairs={{0,64},{32,96},{64,0},{96,32},{128,192},{160,224},{192,128},{224,1... | collective-permute-start | bytes 12296 | tf_op jit(solution)/shard_map/ppermute | solution.py:155
  108.5 4.1 %collective-permute-start.19 = (f32[32,32]{0,1:T(8,128)S(1)}, f32[32,32]{0,1:T(8,128)S(1)}, u32[]{:S(2)}, u32[]{:S(2)}) collective-permute-start(f32[32,32]{0,1:T(8,128)S(1)} %add.42), channel_id=1, source_target_pairs={{0,128},{32,160},{64,192},{96,224},{128,0},{160,32},{192,64},{224,... | collective-permute-start | bytes 12296 | tf_op jit(solution)/shard_map/ppermute | solution.py:155

commit v3 on v2

--- a/solution.py
+++ b/solution.py
@@ -17,26 +17,14 @@
     return [(i, (i + step) % n) for i in range(n)]
 
 
-def face_selector(rows, lanes):
-    r = lax.broadcasted_iota(jnp.int32, (rows, lanes), 0)
-    l = lax.broadcasted_iota(jnp.int32, (rows, lanes), 1)
-    pick = ((r < 2) & (l == r)) | ((r >= 2) & (r < 4) & (l == r + lanes - 4))
-    return jnp.where(pick, 1.0, 0.0).astype(jnp.float32)
+def faces_of(plane):
+    return jnp.transpose(pltpu.roll(plane, 2, 1))[0:8]
 
 
-def placer(rows, lanes, low_side):
-    r = lax.broadcasted_iota(jnp.int32, (rows, lanes), 0)
-    l = lax.broadcasted_iota(jnp.int32, (rows, lanes), 1)
-    if low_side:
-        pick = ((r == 2) & (l == 0)) | ((r == 3) & (l == 1))
-    else:
-        pick = ((r == 0) & (l == lanes - 2)) | ((r == 1) & (l == lanes - 1))
-    return jnp.where(pick, 1.0, 0.0).astype(jnp.float32)
-
-
-def faces_of(plane, selector):
-    return lax.dot_general(selector, plane, (((1,), (1,)), ((), ())), precision=HI,
-                           preferred_element_type=jnp.float32)
+def halo_image(zlo, zhi):
+    rows = zlo.shape[1]
+    pad = jnp.zeros((rows - 2 * zlo.shape[0], rows), jnp.float32)
+    return jnp.transpose(jnp.concatenate([zlo, zhi, pad], axis=0))
 
 
 def stage_kernel(*refs, last):
@@ -48,14 +36,9 @@
          out_ref, face_ref) = refs
     nb, cx, cy, cz = f_ref.shape
     rows = cx * cy
-    frows = zlo_ref.shape[1]
-    t_lo = placer(frows, cz, True)
-    t_hi = placer(frows, cz, False)
-    sel = face_selector(frows, cz)
     lane = lax.broadcasted_iota(jnp.int32, (rows, cz), 1)
     yid = lax.broadcasted_iota(jnp.int32, (cx, cy, cz), 1)
     pot = pot_ref[...]
-    tn = (((0,), (0,)), ((), ()))
     for b in range(nb):
         f3 = f_ref[b]
         summed = 3.0 * TAPS[2] * f3
@@ -71,12 +54,11 @@
         for shifted, weight in ((ym2, TAPS[0]), (ym1, TAPS[1]), (yp1, TAPS[3]), (yp2, TAPS[4])):
             summed = summed + weight * shifted
         f2 = f3.reshape(rows, cz)
-        zl = lax.dot_general(zlo_ref[b], t_lo, tn, precision=HI, preferred_element_type=jnp.float32)
-        zh = lax.dot_general(zhi_ref[b], t_hi, tn, precision=HI, preferred_element_type=jnp.float32)
-        zm2 = jnp.where(lane < 2, zl, pltpu.roll(f2, 2, 1))
-        zm1 = jnp.where(lane < 1, pltpu.roll(zl, cz - 1, 1), pltpu.roll(f2, 1, 1))
-        zp1 = jnp.where(lane >= cz - 1, pltpu.roll(zh, 1, 1), pltpu.roll(f2, cz - 1, 1))
-        zp2 = jnp.where(lane >= cz - 2, zh, pltpu.roll(f2, cz - 2, 1))
+        zim = halo_image(zlo_ref[b], zhi_ref[b])
+        zm2 = jnp.where(lane < 2, zim, pltpu.roll(f2, 2, 1))
+        zm1 = jnp.where(lane < 1, pltpu.roll(zim, cz - 1, 1), pltpu.roll(f2, 1, 1))
+        zp1 = jnp.where(lane >= cz - 1, pltpu.roll(zim, cz - 11, 1), pltpu.roll(f2, cz - 1, 1))
+        zp2 = jnp.where(lane >= cz - 2, pltpu.roll(zim, cz - 12, 1), pltpu.roll(f2, cz - 2, 1))
         summed = summed.reshape(rows, cz)
         for shifted, weight in ((zm2, TAPS[0]), (zm1, TAPS[1]), (zp1, TAPS[3]), (zp2, TAPS[4])):
             summed = summed + weight * shifted
@@ -86,15 +68,14 @@
             res = 2.0 * (h - 5.5 * f2) / 3.5 - orb_ref[b].reshape(rows, cz)
         else:
             res = (h - 5.5 * f2) / 3.5
-            face_ref[b] = faces_of(res, sel)
+            face_ref[b] = faces_of(res)
         out_ref[b] = res.reshape(cx, cy, cz)
 
 
 def z_face_kernel(f_ref, face_ref):
     nb, cx, cy, cz = f_ref.shape
-    sel = face_selector(face_ref.shape[1], cz)
     for b in range(nb):
-        face_ref[b] = faces_of(f_ref[b].reshape(cx * cy, cz), sel)
+        face_ref[b] = faces_of(f_ref[b].reshape(cx * cy, cz))
 
 
 def z_faces(f):

time: 127 us -> 121 us (0.953)
  Pallas kernels: 32.9 us -> 26.9 us
    pallas_call x2, Pallas kernels: 25.5 us -> 20.8 us  [stage(): pl.pallas_call(functools.partial(stage_kernel, last=last), grid=(norb //...]
where the time goes in v3:
time: 121 us; the launch traced here: 120 us
  waiting for transfers between devices  33.5 us (28%)
  starting transfers between devices  30.8 us (25%)
  Pallas kernels  26.9 us (22%)
  local copies, waits for them, and re-layouts  11.5 us (10%)
  matrix products  9.57 us (8%)
  other arithmetic  6.72 us (6%)
    pallas_call x2, Pallas kernels, stage(): pl.pallas_call(functools.partial(stage_kernel, last=last), grid=(norb //...  20.8 us
    ppermute x8, waiting for transfers between devices, butterfly_sum(): c = c + lax.ppermute(c, axis, [(i, i ^ d) for i in range(n)])  20.2 us
    ppermute x8, starting transfers between devices, butterfly_sum(): c = c + lax.ppermute(c, axis, [(i, i ^ d) for i in range(n)])  12.7 us
    ppermute x2, waiting for transfers between devices, exchange(): out.append(lax.ppermute(zface, 'gz', shift_pairs(n, 1)))  9.34 us
    ppermute x4, starting transfers between devices, exchange(): out.append(lax.ppermute(first, axis, shift_pairs(n, -1)))  8.93 us
    unnamed x36, local copies, waits for them, and re-layouts  8.15 us
    dot_general x1, matrix products, per_device(): correlation = jnp.dot(filtered, filtered.T, precision=HI) / all_cells  6.34 us
    pallas_call x1, Pallas kernels, z_faces(): pl.pallas_call(z_face_kernel, grid=(norb // BLOCK,), in_specs=[blk], out_...  6.07 us
  transfers between devices with their start and end apart: 20, of which 12 were waited for; matrix products, arithmetic and copies ran while one was open for 4% of the time, Pallas kernels for 0%

profile of v3, /device:TPU:1, one launch (start us, length us, event | category | flops | bytes accessed | tf_op | source)
XLA Modules:
  0.0 119.9 jit_solution(4040084050321523207)
XLA Ops:
  0.6 6.1 %shard_map.41 = f32[32,8,128]{2,1,0:T(8,128)} custom-call(f32[32,8,16,128]{3,2,1,0:T(8,128)} %refs_8_.1), custom_call_target="tpu_custom_call" | custom-call | tf_op jit(solution)/shard_map/pallas_call | solution.py:85
  6.7 3.6 %collective-permute-start.5 = (f32[32,8,128]{2,1,0:T(8,128)}, f32[32,8,128]{2,1,0:T(8,128)S(1)}, u32[]{:S(2)}, u32[]{:S(2)}) collective-permute-start(f32[32,8,128]{2,1,0:T(8,128)} %shard_map.41), channel_id=1, source_target_pairs={{0,3},{1,0},{2,1},{3,2},{4,7},{5,4},{6,5},{7,6},{8,11},{9,8},{10,9... | collective-permute-start | bytes 393224 | tf_op jit(solution)/shard_map/ppermute | solution.py:101
  10.3 1.0 collective-permute-start.1
  11.3 1.1 collective-permute-start
  12.4 0.2 fusion.15
  12.6 5.7 %collective-permute-start.3 = (f32[32,8,2,128]{3,2,1,0:T(2,128)S(1)}, f32[32,8,2,128]{3,2,1,0:T(2,128)S(1)}, u32[]{:S(2)}, u32[]{:S(2)}) collective-permute-start(f32[32,8,2,128]{3,2,1,0:T(2,128)S(1)} %get-tuple-element.14), channel_id=1, source_target_pairs={{0,28},{4,0},{8,4},{12,8},{16,12},{20,16},{24,20},{28,24},{1,29},{... | collective-permute-start | bytes 786440 | tf_op jit(solution)/shard_map/ppermute | solution.py:98
  18.4 5.0 %collective-permute-done.4.refs_5_ = f32[32,8,128]{2,1,0:T(8,128)S(1)} collective-permute-done((f32[32,8,128]{2,1,0:T(8,128)S(1)}, f32[32,8,128]{2,1,0:T(8,128)S(1)}, u32[]{:S(2)}, u32[]{:S(2)}) %collective-permute-start.4) | collective-permute-done | bytes 131104 | tf_op jit(solution)/shard_map/ppermute | solution.py:100
  23.4 2.9 %collective-permute-done.2.refs_3_ = f32[32,8,2,128]{3,2,1,0:T(2,128)S(1)} collective-permute-done((f32[32,8,2,128]{3,2,1,0:T(2,128)S(1)}, f32[32,8,2,128]{3,2,1,0:T(2,128)S(1)}, u32[]{:S(2)}, u32[]{:S(2)}) %collective-permute-start.2) | collective-permute-done | bytes 262176 | tf_op jit(solution)/shard_map/ppermute | solution.py:97
  26.3 0.7 copy-done.9
  27.0 0.2 copy-done.2
  27.2 0.8 copy-done.4
  28.0 11.5 %shard_map.42 = (f32[32,8,16,128]{3,2,1,0:T(8,128)}, f32[32,8,128]{2,1,0:T(8,128)}) custom-call(f32[32,8,16,128]{3,2,1,0:T(8,128)} %refs_8_.1, f32[32,2,16,128]{3,2,1,0:T(8,128)} %copy-done.4, f32[32,2,16,128]{3,2,1,0:T(8,128)} %copy-done.2, f32[32,8,2,128]{3,2,1,0:T(2,128)} %copy-done.9, f32[32,8,2,128]{3,2,1,0:T(2,128)} %copy-done.8, ...), custom_call_target="tpu_custom_call" | custom-call | tf_op jit(solution)/shard_map/pallas_call | solution.py:124
  39.5 0.5 collective-permute-start.11
  40.0 1.3 %fusion.14 = (f32[32,2,16,128]{3,2,1,0:T(8,128)S(1)}, f32[32,2,16,128]{3,2,1,0:T(8,128)S(1)}) fusion(f32[32,8,16,128]{3,2,1,0:T(8,128)} %get-tuple-element.4.refs_0_), kind=kLoop, calls=%fused_computation.19 | loop fusion | bytes 2097152 | tf_op jit(solution)/shard_map/slice | solution.py:96
  41.3 2.2 %collective-permute-start.7 = (f32[32,2,16,128]{3,2,1,0:T(8,128)S(1)}, f32[32,2,16,128]{3,2,1,0:T(8,128)S(1)}, u32[]{:S(2)}, u32[]{:S(2)}) collective-permute-start(f32[32,2,16,128]{3,2,1,0:T(8,128)S(1)} %get-tuple-element.12), channel_id=1, source_target_pairs={{0,224},{32,0},{64,32},{96,64},{128,96},{160,128},{192,160},{224,1... | collective-permute-start | bytes 1572872 | tf_op jit(solution)/shard_map/ppermute | solution.py:98
  43.5 1.1 collective-permute-start.6
  44.7 1.8 %fusion.13 = (f32[32,8,2,128]{3,2,1,0:T(2,128)S(1)}, f32[32,8,2,128]{3,2,1,0:T(2,128)S(1)}) fusion(f32[32,8,16,128]{3,2,1,0:T(8,128)} %get-tuple-element.4.refs_0_), kind=kLoop, calls=%fused_computation.18 | loop fusion | bytes 1048576 | tf_op jit(solution)/shard_map/slice | solution.py:96
  46.5 1.5 %collective-permute-start.8 = (f32[32,8,2,128]{3,2,1,0:T(2,128)S(1)}, f32[32,8,2,128]{3,2,1,0:T(2,128)S(1)}, u32[]{:S(2)}, u32[]{:S(2)}) collective-permute-start(f32[32,8,2,128]{3,2,1,0:T(2,128)S(1)} %get-tuple-element.11), channel_id=1, source_target_pairs={{0,4},{4,8},{8,12},{12,16},{16,20},{20,24},{24,28},{28,0},{1,5},{5... | collective-permute-start | bytes 786440 | tf_op jit(solution)/shard_map/ppermute | solution.py:97
  48.0 1.3 %collective-permute-start.10 = (f32[32,8,128]{2,1,0:T(8,128)S(1)}, f32[32,8,128]{2,1,0:T(8,128)S(1)}, u32[]{:S(2)}, u32[]{:S(2)}) collective-permute-start(f32[32,8,128]{2,1,0:T(8,128)S(1)} %copy-done.15), channel_id=1, source_target_pairs={{0,1},{1,2},{2,3},{3,0},{4,5},{5,6},{6,7},{7,4},{8,9},{9,10},{10,1... | collective-permute-start | bytes 393224 | tf_op jit(solution)/shard_map/ppermute | solution.py:100
  49.2 4.3 %collective-permute-done.10.refs_5_ = f32[32,8,128]{2,1,0:T(8,128)S(1)} collective-permute-done((f32[32,8,128]{2,1,0:T(8,128)S(1)}, f32[32,8,128]{2,1,0:T(8,128)S(1)}, u32[]{:S(2)}, u32[]{:S(2)}) %collective-permute-start.10) | collective-permute-done | bytes 131104 | tf_op jit(solution)/shard_map/ppermute | solution.py:100
  53.6 1.1 collective-permute-done.8.refs_3_
  54.7 0.7 copy-done.7
  55.4 0.2 copy-done.3
  55.5 0.8 copy-done.5
  56.3 9.4 %shard_map.43 = f32[32,8,16,128]{3,2,1,0:T(8,128)} custom-call(f32[32,8,16,128]{3,2,1,0:T(8,128)} %get-tuple-element.4.refs_0_, f32[32,2,16,128]{3,2,1,0:T(8,128)} %copy-done.5, f32[32,2,16,128]{3,2,1,0:T(8,128)} %copy-done.3, f32[32,8,2,128]{3,2,1,0:T(2,128)} %copy-done.7, f32[32,8,2,128]{3,2,1,0:T(2,128)} %copy-done.6, f32[32,8,128]{2,1,0:T(8,128)} %copy-done.11, ...), custom_call_target="tpu_custom_call" | custom-call | tf_op jit(solution)/shard_map/pallas_call | solution.py:124
  65.7 6.3 %fusion.7 = f32[32,32]{0,1:T(8,128)S(1)} fusion(f32[32,8,16,128]{3,2,1,0:T(8,128)} %shard_map.43), kind=kOutput, calls=%fused_computation.7 | convolution fusion | flops 201327616 | bytes 2101248 | tf_op jit(solution)/shard_map/dot_general | solution.py:147
  72.0 0.7 collective-permute-start.12
  72.7 2.0 %collective-permute-done.12 = f32[32,32]{0,1:T(8,128)S(1)} collective-permute-done((f32[32,32]{0,1:T(8,128)S(1)}, f32[32,32]{0,1:T(8,128)S(1)}, u32[]{:S(2)}, u32[]{:S(2)}) %collective-permute-start.12) | collective-permute-done | bytes 4128 | tf_op jit(solution)/shard_map/ppermute | solution.py:136
  74.7 4.1 %collective-permute-done.13 = f32[32,32]{0,1:T(8,128)S(1)} collective-permute-done((f32[32,32]{0,1:T(8,128)S(1)}, f32[32,32]{0,1:T(8,128)S(1)}, u32[]{:S(2)}, u32[]{:S(2)}) %collective-permute-start.13) | collective-permute-done | bytes 4128 | tf_op jit(solution)/shard_map/ppermute | solution.py:136
  78.8 2.9 %collective-permute-done.14 = f32[32,32]{0,1:T(8,128)S(1)} collective-permute-done((f32[32,32]{0,1:T(8,128)S(1)}, f32[32,32]{0,1:T(8,128)S(1)}, u32[]{:S(2)}, u32[]{:S(2)}) %collective-permute-start.14) | collective-permute-done | bytes 4128 | tf_op jit(solution)/shard_map/ppermute | solution.py:136
  81.7 3.5 %collective-permute-done.15 = f32[32,32]{0,1:T(8,128)S(1)} collective-permute-done((f32[32,32]{0,1:T(8,128)S(1)}, f32[32,32]{0,1:T(8,128)S(1)}, u32[]{:S(2)}, u32[]{:S(2)}) %collective-permute-start.15) | collective-permute-done | bytes 4128 | tf_op jit(solution)/shard_map/ppermute | solution.py:136
  85.2 1.1 collective-permute-start.16
  86.4 5.4 %collective-permute-done.16 = f32[32,32]{0,1:T(8,128)S(1)} collective-permute-done((f32[32,32]{0,1:T(8,128)S(1)}, f32[32,32]{0,1:T(8,128)S(1)}, u32[]{:S(2)}, u32[]{:S(2)}) %collective-permute-start.16) | collective-permute-done | bytes 4128 | tf_op jit(solution)/shard_map/ppermute | solution.py:136
  91.7 7.3 %collective-permute-start.17 = (f32[32,32]{0,1:T(8,128)S(1)}, f32[32,32]{0,1:T(8,128)S(1)}, u32[]{:S(2)}, u32[]{:S(2)}) collective-permute-start(f32[32,32]{0,1:T(8,128)S(1)} %add.40), channel_id=1, source_target_pairs={{0,32},{32,0},{64,96},{96,64},{128,160},{160,128},{192,224},{224,1... | collective-permute-start | bytes 12296 | tf_op jit(solution)/shard_map/ppermute | solution.py:136
  99.1 0.8 collective-permute-done.17
  99.9 1.2 collective-permute-start.18
  101.1 1.4 %collective-permute-done.18 = f32[32,32]{0,1:T(8,128)S(1)} collective-permute-done((f32[32,32]{0,1:T(8,128)S(1)}, f32[32,32]{0,1:T(8,128)S(1)}, u32[]{:S(2)}, u32[]{:S(2)}) %collective-permute-start.18) | collective-permute-done | bytes 4128 | tf_op jit(solution)/shard_map/ppermute | solution.py:136
  102.5 2.4 %collective-permute-start.19 = (f32[32,32]{0,1:T(8,128)S(1)}, f32[32,32]{0,1:T(8,128)S(1)}, u32[]{:S(2)}, u32[]{:S(2)}) collective-permute-start(f32[32,32]{0,1:T(8,128)S(1)} %add.42), channel_id=1, source_target_pairs={{0,128},{32,160},{64,192},{96,224},{128,0},{160,32},{192,64},{224,... | collective-permute-start | bytes 12296 | tf_op jit(solution)/shard_map/ppermute | solution.py:136
  104.9 1.2 %copy.31 = f32[4,8,128,128]{3,1,2,0:T(8,128)S(1)} copy(f32[4,8,128,128]{3,2,1,0:T(8,128)S(1)} %bitcast.33) | data formatting | bytes 4194304
  106.1 0.4 copy.21
  106.7 2.9 %cholesky.17 = f32[32,32]{1,0:T(8,128)S(1)} custom-call(f32[32,32]{1,0:T(8,128)S(1)} %fusion.11), custom_call_target="Cholesky" | custom-call | tf_op jit(solution)/shard_map/jit(cholesky)/cholesky | solution.py:148
  109.7 0.6 compare_reduce_fusion
  110.3 0.7 fusion.12
  111.0 0.7 copy.16
  111.6 2.4 %custom-call.7 = f32[1,32,32]{1,2,0:T(8,128)S(1)} custom-call(f32[1,32,32]{2,1,0:T(8,128)S(1)} %get-tuple-element.19), custom_call_target="InvertDiagBlocksLowerTriangular" | custom-call | tf_op jit(solution)/shard_map/jit(_solve_triangular)/triangular_solve | solution.py:150
  114.1 0.2 convolution_bitcast_fusion
  114.3 3.0 %fusion = f32[32,8,16,128]{3,0,2,1:T(8,128)S(1)} fusion(f32[32,32,1,1]{1,0,3,2:T(8,128)S(1)} %convolution_bitcast_fusion, f32[8,16,128,32]{2,1,0,3:T(8,128)S(1)} %bitcast.34), kind=kOutput, calls=%fused_computation.1 | convolution fusion | flops 201326592 | bytes 4198400 | tf_op jit(solution)/shard_map/dot_general | solution.py:151
  117.3 2.5 %copy.15 = f32[32,8,16,128]{3,2,1,0:T(8,128)} copy(f32[32,8,16,128]{3,0,2,1:T(8,128)S(1)} %fusion) | data formatting | bytes 4194304
  (53 shorter events, 0.6 us)
Async XLA Ops:
  0.6 9.6 %copy-start = (f32[32,8,16,128]{3,2,1,0:T(8,128)S(1)}, f32[32,8,16,128]{3,2,1,0:T(8,128)}, u32[]{:S(2)}) copy-start(f32[32,8,16,128]{3,2,1,0:T(8,128)} %refs_8_.1) | copy-start | bytes 6291460
  6.7 11.6 %copy-start.13 = (f32[32,8,128]{2,1,0:T(8,128)S(1)}, f32[32,8,128]{2,1,0:T(8,128)}, u32[]{:S(2)}) copy-start(f32[32,8,128]{2,1,0:T(8,128)} %shard_map.41) | copy-start | bytes 393220
  6.7 11.6 %collective-permute-start.5 = (f32[32,8,128]{2,1,0:T(8,128)}, f32[32,8,128]{2,1,0:T(8,128)S(1)}, u32[]{:S(2)}, u32[]{:S(2)}) collective-permute-start(f32[32,8,128]{2,1,0:T(8,128)} %shard_map.41), channel_id=1, source_target_pairs={{0,3},{1,0},{2,1},{3,2},{4,7},{5,4},{6,5},{7,6},{8,11},{9,8},{10,9... | collective-permute-start | bytes 393224 | tf_op jit(solution)/shard_map/ppermute | solution.py:101
  10.3 15.9 %collective-permute-start.1 = (f32[32,2,16,128]{3,2,1,0:T(8,128)S(1)}, f32[32,2,16,128]{3,2,1,0:T(8,128)S(1)}, u32[]{:S(2)}, u32[]{:S(2)}) collective-permute-start(f32[32,2,16,128]{3,2,1,0:T(8,128)S(1)} %get-tuple-element.16), channel_id=1, source_target_pairs={{0,224},{32,0},{64,32},{96,64},{128,96},{160,128},{192,160},{224,1... | collective-permute-start | bytes 1572872 | tf_op jit(solution)/shard_map/ppermute | solution.py:98
  11.3 15.0 %collective-permute-start = (f32[32,2,16,128]{3,2,1,0:T(8,128)S(1)}, f32[32,2,16,128]{3,2,1,0:T(8,128)S(1)}, u32[]{:S(2)}, u32[]{:S(2)}) collective-permute-start(f32[32,2,16,128]{3,2,1,0:T(8,128)S(1)} %get-tuple-element.17), channel_id=1, source_target_pairs={{0,32},{32,64},{64,96},{96,128},{128,160},{160,192},{192,224},{224... | collective-permute-start | bytes 1572872 | tf_op jit(solution)/shard_map/ppermute | solution.py:97
  12.6 10.8 %collective-permute-start.3 = (f32[32,8,2,128]{3,2,1,0:T(2,128)S(1)}, f32[32,8,2,128]{3,2,1,0:T(2,128)S(1)}, u32[]{:S(2)}, u32[]{:S(2)}) collective-permute-start(f32[32,8,2,128]{3,2,1,0:T(2,128)S(1)} %get-tuple-element.14), channel_id=1, source_target_pairs={{0,28},{4,0},{8,4},{12,8},{16,12},{20,16},{24,20},{28,24},{1,29},{... | collective-permute-start | bytes 786440 | tf_op jit(solution)/shard_map/ppermute | solution.py:98
  18.3 8.0 %collective-permute-start.2 = (f32[32,8,2,128]{3,2,1,0:T(2,128)S(1)}, f32[32,8,2,128]{3,2,1,0:T(2,128)S(1)}, u32[]{:S(2)}, u32[]{:S(2)}) collective-permute-start(f32[32,8,2,128]{3,2,1,0:T(2,128)S(1)} %get-tuple-element.15), channel_id=1, source_target_pairs={{0,4},{4,8},{8,12},{12,16},{16,20},{20,24},{24,28},{28,0},{1,5},{5... | collective-permute-start | bytes 786440 | tf_op jit(solution)/shard_map/ppermute | solution.py:97
  18.3 8.0 %copy-start.12 = (f32[32,8,128]{2,1,0:T(8,128)}, f32[32,8,128]{2,1,0:T(8,128)S(1)}, u32[]{:S(2)}) copy-start(f32[32,8,128]{2,1,0:T(8,128)S(1)} %collective-permute-done.5.refs_6_) | copy-start | bytes 393220
  18.3 5.1 %collective-permute-start.4 = (f32[32,8,128]{2,1,0:T(8,128)S(1)}, f32[32,8,128]{2,1,0:T(8,128)S(1)}, u32[]{:S(2)}, u32[]{:S(2)}) collective-permute-start(f32[32,8,128]{2,1,0:T(8,128)S(1)} %copy-done.13), channel_id=1, source_target_pairs={{0,1},{1,2},{2,3},{3,0},{4,5},{5,6},{6,7},{7,4},{8,9},{9,10},{10,1... | collective-permute-start | bytes 393224 | tf_op jit(solution)/shard_map/ppermute | solution.py:100
  23.4 2.9 %copy-start.14 = (f32[32,8,128]{2,1,0:T(8,128)}, f32[32,8,128]{2,1,0:T(8,128)S(1)}, u32[]{:S(2)}) copy-start(f32[32,8,128]{2,1,0:T(8,128)S(1)} %collective-permute-done.4.refs_5_) | copy-start | bytes 393220
  23.4 2.9 %copy-start.8 = (f32[32,8,2,128]{3,2,1,0:T(2,128)}, f32[32,8,2,128]{3,2,1,0:T(2,128)S(1)}, u32[]{:S(2)}) copy-start(f32[32,8,2,128]{3,2,1,0:T(2,128)S(1)} %collective-permute-done.3.refs_4_) | copy-start | bytes 786436
  26.3 0.7 copy-start.9
  26.3 0.9 copy-start.2
  27.2 0.8 copy-start.4
  39.5 8.5 %copy-start.15 = (f32[32,8,128]{2,1,0:T(8,128)S(1)}, f32[32,8,128]{2,1,0:T(8,128)}, u32[]{:S(2)}) copy-start(f32[32,8,128]{2,1,0:T(8,128)} %get-tuple-element.5) | copy-start | bytes 393220
  39.5 8.5 %collective-permute-start.11 = (f32[32,8,128]{2,1,0:T(8,128)}, f32[32,8,128]{2,1,0:T(8,128)S(1)}, u32[]{:S(2)}, u32[]{:S(2)}) collective-permute-start(f32[32,8,128]{2,1,0:T(8,128)} %get-tuple-element.5), channel_id=1, source_target_pairs={{0,3},{1,0},{2,1},{3,2},{4,7},{5,4},{6,5},{7,6},{8,11},{9,8},{10,9... | collective-permute-start | bytes 393224 | tf_op jit(solution)/shard_map/ppermute | solution.py:101
  41.3 13.4 %collective-permute-start.7 = (f32[32,2,16,128]{3,2,1,0:T(8,128)S(1)}, f32[32,2,16,128]{3,2,1,0:T(8,128)S(1)}, u32[]{:S(2)}, u32[]{:S(2)}) collective-permute-start(f32[32,2,16,128]{3,2,1,0:T(8,128)S(1)} %get-tuple-element.12), channel_id=1, source_target_pairs={{0,224},{32,0},{64,32},{96,64},{128,96},{160,128},{192,160},{224,1... | collective-permute-start | bytes 1572872 | tf_op jit(solution)/shard_map/ppermute | solution.py:98
  43.5 11.1 %collective-permute-start.6 = (f32[32,2,16,128]{3,2,1,0:T(8,128)S(1)}, f32[32,2,16,128]{3,2,1,0:T(8,128)S(1)}, u32[]{:S(2)}, u32[]{:S(2)}) collective-permute-start(f32[32,2,16,128]{3,2,1,0:T(8,128)S(1)} %get-tuple-element.13), channel_id=1, source_target_pairs={{0,32},{32,64},{64,96},{96,128},{128,160},{160,192},{192,224},{224... | collective-permute-start | bytes 1572872 | tf_op jit(solution)/shard_map/ppermute | solution.py:97
  46.4 7.1 %collective-permute-start.9 = (f32[32,8,2,128]{3,2,1,0:T(2,128)S(1)}, f32[32,8,2,128]{3,2,1,0:T(2,128)S(1)}, u32[]{:S(2)}, u32[]{:S(2)}) collective-permute-start(f32[32,8,2,128]{3,2,1,0:T(2,128)S(1)} %get-tuple-element.10), channel_id=1, source_target_pairs={{0,28},{4,0},{8,4},{12,8},{16,12},{20,16},{24,20},{28,24},{1,29},{... | collective-permute-start | bytes 786440 | tf_op jit(solution)/shard_map/ppermute | solution.py:98
  46.5 8.1 %collective-permute-start.8 = (f32[32,8,2,128]{3,2,1,0:T(2,128)S(1)}, f32[32,8,2,128]{3,2,1,0:T(2,128)S(1)}, u32[]{:S(2)}, u32[]{:S(2)}) collective-permute-start(f32[32,8,2,128]{3,2,1,0:T(2,128)S(1)} %get-tuple-element.11), channel_id=1, source_target_pairs={{0,4},{4,8},{8,12},{12,16},{16,20},{20,24},{24,28},{28,0},{1,5},{5... | collective-permute-start | bytes 786440 | tf_op jit(solution)/shard_map/ppermute | solution.py:97
  48.0 6.7 %copy-start.10 = (f32[32,8,128]{2,1,0:T(8,128)}, f32[32,8,128]{2,1,0:T(8,128)S(1)}, u32[]{:S(2)}) copy-start(f32[32,8,128]{2,1,0:T(8,128)S(1)} %collective-permute-done.11.refs_6_) | copy-start | bytes 393220
  48.0 5.6 %collective-permute-start.10 = (f32[32,8,128]{2,1,0:T(8,128)S(1)}, f32[32,8,128]{2,1,0:T(8,128)S(1)}, u32[]{:S(2)}, u32[]{:S(2)}) collective-permute-start(f32[32,8,128]{2,1,0:T(8,128)S(1)} %copy-done.15), channel_id=1, source_target_pairs={{0,1},{1,2},{2,3},{3,0},{4,5},{5,6},{6,7},{7,4},{8,9},{9,10},{10,1... | collective-permute-start | bytes 393224 | tf_op jit(solution)/shard_map/ppermute | solution.py:100
  53.6 1.1 copy-start.11
  53.6 1.1 copy-start.6
  54.7 0.7 copy-start.7
  54.7 0.9 copy-start.3
  55.5 0.8 copy-start.5
  65.7 39.2 %copy-start.1 = (f32[32,8,16,128]{3,2,1,0:T(8,128)S(1)}, f32[32,8,16,128]{3,2,1,0:T(8,128)}, u32[]{:S(2)}) copy-start(f32[32,8,16,128]{3,2,1,0:T(8,128)} %shard_map.43) | copy-start | bytes 6291460
  72.0 2.7 %collective-permute-start.12 = (f32[32,32]{0,1:T(8,128)S(1)}, f32[32,32]{0,1:T(8,128)S(1)}, u32[]{:S(2)}, u32[]{:S(2)}) collective-permute-start(f32[32,32]{0,1:T(8,128)S(1)} %fusion.7), channel_id=1, source_target_pairs={{0,1},{1,0},{2,3},{3,2},{4,5},{5,4},{6,7},{7,6},{8,9},{9,8},{10,11... | collective-permute-start | bytes 12296 | tf_op jit(solution)/shard_map/ppermute | solution.py:136
  74.7 4.1 %collective-permute-start.13 = (f32[32,32]{0,1:T(8,128)S(1)}, f32[32,32]{0,1:T(8,128)S(1)}, u32[]{:S(2)}, u32[]{:S(2)}) collective-permute-start(f32[32,32]{0,1:T(8,128)S(1)} %add.36), channel_id=1, source_target_pairs={{0,2},{1,3},{2,0},{3,1},{4,6},{5,7},{6,4},{7,5},{8,10},{9,11},{10,... | collective-permute-start | bytes 12296 | tf_op jit(solution)/shard_map/ppermute | solution.py:136
  78.8 2.9 %collective-permute-start.14 = (f32[32,32]{0,1:T(8,128)S(1)}, f32[32,32]{0,1:T(8,128)S(1)}, u32[]{:S(2)}, u32[]{:S(2)}) collective-permute-start(f32[32,32]{0,1:T(8,128)S(1)} %add.37), channel_id=1, source_target_pairs={{0,4},{4,0},{8,12},{12,8},{16,20},{20,16},{24,28},{28,24},{1,5},{5... | collective-permute-start | bytes 12296 | tf_op jit(solution)/shard_map/ppermute | solution.py:136
  81.7 3.5 %collective-permute-start.15 = (f32[32,32]{0,1:T(8,128)S(1)}, f32[32,32]{0,1:T(8,128)S(1)}, u32[]{:S(2)}, u32[]{:S(2)}) collective-permute-start(f32[32,32]{0,1:T(8,128)S(1)} %add.38), channel_id=1, source_target_pairs={{0,8},{4,12},{8,0},{12,4},{16,24},{20,28},{24,16},{28,20},{1,9},{5... | collective-permute-start | bytes 12296 | tf_op jit(solution)/shard_map/ppermute | solution.py:136
  85.2 6.5 %collective-permute-start.16 = (f32[32,32]{0,1:T(8,128)S(1)}, f32[32,32]{0,1:T(8,128)S(1)}, u32[]{:S(2)}, u32[]{:S(2)}) collective-permute-start(f32[32,32]{0,1:T(8,128)S(1)} %add.39), channel_id=1, source_target_pairs={{0,16},{4,20},{8,24},{12,28},{16,0},{20,4},{24,8},{28,12},{1,17},{... | collective-permute-start | bytes 12296 | tf_op jit(solution)/shard_map/ppermute | solution.py:136
  91.7 8.2 %collective-permute-start.17 = (f32[32,32]{0,1:T(8,128)S(1)}, f32[32,32]{0,1:T(8,128)S(1)}, u32[]{:S(2)}, u32[]{:S(2)}) collective-permute-start(f32[32,32]{0,1:T(8,128)S(1)} %add.40), channel_id=1, source_target_pairs={{0,32},{32,0},{64,96},{96,64},{128,160},{160,128},{192,224},{224,1... | collective-permute-start | bytes 12296 | tf_op jit(solution)/shard_map/ppermute | solution.py:136
  99.9 2.6 %collective-permute-start.18 = (f32[32,32]{0,1:T(8,128)S(1)}, f32[32,32]{0,1:T(8,128)S(1)}, u32[]{:S(2)}, u32[]{:S(2)}) collective-permute-start(f32[32,32]{0,1:T(8,128)S(1)} %add.41), channel_id=1, source_target_pairs={{0,64},{32,96},{64,0},{96,32},{128,192},{160,224},{192,128},{224,1... | collective-permute-start | bytes 12296 | tf_op jit(solution)/shard_map/ppermute | solution.py:136
  102.5 4.1 %collective-permute-start.19 = (f32[32,32]{0,1:T(8,128)S(1)}, f32[32,32]{0,1:T(8,128)S(1)}, u32[]{:S(2)}, u32[]{:S(2)}) collective-permute-start(f32[32,32]{0,1:T(8,128)S(1)} %add.42), channel_id=1, source_target_pairs={{0,128},{32,160},{64,192},{96,224},{128,0},{160,32},{192,64},{224,... | collective-permute-start | bytes 12296 | tf_op jit(solution)/shard_map/ppermute | solution.py:136

commit v4 on v3

--- a/solution.py
+++ b/solution.py
@@ -8,7 +8,7 @@
 from jax.sharding import PartitionSpec as P
 
 TAPS = (-1.0 / 12.0, 4.0 / 3.0, -2.5, 4.0 / 3.0, -1.0 / 12.0)
-BLOCK = 4
+BLOCK = 8
 INTERPRET = False
 HI = lax.Precision.HIGHEST
 
@@ -142,14 +142,13 @@
     first, first_z = stage(orbitals, exchange(orbitals, z_faces(orbitals)), potential)
     second = stage(first, exchange(first, first_z), potential, orbitals)
     norb_count = orbitals.shape[0]
-    filtered = second.reshape(norb_count, -1)
-    all_cells = filtered.shape[1] * lax.axis_size("gx") * lax.axis_size("gy") * lax.axis_size("gz")
-    correlation = jnp.dot(filtered, filtered.T, precision=HI) / all_cells
+    all_cells = second[0].size * lax.axis_size("gx") * lax.axis_size("gy") * lax.axis_size("gz")
+    correlation = jnp.einsum("axyz,bxyz->ab", second, second, precision=HI) / all_cells
     lower = jnp.linalg.cholesky(butterfly_sum(correlation))
     eye = jnp.eye(norb_count, dtype=lower.dtype)
     inverse = jax.scipy.linalg.solve_triangular(lower, eye, lower=True)
-    basis = jnp.dot(inverse, filtered, precision=HI)
-    return (basis.reshape(orbitals.shape), lower.T)
+    basis = jnp.einsum("ab,bxyz->axyz", inverse, second, precision=HI)
+    return (basis, lower.T)
 
 
 def solution(mesh):

time: 121 us -> 118 us (0.975)
  Pallas kernels: 26.9 us -> 23.5 us
  waiting for transfers between devices: 33.5 us -> 35.1 us
  local copies, waits for them, and re-layouts: 11.5 us -> 9.94 us
    pallas_call x1, Pallas kernels: 6.07 us -> 4.2 us  [z_faces(): pl.pallas_call(z_face_kernel, grid=(norb // BLOCK,), in_specs=[blk], out_...]
    ppermute x8, waiting for transfers between devices: 20.2 us -> 21.8 us  [butterfly_sum(): c = c + lax.ppermute(c, axis, [(i, i ^ d) for i in range(n)])]
    unnamed x36 -> x34, local copies, waits for them, and re-layouts: 8.15 us -> 6.56 us
    pallas_call x2, Pallas kernels: 20.8 us -> 19.3 us  [stage(): pl.pallas_call(functools.partial(stage_kernel, last=last), grid=(norb //...]
  transfers between devices with their start and end apart: 20 -> 20, of which waited for: 12 -> 12; matrix products, arithmetic and copies ran while one was open for 4% -> 3% of each run, Pallas kernels for 0% -> 0%
where the time goes in v4:
time: 118 us; the launch traced here: 116 us
  waiting for transfers between devices  35.1 us (30%)
  starting transfers between devices  30.8 us (26%)
  Pallas kernels  23.5 us (20%)
  local copies, waits for them, and re-layouts  9.94 us (8%)
  matrix products  9.56 us (8%)
  other arithmetic  6.72 us (6%)
    ppermute x8, waiting for transfers between devices, butterfly_sum(): c = c + lax.ppermute(c, axis, [(i, i ^ d) for i in range(n)])  21.8 us
    pallas_call x2, Pallas kernels, stage(): pl.pallas_call(functools.partial(stage_kernel, last=last), grid=(norb //...  19.3 us
    ppermute x8, starting transfers between devices, butterfly_sum(): c = c + lax.ppermute(c, axis, [(i, i ^ d) for i in range(n)])  12.7 us
    ppermute x2, waiting for transfers between devices, exchange(): out.append(lax.ppermute(zface, 'gz', shift_pairs(n, 1)))  9.34 us
    ppermute x4, starting transfers between devices, exchange(): out.append(lax.ppermute(first, axis, shift_pairs(n, -1)))  8.93 us
    unnamed x34, local copies, waits for them, and re-layouts  6.56 us
    dot_general x1, matrix products, per_device(): jnp.einsum('axyz,bxyz->ab', second, second, precision=HI) / all_cells  6.34 us
    pallas_call x1, Pallas kernels, z_faces(): pl.pallas_call(z_face_kernel, grid=(norb // BLOCK,), in_specs=[blk], out_...  4.2 us
  transfers between devices with their start and end apart: 20, of which 12 were waited for; matrix products, arithmetic and copies ran while one was open for 3% of the time, Pallas kernels for 0%

profile of v4, /device:TPU:1, one launch (start us, length us, event | category | flops | bytes accessed | tf_op | source)
XLA Modules:
  0.0 116.5 jit_solution(16972093365763732256)
XLA Ops:
  0.6 4.2 %shard_map.41 = f32[32,8,128]{2,1,0:T(8,128)} custom-call(f32[32,8,16,128]{3,2,1,0:T(8,128)} %refs_8_.1), custom_call_target="tpu_custom_call" | custom-call | tf_op jit(solution)/shard_map/pallas_call | solution.py:85
  4.8 3.6 %collective-permute-start.5 = (f32[32,8,128]{2,1,0:T(8,128)}, f32[32,8,128]{2,1,0:T(8,128)S(1)}, u32[]{:S(2)}, u32[]{:S(2)}) collective-permute-start(f32[32,8,128]{2,1,0:T(8,128)} %shard_map.41), channel_id=1, source_target_pairs={{0,3},{1,0},{2,1},{3,2},{4,7},{5,4},{6,5},{7,6},{8,11},{9,8},{10,9... | collective-permute-start | bytes 393224 | tf_op jit(solution)/shard_map/ppermute | solution.py:101
  8.5 1.0 collective-permute-start.1
  9.4 1.1 collective-permute-start
  10.6 0.2 fusion.15
  10.8 5.7 %collective-permute-start.3 = (f32[32,8,2,128]{3,2,1,0:T(2,128)S(1)}, f32[32,8,2,128]{3,2,1,0:T(2,128)S(1)}, u32[]{:S(2)}, u32[]{:S(2)}) collective-permute-start(f32[32,8,2,128]{3,2,1,0:T(2,128)S(1)} %get-tuple-element.12), channel_id=1, source_target_pairs={{0,28},{4,0},{8,4},{12,8},{16,12},{20,16},{24,20},{28,24},{1,29},{... | collective-permute-start | bytes 786440 | tf_op jit(solution)/shard_map/ppermute | solution.py:98
  16.5 5.0 %collective-permute-done.4.refs_5_ = f32[32,8,128]{2,1,0:T(8,128)S(1)} collective-permute-done((f32[32,8,128]{2,1,0:T(8,128)S(1)}, f32[32,8,128]{2,1,0:T(8,128)S(1)}, u32[]{:S(2)}, u32[]{:S(2)}) %collective-permute-start.4) | collective-permute-done | bytes 131104 | tf_op jit(solution)/shard_map/ppermute | solution.py:100
  21.5 2.9 %collective-permute-done.2.refs_3_ = f32[32,8,2,128]{3,2,1,0:T(2,128)S(1)} collective-permute-done((f32[32,8,2,128]{3,2,1,0:T(2,128)S(1)}, f32[32,8,2,128]{3,2,1,0:T(2,128)S(1)}, u32[]{:S(2)}, u32[]{:S(2)}) %collective-permute-start.2) | collective-permute-done | bytes 262176 | tf_op jit(solution)/shard_map/ppermute | solution.py:97
  24.5 0.7 copy-done.9
  25.1 0.2 copy-done.2
  25.3 0.8 copy-done.4
  26.1 11.5 %shard_map.42 = (f32[32,8,16,128]{3,2,1,0:T(8,128)}, f32[32,8,128]{2,1,0:T(8,128)}) custom-call(f32[32,8,16,128]{3,2,1,0:T(8,128)} %refs_8_.1, f32[32,2,16,128]{3,2,1,0:T(8,128)} %copy-done.4, f32[32,2,16,128]{3,2,1,0:T(8,128)} %copy-done.2, f32[32,8,2,128]{3,2,1,0:T(2,128)} %copy-done.9, f32[32,8,2,128]{3,2,1,0:T(2,128)} %copy-done.8, ...), custom_call_target="tpu_custom_call" | custom-call | tf_op jit(solution)/shard_map/pallas_call | solution.py:124
  37.6 0.5 collective-permute-start.11
  38.1 1.3 %fusion.14 = (f32[32,2,16,128]{3,2,1,0:T(8,128)S(1)}, f32[32,2,16,128]{3,2,1,0:T(8,128)S(1)}) fusion(f32[32,8,16,128]{3,2,1,0:T(8,128)} %get-tuple-element.4.refs_0_), kind=kLoop, calls=%fused_computation.18 | loop fusion | bytes 2097152 | tf_op jit(solution)/shard_map/slice | solution.py:96
  39.4 2.2 %collective-permute-start.7 = (f32[32,2,16,128]{3,2,1,0:T(8,128)S(1)}, f32[32,2,16,128]{3,2,1,0:T(8,128)S(1)}, u32[]{:S(2)}, u32[]{:S(2)}) collective-permute-start(f32[32,2,16,128]{3,2,1,0:T(8,128)S(1)} %get-tuple-element.10), channel_id=1, source_target_pairs={{0,224},{32,0},{64,32},{96,64},{128,96},{160,128},{192,160},{224,1... | collective-permute-start | bytes 1572872 | tf_op jit(solution)/shard_map/ppermute | solution.py:98
  41.6 1.1 collective-permute-start.6
  42.8 1.8 %fusion.13 = (f32[32,8,2,128]{3,2,1,0:T(2,128)S(1)}, f32[32,8,2,128]{3,2,1,0:T(2,128)S(1)}) fusion(f32[32,8,16,128]{3,2,1,0:T(8,128)} %get-tuple-element.4.refs_0_), kind=kLoop, calls=%fused_computation.17 | loop fusion | bytes 1048576 | tf_op jit(solution)/shard_map/slice | solution.py:96
  44.5 0.1 collective-permute-start.9
  44.6 1.5 %collective-permute-start.8 = (f32[32,8,2,128]{3,2,1,0:T(2,128)S(1)}, f32[32,8,2,128]{3,2,1,0:T(2,128)S(1)}, u32[]{:S(2)}, u32[]{:S(2)}) collective-permute-start(f32[32,8,2,128]{3,2,1,0:T(2,128)S(1)} %get-tuple-element.9), channel_id=1, source_target_pairs={{0,4},{4,8},{8,12},{12,16},{16,20},{20,24},{24,28},{28,0},{1,5},{5... | collective-permute-start | bytes 786440 | tf_op jit(solution)/shard_map/ppermute | solution.py:97
  46.1 1.3 %collective-permute-start.10 = (f32[32,8,128]{2,1,0:T(8,128)S(1)}, f32[32,8,128]{2,1,0:T(8,128)S(1)}, u32[]{:S(2)}, u32[]{:S(2)}) collective-permute-start(f32[32,8,128]{2,1,0:T(8,128)S(1)} %copy-done.15), channel_id=1, source_target_pairs={{0,1},{1,2},{2,3},{3,0},{4,5},{5,6},{6,7},{7,4},{8,9},{9,10},{10,1... | collective-permute-start | bytes 393224 | tf_op jit(solution)/shard_map/ppermute | solution.py:100
  47.3 4.3 %collective-permute-done.10.refs_5_ = f32[32,8,128]{2,1,0:T(8,128)S(1)} collective-permute-done((f32[32,8,128]{2,1,0:T(8,128)S(1)}, f32[32,8,128]{2,1,0:T(8,128)S(1)}, u32[]{:S(2)}, u32[]{:S(2)}) %collective-permute-start.10) | collective-permute-done | bytes 131104 | tf_op jit(solution)/shard_map/ppermute | solution.py:100
  51.7 1.1 collective-permute-done.8.refs_3_
  52.8 0.7 copy-done.7
  53.4 0.2 copy-done.3
  53.6 0.8 copy-done.5
  54.4 7.9 %shard_map.43 = f32[32,8,16,128]{3,2,1,0:T(8,128)} custom-call(f32[32,8,16,128]{3,2,1,0:T(8,128)} %get-tuple-element.4.refs_0_, f32[32,2,16,128]{3,2,1,0:T(8,128)} %copy-done.5, f32[32,2,16,128]{3,2,1,0:T(8,128)} %copy-done.3, f32[32,8,2,128]{3,2,1,0:T(2,128)} %copy-done.7, f32[32,8,2,128]{3,2,1,0:T(2,128)} %copy-done.6, f32[32,8,128]{2,1,0:T(8,128)} %copy-done.11, ...), custom_call_target="tpu_custom_call" | custom-call | tf_op jit(solution)/shard_map/pallas_call | solution.py:124
  62.3 6.3 %fusion.7 = f32[32,32]{0,1:T(8,128)S(1)} fusion(f32[32,8,16,128]{3,2,1,0:T(8,128)} %shard_map.43), kind=kOutput, calls=%fused_computation.6 | convolution fusion | flops 201327616 | bytes 2101248 | tf_op jit(solution)/shard_map/axyz,bxyz->ab/dot_general | solution.py:146
  68.7 0.7 collective-permute-start.12
  69.3 2.0 %collective-permute-done.12 = f32[32,32]{0,1:T(8,128)S(1)} collective-permute-done((f32[32,32]{0,1:T(8,128)S(1)}, f32[32,32]{0,1:T(8,128)S(1)}, u32[]{:S(2)}, u32[]{:S(2)}) %collective-permute-start.12) | collective-permute-done | bytes 4128 | tf_op jit(solution)/shard_map/ppermute | solution.py:136
  71.4 4.1 %collective-permute-done.13 = f32[32,32]{0,1:T(8,128)S(1)} collective-permute-done((f32[32,32]{0,1:T(8,128)S(1)}, f32[32,32]{0,1:T(8,128)S(1)}, u32[]{:S(2)}, u32[]{:S(2)}) %collective-permute-start.13) | collective-permute-done | bytes 4128 | tf_op jit(solution)/shard_map/ppermute | solution.py:136
  75.5 2.9 %collective-permute-done.14 = f32[32,32]{0,1:T(8,128)S(1)} collective-permute-done((f32[32,32]{0,1:T(8,128)S(1)}, f32[32,32]{0,1:T(8,128)S(1)}, u32[]{:S(2)}, u32[]{:S(2)}) %collective-permute-start.14) | collective-permute-done | bytes 4128 | tf_op jit(solution)/shard_map/ppermute | solution.py:136
  78.3 3.5 %collective-permute-done.15 = f32[32,32]{0,1:T(8,128)S(1)} collective-permute-done((f32[32,32]{0,1:T(8,128)S(1)}, f32[32,32]{0,1:T(8,128)S(1)}, u32[]{:S(2)}, u32[]{:S(2)}) %collective-permute-start.15) | collective-permute-done | bytes 4128 | tf_op jit(solution)/shard_map/ppermute | solution.py:136
  81.8 1.1 collective-permute-start.16
  83.0 5.4 %collective-permute-done.16 = f32[32,32]{0,1:T(8,128)S(1)} collective-permute-done((f32[32,32]{0,1:T(8,128)S(1)}, f32[32,32]{0,1:T(8,128)S(1)}, u32[]{:S(2)}, u32[]{:S(2)}) %collective-permute-start.16) | collective-permute-done | bytes 4128 | tf_op jit(solution)/shard_map/ppermute | solution.py:136
  88.4 7.3 %collective-permute-start.17 = (f32[32,32]{0,1:T(8,128)S(1)}, f32[32,32]{0,1:T(8,128)S(1)}, u32[]{:S(2)}, u32[]{:S(2)}) collective-permute-start(f32[32,32]{0,1:T(8,128)S(1)} %add.40), channel_id=1, source_target_pairs={{0,32},{32,0},{64,96},{96,64},{128,160},{160,128},{192,224},{224,1... | collective-permute-start | bytes 12296 | tf_op jit(solution)/shard_map/ppermute | solution.py:136
  95.7 0.8 collective-permute-done.17
  96.6 1.2 %collective-permute-start.18 = (f32[32,32]{0,1:T(8,128)S(1)}, f32[32,32]{0,1:T(8,128)S(1)}, u32[]{:S(2)}, u32[]{:S(2)}) collective-permute-start(f32[32,32]{0,1:T(8,128)S(1)} %add.41), channel_id=1, source_target_pairs={{0,64},{32,96},{64,0},{96,32},{128,192},{160,224},{192,128},{224,1... | collective-permute-start | bytes 12296 | tf_op jit(solution)/shard_map/ppermute | solution.py:136
  97.8 1.4 %collective-permute-done.18 = f32[32,32]{0,1:T(8,128)S(1)} collective-permute-done((f32[32,32]{0,1:T(8,128)S(1)}, f32[32,32]{0,1:T(8,128)S(1)}, u32[]{:S(2)}, u32[]{:S(2)}) %collective-permute-start.18) | collective-permute-done | bytes 4128 | tf_op jit(solution)/shard_map/ppermute | solution.py:136
  99.2 2.4 %collective-permute-start.19 = (f32[32,32]{0,1:T(8,128)S(1)}, f32[32,32]{0,1:T(8,128)S(1)}, u32[]{:S(2)}, u32[]{:S(2)}) collective-permute-start(f32[32,32]{0,1:T(8,128)S(1)} %add.42), channel_id=1, source_target_pairs={{0,128},{32,160},{64,192},{96,224},{128,0},{160,32},{192,64},{224,... | collective-permute-start | bytes 12296 | tf_op jit(solution)/shard_map/ppermute | solution.py:136
  101.5 1.7 %collective-permute-done.19 = f32[32,32]{0,1:T(8,128)S(1)} collective-permute-done((f32[32,32]{0,1:T(8,128)S(1)}, f32[32,32]{0,1:T(8,128)S(1)}, u32[]{:S(2)}, u32[]{:S(2)}) %collective-permute-start.19) | collective-permute-done | bytes 4128 | tf_op jit(solution)/shard_map/ppermute | solution.py:136
  103.3 2.9 %cholesky.17 = f32[32,32]{1,0:T(8,128)S(1)} custom-call(f32[32,32]{1,0:T(8,128)S(1)} %fusion.11), custom_call_target="Cholesky" | custom-call | tf_op jit(solution)/shard_map/jit(cholesky)/cholesky | solution.py:147
  106.3 0.6 compare_reduce_fusion
  106.9 0.7 fusion.12
  107.6 0.7 copy.10
  108.3 2.4 %custom-call.7 = f32[1,32,32]{1,2,0:T(8,128)S(1)} custom-call(f32[1,32,32]{2,1,0:T(8,128)S(1)} %get-tuple-element.17), custom_call_target="InvertDiagBlocksLowerTriangular" | custom-call | tf_op jit(solution)/shard_map/jit(_solve_triangular)/triangular_solve | solution.py:149
  110.7 0.2 convolution_bitcast_fusion
  110.9 3.0 %fusion = f32[32,8,16,128]{3,0,2,1:T(8,128)S(1)} fusion(f32[32,32,1,1]{1,0,3,2:T(8,128)S(1)} %convolution_bitcast_fusion, f32[32,8,16,128]{3,2,1,0:T(8,128)S(1)} %copy-done.1), kind=kOutput, calls=%fused_computation | convolution fusion | flops 201326592 | bytes 4198400 | tf_op jit(solution)/shard_map/ab,bxyz->axyz/dot_general | solution.py:150
  114.0 2.5 %copy.9 = f32[32,8,16,128]{3,2,1,0:T(8,128)} copy(f32[32,8,16,128]{3,0,2,1:T(8,128)S(1)} %fusion) | data formatting | bytes 4194304
  (51 shorter events, 0.4 us)
Async XLA Ops:
  0.6 7.8 %copy-start = (f32[32,8,16,128]{3,2,1,0:T(8,128)S(1)}, f32[32,8,16,128]{3,2,1,0:T(8,128)}, u32[]{:S(2)}) copy-start(f32[32,8,16,128]{3,2,1,0:T(8,128)} %refs_8_.1) | copy-start | bytes 6291460
  4.8 11.6 %copy-start.13 = (f32[32,8,128]{2,1,0:T(8,128)S(1)}, f32[32,8,128]{2,1,0:T(8,128)}, u32[]{:S(2)}) copy-start(f32[32,8,128]{2,1,0:T(8,128)} %shard_map.41) | copy-start | bytes 393220
  4.8 11.6 %collective-permute-start.5 = (f32[32,8,128]{2,1,0:T(8,128)}, f32[32,8,128]{2,1,0:T(8,128)S(1)}, u32[]{:S(2)}, u32[]{:S(2)}) collective-permute-start(f32[32,8,128]{2,1,0:T(8,128)} %shard_map.41), channel_id=1, source_target_pairs={{0,3},{1,0},{2,1},{3,2},{4,7},{5,4},{6,5},{7,6},{8,11},{9,8},{10,9... | collective-permute-start | bytes 393224 | tf_op jit(solution)/shard_map/ppermute | solution.py:101
  8.5 15.9 %collective-permute-start.1 = (f32[32,2,16,128]{3,2,1,0:T(8,128)S(1)}, f32[32,2,16,128]{3,2,1,0:T(8,128)S(1)}, u32[]{:S(2)}, u32[]{:S(2)}) collective-permute-start(f32[32,2,16,128]{3,2,1,0:T(8,128)S(1)} %get-tuple-element.14), channel_id=1, source_target_pairs={{0,224},{32,0},{64,32},{96,64},{128,96},{160,128},{192,160},{224,1... | collective-permute-start | bytes 1572872 | tf_op jit(solution)/shard_map/ppermute | solution.py:98
  9.4 15.0 %collective-permute-start = (f32[32,2,16,128]{3,2,1,0:T(8,128)S(1)}, f32[32,2,16,128]{3,2,1,0:T(8,128)S(1)}, u32[]{:S(2)}, u32[]{:S(2)}) collective-permute-start(f32[32,2,16,128]{3,2,1,0:T(8,128)S(1)} %get-tuple-element.15), channel_id=1, source_target_pairs={{0,32},{32,64},{64,96},{96,128},{128,160},{160,192},{192,224},{224... | collective-permute-start | bytes 1572872 | tf_op jit(solution)/shard_map/ppermute | solution.py:97
  10.8 10.8 %collective-permute-start.3 = (f32[32,8,2,128]{3,2,1,0:T(2,128)S(1)}, f32[32,8,2,128]{3,2,1,0:T(2,128)S(1)}, u32[]{:S(2)}, u32[]{:S(2)}) collective-permute-start(f32[32,8,2,128]{3,2,1,0:T(2,128)S(1)} %get-tuple-element.12), channel_id=1, source_target_pairs={{0,28},{4,0},{8,4},{12,8},{16,12},{20,16},{24,20},{28,24},{1,29},{... | collective-permute-start | bytes 786440 | tf_op jit(solution)/shard_map/ppermute | solution.py:98
  16.4 8.0 %collective-permute-start.2 = (f32[32,8,2,128]{3,2,1,0:T(2,128)S(1)}, f32[32,8,2,128]{3,2,1,0:T(2,128)S(1)}, u32[]{:S(2)}, u32[]{:S(2)}) collective-permute-start(f32[32,8,2,128]{3,2,1,0:T(2,128)S(1)} %get-tuple-element.13), channel_id=1, source_target_pairs={{0,4},{4,8},{8,12},{12,16},{16,20},{20,24},{24,28},{28,0},{1,5},{5... | collective-permute-start | bytes 786440 | tf_op jit(solution)/shard_map/ppermute | solution.py:97
  16.4 8.0 %copy-start.12 = (f32[32,8,128]{2,1,0:T(8,128)}, f32[32,8,128]{2,1,0:T(8,128)S(1)}, u32[]{:S(2)}) copy-start(f32[32,8,128]{2,1,0:T(8,128)S(1)} %collective-permute-done.5.refs_6_) | copy-start | bytes 393220
  16.4 5.1 %collective-permute-start.4 = (f32[32,8,128]{2,1,0:T(8,128)S(1)}, f32[32,8,128]{2,1,0:T(8,128)S(1)}, u32[]{:S(2)}, u32[]{:S(2)}) collective-permute-start(f32[32,8,128]{2,1,0:T(8,128)S(1)} %copy-done.13), channel_id=1, source_target_pairs={{0,1},{1,2},{2,3},{3,0},{4,5},{5,6},{6,7},{7,4},{8,9},{9,10},{10,1... | collective-permute-start | bytes 393224 | tf_op jit(solution)/shard_map/ppermute | solution.py:100
  21.5 2.9 %copy-start.14 = (f32[32,8,128]{2,1,0:T(8,128)}, f32[32,8,128]{2,1,0:T(8,128)S(1)}, u32[]{:S(2)}) copy-start(f32[32,8,128]{2,1,0:T(8,128)S(1)} %collective-permute-done.4.refs_5_) | copy-start | bytes 393220
  21.5 2.9 %copy-start.8 = (f32[32,8,2,128]{3,2,1,0:T(2,128)}, f32[32,8,2,128]{3,2,1,0:T(2,128)S(1)}, u32[]{:S(2)}) copy-start(f32[32,8,2,128]{3,2,1,0:T(2,128)S(1)} %collective-permute-done.3.refs_4_) | copy-start | bytes 786436
  24.4 0.7 copy-start.9
  24.4 0.9 copy-start.2
  25.3 0.8 copy-start.4
  37.6 8.5 %copy-start.15 = (f32[32,8,128]{2,1,0:T(8,128)S(1)}, f32[32,8,128]{2,1,0:T(8,128)}, u32[]{:S(2)}) copy-start(f32[32,8,128]{2,1,0:T(8,128)} %get-tuple-element.5) | copy-start | bytes 393220
  37.6 8.5 %collective-permute-start.11 = (f32[32,8,128]{2,1,0:T(8,128)}, f32[32,8,128]{2,1,0:T(8,128)S(1)}, u32[]{:S(2)}, u32[]{:S(2)}) collective-permute-start(f32[32,8,128]{2,1,0:T(8,128)} %get-tuple-element.5), channel_id=1, source_target_pairs={{0,3},{1,0},{2,1},{3,2},{4,7},{5,4},{6,5},{7,6},{8,11},{9,8},{10,9... | collective-permute-start | bytes 393224 | tf_op jit(solution)/shard_map/ppermute | solution.py:101
  39.4 13.4 %collective-permute-start.7 = (f32[32,2,16,128]{3,2,1,0:T(8,128)S(1)}, f32[32,2,16,128]{3,2,1,0:T(8,128)S(1)}, u32[]{:S(2)}, u32[]{:S(2)}) collective-permute-start(f32[32,2,16,128]{3,2,1,0:T(8,128)S(1)} %get-tuple-element.10), channel_id=1, source_target_pairs={{0,224},{32,0},{64,32},{96,64},{128,96},{160,128},{192,160},{224,1... | collective-permute-start | bytes 1572872 | tf_op jit(solution)/shard_map/ppermute | solution.py:98
  41.6 11.1 %collective-permute-start.6 = (f32[32,2,16,128]{3,2,1,0:T(8,128)S(1)}, f32[32,2,16,128]{3,2,1,0:T(8,128)S(1)}, u32[]{:S(2)}, u32[]{:S(2)}) collective-permute-start(f32[32,2,16,128]{3,2,1,0:T(8,128)S(1)} %get-tuple-element.11), channel_id=1, source_target_pairs={{0,32},{32,64},{64,96},{96,128},{128,160},{160,192},{192,224},{224... | collective-permute-start | bytes 1572872 | tf_op jit(solution)/shard_map/ppermute | solution.py:97
  44.5 7.1 %collective-permute-start.9 = (f32[32,8,2,128]{3,2,1,0:T(2,128)S(1)}, f32[32,8,2,128]{3,2,1,0:T(2,128)S(1)}, u32[]{:S(2)}, u32[]{:S(2)}) collective-permute-start(f32[32,8,2,128]{3,2,1,0:T(2,128)S(1)} %get-tuple-element.8), channel_id=1, source_target_pairs={{0,28},{4,0},{8,4},{12,8},{16,12},{20,16},{24,20},{28,24},{1,29},{... | collective-permute-start | bytes 786440 | tf_op jit(solution)/shard_map/ppermute | solution.py:98
  44.6 8.1 %collective-permute-start.8 = (f32[32,8,2,128]{3,2,1,0:T(2,128)S(1)}, f32[32,8,2,128]{3,2,1,0:T(2,128)S(1)}, u32[]{:S(2)}, u32[]{:S(2)}) collective-permute-start(f32[32,8,2,128]{3,2,1,0:T(2,128)S(1)} %get-tuple-element.9), channel_id=1, source_target_pairs={{0,4},{4,8},{8,12},{12,16},{16,20},{20,24},{24,28},{28,0},{1,5},{5... | collective-permute-start | bytes 786440 | tf_op jit(solution)/shard_map/ppermute | solution.py:97
  46.1 6.7 %copy-start.10 = (f32[32,8,128]{2,1,0:T(8,128)}, f32[32,8,128]{2,1,0:T(8,128)S(1)}, u32[]{:S(2)}) copy-start(f32[32,8,128]{2,1,0:T(8,128)S(1)} %collective-permute-done.11.refs_6_) | copy-start | bytes 393220
  46.1 5.6 %collective-permute-start.10 = (f32[32,8,128]{2,1,0:T(8,128)S(1)}, f32[32,8,128]{2,1,0:T(8,128)S(1)}, u32[]{:S(2)}, u32[]{:S(2)}) collective-permute-start(f32[32,8,128]{2,1,0:T(8,128)S(1)} %copy-done.15), channel_id=1, source_target_pairs={{0,1},{1,2},{2,3},{3,0},{4,5},{5,6},{6,7},{7,4},{8,9},{9,10},{10,1... | collective-permute-start | bytes 393224 | tf_op jit(solution)/shard_map/ppermute | solution.py:100
  51.7 1.1 copy-start.11
  51.7 1.1 copy-start.6
  52.8 0.7 copy-start.7
  52.8 0.9 copy-start.3
  53.6 0.8 copy-start.5
  62.3 48.6 %copy-start.1 = (f32[32,8,16,128]{3,2,1,0:T(8,128)S(1)}, f32[32,8,16,128]{3,2,1,0:T(8,128)}, u32[]{:S(2)}) copy-start(f32[32,8,16,128]{3,2,1,0:T(8,128)} %shard_map.43) | copy-start | bytes 6291460
  68.7 2.7 %collective-permute-start.12 = (f32[32,32]{0,1:T(8,128)S(1)}, f32[32,32]{0,1:T(8,128)S(1)}, u32[]{:S(2)}, u32[]{:S(2)}) collective-permute-start(f32[32,32]{0,1:T(8,128)S(1)} %fusion.7), channel_id=1, source_target_pairs={{0,1},{1,0},{2,3},{3,2},{4,5},{5,4},{6,7},{7,6},{8,9},{9,8},{10,11... | collective-permute-start | bytes 12296 | tf_op jit(solution)/shard_map/ppermute | solution.py:136
  71.4 4.1 %collective-permute-start.13 = (f32[32,32]{0,1:T(8,128)S(1)}, f32[32,32]{0,1:T(8,128)S(1)}, u32[]{:S(2)}, u32[]{:S(2)}) collective-permute-start(f32[32,32]{0,1:T(8,128)S(1)} %add.36), channel_id=1, source_target_pairs={{0,2},{1,3},{2,0},{3,1},{4,6},{5,7},{6,4},{7,5},{8,10},{9,11},{10,... | collective-permute-start | bytes 12296 | tf_op jit(solution)/shard_map/ppermute | solution.py:136
  75.5 2.9 %collective-permute-start.14 = (f32[32,32]{0,1:T(8,128)S(1)}, f32[32,32]{0,1:T(8,128)S(1)}, u32[]{:S(2)}, u32[]{:S(2)}) collective-permute-start(f32[32,32]{0,1:T(8,128)S(1)} %add.37), channel_id=1, source_target_pairs={{0,4},{4,0},{8,12},{12,8},{16,20},{20,16},{24,28},{28,24},{1,5},{5... | collective-permute-start | bytes 12296 | tf_op jit(solution)/shard_map/ppermute | solution.py:136
  78.3 3.5 %collective-permute-start.15 = (f32[32,32]{0,1:T(8,128)S(1)}, f32[32,32]{0,1:T(8,128)S(1)}, u32[]{:S(2)}, u32[]{:S(2)}) collective-permute-start(f32[32,32]{0,1:T(8,128)S(1)} %add.38), channel_id=1, source_target_pairs={{0,8},{4,12},{8,0},{12,4},{16,24},{20,28},{24,16},{28,20},{1,9},{5... | collective-permute-start | bytes 12296 | tf_op jit(solution)/shard_map/ppermute | solution.py:136
  81.8 6.5 %collective-permute-start.16 = (f32[32,32]{0,1:T(8,128)S(1)}, f32[32,32]{0,1:T(8,128)S(1)}, u32[]{:S(2)}, u32[]{:S(2)}) collective-permute-start(f32[32,32]{0,1:T(8,128)S(1)} %add.39), channel_id=1, source_target_pairs={{0,16},{4,20},{8,24},{12,28},{16,0},{20,4},{24,8},{28,12},{1,17},{... | collective-permute-start | bytes 12296 | tf_op jit(solution)/shard_map/ppermute | solution.py:136
  88.4 8.2 %collective-permute-start.17 = (f32[32,32]{0,1:T(8,128)S(1)}, f32[32,32]{0,1:T(8,128)S(1)}, u32[]{:S(2)}, u32[]{:S(2)}) collective-permute-start(f32[32,32]{0,1:T(8,128)S(1)} %add.40), channel_id=1, source_target_pairs={{0,32},{32,0},{64,96},{96,64},{128,160},{160,128},{192,224},{224,1... | collective-permute-start | bytes 12296 | tf_op jit(solution)/shard_map/ppermute | solution.py:136
  96.6 2.6 %collective-permute-start.18 = (f32[32,32]{0,1:T(8,128)S(1)}, f32[32,32]{0,1:T(8,128)S(1)}, u32[]{:S(2)}, u32[]{:S(2)}) collective-permute-start(f32[32,32]{0,1:T(8,128)S(1)} %add.41), channel_id=1, source_target_pairs={{0,64},{32,96},{64,0},{96,32},{128,192},{160,224},{192,128},{224,1... | collective-permute-start | bytes 12296 | tf_op jit(solution)/shard_map/ppermute | solution.py:136
  99.2 4.1 %collective-permute-start.19 = (f32[32,32]{0,1:T(8,128)S(1)}, f32[32,32]{0,1:T(8,128)S(1)}, u32[]{:S(2)}, u32[]{:S(2)}) collective-permute-start(f32[32,32]{0,1:T(8,128)S(1)} %add.42), channel_id=1, source_target_pairs={{0,128},{32,160},{64,192},{96,224},{128,0},{160,32},{192,64},{224,... | collective-permute-start | bytes 12296 | tf_op jit(solution)/shard_map/ppermute | solution.py:136

commit v5 on v4

--- a/solution.py
+++ b/solution.py
@@ -9,6 +9,7 @@
 
 TAPS = (-1.0 / 12.0, 4.0 / 3.0, -2.5, 4.0 / 3.0, -1.0 / 12.0)
 BLOCK = 8
+CHUNKS = 2
 INTERPRET = False
 HI = lax.Precision.HIGHEST
 
@@ -139,8 +140,14 @@
 
 
 def per_device(orbitals, potential):
-    first, first_z = stage(orbitals, exchange(orbitals, z_faces(orbitals)), potential)
-    second = stage(first, exchange(first, first_z), potential, orbitals)
+    norb = orbitals.shape[0]
+    step = norb // CHUNKS
+    parts = [orbitals[c * step:(c + 1) * step] for c in range(CHUNKS)]
+    rims = [exchange(part, z_faces(part)) for part in parts]
+    firsts = [stage(part, rim, potential) for part, rim in zip(parts, rims)]
+    rims = [exchange(first, first_z) for first, first_z in firsts]
+    second = jnp.concatenate(
+        [stage(first, rim, potential, part) for (first, _), rim, part in zip(firsts, rims, parts)], axis=0)
     norb_count = orbitals.shape[0]
     all_cells = second[0].size * lax.axis_size("gx") * lax.axis_size("gy") * lax.axis_size("gz")
     correlation = jnp.einsum("axyz,bxyz->ab", second, second, precision=HI) / all_cells

time: 118 us -> 134 us (1.14)
  starting transfers between devices: 30.8 us -> 51.8 us
  waiting for transfers between devices: 35.1 us -> 21.5 us
  local copies, waits for them, and re-layouts: 9.94 us -> 16.5 us
  Pallas kernels: 23.5 us -> 28.3 us
  matrix products: 9.56 us -> 6.07 us
  other arithmetic: 6.72 us -> 8.11 us
    ppermute x2 -> x4, waiting for transfers between devices: 9.34 us -> 0.01 us  [exchange(): out.append(lax.ppermute(zface, 'gz', shift_pairs(n, 1)))]
    ppermute x4 -> x8, starting transfers between devices: 3.7 us -> 10.6 us  [exchange(): out.append(lax.ppermute(last, axis, shift_pairs(n, 1)))]
    ppermute x4 -> x8, starting transfers between devices: 8.93 us -> 15.3 us  [exchange(): out.append(lax.ppermute(first, axis, shift_pairs(n, -1)))]
    pallas_call x2 -> x4, Pallas kernels: 19.3 us -> 23.6 us  [stage(): pl.pallas_call(functools.partial(stage_kernel, last=last), grid=(norb //...]
    ppermute x2 -> x4, starting transfers between devices: 4.09 us -> 8.11 us  [exchange(): out.append(lax.ppermute(zface, 'gz', shift_pairs(n, -1)))]
    ppermute x4 -> x8, waiting for transfers between devices: 3.95 us -> 0.02 us  [exchange(): out.append(lax.ppermute(last, axis, shift_pairs(n, 1)))]
    dot_general x1, matrix products: 6.34 us -> 2.84 us  [per_device(): jnp.einsum('axyz,bxyz->ab', second, second, precision=HI) / all_cells]
    slice x0 -> x1, local copies, waits for them, and re-layouts: none -> 3.28 us  [per_device(): parts = [orbitals[c * step:(c + 1) * step] for c in range(CHUNKS)]]
  transfers between devices with their start and end apart: 20 -> 32, of which waited for: 12 -> 8; matrix products, arithmetic and copies ran while one was open for 3% -> 5% of each run, Pallas kernels for 0% -> 16%
where the time goes in v5:
time: 134 us; the launch traced here: 133 us
  starting transfers between devices  51.8 us (39%)
  Pallas kernels  28.3 us (21%)
  waiting for transfers between devices  21.5 us (16%)
  local copies, waits for them, and re-layouts  16.5 us (12%)
  other arithmetic  8.11 us (6%)
  matrix products  6.07 us (5%)
    pallas_call x4, Pallas kernels, stage(): pl.pallas_call(functools.partial(stage_kernel, last=last), grid=(norb //...  23.6 us
    ppermute x8, waiting for transfers between devices, butterfly_sum(): c = c + lax.ppermute(c, axis, [(i, i ^ d) for i in range(n)])  21.5 us
    ppermute x8, starting transfers between devices, exchange(): out.append(lax.ppermute(first, axis, shift_pairs(n, -1)))  15.3 us
    ppermute x8, starting transfers between devices, butterfly_sum(): c = c + lax.ppermute(c, axis, [(i, i ^ d) for i in range(n)])  14.3 us
    ppermute x8, starting transfers between devices, exchange(): out.append(lax.ppermute(last, axis, shift_pairs(n, 1)))  10.6 us
    ppermute x4, starting transfers between devices, exchange(): out.append(lax.ppermute(zface, 'gz', shift_pairs(n, -1)))  8.11 us
    unnamed x52, local copies, waits for them, and re-layouts  6.71 us
    slice x6, local copies, waits for them, and re-layouts, exchange(): first = lax.slice_in_dim(f, 0, 2, axis=dim)  6.43 us
  transfers between devices with their start and end apart: 32, of which 8 were waited for; matrix products, arithmetic and copies ran while one was open for 5% of the time, Pallas kernels for 16%

profile of v5, /device:TPU:1, one launch (start us, length us, event | category | flops | bytes accessed | tf_op | source)
XLA Modules:
  0.0 133.3 jit_solution(15274922467591129353)
XLA Ops:
  0.6 3.3 %fusion.15 = (f32[16,8,16,128]{3,2,1,0:T(8,128)}, f32[16,8,16,128]{3,2,1,0:T(8,128)}) fusion(f32[32,8,16,128]{3,2,1,0:T(8,128)} %param.2), kind=kLoop, calls=%fused_computation.20 | loop fusion | bytes 4194304 | tf_op jit(solution)/shard_map/slice | solution.py:145
  3.9 2.3 %shard_map.41 = f32[16,8,128]{2,1,0:T(8,128)} custom-call(f32[16,8,16,128]{3,2,1,0:T(8,128)} %get-tuple-element.20.f_ref.refs_0_.refs_8_), custom_call_target="tpu_custom_call" | custom-call | tf_op jit(solution)/shard_map/pallas_call | solution.py:86
  6.3 2.1 %collective-permute-start.4 = (f32[16,8,128]{2,1,0:T(8,128)}, f32[16,8,128]{2,1,0:T(8,128)}, u32[]{:S(2)}, u32[]{:S(2)}) collective-permute-start(f32[16,8,128]{2,1,0:T(8,128)} %shard_map.41), channel_id=1, source_target_pairs={{0,1},{1,2},{2,3},{3,0},{4,5},{5,6},{6,7},{7,4},{8,9},{9,10},{10,1... | collective-permute-start | bytes 196616 | tf_op jit(solution)/shard_map/ppermute | solution.py:101
  8.4 0.8 fusion.14
  9.2 2.1 %collective-permute-start = (f32[16,2,16,128]{3,2,1,0:T(8,128)}, f32[16,2,16,128]{3,2,1,0:T(8,128)S(1)}, u32[]{:S(2)}, u32[]{:S(2)}) collective-permute-start(f32[16,2,16,128]{3,2,1,0:T(8,128)} %get-tuple-element.19), channel_id=1, source_target_pairs={{0,32},{32,64},{64,96},{96,128},{128,160},{160,192},{192,224},{224... | collective-permute-start | bytes 786440 | tf_op jit(solution)/shard_map/ppermute | solution.py:98
  11.2 0.9 fusion.13
  12.1 1.6 %collective-permute-start.2 = (f32[16,8,2,128]{3,2,1,0:T(2,128)}, f32[16,8,2,128]{3,2,1,0:T(2,128)S(1)}, u32[]{:S(2)}, u32[]{:S(2)}) collective-permute-start(f32[16,8,2,128]{3,2,1,0:T(2,128)} %get-tuple-element.13), channel_id=1, source_target_pairs={{0,4},{4,8},{8,12},{12,16},{16,20},{20,24},{24,28},{28,0},{1,5},{5... | collective-permute-start | bytes 393224 | tf_op jit(solution)/shard_map/ppermute | solution.py:98
  13.8 3.9 %collective-permute-start.3 = (f32[16,8,2,128]{3,2,1,0:T(2,128)}, f32[16,8,2,128]{3,2,1,0:T(2,128)S(1)}, u32[]{:S(2)}, u32[]{:S(2)}) collective-permute-start(f32[16,8,2,128]{3,2,1,0:T(2,128)} %get-tuple-element.12), channel_id=1, source_target_pairs={{0,28},{4,0},{8,4},{12,8},{16,12},{20,16},{24,20},{28,24},{1,29},{... | collective-permute-start | bytes 393224 | tf_op jit(solution)/shard_map/ppermute | solution.py:99
  17.7 1.4 %collective-permute-start.5 = (f32[16,8,128]{2,1,0:T(8,128)}, f32[16,8,128]{2,1,0:T(8,128)S(1)}, u32[]{:S(2)}, u32[]{:S(2)}) collective-permute-start(f32[16,8,128]{2,1,0:T(8,128)} %shard_map.41), channel_id=1, source_target_pairs={{0,3},{1,0},{2,1},{3,2},{4,7},{5,4},{6,5},{7,6},{8,11},{9,8},{10,9... | collective-permute-start | bytes 196616 | tf_op jit(solution)/shard_map/ppermute | solution.py:102
  19.1 2.3 %shard_map.44 = f32[16,8,128]{2,1,0:T(8,128)} custom-call(f32[16,8,16,128]{3,2,1,0:T(8,128)} %get-tuple-element.21.f_ref.refs_0_.refs_8_), custom_call_target="tpu_custom_call" | custom-call | tf_op jit(solution)/shard_map/pallas_call | solution.py:86
  21.4 1.2 collective-permute-start.16
  22.6 1.5 %collective-permute-start.17 = (f32[16,8,128]{2,1,0:T(8,128)}, f32[16,8,128]{2,1,0:T(8,128)S(1)}, u32[]{:S(2)}, u32[]{:S(2)}) collective-permute-start(f32[16,8,128]{2,1,0:T(8,128)} %shard_map.44), channel_id=1, source_target_pairs={{0,3},{1,0},{2,1},{3,2},{4,7},{5,4},{6,5},{7,6},{8,11},{9,8},{10,9... | collective-permute-start | bytes 196616 | tf_op jit(solution)/shard_map/ppermute | solution.py:102
  24.1 3.3 %collective-permute-start.12 = (f32[16,2,16,128]{3,2,1,0:T(8,128)S(1)}, f32[16,2,16,128]{3,2,1,0:T(8,128)S(1)}, u32[]{:S(2)}, u32[]{:S(2)}) collective-permute-start(f32[16,2,16,128]{3,2,1,0:T(8,128)S(1)} %get-tuple-element.18), channel_id=1, source_target_pairs={{0,32},{32,64},{64,96},{96,128},{128,160},{160,192},{192,224},{224... | collective-permute-start | bytes 786440 | tf_op jit(solution)/shard_map/ppermute | solution.py:98
  28.3 6.8 %shard_map.42 = (f32[16,8,16,128]{3,2,1,0:T(8,128)}, f32[16,8,128]{2,1,0:T(8,128)}) custom-call(f32[16,8,16,128]{3,2,1,0:T(8,128)} %get-tuple-element.20.f_ref.refs_0_.refs_8_, f32[16,2,16,128]{3,2,1,0:T(8,128)} %copy-done.8, f32[16,2,16,128]{3,2,1,0:T(8,128)} %copy-done.9, f32[16,8,2,128]{3,2,1,0:T(2,128)} %copy-done.12, f32[16,8,2,128]{3,2,1,0:T(2,128)} %copy-done.13, ...), custom_call_target="tpu_custom_call" | custom-call | tf_op jit(solution)/shard_map/pallas_call | solution.py:125
  35.1 1.1 fusion.17
  36.2 2.1 %collective-permute-start.15 = (f32[16,8,2,128]{3,2,1,0:T(2,128)S(1)}, f32[16,8,2,128]{3,2,1,0:T(2,128)S(1)}, u32[]{:S(2)}, u32[]{:S(2)}) collective-permute-start(f32[16,8,2,128]{3,2,1,0:T(2,128)S(1)} %get-tuple-element.14), channel_id=1, source_target_pairs={{0,28},{4,0},{8,4},{12,8},{16,12},{20,16},{24,20},{28,24},{1,29},{... | collective-permute-start | bytes 393224 | tf_op jit(solution)/shard_map/ppermute | solution.py:99
  38.3 1.3 fusion.16
  39.8 2.6 %collective-permute-start.11 = (f32[16,8,128]{2,1,0:T(8,128)}, f32[16,8,128]{2,1,0:T(8,128)S(1)}, u32[]{:S(2)}, u32[]{:S(2)}) collective-permute-start(f32[16,8,128]{2,1,0:T(8,128)} %get-tuple-element.7), channel_id=1, source_target_pairs={{0,3},{1,0},{2,1},{3,2},{4,7},{5,4},{6,5},{7,6},{8,11},{9,8},{10,9... | collective-permute-start | bytes 196616 | tf_op jit(solution)/shard_map/ppermute | solution.py:102
  42.4 2.7 %collective-permute-start.6 = (f32[16,2,16,128]{3,2,1,0:T(8,128)S(1)}, f32[16,2,16,128]{3,2,1,0:T(8,128)S(1)}, u32[]{:S(2)}, u32[]{:S(2)}) collective-permute-start(f32[16,2,16,128]{3,2,1,0:T(8,128)S(1)} %get-tuple-element.25), channel_id=1, source_target_pairs={{0,32},{32,64},{64,96},{96,128},{128,160},{160,192},{192,224},{224... | collective-permute-start | bytes 786440 | tf_op jit(solution)/shard_map/ppermute | solution.py:98
  45.8 0.7 copy-done.7
  46.5 6.8 %shard_map.45 = (f32[16,8,16,128]{3,2,1,0:T(8,128)}, f32[16,8,128]{2,1,0:T(8,128)}) custom-call(f32[16,8,16,128]{3,2,1,0:T(8,128)} %get-tuple-element.21.f_ref.refs_0_.refs_8_, f32[16,2,16,128]{3,2,1,0:T(8,128)} %copy-done.6, f32[16,2,16,128]{3,2,1,0:T(8,128)} %copy-done.7, f32[16,8,2,128]{3,2,1,0:T(2,128)} %copy-done.11, f32[16,8,2,128]{3,2,1,0:T(2,128)} %copy-done.16, ...), custom_call_target="tpu_custom_call" | custom-call | tf_op jit(solution)/shard_map/pallas_call | solution.py:125
  53.3 1.1 fusion.19
  54.4 1.4 %collective-permute-start.7 = (f32[16,2,16,128]{3,2,1,0:T(8,128)S(1)}, f32[16,2,16,128]{3,2,1,0:T(8,128)S(1)}, u32[]{:S(2)}, u32[]{:S(2)}) collective-permute-start(f32[16,2,16,128]{3,2,1,0:T(8,128)S(1)} %get-tuple-element.24), channel_id=1, source_target_pairs={{0,224},{32,0},{64,32},{96,64},{128,96},{160,128},{192,160},{224,1... | collective-permute-start | bytes 786440 | tf_op jit(solution)/shard_map/ppermute | solution.py:99
  55.8 2.6 %collective-permute-start.9 = (f32[16,8,2,128]{3,2,1,0:T(2,128)S(1)}, f32[16,8,2,128]{3,2,1,0:T(2,128)S(1)}, u32[]{:S(2)}, u32[]{:S(2)}) collective-permute-start(f32[16,8,2,128]{3,2,1,0:T(2,128)S(1)} %get-tuple-element.22), channel_id=1, source_target_pairs={{0,28},{4,0},{8,4},{12,8},{16,12},{20,16},{24,20},{28,24},{1,29},{... | collective-permute-start | bytes 393224 | tf_op jit(solution)/shard_map/ppermute | solution.py:99
  58.3 0.8 collective-permute-start.18
  59.1 2.5 %collective-permute-start.19 = (f32[16,2,16,128]{3,2,1,0:T(8,128)S(1)}, f32[16,2,16,128]{3,2,1,0:T(8,128)S(1)}, u32[]{:S(2)}, u32[]{:S(2)}) collective-permute-start(f32[16,2,16,128]{3,2,1,0:T(8,128)S(1)} %get-tuple-element.28), channel_id=1, source_target_pairs={{0,224},{32,0},{64,32},{96,64},{128,96},{160,128},{192,160},{224,1... | collective-permute-start | bytes 786440 | tf_op jit(solution)/shard_map/ppermute | solution.py:99
  61.6 1.3 fusion.18
  63.1 2.6 %collective-permute-start.21 = (f32[16,8,2,128]{3,2,1,0:T(2,128)S(1)}, f32[16,8,2,128]{3,2,1,0:T(2,128)S(1)}, u32[]{:S(2)}, u32[]{:S(2)}) collective-permute-start(f32[16,8,2,128]{3,2,1,0:T(2,128)S(1)} %get-tuple-element.26), channel_id=1, source_target_pairs={{0,28},{4,0},{8,4},{12,8},{16,12},{20,16},{24,20},{28,24},{1,29},{... | collective-permute-start | bytes 393224 | tf_op jit(solution)/shard_map/ppermute | solution.py:99
  65.7 2.7 %collective-permute-start.23 = (f32[16,8,128]{2,1,0:T(8,128)}, f32[16,8,128]{2,1,0:T(8,128)S(1)}, u32[]{:S(2)}, u32[]{:S(2)}) collective-permute-start(f32[16,8,128]{2,1,0:T(8,128)} %get-tuple-element.9), channel_id=1, source_target_pairs={{0,3},{1,0},{2,1},{3,2},{4,7},{5,4},{6,5},{7,6},{8,11},{9,8},{10,9... | collective-permute-start | bytes 196616 | tf_op jit(solution)/shard_map/ppermute | solution.py:102
  68.4 5.1 %shard_map.43 = f32[16,8,16,128]{3,2,1,0:T(8,128)} custom-call(f32[16,8,16,128]{3,2,1,0:T(8,128)} %get-tuple-element.6.refs_0_, f32[16,2,16,128]{3,2,1,0:T(8,128)} %copy-done.2, f32[16,2,16,128]{3,2,1,0:T(8,128)} %copy-done.5, f32[16,8,2,128]{3,2,1,0:T(2,128)} %copy-done.10, f32[16,8,2,128]{3,2,1,0:T(2,128)} %copy-done.14, f32[16,8,128]{2,1,0:T(8,128)} %copy-done.18, ...), custom_call_target="tpu_custom_call" | custom-call | tf_op jit(solution)/shard_map/pallas_call | solution.py:125
  75.0 5.0 %shard_map.46 = f32[16,8,16,128]{3,2,1,0:T(8,128)} custom-call(f32[16,8,16,128]{3,2,1,0:T(8,128)} %get-tuple-element.8.refs_0_, f32[16,2,16,128]{3,2,1,0:T(8,128)} %copy-done.3, f32[16,2,16,128]{3,2,1,0:T(8,128)} %copy-done.4, f32[16,8,2,128]{3,2,1,0:T(2,128)} %copy-done.15, f32[16,8,2,128]{3,2,1,0:T(2,128)} %copy-done.17, f32[16,8,128]{2,1,0:T(8,128)} %copy-done.20, ...), custom_call_target="tpu_custom_call" | custom-call | tf_op jit(solution)/shard_map/pallas_call | solution.py:125
  80.0 1.4 %pad_maximum_fusion = f32[32,8,16,128]{3,2,1,0:T(8,128)S(1)} fusion(f32[16,8,16,128]{3,2,1,0:T(8,128)} %shard_map.46, f32[16,8,16,128]{3,2,1,0:T(8,128)S(1)} %copy-done.1), kind=kLoop, calls=%fused_computation | loop fusion | flops 524288 | bytes 4194304 | tf_op jit(solution)/shard_map/concatenate | solution.py:149
  81.4 2.8 %fusion.7 = f32[32,32]{0,1:T(8,128)S(1)} fusion(f32[32,8,16,128]{3,2,1,0:T(8,128)S(1)} %pad_maximum_fusion), kind=kOutput, calls=%fused_computation.7 | convolution fusion | flops 201327616 | bytes 2101248 | tf_op jit(solution)/shard_map/axyz,bxyz->ab/dot_general | solution.py:153
  84.4 2.6 %collective-permute-done.24 = f32[32,32]{0,1:T(8,128)S(1)} collective-permute-done((f32[32,32]{0,1:T(8,128)S(1)}, f32[32,32]{0,1:T(8,128)S(1)}, u32[]{:S(2)}, u32[]{:S(2)}) %collective-permute-start.24) | collective-permute-done | bytes 4128 | tf_op jit(solution)/shard_map/ppermute | solution.py:137
  87.3 3.7 %collective-permute-done.25 = f32[32,32]{0,1:T(8,128)S(1)} collective-permute-done((f32[32,32]{0,1:T(8,128)S(1)}, f32[32,32]{0,1:T(8,128)S(1)}, u32[]{:S(2)}, u32[]{:S(2)}) %collective-permute-start.25) | collective-permute-done | bytes 4128 | tf_op jit(solution)/shard_map/ppermute | solution.py:137
  91.1 2.6 %collective-permute-done.26 = f32[32,32]{0,1:T(8,128)S(1)} collective-permute-done((f32[32,32]{0,1:T(8,128)S(1)}, f32[32,32]{0,1:T(8,128)S(1)}, u32[]{:S(2)}, u32[]{:S(2)}) %collective-permute-start.26) | collective-permute-done | bytes 4128 | tf_op jit(solution)/shard_map/ppermute | solution.py:137
  93.6 0.8 collective-permute-start.27
  94.5 2.8 %collective-permute-done.27 = f32[32,32]{0,1:T(8,128)S(1)} collective-permute-done((f32[32,32]{0,1:T(8,128)S(1)}, f32[32,32]{0,1:T(8,128)S(1)}, u32[]{:S(2)}, u32[]{:S(2)}) %collective-permute-start.27) | collective-permute-done | bytes 4128 | tf_op jit(solution)/shard_map/ppermute | solution.py:137
  97.3 4.2 %collective-permute-start.28 = (f32[32,32]{0,1:T(8,128)S(1)}, f32[32,32]{0,1:T(8,128)S(1)}, u32[]{:S(2)}, u32[]{:S(2)}) collective-permute-start(f32[32,32]{0,1:T(8,128)S(1)} %add.39), channel_id=1, source_target_pairs={{0,16},{4,20},{8,24},{12,28},{16,0},{20,4},{24,8},{28,12},{1,17},{... | collective-permute-start | bytes 12296 | tf_op jit(solution)/shard_map/ppermute | solution.py:137
  101.5 2.3 %collective-permute-done.28 = f32[32,32]{0,1:T(8,128)S(1)} collective-permute-done((f32[32,32]{0,1:T(8,128)S(1)}, f32[32,32]{0,1:T(8,128)S(1)}, u32[]{:S(2)}, u32[]{:S(2)}) %collective-permute-start.28) | collective-permute-done | bytes 4128 | tf_op jit(solution)/shard_map/ppermute | solution.py:137
  103.8 8.8 %collective-permute-start.29 = (f32[32,32]{0,1:T(8,128)S(1)}, f32[32,32]{0,1:T(8,128)S(1)}, u32[]{:S(2)}, u32[]{:S(2)}) collective-permute-start(f32[32,32]{0,1:T(8,128)S(1)} %add.40), channel_id=1, source_target_pairs={{0,32},{32,0},{64,96},{96,64},{128,160},{160,128},{192,224},{224,1... | collective-permute-start | bytes 12296 | tf_op jit(solution)/shard_map/ppermute | solution.py:137
  112.6 0.8 collective-permute-done.29
  113.4 2.6 %collective-permute-done.30 = f32[32,32]{0,1:T(8,128)S(1)} collective-permute-done((f32[32,32]{0,1:T(8,128)S(1)}, f32[32,32]{0,1:T(8,128)S(1)}, u32[]{:S(2)}, u32[]{:S(2)}) %collective-permute-start.30) | collective-permute-done | bytes 4128 | tf_op jit(solution)/shard_map/ppermute | solution.py:137
  116.0 4.1 %collective-permute-done.31 = f32[32,32]{0,1:T(8,128)S(1)} collective-permute-done((f32[32,32]{0,1:T(8,128)S(1)}, f32[32,32]{0,1:T(8,128)S(1)}, u32[]{:S(2)}, u32[]{:S(2)}) %collective-permute-start.31) | collective-permute-done | bytes 4128 | tf_op jit(solution)/shard_map/ppermute | solution.py:137
  120.2 2.9 %cholesky.17 = f32[32,32]{1,0:T(8,128)S(1)} custom-call(f32[32,32]{1,0:T(8,128)S(1)} %fusion.11), custom_call_target="Cholesky" | custom-call | tf_op jit(solution)/shard_map/jit(cholesky)/cholesky | solution.py:154
  124.5 2.4 %custom-call.7 = f32[1,32,32]{1,2,0:T(8,128)S(1)} custom-call(f32[1,32,32]{2,1,0:T(8,128)S(1)} %get-tuple-element.31), custom_call_target="InvertDiagBlocksLowerTriangular" | custom-call | tf_op jit(solution)/shard_map/jit(_solve_triangular)/triangular_solve | solution.py:156
  127.1 3.0 %fusion = f32[32,8,16,128]{3,0,2,1:T(8,128)S(1)} fusion(f32[32,32,1,1]{1,0,3,2:T(8,128)S(1)} %convolution_bitcast_fusion, f32[32,8,16,128]{3,2,1,0:T(8,128)S(1)} %pad_maximum_fusion), kind=kOutput, calls=%fused_computation.1 | convolution fusion | flops 201326592 | bytes 4198400 | tf_op jit(solution)/shard_map/ab,bxyz->axyz/dot_general | solution.py:157
  130.1 2.5 %copy.9 = f32[32,8,16,128]{3,2,1,0:T(8,128)} copy(f32[32,8,16,128]{3,0,2,1:T(8,128)S(1)} %fusion) | data formatting | bytes 4194304
  (100 shorter events, 6.1 us)
Async XLA Ops:
  0.6 7.7 %copy-start = (f32[32,8,16,128]{3,2,1,0:T(8,128)S(1)}, f32[32,8,16,128]{3,2,1,0:T(8,128)}, u32[]{:S(2)}) copy-start(f32[32,8,16,128]{3,2,1,0:T(8,128)} %param.2) | copy-start | bytes 6291460
  6.3 11.5 %collective-permute-start.4 = (f32[16,8,128]{2,1,0:T(8,128)}, f32[16,8,128]{2,1,0:T(8,128)}, u32[]{:S(2)}, u32[]{:S(2)}) collective-permute-start(f32[16,8,128]{2,1,0:T(8,128)} %shard_map.41), channel_id=1, source_target_pairs={{0,1},{1,2},{2,3},{3,0},{4,5},{5,6},{6,7},{7,4},{8,9},{9,10},{10,1... | collective-permute-start | bytes 196616 | tf_op jit(solution)/shard_map/ppermute | solution.py:101
  9.2 18.3 %collective-permute-start = (f32[16,2,16,128]{3,2,1,0:T(8,128)}, f32[16,2,16,128]{3,2,1,0:T(8,128)S(1)}, u32[]{:S(2)}, u32[]{:S(2)}) collective-permute-start(f32[16,2,16,128]{3,2,1,0:T(8,128)} %get-tuple-element.19), channel_id=1, source_target_pairs={{0,32},{32,64},{64,96},{96,128},{128,160},{160,192},{192,224},{224... | collective-permute-start | bytes 786440 | tf_op jit(solution)/shard_map/ppermute | solution.py:98
  11.2 16.4 %collective-permute-start.1 = (f32[16,2,16,128]{3,2,1,0:T(8,128)S(1)}, f32[16,2,16,128]{3,2,1,0:T(8,128)S(1)}, u32[]{:S(2)}, u32[]{:S(2)}) collective-permute-start(f32[16,2,16,128]{3,2,1,0:T(8,128)S(1)} %get-tuple-element.16), channel_id=1, source_target_pairs={{0,224},{32,0},{64,32},{96,64},{128,96},{160,128},{192,160},{224,1... | collective-permute-start | bytes 786440 | tf_op jit(solution)/shard_map/ppermute | solution.py:99
  12.1 10.5 %collective-permute-start.2 = (f32[16,8,2,128]{3,2,1,0:T(2,128)}, f32[16,8,2,128]{3,2,1,0:T(2,128)S(1)}, u32[]{:S(2)}, u32[]{:S(2)}) collective-permute-start(f32[16,8,2,128]{3,2,1,0:T(2,128)} %get-tuple-element.13), channel_id=1, source_target_pairs={{0,4},{4,8},{8,12},{12,16},{16,20},{20,24},{24,28},{28,0},{1,5},{5... | collective-permute-start | bytes 393224 | tf_op jit(solution)/shard_map/ppermute | solution.py:98
  13.8 10.4 %collective-permute-start.3 = (f32[16,8,2,128]{3,2,1,0:T(2,128)}, f32[16,8,2,128]{3,2,1,0:T(2,128)S(1)}, u32[]{:S(2)}, u32[]{:S(2)}) collective-permute-start(f32[16,8,2,128]{3,2,1,0:T(2,128)} %get-tuple-element.12), channel_id=1, source_target_pairs={{0,28},{4,0},{8,4},{12,8},{16,12},{20,16},{24,20},{28,24},{1,29},{... | collective-permute-start | bytes 393224 | tf_op jit(solution)/shard_map/ppermute | solution.py:99
  17.7 3.7 %collective-permute-start.5 = (f32[16,8,128]{2,1,0:T(8,128)}, f32[16,8,128]{2,1,0:T(8,128)S(1)}, u32[]{:S(2)}, u32[]{:S(2)}) collective-permute-start(f32[16,8,128]{2,1,0:T(8,128)} %shard_map.41), channel_id=1, source_target_pairs={{0,3},{1,0},{2,1},{3,2},{4,7},{5,4},{6,5},{7,6},{8,11},{9,8},{10,9... | collective-permute-start | bytes 196616 | tf_op jit(solution)/shard_map/ppermute | solution.py:102
  21.4 6.2 %copy-start.24 = (f32[16,8,128]{2,1,0:T(8,128)}, f32[16,8,128]{2,1,0:T(8,128)S(1)}, u32[]{:S(2)}) copy-start(f32[16,8,128]{2,1,0:T(8,128)S(1)} %collective-permute-done.5.refs_6_) | copy-start | bytes 196612
  21.4 14.7 %collective-permute-start.16 = (f32[16,8,128]{2,1,0:T(8,128)}, f32[16,8,128]{2,1,0:T(8,128)S(1)}, u32[]{:S(2)}, u32[]{:S(2)}) collective-permute-start(f32[16,8,128]{2,1,0:T(8,128)} %shard_map.44), channel_id=1, source_target_pairs={{0,1},{1,2},{2,3},{3,0},{4,5},{5,6},{6,7},{7,4},{8,9},{9,10},{10,1... | collective-permute-start | bytes 196616 | tf_op jit(solution)/shard_map/ppermute | solution.py:101
  22.6 5.0 %copy-start.12 = (f32[16,8,2,128]{3,2,1,0:T(2,128)}, f32[16,8,2,128]{3,2,1,0:T(2,128)S(1)}, u32[]{:S(2)}) copy-start(f32[16,8,2,128]{3,2,1,0:T(2,128)S(1)} %collective-permute-done.2.refs_3_) | copy-start | bytes 393220
  22.6 17.0 %collective-permute-start.17 = (f32[16,8,128]{2,1,0:T(8,128)}, f32[16,8,128]{2,1,0:T(8,128)S(1)}, u32[]{:S(2)}, u32[]{:S(2)}) collective-permute-start(f32[16,8,128]{2,1,0:T(8,128)} %shard_map.44), channel_id=1, source_target_pairs={{0,3},{1,0},{2,1},{3,2},{4,7},{5,4},{6,5},{7,6},{8,11},{9,8},{10,9... | collective-permute-start | bytes 196616 | tf_op jit(solution)/shard_map/ppermute | solution.py:102
  24.1 3.5 %copy-start.13 = (f32[16,8,2,128]{3,2,1,0:T(2,128)}, f32[16,8,2,128]{3,2,1,0:T(2,128)S(1)}, u32[]{:S(2)}) copy-start(f32[16,8,2,128]{3,2,1,0:T(2,128)S(1)} %collective-permute-done.3.refs_4_) | copy-start | bytes 393220
  24.1 21.0 %collective-permute-start.12 = (f32[16,2,16,128]{3,2,1,0:T(8,128)S(1)}, f32[16,2,16,128]{3,2,1,0:T(8,128)S(1)}, u32[]{:S(2)}, u32[]{:S(2)}) collective-permute-start(f32[16,2,16,128]{3,2,1,0:T(8,128)S(1)} %get-tuple-element.18), channel_id=1, source_target_pairs={{0,32},{32,64},{64,96},{96,128},{128,160},{160,192},{192,224},{224... | collective-permute-start | bytes 786440 | tf_op jit(solution)/shard_map/ppermute | solution.py:98
  27.5 17.7 %collective-permute-start.13 = (f32[16,2,16,128]{3,2,1,0:T(8,128)S(1)}, f32[16,2,16,128]{3,2,1,0:T(8,128)S(1)}, u32[]{:S(2)}, u32[]{:S(2)}) collective-permute-start(f32[16,2,16,128]{3,2,1,0:T(8,128)S(1)} %get-tuple-element.17), channel_id=1, source_target_pairs={{0,224},{32,0},{64,32},{96,64},{128,96},{160,128},{192,160},{224,1... | collective-permute-start | bytes 786440 | tf_op jit(solution)/shard_map/ppermute | solution.py:99
  27.6 12.2 %collective-permute-start.14 = (f32[16,8,2,128]{3,2,1,0:T(2,128)}, f32[16,8,2,128]{3,2,1,0:T(2,128)S(1)}, u32[]{:S(2)}, u32[]{:S(2)}) collective-permute-start(f32[16,8,2,128]{3,2,1,0:T(2,128)} %get-tuple-element.15), channel_id=1, source_target_pairs={{0,4},{4,8},{8,12},{12,16},{16,20},{20,24},{24,28},{28,0},{1,5},{5... | collective-permute-start | bytes 393224 | tf_op jit(solution)/shard_map/ppermute | solution.py:98
  36.2 8.9 %copy-start.22 = (f32[16,8,128]{2,1,0:T(8,128)}, f32[16,8,128]{2,1,0:T(8,128)S(1)}, u32[]{:S(2)}) copy-start(f32[16,8,128]{2,1,0:T(8,128)S(1)} %collective-permute-done.16.refs_5_) | copy-start | bytes 196612
  36.2 6.2 %collective-permute-start.15 = (f32[16,8,2,128]{3,2,1,0:T(2,128)S(1)}, f32[16,8,2,128]{3,2,1,0:T(2,128)S(1)}, u32[]{:S(2)}, u32[]{:S(2)}) collective-permute-start(f32[16,8,2,128]{3,2,1,0:T(2,128)S(1)} %get-tuple-element.14), channel_id=1, source_target_pairs={{0,28},{4,0},{8,4},{12,8},{16,12},{20,16},{24,20},{28,24},{1,29},{... | collective-permute-start | bytes 393224 | tf_op jit(solution)/shard_map/ppermute | solution.py:99
  39.6 5.5 %copy-start.23 = (f32[16,8,128]{2,1,0:T(8,128)}, f32[16,8,128]{2,1,0:T(8,128)S(1)}, u32[]{:S(2)}) copy-start(f32[16,8,128]{2,1,0:T(8,128)S(1)} %collective-permute-done.17.refs_6_) | copy-start | bytes 196612
  39.6 14.7 %collective-permute-start.10 = (f32[16,8,128]{2,1,0:T(8,128)}, f32[16,8,128]{2,1,0:T(8,128)S(1)}, u32[]{:S(2)}, u32[]{:S(2)}) collective-permute-start(f32[16,8,128]{2,1,0:T(8,128)} %get-tuple-element.7), channel_id=1, source_target_pairs={{0,1},{1,2},{2,3},{3,0},{4,5},{5,6},{6,7},{7,4},{8,9},{9,10},{10,1... | collective-permute-start | bytes 196616 | tf_op jit(solution)/shard_map/ppermute | solution.py:101
  39.8 5.4 %copy-start.11 = (f32[16,8,2,128]{3,2,1,0:T(2,128)}, f32[16,8,2,128]{3,2,1,0:T(2,128)S(1)}, u32[]{:S(2)}) copy-start(f32[16,8,2,128]{3,2,1,0:T(2,128)S(1)} %collective-permute-done.14.refs_3_) | copy-start | bytes 393220
  39.8 16.0 %collective-permute-start.11 = (f32[16,8,128]{2,1,0:T(8,128)}, f32[16,8,128]{2,1,0:T(8,128)S(1)}, u32[]{:S(2)}, u32[]{:S(2)}) collective-permute-start(f32[16,8,128]{2,1,0:T(8,128)} %get-tuple-element.7), channel_id=1, source_target_pairs={{0,3},{1,0},{2,1},{3,2},{4,7},{5,4},{6,5},{7,6},{8,11},{9,8},{10,9... | collective-permute-start | bytes 196616 | tf_op jit(solution)/shard_map/ppermute | solution.py:102
  42.4 2.8 %copy-start.16 = (f32[16,8,2,128]{3,2,1,0:T(2,128)}, f32[16,8,2,128]{3,2,1,0:T(2,128)S(1)}, u32[]{:S(2)}) copy-start(f32[16,8,2,128]{3,2,1,0:T(2,128)S(1)} %collective-permute-done.15.refs_4_) | copy-start | bytes 393220
  42.4 20.7 %collective-permute-start.6 = (f32[16,2,16,128]{3,2,1,0:T(8,128)S(1)}, f32[16,2,16,128]{3,2,1,0:T(8,128)S(1)}, u32[]{:S(2)}, u32[]{:S(2)}) collective-permute-start(f32[16,2,16,128]{3,2,1,0:T(8,128)S(1)} %get-tuple-element.25), channel_id=1, source_target_pairs={{0,32},{32,64},{64,96},{96,128},{128,160},{160,192},{192,224},{224... | collective-permute-start | bytes 786440 | tf_op jit(solution)/shard_map/ppermute | solution.py:98
  45.1 14.0 %collective-permute-start.8 = (f32[16,8,2,128]{3,2,1,0:T(2,128)S(1)}, f32[16,8,2,128]{3,2,1,0:T(2,128)S(1)}, u32[]{:S(2)}, u32[]{:S(2)}) collective-permute-start(f32[16,8,2,128]{3,2,1,0:T(2,128)S(1)} %get-tuple-element.23), channel_id=1, source_target_pairs={{0,4},{4,8},{8,12},{12,16},{16,20},{20,24},{24,28},{28,0},{1,5},{5... | collective-permute-start | bytes 393224 | tf_op jit(solution)/shard_map/ppermute | solution.py:98
  53.3 5.0 %collective-permute-start.22 = (f32[16,8,128]{2,1,0:T(8,128)}, f32[16,8,128]{2,1,0:T(8,128)S(1)}, u32[]{:S(2)}, u32[]{:S(2)}) collective-permute-start(f32[16,8,128]{2,1,0:T(8,128)} %get-tuple-element.9), channel_id=1, source_target_pairs={{0,1},{1,2},{2,3},{3,0},{4,5},{5,6},{6,7},{7,4},{8,9},{9,10},{10,1... | collective-permute-start | bytes 196616 | tf_op jit(solution)/shard_map/ppermute | solution.py:101
  54.4 14.0 %copy-start.18 = (f32[16,8,128]{2,1,0:T(8,128)}, f32[16,8,128]{2,1,0:T(8,128)S(1)}, u32[]{:S(2)}) copy-start(f32[16,8,128]{2,1,0:T(8,128)S(1)} %collective-permute-done.10.refs_5_) | copy-start | bytes 196612
  54.4 11.3 %collective-permute-start.7 = (f32[16,2,16,128]{3,2,1,0:T(8,128)S(1)}, f32[16,2,16,128]{3,2,1,0:T(8,128)S(1)}, u32[]{:S(2)}, u32[]{:S(2)}) collective-permute-start(f32[16,2,16,128]{3,2,1,0:T(8,128)S(1)} %get-tuple-element.24), channel_id=1, source_target_pairs={{0,224},{32,0},{64,32},{96,64},{128,96},{160,128},{192,160},{224,1... | collective-permute-start | bytes 786440 | tf_op jit(solution)/shard_map/ppermute | solution.py:99
  55.8 12.6 %copy-start.19 = (f32[16,8,128]{2,1,0:T(8,128)}, f32[16,8,128]{2,1,0:T(8,128)S(1)}, u32[]{:S(2)}) copy-start(f32[16,8,128]{2,1,0:T(8,128)S(1)} %collective-permute-done.11.refs_6_) | copy-start | bytes 196612
  55.8 7.2 %collective-permute-start.9 = (f32[16,8,2,128]{3,2,1,0:T(2,128)S(1)}, f32[16,8,2,128]{3,2,1,0:T(2,128)S(1)}, u32[]{:S(2)}, u32[]{:S(2)}) collective-permute-start(f32[16,8,2,128]{3,2,1,0:T(2,128)S(1)} %get-tuple-element.22), channel_id=1, source_target_pairs={{0,28},{4,0},{8,4},{12,8},{16,12},{20,16},{24,20},{28,24},{1,29},{... | collective-permute-start | bytes 393224 | tf_op jit(solution)/shard_map/ppermute | solution.py:99
  58.3 0.8 copy-start.20
  58.3 15.2 %collective-permute-start.18 = (f32[16,2,16,128]{3,2,1,0:T(8,128)S(1)}, f32[16,2,16,128]{3,2,1,0:T(8,128)S(1)}, u32[]{:S(2)}, u32[]{:S(2)}) collective-permute-start(f32[16,2,16,128]{3,2,1,0:T(8,128)S(1)} %get-tuple-element.29), channel_id=1, source_target_pairs={{0,32},{32,64},{64,96},{96,128},{128,160},{160,192},{192,224},{224... | collective-permute-start | bytes 786440 | tf_op jit(solution)/shard_map/ppermute | solution.py:98
  59.1 9.3 %copy-start.10 = (f32[16,8,2,128]{3,2,1,0:T(2,128)}, f32[16,8,2,128]{3,2,1,0:T(2,128)S(1)}, u32[]{:S(2)}) copy-start(f32[16,8,2,128]{3,2,1,0:T(2,128)S(1)} %collective-permute-done.8.refs_3_) | copy-start | bytes 393220
  59.1 14.4 %collective-permute-start.19 = (f32[16,2,16,128]{3,2,1,0:T(8,128)S(1)}, f32[16,2,16,128]{3,2,1,0:T(8,128)S(1)}, u32[]{:S(2)}, u32[]{:S(2)}) collective-permute-start(f32[16,2,16,128]{3,2,1,0:T(8,128)S(1)} %get-tuple-element.28), channel_id=1, source_target_pairs={{0,224},{32,0},{64,32},{96,64},{128,96},{160,128},{192,160},{224,1... | collective-permute-start | bytes 786440 | tf_op jit(solution)/shard_map/ppermute | solution.py:99
  62.9 5.4 %copy-start.14 = (f32[16,8,2,128]{3,2,1,0:T(2,128)}, f32[16,8,2,128]{3,2,1,0:T(2,128)S(1)}, u32[]{:S(2)}) copy-start(f32[16,8,2,128]{3,2,1,0:T(2,128)S(1)} %collective-permute-done.9.refs_4_) | copy-start | bytes 393220
  63.0 10.5 %collective-permute-start.20 = (f32[16,8,2,128]{3,2,1,0:T(2,128)S(1)}, f32[16,8,2,128]{3,2,1,0:T(2,128)S(1)}, u32[]{:S(2)}, u32[]{:S(2)}) collective-permute-start(f32[16,8,2,128]{3,2,1,0:T(2,128)S(1)} %get-tuple-element.27), channel_id=1, source_target_pairs={{0,4},{4,8},{8,12},{12,16},{16,20},{20,24},{24,28},{28,0},{1,5},{5... | collective-permute-start | bytes 393224 | tf_op jit(solution)/shard_map/ppermute | solution.py:98
  63.1 5.3 %copy-start.2 = (f32[16,2,16,128]{3,2,1,0:T(8,128)}, f32[16,2,16,128]{3,2,1,0:T(8,128)S(1)}, u32[]{:S(2)}) copy-start(f32[16,2,16,128]{3,2,1,0:T(8,128)S(1)} %collective-permute-done.6.refs_1_) | copy-start | bytes 786436
  63.1 10.5 %collective-permute-start.21 = (f32[16,8,2,128]{3,2,1,0:T(2,128)S(1)}, f32[16,8,2,128]{3,2,1,0:T(2,128)S(1)}, u32[]{:S(2)}, u32[]{:S(2)}) collective-permute-start(f32[16,8,2,128]{3,2,1,0:T(2,128)S(1)} %get-tuple-element.26), channel_id=1, source_target_pairs={{0,28},{4,0},{8,4},{12,8},{16,12},{20,16},{24,20},{28,24},{1,29},{... | collective-permute-start | bytes 393224 | tf_op jit(solution)/shard_map/ppermute | solution.py:99
  65.7 2.7 %copy-start.5 = (f32[16,2,16,128]{3,2,1,0:T(8,128)}, f32[16,2,16,128]{3,2,1,0:T(8,128)S(1)}, u32[]{:S(2)}) copy-start(f32[16,2,16,128]{3,2,1,0:T(8,128)S(1)} %collective-permute-done.7.refs_2_) | copy-start | bytes 786436
  65.7 7.8 %collective-permute-start.23 = (f32[16,8,128]{2,1,0:T(8,128)}, f32[16,8,128]{2,1,0:T(8,128)S(1)}, u32[]{:S(2)}, u32[]{:S(2)}) collective-permute-start(f32[16,8,128]{2,1,0:T(8,128)} %get-tuple-element.9), channel_id=1, source_target_pairs={{0,3},{1,0},{2,1},{3,2},{4,7},{5,4},{6,5},{7,6},{8,11},{9,8},{10,9... | collective-permute-start | bytes 196616 | tf_op jit(solution)/shard_map/ppermute | solution.py:102
  73.5 6.6 %copy-start.1 = (f32[16,8,16,128]{3,2,1,0:T(8,128)S(1)}, f32[16,8,16,128]{3,2,1,0:T(8,128)}, u32[]{:S(2)}) copy-start(f32[16,8,16,128]{3,2,1,0:T(8,128)} %shard_map.43) | copy-start | bytes 3145732
  84.3 2.7 %collective-permute-start.24 = (f32[32,32]{0,1:T(8,128)S(1)}, f32[32,32]{0,1:T(8,128)S(1)}, u32[]{:S(2)}, u32[]{:S(2)}) collective-permute-start(f32[32,32]{0,1:T(8,128)S(1)} %fusion.7), channel_id=1, source_target_pairs={{0,1},{1,0},{2,3},{3,2},{4,5},{5,4},{6,7},{7,6},{8,9},{9,8},{10,11... | collective-permute-start | bytes 12296 | tf_op jit(solution)/shard_map/ppermute | solution.py:137
  87.0 4.1 %collective-permute-start.25 = (f32[32,32]{0,1:T(8,128)S(1)}, f32[32,32]{0,1:T(8,128)S(1)}, u32[]{:S(2)}, u32[]{:S(2)}) collective-permute-start(f32[32,32]{0,1:T(8,128)S(1)} %add.36), channel_id=1, source_target_pairs={{0,2},{1,3},{2,0},{3,1},{4,6},{5,7},{6,4},{7,5},{8,10},{9,11},{10,... | collective-permute-start | bytes 12296 | tf_op jit(solution)/shard_map/ppermute | solution.py:137
  91.0 2.6 %collective-permute-start.26 = (f32[32,32]{0,1:T(8,128)S(1)}, f32[32,32]{0,1:T(8,128)S(1)}, u32[]{:S(2)}, u32[]{:S(2)}) collective-permute-start(f32[32,32]{0,1:T(8,128)S(1)} %add.37), channel_id=1, source_target_pairs={{0,4},{4,0},{8,12},{12,8},{16,20},{20,16},{24,28},{28,24},{1,5},{5... | collective-permute-start | bytes 12296 | tf_op jit(solution)/shard_map/ppermute | solution.py:137
  93.6 3.7 %collective-permute-start.27 = (f32[32,32]{0,1:T(8,128)S(1)}, f32[32,32]{0,1:T(8,128)S(1)}, u32[]{:S(2)}, u32[]{:S(2)}) collective-permute-start(f32[32,32]{0,1:T(8,128)S(1)} %add.38), channel_id=1, source_target_pairs={{0,8},{4,12},{8,0},{12,4},{16,24},{20,28},{24,16},{28,20},{1,9},{5... | collective-permute-start | bytes 12296 | tf_op jit(solution)/shard_map/ppermute | solution.py:137
  97.3 6.5 %collective-permute-start.28 = (f32[32,32]{0,1:T(8,128)S(1)}, f32[32,32]{0,1:T(8,128)S(1)}, u32[]{:S(2)}, u32[]{:S(2)}) collective-permute-start(f32[32,32]{0,1:T(8,128)S(1)} %add.39), channel_id=1, source_target_pairs={{0,16},{4,20},{8,24},{12,28},{16,0},{20,4},{24,8},{28,12},{1,17},{... | collective-permute-start | bytes 12296 | tf_op jit(solution)/shard_map/ppermute | solution.py:137
  103.8 9.6 %collective-permute-start.29 = (f32[32,32]{0,1:T(8,128)S(1)}, f32[32,32]{0,1:T(8,128)S(1)}, u32[]{:S(2)}, u32[]{:S(2)}) collective-permute-start(f32[32,32]{0,1:T(8,128)S(1)} %add.40), channel_id=1, source_target_pairs={{0,32},{32,0},{64,96},{96,64},{128,160},{160,128},{192,224},{224,1... | collective-permute-start | bytes 12296 | tf_op jit(solution)/shard_map/ppermute | solution.py:137
  113.4 2.6 %collective-permute-start.30 = (f32[32,32]{0,1:T(8,128)S(1)}, f32[32,32]{0,1:T(8,128)S(1)}, u32[]{:S(2)}, u32[]{:S(2)}) collective-permute-start(f32[32,32]{0,1:T(8,128)S(1)} %add.41), channel_id=1, source_target_pairs={{0,64},{32,96},{64,0},{96,32},{128,192},{160,224},{192,128},{224,1... | collective-permute-start | bytes 12296 | tf_op jit(solution)/shard_map/ppermute | solution.py:137
  116.0 4.1 %collective-permute-start.31 = (f32[32,32]{0,1:T(8,128)S(1)}, f32[32,32]{0,1:T(8,128)S(1)}, u32[]{:S(2)}, u32[]{:S(2)}) collective-permute-start(f32[32,32]{0,1:T(8,128)S(1)} %add.42), channel_id=1, source_target_pairs={{0,128},{32,160},{64,192},{96,224},{128,0},{160,32},{192,64},{224,... | collective-permute-start | bytes 12296 | tf_op jit(solution)/shard_map/ppermute | solution.py:137
  (9 other events, 6.2 us)

commit v6 on v4

--- a/solution.py
+++ b/solution.py
@@ -128,6 +128,26 @@
     )(*args)
 
 
+def solve_kernel(l_ref, y_ref, o_ref):
+    n = y_ref.shape[0]
+    for j in range(n):
+        acc = y_ref[j]
+        for k in range(j):
+            acc = acc - l_ref[j, k] * o_ref[k]
+        o_ref[j] = acc / l_ref[j, j]
+
+
+def solve_lower(lower, y):
+    norb, cx, cy, cz = y.shape
+    xb = 2
+    blk = pl.BlockSpec((norb, xb, cy, cz), lambda i: (0, i, 0, 0))
+    return pl.pallas_call(
+        solve_kernel, grid=(cx // xb,),
+        in_specs=[pl.BlockSpec(memory_space=pltpu.SMEM), blk], out_specs=blk,
+        out_shape=jax.ShapeDtypeStruct(y.shape, jnp.float32), interpret=INTERPRET,
+    )(lower, y)
+
+
 def butterfly_sum(c):
     for axis in ("gz", "gy", "gx"):
         n = lax.axis_size(axis)
@@ -145,9 +165,7 @@
     all_cells = second[0].size * lax.axis_size("gx") * lax.axis_size("gy") * lax.axis_size("gz")
     correlation = jnp.einsum("axyz,bxyz->ab", second, second, precision=HI) / all_cells
     lower = jnp.linalg.cholesky(butterfly_sum(correlation))
-    eye = jnp.eye(norb_count, dtype=lower.dtype)
-    inverse = jax.scipy.linalg.solve_triangular(lower, eye, lower=True)
-    basis = jnp.einsum("ab,bxyz->axyz", inverse, second, precision=HI)
+    basis = solve_lower(lower, second)
     return (basis, lower.T)
 
 

time: 118 us -> 116 us (0.983)
  Pallas kernels: 23.5 us -> 28.6 us
  matrix products: 9.56 us -> 6.19 us
  local copies, waits for them, and re-layouts: 9.94 us -> 7.37 us
    pallas_call x0 -> x1, Pallas kernels: none -> 5.07 us  [solve_lower(): pl.pallas_call(solve_kernel, grid=(cx // xb,), in_specs=[pl.BlockSpec(mem...]
    dot_general x1 -> x0, matrix products: 3 us -> none  [per_device(): basis = jnp.einsum('ab,bxyz->axyz', inverse, second, precision=HI)]
    unnamed x34 -> x31, local copies, waits for them, and re-layouts: 6.56 us -> 4 us
    another operation x1 -> x0, other arithmetic: 2.44 us -> none  [per_device(): inverse = jax.scipy.linalg.solve_triangular(lower, eye, lower=True)]
    select_n x0 -> x1, other arithmetic: none -> 1.26 us  [per_device(): lower = jnp.linalg.cholesky(butterfly_sum(correlation))]
where the time goes in v6:
time: 116 us; the launch traced here: 114 us
  waiting for transfers between devices  35.1 us (30%)
  starting transfers between devices  30.8 us (27%)
  Pallas kernels  28.6 us (25%)
  local copies, waits for them, and re-layouts  7.37 us (6%)
  matrix products  6.19 us (5%)
  other arithmetic  5.54 us (5%)
    ppermute x8, waiting for transfers between devices, butterfly_sum(): c = c + lax.ppermute(c, axis, [(i, i ^ d) for i in range(n)])  21.9 us
    pallas_call x2, Pallas kernels, stage(): pl.pallas_call(functools.partial(stage_kernel, last=last), grid=(norb //...  19.3 us
    ppermute x8, starting transfers between devices, butterfly_sum(): c = c + lax.ppermute(c, axis, [(i, i ^ d) for i in range(n)])  12.7 us
    ppermute x2, waiting for transfers between devices, exchange(): out.append(lax.ppermute(zface, 'gz', shift_pairs(n, 1)))  9.34 us
    ppermute x4, starting transfers between devices, exchange(): out.append(lax.ppermute(first, axis, shift_pairs(n, -1)))  8.93 us
    dot_general x1, matrix products, per_device(): jnp.einsum('axyz,bxyz->ab', second, second, precision=HI) / all_cells  6.19 us
    pallas_call x1, Pallas kernels, solve_lower(): pl.pallas_call(solve_kernel, grid=(cx // xb,), in_specs=[pl.BlockSpec(mem...  5.07 us
    pallas_call x1, Pallas kernels, z_faces(): pl.pallas_call(z_face_kernel, grid=(norb // BLOCK,), in_specs=[blk], out_...  4.2 us
  transfers between devices with their start and end apart: 20, of which 12 were waited for; matrix products, arithmetic and copies ran while one was open for 3% of the time, Pallas kernels for 0%

profile of v6, /device:TPU:1, one launch (start us, length us, event | category | flops | bytes accessed | tf_op | source)
XLA Modules:
  0.0 114.4 jit_solution(4135358603456551227)
XLA Ops:
  0.6 4.2 %shard_map.41 = f32[32,8,128]{2,1,0:T(8,128)} custom-call(f32[32,8,16,128]{3,2,1,0:T(8,128)} %refs_8_.1), custom_call_target="tpu_custom_call" | custom-call | tf_op jit(solution)/shard_map/pallas_call | solution.py:85
  4.8 3.6 %collective-permute-start.5 = (f32[32,8,128]{2,1,0:T(8,128)}, f32[32,8,128]{2,1,0:T(8,128)S(1)}, u32[]{:S(2)}, u32[]{:S(2)}) collective-permute-start(f32[32,8,128]{2,1,0:T(8,128)} %shard_map.41), channel_id=1, source_target_pairs={{0,3},{1,0},{2,1},{3,2},{4,7},{5,4},{6,5},{7,6},{8,11},{9,8},{10,9... | collective-permute-start | bytes 393224 | tf_op jit(solution)/shard_map/ppermute | solution.py:101
  8.4 0.1 fusion.12
  8.5 1.0 collective-permute-start.1
  9.4 1.1 collective-permute-start
  10.6 0.2 fusion.11
  10.8 5.7 %collective-permute-start.3 = (f32[32,8,2,128]{3,2,1,0:T(2,128)S(1)}, f32[32,8,2,128]{3,2,1,0:T(2,128)S(1)}, u32[]{:S(2)}, u32[]{:S(2)}) collective-permute-start(f32[32,8,2,128]{3,2,1,0:T(2,128)S(1)} %get-tuple-element.12), channel_id=1, source_target_pairs={{0,28},{4,0},{8,4},{12,8},{16,12},{20,16},{24,20},{28,24},{1,29},{... | collective-permute-start | bytes 786440 | tf_op jit(solution)/shard_map/ppermute | solution.py:98
  16.4 0.1 collective-permute-start.4
  16.5 5.0 %collective-permute-done.4.refs_5_ = f32[32,8,128]{2,1,0:T(8,128)S(1)} collective-permute-done((f32[32,8,128]{2,1,0:T(8,128)S(1)}, f32[32,8,128]{2,1,0:T(8,128)S(1)}, u32[]{:S(2)}, u32[]{:S(2)}) %collective-permute-start.4) | collective-permute-done | bytes 131104 | tf_op jit(solution)/shard_map/ppermute | solution.py:100
  21.5 2.9 %collective-permute-done.2.refs_3_ = f32[32,8,2,128]{3,2,1,0:T(2,128)S(1)} collective-permute-done((f32[32,8,2,128]{3,2,1,0:T(2,128)S(1)}, f32[32,8,2,128]{3,2,1,0:T(2,128)S(1)}, u32[]{:S(2)}, u32[]{:S(2)}) %collective-permute-start.2) | collective-permute-done | bytes 262176 | tf_op jit(solution)/shard_map/ppermute | solution.py:97
  24.5 0.7 copy-done.8
  25.1 0.2 copy-done.1
  25.3 0.8 copy-done.3
  26.1 11.4 %shard_map.42 = (f32[32,8,16,128]{3,2,1,0:T(8,128)}, f32[32,8,128]{2,1,0:T(8,128)}) custom-call(f32[32,8,16,128]{3,2,1,0:T(8,128)} %refs_8_.1, f32[32,2,16,128]{3,2,1,0:T(8,128)} %copy-done.3, f32[32,2,16,128]{3,2,1,0:T(8,128)} %copy-done.1, f32[32,8,2,128]{3,2,1,0:T(2,128)} %copy-done.8, f32[32,8,2,128]{3,2,1,0:T(2,128)} %copy-done.7, ...), custom_call_target="tpu_custom_call" | custom-call | tf_op jit(solution)/shard_map/pallas_call | solution.py:124
  37.6 0.5 collective-permute-start.11
  38.1 1.3 %fusion.10 = (f32[32,2,16,128]{3,2,1,0:T(8,128)S(1)}, f32[32,2,16,128]{3,2,1,0:T(8,128)S(1)}) fusion(f32[32,8,16,128]{3,2,1,0:T(8,128)} %get-tuple-element.4.refs_0_), kind=kLoop, calls=%fused_computation.12 | loop fusion | bytes 2097152 | tf_op jit(solution)/shard_map/slice | solution.py:96
  39.4 2.2 %collective-permute-start.7 = (f32[32,2,16,128]{3,2,1,0:T(8,128)S(1)}, f32[32,2,16,128]{3,2,1,0:T(8,128)S(1)}, u32[]{:S(2)}, u32[]{:S(2)}) collective-permute-start(f32[32,2,16,128]{3,2,1,0:T(8,128)S(1)} %get-tuple-element.10), channel_id=1, source_target_pairs={{0,224},{32,0},{64,32},{96,64},{128,96},{160,128},{192,160},{224,1... | collective-permute-start | bytes 1572872 | tf_op jit(solution)/shard_map/ppermute | solution.py:98
  41.6 1.1 collective-permute-start.6
  42.7 1.8 %fusion.9 = (f32[32,8,2,128]{3,2,1,0:T(2,128)S(1)}, f32[32,8,2,128]{3,2,1,0:T(2,128)S(1)}) fusion(f32[32,8,16,128]{3,2,1,0:T(8,128)} %get-tuple-element.4.refs_0_), kind=kLoop, calls=%fused_computation.11 | loop fusion | bytes 1048576 | tf_op jit(solution)/shard_map/slice | solution.py:96
  44.5 0.1 collective-permute-start.9
  44.6 1.5 %collective-permute-start.8 = (f32[32,8,2,128]{3,2,1,0:T(2,128)S(1)}, f32[32,8,2,128]{3,2,1,0:T(2,128)S(1)}, u32[]{:S(2)}, u32[]{:S(2)}) collective-permute-start(f32[32,8,2,128]{3,2,1,0:T(2,128)S(1)} %get-tuple-element.9), channel_id=1, source_target_pairs={{0,4},{4,8},{8,12},{12,16},{16,20},{20,24},{24,28},{28,0},{1,5},{5... | collective-permute-start | bytes 786440 | tf_op jit(solution)/shard_map/ppermute | solution.py:97
  46.0 1.3 %collective-permute-start.10 = (f32[32,8,128]{2,1,0:T(8,128)S(1)}, f32[32,8,128]{2,1,0:T(8,128)S(1)}, u32[]{:S(2)}, u32[]{:S(2)}) collective-permute-start(f32[32,8,128]{2,1,0:T(8,128)S(1)} %copy-done.14), channel_id=1, source_target_pairs={{0,1},{1,2},{2,3},{3,0},{4,5},{5,6},{6,7},{7,4},{8,9},{9,10},{10,1... | collective-permute-start | bytes 393224 | tf_op jit(solution)/shard_map/ppermute | solution.py:100
  47.3 4.3 %collective-permute-done.10.refs_5_ = f32[32,8,128]{2,1,0:T(8,128)S(1)} collective-permute-done((f32[32,8,128]{2,1,0:T(8,128)S(1)}, f32[32,8,128]{2,1,0:T(8,128)S(1)}, u32[]{:S(2)}, u32[]{:S(2)}) %collective-permute-start.10) | collective-permute-done | bytes 131104 | tf_op jit(solution)/shard_map/ppermute | solution.py:100
  51.6 1.1 collective-permute-done.8.refs_3_
  52.7 0.7 copy-done.6
  53.4 0.2 copy-done.2
  53.6 0.8 copy-done.4
  54.4 7.9 %shard_map.43.y_ref = f32[32,8,16,128]{3,2,1,0:T(8,128)} custom-call(f32[32,8,16,128]{3,2,1,0:T(8,128)} %get-tuple-element.4.refs_0_, f32[32,2,16,128]{3,2,1,0:T(8,128)} %copy-done.4, f32[32,2,16,128]{3,2,1,0:T(8,128)} %copy-done.2, f32[32,8,2,128]{3,2,1,0:T(2,128)} %copy-done.6, f32[32,8,2,128]{3,2,1,0:T(2,128)} %copy-done.5, f32[32,8,128]{2,1,0:T(8,128)} %copy-done.10, ...), custom_call_target="tpu_custom_call" | custom-call | tf_op jit(solution)/shard_map/pallas_call | solution.py:124
  62.3 6.2 %fusion.5 = f32[32,32]{0,1:T(8,128)S(1)} fusion(f32[32,8,16,128]{3,2,1,0:T(8,128)} %shard_map.43.y_ref), kind=kOutput, calls=%fused_computation.3 | convolution fusion | flops 201327616 | bytes 2101248 | tf_op jit(solution)/shard_map/axyz,bxyz->ab/dot_general | solution.py:166
  68.5 0.7 collective-permute-start.12
  69.1 2.0 %collective-permute-done.12 = f32[32,32]{0,1:T(8,128)S(1)} collective-permute-done((f32[32,32]{0,1:T(8,128)S(1)}, f32[32,32]{0,1:T(8,128)S(1)}, u32[]{:S(2)}, u32[]{:S(2)}) %collective-permute-start.12) | collective-permute-done | bytes 4128 | tf_op jit(solution)/shard_map/ppermute | solution.py:156
  71.1 4.1 %collective-permute-done.13 = f32[32,32]{0,1:T(8,128)S(1)} collective-permute-done((f32[32,32]{0,1:T(8,128)S(1)}, f32[32,32]{0,1:T(8,128)S(1)}, u32[]{:S(2)}, u32[]{:S(2)}) %collective-permute-start.13) | collective-permute-done | bytes 4128 | tf_op jit(solution)/shard_map/ppermute | solution.py:156
  75.2 2.9 %collective-permute-done.14 = f32[32,32]{0,1:T(8,128)S(1)} collective-permute-done((f32[32,32]{0,1:T(8,128)S(1)}, f32[32,32]{0,1:T(8,128)S(1)}, u32[]{:S(2)}, u32[]{:S(2)}) %collective-permute-start.14) | collective-permute-done | bytes 4128 | tf_op jit(solution)/shard_map/ppermute | solution.py:156
  78.1 3.5 %collective-permute-done.15 = f32[32,32]{0,1:T(8,128)S(1)} collective-permute-done((f32[32,32]{0,1:T(8,128)S(1)}, f32[32,32]{0,1:T(8,128)S(1)}, u32[]{:S(2)}, u32[]{:S(2)}) %collective-permute-start.15) | collective-permute-done | bytes 4128 | tf_op jit(solution)/shard_map/ppermute | solution.py:156
  81.6 1.1 %collective-permute-start.16 = (f32[32,32]{0,1:T(8,128)S(1)}, f32[32,32]{0,1:T(8,128)S(1)}, u32[]{:S(2)}, u32[]{:S(2)}) collective-permute-start(f32[32,32]{0,1:T(8,128)S(1)} %add.36), channel_id=1, source_target_pairs={{0,16},{4,20},{8,24},{12,28},{16,0},{20,4},{24,8},{28,12},{1,17},{... | collective-permute-start | bytes 12296 | tf_op jit(solution)/shard_map/ppermute | solution.py:156
  82.8 5.5 %collective-permute-done.16 = f32[32,32]{0,1:T(8,128)S(1)} collective-permute-done((f32[32,32]{0,1:T(8,128)S(1)}, f32[32,32]{0,1:T(8,128)S(1)}, u32[]{:S(2)}, u32[]{:S(2)}) %collective-permute-start.16) | collective-permute-done | bytes 4128 | tf_op jit(solution)/shard_map/ppermute | solution.py:156
  88.2 7.3 %collective-permute-start.17 = (f32[32,32]{0,1:T(8,128)S(1)}, f32[32,32]{0,1:T(8,128)S(1)}, u32[]{:S(2)}, u32[]{:S(2)}) collective-permute-start(f32[32,32]{0,1:T(8,128)S(1)} %add.37), channel_id=1, source_target_pairs={{0,32},{32,0},{64,96},{96,64},{128,160},{160,128},{192,224},{224,1... | collective-permute-start | bytes 12296 | tf_op jit(solution)/shard_map/ppermute | solution.py:156
  95.5 0.8 collective-permute-done.17
  96.4 1.2 %collective-permute-start.18 = (f32[32,32]{0,1:T(8,128)S(1)}, f32[32,32]{0,1:T(8,128)S(1)}, u32[]{:S(2)}, u32[]{:S(2)}) collective-permute-start(f32[32,32]{0,1:T(8,128)S(1)} %add.38), channel_id=1, source_target_pairs={{0,64},{32,96},{64,0},{96,32},{128,192},{160,224},{192,128},{224,1... | collective-permute-start | bytes 12296 | tf_op jit(solution)/shard_map/ppermute | solution.py:156
  97.6 1.4 %collective-permute-done.18 = f32[32,32]{0,1:T(8,128)S(1)} collective-permute-done((f32[32,32]{0,1:T(8,128)S(1)}, f32[32,32]{0,1:T(8,128)S(1)}, u32[]{:S(2)}, u32[]{:S(2)}) %collective-permute-start.18) | collective-permute-done | bytes 4128 | tf_op jit(solution)/shard_map/ppermute | solution.py:156
  99.0 2.4 %collective-permute-start.19 = (f32[32,32]{0,1:T(8,128)S(1)}, f32[32,32]{0,1:T(8,128)S(1)}, u32[]{:S(2)}, u32[]{:S(2)}) collective-permute-start(f32[32,32]{0,1:T(8,128)S(1)} %add.39), channel_id=1, source_target_pairs={{0,128},{32,160},{64,192},{96,224},{128,0},{160,32},{192,64},{224,... | collective-permute-start | bytes 12296 | tf_op jit(solution)/shard_map/ppermute | solution.py:156
  101.3 1.7 %collective-permute-done.19 = f32[32,32]{0,1:T(8,128)S(1)} collective-permute-done((f32[32,32]{0,1:T(8,128)S(1)}, f32[32,32]{0,1:T(8,128)S(1)}, u32[]{:S(2)}, u32[]{:S(2)}) %collective-permute-start.19) | collective-permute-done | bytes 4128 | tf_op jit(solution)/shard_map/ppermute | solution.py:156
  103.1 2.9 %cholesky.18 = f32[32,32]{1,0:T(8,128)S(1)} custom-call(f32[32,32]{1,0:T(8,128)S(1)} %fusion.8), custom_call_target="Cholesky" | custom-call | tf_op jit(solution)/shard_map/jit(cholesky)/cholesky | solution.py:167
  106.1 0.6 compare_reduce_fusion
  106.7 0.6 fusion.13
  107.4 1.3 %select_select_fusion.l_ref = f32[32,32]{1,0:T(8,128)} fusion(f32[32,32]{1,0:T(8,128)S(1)} %cholesky.18, pred[]{:T(512)} %compare_reduce_fusion), kind=kLoop, calls=%fused_computation.6 | loop fusion | flops 3072 | bytes 8193 | tf_op jit(solution)/shard_map/jit(cholesky)/select_n | solution.py:167
  108.7 5.1 %shard_map.44 = f32[32,8,16,128]{3,2,1,0:T(8,128)} custom-call(f32[32,32]{1,0:T(8,128)} %select_select_fusion.l_ref, f32[32,8,16,128]{3,2,1,0:T(8,128)} %shard_map.43.y_ref), custom_call_target="tpu_custom_call" | custom-call | tf_op jit(solution)/shard_map/pallas_call | solution.py:144
  113.7 0.7 copy.8
  (47 shorter events, 0.2 us)
Async XLA Ops:
  0.6 7.8 %copy-start = (f32[32,8,16,128]{3,2,1,0:T(8,128)S(1)}, f32[32,8,16,128]{3,2,1,0:T(8,128)}, u32[]{:S(2)}) copy-start(f32[32,8,16,128]{3,2,1,0:T(8,128)} %refs_8_.1) | copy-start | bytes 6291460
  4.8 11.6 %copy-start.12 = (f32[32,8,128]{2,1,0:T(8,128)S(1)}, f32[32,8,128]{2,1,0:T(8,128)}, u32[]{:S(2)}) copy-start(f32[32,8,128]{2,1,0:T(8,128)} %shard_map.41) | copy-start | bytes 393220
  4.8 11.6 %collective-permute-start.5 = (f32[32,8,128]{2,1,0:T(8,128)}, f32[32,8,128]{2,1,0:T(8,128)S(1)}, u32[]{:S(2)}, u32[]{:S(2)}) collective-permute-start(f32[32,8,128]{2,1,0:T(8,128)} %shard_map.41), channel_id=1, source_target_pairs={{0,3},{1,0},{2,1},{3,2},{4,7},{5,4},{6,5},{7,6},{8,11},{9,8},{10,9... | collective-permute-start | bytes 393224 | tf_op jit(solution)/shard_map/ppermute | solution.py:101
  8.5 15.9 %collective-permute-start.1 = (f32[32,2,16,128]{3,2,1,0:T(8,128)S(1)}, f32[32,2,16,128]{3,2,1,0:T(8,128)S(1)}, u32[]{:S(2)}, u32[]{:S(2)}) collective-permute-start(f32[32,2,16,128]{3,2,1,0:T(8,128)S(1)} %get-tuple-element.14), channel_id=1, source_target_pairs={{0,224},{32,0},{64,32},{96,64},{128,96},{160,128},{192,160},{224,1... | collective-permute-start | bytes 1572872 | tf_op jit(solution)/shard_map/ppermute | solution.py:98
  9.4 15.0 %collective-permute-start = (f32[32,2,16,128]{3,2,1,0:T(8,128)S(1)}, f32[32,2,16,128]{3,2,1,0:T(8,128)S(1)}, u32[]{:S(2)}, u32[]{:S(2)}) collective-permute-start(f32[32,2,16,128]{3,2,1,0:T(8,128)S(1)} %get-tuple-element.15), channel_id=1, source_target_pairs={{0,32},{32,64},{64,96},{96,128},{128,160},{160,192},{192,224},{224... | collective-permute-start | bytes 1572872 | tf_op jit(solution)/shard_map/ppermute | solution.py:97
  10.8 10.8 %collective-permute-start.3 = (f32[32,8,2,128]{3,2,1,0:T(2,128)S(1)}, f32[32,8,2,128]{3,2,1,0:T(2,128)S(1)}, u32[]{:S(2)}, u32[]{:S(2)}) collective-permute-start(f32[32,8,2,128]{3,2,1,0:T(2,128)S(1)} %get-tuple-element.12), channel_id=1, source_target_pairs={{0,28},{4,0},{8,4},{12,8},{16,12},{20,16},{24,20},{28,24},{1,29},{... | collective-permute-start | bytes 786440 | tf_op jit(solution)/shard_map/ppermute | solution.py:98
  16.4 8.0 %collective-permute-start.2 = (f32[32,8,2,128]{3,2,1,0:T(2,128)S(1)}, f32[32,8,2,128]{3,2,1,0:T(2,128)S(1)}, u32[]{:S(2)}, u32[]{:S(2)}) collective-permute-start(f32[32,8,2,128]{3,2,1,0:T(2,128)S(1)} %get-tuple-element.13), channel_id=1, source_target_pairs={{0,4},{4,8},{8,12},{12,16},{16,20},{20,24},{24,28},{28,0},{1,5},{5... | collective-permute-start | bytes 786440 | tf_op jit(solution)/shard_map/ppermute | solution.py:97
  16.4 8.0 %copy-start.11 = (f32[32,8,128]{2,1,0:T(8,128)}, f32[32,8,128]{2,1,0:T(8,128)S(1)}, u32[]{:S(2)}) copy-start(f32[32,8,128]{2,1,0:T(8,128)S(1)} %collective-permute-done.5.refs_6_) | copy-start | bytes 393220
  16.4 5.1 %collective-permute-start.4 = (f32[32,8,128]{2,1,0:T(8,128)S(1)}, f32[32,8,128]{2,1,0:T(8,128)S(1)}, u32[]{:S(2)}, u32[]{:S(2)}) collective-permute-start(f32[32,8,128]{2,1,0:T(8,128)S(1)} %copy-done.12), channel_id=1, source_target_pairs={{0,1},{1,2},{2,3},{3,0},{4,5},{5,6},{6,7},{7,4},{8,9},{9,10},{10,1... | collective-permute-start | bytes 393224 | tf_op jit(solution)/shard_map/ppermute | solution.py:100
  21.5 2.9 %copy-start.13 = (f32[32,8,128]{2,1,0:T(8,128)}, f32[32,8,128]{2,1,0:T(8,128)S(1)}, u32[]{:S(2)}) copy-start(f32[32,8,128]{2,1,0:T(8,128)S(1)} %collective-permute-done.4.refs_5_) | copy-start | bytes 393220
  21.5 2.9 %copy-start.7 = (f32[32,8,2,128]{3,2,1,0:T(2,128)}, f32[32,8,2,128]{3,2,1,0:T(2,128)S(1)}, u32[]{:S(2)}) copy-start(f32[32,8,2,128]{3,2,1,0:T(2,128)S(1)} %collective-permute-done.3.refs_4_) | copy-start | bytes 786436
  24.4 0.7 copy-start.8
  24.4 0.9 copy-start.1
  25.3 0.8 copy-start.3
  37.6 8.5 %copy-start.14 = (f32[32,8,128]{2,1,0:T(8,128)S(1)}, f32[32,8,128]{2,1,0:T(8,128)}, u32[]{:S(2)}) copy-start(f32[32,8,128]{2,1,0:T(8,128)} %get-tuple-element.5) | copy-start | bytes 393220
  37.6 8.5 %collective-permute-start.11 = (f32[32,8,128]{2,1,0:T(8,128)}, f32[32,8,128]{2,1,0:T(8,128)S(1)}, u32[]{:S(2)}, u32[]{:S(2)}) collective-permute-start(f32[32,8,128]{2,1,0:T(8,128)} %get-tuple-element.5), channel_id=1, source_target_pairs={{0,3},{1,0},{2,1},{3,2},{4,7},{5,4},{6,5},{7,6},{8,11},{9,8},{10,9... | collective-permute-start | bytes 393224 | tf_op jit(solution)/shard_map/ppermute | solution.py:101
  39.4 13.3 %collective-permute-start.7 = (f32[32,2,16,128]{3,2,1,0:T(8,128)S(1)}, f32[32,2,16,128]{3,2,1,0:T(8,128)S(1)}, u32[]{:S(2)}, u32[]{:S(2)}) collective-permute-start(f32[32,2,16,128]{3,2,1,0:T(8,128)S(1)} %get-tuple-element.10), channel_id=1, source_target_pairs={{0,224},{32,0},{64,32},{96,64},{128,96},{160,128},{192,160},{224,1... | collective-permute-start | bytes 1572872 | tf_op jit(solution)/shard_map/ppermute | solution.py:98
  41.6 11.1 %collective-permute-start.6 = (f32[32,2,16,128]{3,2,1,0:T(8,128)S(1)}, f32[32,2,16,128]{3,2,1,0:T(8,128)S(1)}, u32[]{:S(2)}, u32[]{:S(2)}) collective-permute-start(f32[32,2,16,128]{3,2,1,0:T(8,128)S(1)} %get-tuple-element.11), channel_id=1, source_target_pairs={{0,32},{32,64},{64,96},{96,128},{128,160},{160,192},{192,224},{224... | collective-permute-start | bytes 1572872 | tf_op jit(solution)/shard_map/ppermute | solution.py:97
  44.5 7.1 %collective-permute-start.9 = (f32[32,8,2,128]{3,2,1,0:T(2,128)S(1)}, f32[32,8,2,128]{3,2,1,0:T(2,128)S(1)}, u32[]{:S(2)}, u32[]{:S(2)}) collective-permute-start(f32[32,8,2,128]{3,2,1,0:T(2,128)S(1)} %get-tuple-element.8), channel_id=1, source_target_pairs={{0,28},{4,0},{8,4},{12,8},{16,12},{20,16},{24,20},{28,24},{1,29},{... | collective-permute-start | bytes 786440 | tf_op jit(solution)/shard_map/ppermute | solution.py:98
  44.6 8.1 %collective-permute-start.8 = (f32[32,8,2,128]{3,2,1,0:T(2,128)S(1)}, f32[32,8,2,128]{3,2,1,0:T(2,128)S(1)}, u32[]{:S(2)}, u32[]{:S(2)}) collective-permute-start(f32[32,8,2,128]{3,2,1,0:T(2,128)S(1)} %get-tuple-element.9), channel_id=1, source_target_pairs={{0,4},{4,8},{8,12},{12,16},{16,20},{20,24},{24,28},{28,0},{1,5},{5... | collective-permute-start | bytes 786440 | tf_op jit(solution)/shard_map/ppermute | solution.py:97
  46.0 6.7 %copy-start.9 = (f32[32,8,128]{2,1,0:T(8,128)}, f32[32,8,128]{2,1,0:T(8,128)S(1)}, u32[]{:S(2)}) copy-start(f32[32,8,128]{2,1,0:T(8,128)S(1)} %collective-permute-done.11.refs_6_) | copy-start | bytes 393220
  46.0 5.6 %collective-permute-start.10 = (f32[32,8,128]{2,1,0:T(8,128)S(1)}, f32[32,8,128]{2,1,0:T(8,128)S(1)}, u32[]{:S(2)}, u32[]{:S(2)}) collective-permute-start(f32[32,8,128]{2,1,0:T(8,128)S(1)} %copy-done.14), channel_id=1, source_target_pairs={{0,1},{1,2},{2,3},{3,0},{4,5},{5,6},{6,7},{7,4},{8,9},{9,10},{10,1... | collective-permute-start | bytes 393224 | tf_op jit(solution)/shard_map/ppermute | solution.py:100
  51.6 1.1 copy-start.10
  51.6 1.1 copy-start.5
  52.7 0.7 copy-start.6
  52.7 0.9 copy-start.2
  53.6 0.8 copy-start.4
  68.5 2.7 %collective-permute-start.12 = (f32[32,32]{0,1:T(8,128)S(1)}, f32[32,32]{0,1:T(8,128)S(1)}, u32[]{:S(2)}, u32[]{:S(2)}) collective-permute-start(f32[32,32]{0,1:T(8,128)S(1)} %fusion.5), channel_id=1, source_target_pairs={{0,1},{1,0},{2,3},{3,2},{4,5},{5,4},{6,7},{7,6},{8,9},{9,8},{10,11... | collective-permute-start | bytes 12296 | tf_op jit(solution)/shard_map/ppermute | solution.py:156
  71.1 4.1 %collective-permute-start.13 = (f32[32,32]{0,1:T(8,128)S(1)}, f32[32,32]{0,1:T(8,128)S(1)}, u32[]{:S(2)}, u32[]{:S(2)}) collective-permute-start(f32[32,32]{0,1:T(8,128)S(1)} %add.33), channel_id=1, source_target_pairs={{0,2},{1,3},{2,0},{3,1},{4,6},{5,7},{6,4},{7,5},{8,10},{9,11},{10,... | collective-permute-start | bytes 12296 | tf_op jit(solution)/shard_map/ppermute | solution.py:156
  75.2 2.9 %collective-permute-start.14 = (f32[32,32]{0,1:T(8,128)S(1)}, f32[32,32]{0,1:T(8,128)S(1)}, u32[]{:S(2)}, u32[]{:S(2)}) collective-permute-start(f32[32,32]{0,1:T(8,128)S(1)} %add.34), channel_id=1, source_target_pairs={{0,4},{4,0},{8,12},{12,8},{16,20},{20,16},{24,28},{28,24},{1,5},{5... | collective-permute-start | bytes 12296 | tf_op jit(solution)/shard_map/ppermute | solution.py:156
  78.1 3.5 %collective-permute-start.15 = (f32[32,32]{0,1:T(8,128)S(1)}, f32[32,32]{0,1:T(8,128)S(1)}, u32[]{:S(2)}, u32[]{:S(2)}) collective-permute-start(f32[32,32]{0,1:T(8,128)S(1)} %add.35), channel_id=1, source_target_pairs={{0,8},{4,12},{8,0},{12,4},{16,24},{20,28},{24,16},{28,20},{1,9},{5... | collective-permute-start | bytes 12296 | tf_op jit(solution)/shard_map/ppermute | solution.py:156
  81.6 6.6 %collective-permute-start.16 = (f32[32,32]{0,1:T(8,128)S(1)}, f32[32,32]{0,1:T(8,128)S(1)}, u32[]{:S(2)}, u32[]{:S(2)}) collective-permute-start(f32[32,32]{0,1:T(8,128)S(1)} %add.36), channel_id=1, source_target_pairs={{0,16},{4,20},{8,24},{12,28},{16,0},{20,4},{24,8},{28,12},{1,17},{... | collective-permute-start | bytes 12296 | tf_op jit(solution)/shard_map/ppermute | solution.py:156
  88.2 8.1 %collective-permute-start.17 = (f32[32,32]{0,1:T(8,128)S(1)}, f32[32,32]{0,1:T(8,128)S(1)}, u32[]{:S(2)}, u32[]{:S(2)}) collective-permute-start(f32[32,32]{0,1:T(8,128)S(1)} %add.37), channel_id=1, source_target_pairs={{0,32},{32,0},{64,96},{96,64},{128,160},{160,128},{192,224},{224,1... | collective-permute-start | bytes 12296 | tf_op jit(solution)/shard_map/ppermute | solution.py:156
  96.4 2.6 %collective-permute-start.18 = (f32[32,32]{0,1:T(8,128)S(1)}, f32[32,32]{0,1:T(8,128)S(1)}, u32[]{:S(2)}, u32[]{:S(2)}) collective-permute-start(f32[32,32]{0,1:T(8,128)S(1)} %add.38), channel_id=1, source_target_pairs={{0,64},{32,96},{64,0},{96,32},{128,192},{160,224},{192,128},{224,1... | collective-permute-start | bytes 12296 | tf_op jit(solution)/shard_map/ppermute | solution.py:156
  99.0 4.1 %collective-permute-start.19 = (f32[32,32]{0,1:T(8,128)S(1)}, f32[32,32]{0,1:T(8,128)S(1)}, u32[]{:S(2)}, u32[]{:S(2)}) collective-permute-start(f32[32,32]{0,1:T(8,128)S(1)} %add.39), channel_id=1, source_target_pairs={{0,128},{32,160},{64,192},{96,224},{128,0},{160,32},{192,64},{224,... | collective-permute-start | bytes 12296 | tf_op jit(solution)/shard_map/ppermute | solution.py:156

commit v7 on v6

--- a/solution.py
+++ b/solution.py
@@ -17,14 +17,10 @@
     return [(i, (i + step) % n) for i in range(n)]
 
 
-def faces_of(plane):
-    return jnp.transpose(pltpu.roll(plane, 2, 1))[0:8]
-
-
-def halo_image(zlo, zhi):
-    rows = zlo.shape[1]
-    pad = jnp.zeros((rows - 2 * zlo.shape[0], rows), jnp.float32)
-    return jnp.transpose(jnp.concatenate([zlo, zhi, pad], axis=0))
+def face_lanes(plane, orbital, lane, packed):
+    cz = plane.shape[1]
+    rolled = pltpu.roll(plane, (4 * orbital + 2) % cz, 1)
+    return jnp.where(lane // 4 == orbital, rolled, packed)
 
 
 def stage_kernel(*refs, last):
@@ -36,10 +32,19 @@
          out_ref, face_ref) = refs
     nb, cx, cy, cz = f_ref.shape
     rows = cx * cy
+    step = pl.program_id(0)
     lane = lax.broadcasted_iota(jnp.int32, (rows, cz), 1)
     yid = lax.broadcasted_iota(jnp.int32, (cx, cy, cz), 1)
     pot = pot_ref[...]
+    zlo = zlo_ref[...]
+    zhi = zhi_ref[...]
+    if not last:
+        @pl.when(step == 0)
+        def _():
+            face_ref[...] = jnp.zeros(face_ref.shape, jnp.float32)
+        packed = face_ref[...]
     for b in range(nb):
+        orbital = step * nb + b
         f3 = f_ref[b]
         summed = 3.0 * TAPS[2] * f3
         ext = jnp.concatenate([xlo_ref[b], f3, xhi_ref[b]], axis=0)
@@ -54,11 +59,11 @@
         for shifted, weight in ((ym2, TAPS[0]), (ym1, TAPS[1]), (yp1, TAPS[3]), (yp2, TAPS[4])):
             summed = summed + weight * shifted
         f2 = f3.reshape(rows, cz)
-        zim = halo_image(zlo_ref[b], zhi_ref[b])
-        zm2 = jnp.where(lane < 2, zim, pltpu.roll(f2, 2, 1))
-        zm1 = jnp.where(lane < 1, pltpu.roll(zim, cz - 1, 1), pltpu.roll(f2, 1, 1))
-        zp1 = jnp.where(lane >= cz - 1, pltpu.roll(zim, cz - 11, 1), pltpu.roll(f2, cz - 1, 1))
-        zp2 = jnp.where(lane >= cz - 2, pltpu.roll(zim, cz - 12, 1), pltpu.roll(f2, cz - 2, 1))
+        base = 4 * orbital
+        zm2 = jnp.where(lane < 2, pltpu.roll(zlo, (cz - base) % cz, 1), pltpu.roll(f2, 2, 1))
+        zm1 = jnp.where(lane < 1, pltpu.roll(zlo, cz - 1 - base, 1), pltpu.roll(f2, 1, 1))
+        zp1 = jnp.where(lane >= cz - 1, pltpu.roll(zhi, cz - 3 - base, 1), pltpu.roll(f2, cz - 1, 1))
+        zp2 = jnp.where(lane >= cz - 2, pltpu.roll(zhi, cz - 4 - base, 1), pltpu.roll(f2, cz - 2, 1))
         summed = summed.reshape(rows, cz)
         for shifted, weight in ((zm2, TAPS[0]), (zm1, TAPS[1]), (zp1, TAPS[3]), (zp2, TAPS[4])):
             summed = summed + weight * shifted
@@ -68,23 +73,35 @@
             res = 2.0 * (h - 5.5 * f2) / 3.5 - orb_ref[b].reshape(rows, cz)
         else:
             res = (h - 5.5 * f2) / 3.5
-            face_ref[b] = faces_of(res)
+            packed = face_lanes(res, orbital, lane, packed)
         out_ref[b] = res.reshape(cx, cy, cz)
+    if not last:
+        face_ref[...] = packed
 
 
 def z_face_kernel(f_ref, face_ref):
     nb, cx, cy, cz = f_ref.shape
+    step = pl.program_id(0)
+    lane = lax.broadcasted_iota(jnp.int32, (cx * cy, cz), 1)
+
+    @pl.when(step == 0)
+    def _():
+        face_ref[...] = jnp.zeros(face_ref.shape, jnp.float32)
+
+    packed = face_ref[...]
     for b in range(nb):
-        face_ref[b] = faces_of(f_ref[b].reshape(cx * cy, cz))
+        packed = face_lanes(f_ref[b].reshape(cx * cy, cz), step * nb + b, lane, packed)
+    face_ref[...] = packed
 
 
 def z_faces(f):
     norb, cx, cy, cz = f.shape
     blk = pl.BlockSpec((BLOCK, cx, cy, cz), lambda i: (i, 0, 0, 0))
-    fblk = pl.BlockSpec((BLOCK, 8, cx * cy), lambda i: (i, 0, 0))
+    fblk = pl.BlockSpec((cx * cy, 4 * norb), lambda i: (0, 0))
     return pl.pallas_call(
         z_face_kernel, grid=(norb // BLOCK,), in_specs=[blk], out_specs=fblk,
-        out_shape=jax.ShapeDtypeStruct((norb, 8, cx * cy), jnp.float32), interpret=INTERPRET,
+        out_shape=jax.ShapeDtypeStruct((cx * cy, 4 * norb), jnp.float32), interpret=INTERPRET,
+        compiler_params=pltpu.CompilerParams(dimension_semantics=("arbitrary",)),
     )(f)
 
 
@@ -108,7 +125,7 @@
     blk = pl.BlockSpec((BLOCK, cx, cy, cz), lambda i: (i, 0, 0, 0))
     xblk = pl.BlockSpec((BLOCK, 2, cy, cz), lambda i: (i, 0, 0, 0))
     yblk = pl.BlockSpec((BLOCK, cx, 2, cz), lambda i: (i, 0, 0, 0))
-    fblk = pl.BlockSpec((BLOCK, 8, cx * cy), lambda i: (i, 0, 0))
+    fblk = pl.BlockSpec((cx * cy, 4 * norb), lambda i: (0, 0))
     pblk = pl.BlockSpec((cx, cy, cz), lambda i: (0, 0, 0))
     in_specs = [blk, xblk, xblk, yblk, yblk, fblk, fblk, pblk]
     args = [f, *rims, potential]
@@ -120,7 +137,7 @@
     else:
         out_specs = (blk, fblk)
         out_shape = (jax.ShapeDtypeStruct(f.shape, jnp.float32),
-                     jax.ShapeDtypeStruct((norb, 8, cx * cy), jnp.float32))
+                     jax.ShapeDtypeStruct((cx * cy, 4 * norb), jnp.float32))
     return pl.pallas_call(
         functools.partial(stage_kernel, last=last), grid=(norb // BLOCK,), in_specs=in_specs,
         out_specs=out_specs, out_shape=out_shape, interpret=INTERPRET,

time: 116 us -> 117 us (level)
  Pallas kernels: 28.6 us -> 25.5 us
  local copies, waits for them, and re-layouts: 7.37 us -> 10.4 us
  starting transfers between devices: 30.8 us -> 32.1 us
    ppermute x4, starting transfers between devices: 8.93 us -> 14.4 us  [exchange(): out.append(lax.ppermute(first, axis, shift_pairs(n, -1)))]
    ppermute x4, waiting for transfers between devices: 3.93 us -> 0.01 us  [exchange(): out.append(lax.ppermute(last, axis, shift_pairs(n, 1)))]
    ppermute x4, starting transfers between devices: 3.7 us -> 0.01 us  [exchange(): out.append(lax.ppermute(last, axis, shift_pairs(n, 1)))]
    ppermute x2, waiting for transfers between devices: 0.01 us -> 3.32 us  [exchange(): out.append(lax.ppermute(zface, 'gz', shift_pairs(n, -1)))]
    slice x4, local copies, waits for them, and re-layouts: 3.3 us -> 6.12 us  [exchange(): first = lax.slice_in_dim(f, 0, 2, axis=dim)]
    pallas_call x2, Pallas kernels: 19.3 us -> 17 us  [stage(): pl.pallas_call(functools.partial(stage_kernel, last=last), grid=(norb //...]
    unnamed x31 -> x27, local copies, waits for them, and re-layouts: 4 us -> 4.23 us
  transfers between devices with their start and end apart: 20 -> 20, of which waited for: 12 -> 12; matrix products, arithmetic and copies ran while one was open for 3% -> 3% of each run, Pallas kernels for 0% -> 3%
where the time goes in v7:
time: 117 us; the launch traced here: 116 us
  waiting for transfers between devices  35.7 us (31%)
  starting transfers between devices  32.1 us (27%)
  Pallas kernels  25.5 us (22%)
  local copies, waits for them, and re-layouts  10.4 us (9%)
  matrix products  6.19 us (5%)
  other arithmetic  5.54 us (5%)
    ppermute x8, waiting for transfers between devices, butterfly_sum(): c = c + lax.ppermute(c, axis, [(i, i ^ d) for i in range(n)])  22.9 us
    pallas_call x2, Pallas kernels, stage(): pl.pallas_call(functools.partial(stage_kernel, last=last), grid=(norb //...  17 us
    ppermute x4, starting transfers between devices, exchange(): out.append(lax.ppermute(first, axis, shift_pairs(n, -1)))  14.4 us
    ppermute x8, starting transfers between devices, butterfly_sum(): c = c + lax.ppermute(c, axis, [(i, i ^ d) for i in range(n)])  12.6 us
    ppermute x2, waiting for transfers between devices, exchange(): out.append(lax.ppermute(zface, 'gz', shift_pairs(n, 1)))  9.41 us
    dot_general x1, matrix products, per_device(): jnp.einsum('axyz,bxyz->ab', second, second, precision=HI) / all_cells  6.19 us
    slice x4, local copies, waits for them, and re-layouts, exchange(): first = lax.slice_in_dim(f, 0, 2, axis=dim)  6.12 us
    pallas_call x1, Pallas kernels, solve_lower(): pl.pallas_call(solve_kernel, grid=(cx // xb,), in_specs=[pl.BlockSpec(mem...  5.07 us
  transfers between devices with their start and end apart: 20, of which 12 were waited for; matrix products, arithmetic and copies ran while one was open for 3% of the time, Pallas kernels for 3%

profile of v7, /device:TPU:1, one launch (start us, length us, event | category | flops | bytes accessed | tf_op | source)
XLA Modules:
  0.0 116.2 jit_solution(7965015936859772713)
XLA Ops:
  0.6 1.3 %fusion.12 = (f32[32,2,16,128]{3,2,1,0:T(8,128)S(1)}, f32[32,2,16,128]{3,2,1,0:T(8,128)S(1)}) fusion(f32[32,8,16,128]{3,2,1,0:T(8,128)} %refs_8_.1), kind=kLoop, calls=%fused_computation.14 | loop fusion | bytes 2097152 | tf_op jit(solution)/shard_map/slice | solution.py:113
  1.9 3.2 %collective-permute-start.1 = (f32[32,2,16,128]{3,2,1,0:T(8,128)S(1)}, f32[32,2,16,128]{3,2,1,0:T(8,128)S(1)}, u32[]{:S(2)}, u32[]{:S(2)}) collective-permute-start(f32[32,2,16,128]{3,2,1,0:T(8,128)S(1)} %get-tuple-element.14), channel_id=1, source_target_pairs={{0,224},{32,0},{64,32},{96,64},{128,96},{160,128},{192,160},{224,1... | collective-permute-start | bytes 1572872 | tf_op jit(solution)/shard_map/ppermute | solution.py:115
  5.1 1.8 %fusion.11 = (f32[32,8,2,128]{3,2,1,0:T(2,128)S(1)}, f32[32,8,2,128]{3,2,1,0:T(2,128)S(1)}) fusion(f32[32,8,16,128]{3,2,1,0:T(8,128)} %refs_8_.1), kind=kLoop, calls=%fused_computation.13 | loop fusion | bytes 1048576 | tf_op jit(solution)/shard_map/slice | solution.py:113
  6.9 5.1 %collective-permute-start.3 = (f32[32,8,2,128]{3,2,1,0:T(2,128)S(1)}, f32[32,8,2,128]{3,2,1,0:T(2,128)S(1)}, u32[]{:S(2)}, u32[]{:S(2)}) collective-permute-start(f32[32,8,2,128]{3,2,1,0:T(2,128)S(1)} %get-tuple-element.12), channel_id=1, source_target_pairs={{0,28},{4,0},{8,4},{12,8},{16,12},{20,16},{24,20},{28,24},{1,29},{... | collective-permute-start | bytes 786440 | tf_op jit(solution)/shard_map/ppermute | solution.py:115
  12.0 3.4 %shard_map.41 = f32[128,128]{1,0:T(8,128)} custom-call(f32[32,8,16,128]{3,2,1,0:T(8,128)} %refs_8_.1), custom_call_target="tpu_custom_call" | custom-call | tf_op jit(solution)/shard_map/pallas_call | solution.py:101
  15.4 2.7 %collective-permute-start.5 = (f32[128,128]{1,0:T(8,128)}, f32[128,128]{1,0:T(8,128)S(1)}, u32[]{:S(2)}, u32[]{:S(2)}) collective-permute-start(f32[128,128]{1,0:T(8,128)} %shard_map.41), channel_id=1, source_target_pairs={{0,3},{1,0},{2,1},{3,2},{4,7},{5,4},{6,5},{7,6},{8,11},{9,8},{10,9... | collective-permute-start | bytes 196616 | tf_op jit(solution)/shard_map/ppermute | solution.py:118
  18.1 1.6 %collective-permute-done.5.refs_6_ = f32[128,128]{1,0:T(8,128)S(1)} collective-permute-done((f32[128,128]{1,0:T(8,128)}, f32[128,128]{1,0:T(8,128)S(1)}, u32[]{:S(2)}, u32[]{:S(2)}) %collective-permute-start.5) | collective-permute-done | bytes 65568 | tf_op jit(solution)/shard_map/ppermute | solution.py:118
  19.8 0.5 collective-permute-start.4
  20.3 4.5 %collective-permute-done.4.refs_5_ = f32[128,128]{1,0:T(8,128)S(1)} collective-permute-done((f32[128,128]{1,0:T(8,128)}, f32[128,128]{1,0:T(8,128)S(1)}, u32[]{:S(2)}, u32[]{:S(2)}) %collective-permute-start.4) | collective-permute-done | bytes 65568 | tf_op jit(solution)/shard_map/ppermute | solution.py:117
  24.9 0.6 copy-done.10
  25.4 0.1 copy-done.6
  25.5 0.1 copy-done.7
  25.6 0.2 copy-done
  25.8 0.8 copy-done.1
  26.7 9.5 %shard_map.42 = (f32[32,8,16,128]{3,2,1,0:T(8,128)}, f32[128,128]{1,0:T(8,128)}) custom-call(f32[32,8,16,128]{3,2,1,0:T(8,128)} %refs_8_.1, f32[32,2,16,128]{3,2,1,0:T(8,128)} %copy-done.1, f32[32,2,16,128]{3,2,1,0:T(8,128)} %copy-done, f32[32,8,2,128]{3,2,1,0:T(2,128)} %copy-done.7, f32[32,8,2,128]{3,2,1,0:T(2,128)} %copy-done.6, f32[128,128]{1,0:T(8,128)} %copy-done.10, ...), custom_call_target="tpu_custom_call" | custom-call | tf_op jit(solution)/shard_map/pallas_call | solution.py:141
  36.1 1.3 %fusion.10 = (f32[32,2,16,128]{3,2,1,0:T(8,128)S(1)}, f32[32,2,16,128]{3,2,1,0:T(8,128)S(1)}) fusion(f32[32,8,16,128]{3,2,1,0:T(8,128)} %get-tuple-element.4.refs_0_), kind=kLoop, calls=%fused_computation.12 | loop fusion | bytes 2097152 | tf_op jit(solution)/shard_map/slice | solution.py:113
  37.4 3.1 %collective-permute-start.7 = (f32[32,2,16,128]{3,2,1,0:T(8,128)S(1)}, f32[32,2,16,128]{3,2,1,0:T(8,128)S(1)}, u32[]{:S(2)}, u32[]{:S(2)}) collective-permute-start(f32[32,2,16,128]{3,2,1,0:T(8,128)S(1)} %get-tuple-element.10), channel_id=1, source_target_pairs={{0,224},{32,0},{64,32},{96,64},{128,96},{160,128},{192,160},{224,1... | collective-permute-start | bytes 1572872 | tf_op jit(solution)/shard_map/ppermute | solution.py:115
  40.5 1.8 %fusion.9 = (f32[32,8,2,128]{3,2,1,0:T(2,128)S(1)}, f32[32,8,2,128]{3,2,1,0:T(2,128)S(1)}) fusion(f32[32,8,16,128]{3,2,1,0:T(8,128)} %get-tuple-element.4.refs_0_), kind=kLoop, calls=%fused_computation.11 | loop fusion | bytes 1048576 | tf_op jit(solution)/shard_map/slice | solution.py:113
  42.3 3.0 %collective-permute-start.9 = (f32[32,8,2,128]{3,2,1,0:T(2,128)S(1)}, f32[32,8,2,128]{3,2,1,0:T(2,128)S(1)}, u32[]{:S(2)}, u32[]{:S(2)}) collective-permute-start(f32[32,8,2,128]{3,2,1,0:T(2,128)S(1)} %get-tuple-element.8), channel_id=1, source_target_pairs={{0,28},{4,0},{8,4},{12,8},{16,12},{20,16},{24,20},{28,24},{1,29},{... | collective-permute-start | bytes 786440 | tf_op jit(solution)/shard_map/ppermute | solution.py:115
  45.3 1.7 %collective-permute-start.11 = (f32[128,128]{1,0:T(8,128)S(1)}, f32[128,128]{1,0:T(8,128)S(1)}, u32[]{:S(2)}, u32[]{:S(2)}) collective-permute-start(f32[128,128]{1,0:T(8,128)S(1)} %copy-done.12), channel_id=1, source_target_pairs={{0,3},{1,0},{2,1},{3,2},{4,7},{5,4},{6,5},{7,6},{8,11},{9,8},{10,9... | collective-permute-start | bytes 196616 | tf_op jit(solution)/shard_map/ppermute | solution.py:118
  47.1 1.7 %collective-permute-done.11.refs_6_ = f32[128,128]{1,0:T(8,128)S(1)} collective-permute-done((f32[128,128]{1,0:T(8,128)S(1)}, f32[128,128]{1,0:T(8,128)S(1)}, u32[]{:S(2)}, u32[]{:S(2)}) %collective-permute-start.11) | collective-permute-done | bytes 65568 | tf_op jit(solution)/shard_map/ppermute | solution.py:118
  48.8 4.9 %collective-permute-done.10.refs_5_ = f32[128,128]{1,0:T(8,128)S(1)} collective-permute-done((f32[128,128]{1,0:T(8,128)S(1)}, f32[128,128]{1,0:T(8,128)S(1)}, u32[]{:S(2)}, u32[]{:S(2)}) %collective-permute-start.10) | collective-permute-done | bytes 65568 | tf_op jit(solution)/shard_map/ppermute | solution.py:117
  53.7 0.6 copy-done.11
  54.3 0.1 copy-done.4
  54.4 0.1 copy-done.5
  54.5 0.2 copy-done.2
  54.7 0.8 copy-done.3
  55.5 7.5 %shard_map.43.y_ref = f32[32,8,16,128]{3,2,1,0:T(8,128)} custom-call(f32[32,8,16,128]{3,2,1,0:T(8,128)} %get-tuple-element.4.refs_0_, f32[32,2,16,128]{3,2,1,0:T(8,128)} %copy-done.3, f32[32,2,16,128]{3,2,1,0:T(8,128)} %copy-done.2, f32[32,8,2,128]{3,2,1,0:T(2,128)} %copy-done.5, f32[32,8,2,128]{3,2,1,0:T(2,128)} %copy-done.4, f32[128,128]{1,0:T(8,128)} %copy-done.11, ...), custom_call_target="tpu_custom_call" | custom-call | tf_op jit(solution)/shard_map/pallas_call | solution.py:141
  63.0 6.2 %fusion.5 = f32[32,32]{0,1:T(8,128)S(1)} fusion(f32[32,8,16,128]{3,2,1,0:T(8,128)} %shard_map.43.y_ref), kind=kOutput, calls=%fused_computation.3 | convolution fusion | flops 201327616 | bytes 2101248 | tf_op jit(solution)/shard_map/axyz,bxyz->ab/dot_general | solution.py:183
  69.2 0.1 collective-permute-start.12
  69.3 2.6 %collective-permute-done.12 = f32[32,32]{0,1:T(8,128)S(1)} collective-permute-done((f32[32,32]{0,1:T(8,128)S(1)}, f32[32,32]{0,1:T(8,128)S(1)}, u32[]{:S(2)}, u32[]{:S(2)}) %collective-permute-start.12) | collective-permute-done | bytes 4128 | tf_op jit(solution)/shard_map/ppermute | solution.py:173
  71.9 1.2 %collective-permute-start.13 = (f32[32,32]{0,1:T(8,128)S(1)}, f32[32,32]{0,1:T(8,128)S(1)}, u32[]{:S(2)}, u32[]{:S(2)}) collective-permute-start(f32[32,32]{0,1:T(8,128)S(1)} %add.33), channel_id=1, source_target_pairs={{0,2},{1,3},{2,0},{3,1},{4,6},{5,7},{6,4},{7,5},{8,10},{9,11},{10,... | collective-permute-start | bytes 12296 | tf_op jit(solution)/shard_map/ppermute | solution.py:173
  73.1 2.9 %collective-permute-done.13 = f32[32,32]{0,1:T(8,128)S(1)} collective-permute-done((f32[32,32]{0,1:T(8,128)S(1)}, f32[32,32]{0,1:T(8,128)S(1)}, u32[]{:S(2)}, u32[]{:S(2)}) %collective-permute-start.13) | collective-permute-done | bytes 4128 | tf_op jit(solution)/shard_map/ppermute | solution.py:173
  76.0 2.6 %collective-permute-done.14 = f32[32,32]{0,1:T(8,128)S(1)} collective-permute-done((f32[32,32]{0,1:T(8,128)S(1)}, f32[32,32]{0,1:T(8,128)S(1)}, u32[]{:S(2)}, u32[]{:S(2)}) %collective-permute-start.14) | collective-permute-done | bytes 4128 | tf_op jit(solution)/shard_map/ppermute | solution.py:173
  78.6 3.7 %collective-permute-done.15 = f32[32,32]{0,1:T(8,128)S(1)} collective-permute-done((f32[32,32]{0,1:T(8,128)S(1)}, f32[32,32]{0,1:T(8,128)S(1)}, u32[]{:S(2)}, u32[]{:S(2)}) %collective-permute-start.15) | collective-permute-done | bytes 4128 | tf_op jit(solution)/shard_map/ppermute | solution.py:173
  82.3 1.6 %collective-permute-start.16 = (f32[32,32]{0,1:T(8,128)S(1)}, f32[32,32]{0,1:T(8,128)S(1)}, u32[]{:S(2)}, u32[]{:S(2)}) collective-permute-start(f32[32,32]{0,1:T(8,128)S(1)} %add.36), channel_id=1, source_target_pairs={{0,16},{4,20},{8,24},{12,28},{16,0},{20,4},{24,8},{28,12},{1,17},{... | collective-permute-start | bytes 12296 | tf_op jit(solution)/shard_map/ppermute | solution.py:173
  83.9 4.9 %collective-permute-done.16 = f32[32,32]{0,1:T(8,128)S(1)} collective-permute-done((f32[32,32]{0,1:T(8,128)S(1)}, f32[32,32]{0,1:T(8,128)S(1)}, u32[]{:S(2)}, u32[]{:S(2)}) %collective-permute-start.16) | collective-permute-done | bytes 4128 | tf_op jit(solution)/shard_map/ppermute | solution.py:173
  88.8 8.5 %collective-permute-start.17 = (f32[32,32]{0,1:T(8,128)S(1)}, f32[32,32]{0,1:T(8,128)S(1)}, u32[]{:S(2)}, u32[]{:S(2)}) collective-permute-start(f32[32,32]{0,1:T(8,128)S(1)} %add.37), channel_id=1, source_target_pairs={{0,32},{32,0},{64,96},{96,64},{128,160},{160,128},{192,224},{224,1... | collective-permute-start | bytes 12296 | tf_op jit(solution)/shard_map/ppermute | solution.py:173
  97.3 0.8 collective-permute-done.17
  98.1 2.6 %collective-permute-done.18 = f32[32,32]{0,1:T(8,128)S(1)} collective-permute-done((f32[32,32]{0,1:T(8,128)S(1)}, f32[32,32]{0,1:T(8,128)S(1)}, u32[]{:S(2)}, u32[]{:S(2)}) %collective-permute-start.18) | collective-permute-done | bytes 4128 | tf_op jit(solution)/shard_map/ppermute | solution.py:173
  100.7 1.2 %collective-permute-start.19 = (f32[32,32]{0,1:T(8,128)S(1)}, f32[32,32]{0,1:T(8,128)S(1)}, u32[]{:S(2)}, u32[]{:S(2)}) collective-permute-start(f32[32,32]{0,1:T(8,128)S(1)} %add.39), channel_id=1, source_target_pairs={{0,128},{32,160},{64,192},{96,224},{128,0},{160,32},{192,64},{224,... | collective-permute-start | bytes 12296 | tf_op jit(solution)/shard_map/ppermute | solution.py:173
  101.9 2.9 %collective-permute-done.19 = f32[32,32]{0,1:T(8,128)S(1)} collective-permute-done((f32[32,32]{0,1:T(8,128)S(1)}, f32[32,32]{0,1:T(8,128)S(1)}, u32[]{:S(2)}, u32[]{:S(2)}) %collective-permute-start.19) | collective-permute-done | bytes 4128 | tf_op jit(solution)/shard_map/ppermute | solution.py:173
  104.9 2.9 %cholesky.18 = f32[32,32]{1,0:T(8,128)S(1)} custom-call(f32[32,32]{1,0:T(8,128)S(1)} %fusion.8), custom_call_target="Cholesky" | custom-call | tf_op jit(solution)/shard_map/jit(cholesky)/cholesky | solution.py:184
  107.9 0.6 compare_reduce_fusion
  108.5 0.6 fusion.13
  109.2 1.3 %select_select_fusion.l_ref = f32[32,32]{1,0:T(8,128)} fusion(f32[32,32]{1,0:T(8,128)S(1)} %cholesky.18, pred[]{:T(512)} %compare_reduce_fusion), kind=kLoop, calls=%fused_computation.6 | loop fusion | flops 3072 | bytes 8193 | tf_op jit(solution)/shard_map/jit(cholesky)/select_n | solution.py:184
  110.4 5.1 %shard_map.44 = f32[32,8,16,128]{3,2,1,0:T(8,128)} custom-call(f32[32,32]{1,0:T(8,128)} %select_select_fusion.l_ref, f32[32,8,16,128]{3,2,1,0:T(8,128)} %shard_map.43.y_ref), custom_call_target="tpu_custom_call" | custom-call | tf_op jit(solution)/shard_map/pallas_call | solution.py:161
  115.5 0.7 copy.8
  (43 shorter events, 0.2 us)
Async XLA Ops:
  1.9 22.9 %collective-permute-start.1 = (f32[32,2,16,128]{3,2,1,0:T(8,128)S(1)}, f32[32,2,16,128]{3,2,1,0:T(8,128)S(1)}, u32[]{:S(2)}, u32[]{:S(2)}) collective-permute-start(f32[32,2,16,128]{3,2,1,0:T(8,128)S(1)} %get-tuple-element.14), channel_id=1, source_target_pairs={{0,224},{32,0},{64,32},{96,64},{128,96},{160,128},{192,160},{224,1... | collective-permute-start | bytes 1572872 | tf_op jit(solution)/shard_map/ppermute | solution.py:115
  5.1 19.7 %collective-permute-start = (f32[32,2,16,128]{3,2,1,0:T(8,128)S(1)}, f32[32,2,16,128]{3,2,1,0:T(8,128)S(1)}, u32[]{:S(2)}, u32[]{:S(2)}) collective-permute-start(f32[32,2,16,128]{3,2,1,0:T(8,128)S(1)} %get-tuple-element.15), channel_id=1, source_target_pairs={{0,32},{32,64},{64,96},{96,128},{128,160},{160,192},{192,224},{224... | collective-permute-start | bytes 1572872 | tf_op jit(solution)/shard_map/ppermute | solution.py:114
  6.9 17.9 %collective-permute-start.3 = (f32[32,8,2,128]{3,2,1,0:T(2,128)S(1)}, f32[32,8,2,128]{3,2,1,0:T(2,128)S(1)}, u32[]{:S(2)}, u32[]{:S(2)}) collective-permute-start(f32[32,8,2,128]{3,2,1,0:T(2,128)S(1)} %get-tuple-element.12), channel_id=1, source_target_pairs={{0,28},{4,0},{8,4},{12,8},{16,12},{20,16},{24,20},{28,24},{1,29},{... | collective-permute-start | bytes 786440 | tf_op jit(solution)/shard_map/ppermute | solution.py:115
  12.0 12.9 %collective-permute-start.2 = (f32[32,8,2,128]{3,2,1,0:T(2,128)S(1)}, f32[32,8,2,128]{3,2,1,0:T(2,128)S(1)}, u32[]{:S(2)}, u32[]{:S(2)}) collective-permute-start(f32[32,8,2,128]{3,2,1,0:T(2,128)S(1)} %get-tuple-element.13), channel_id=1, source_target_pairs={{0,4},{4,8},{8,12},{12,16},{16,20},{20,24},{24,28},{28,0},{1,5},{5... | collective-permute-start | bytes 786440 | tf_op jit(solution)/shard_map/ppermute | solution.py:114
  15.4 4.4 %collective-permute-start.5 = (f32[128,128]{1,0:T(8,128)}, f32[128,128]{1,0:T(8,128)S(1)}, u32[]{:S(2)}, u32[]{:S(2)}) collective-permute-start(f32[128,128]{1,0:T(8,128)} %shard_map.41), channel_id=1, source_target_pairs={{0,3},{1,0},{2,1},{3,2},{4,7},{5,4},{6,5},{7,6},{8,11},{9,8},{10,9... | collective-permute-start | bytes 196616 | tf_op jit(solution)/shard_map/ppermute | solution.py:118
  19.8 5.1 %copy-start.8 = (f32[128,128]{1,0:T(8,128)}, f32[128,128]{1,0:T(8,128)S(1)}, u32[]{:S(2)}) copy-start(f32[128,128]{1,0:T(8,128)S(1)} %collective-permute-done.5.refs_6_) | copy-start | bytes 196612
  19.8 5.0 %collective-permute-start.4 = (f32[128,128]{1,0:T(8,128)}, f32[128,128]{1,0:T(8,128)S(1)}, u32[]{:S(2)}, u32[]{:S(2)}) collective-permute-start(f32[128,128]{1,0:T(8,128)} %shard_map.41), channel_id=1, source_target_pairs={{0,1},{1,2},{2,3},{3,0},{4,5},{5,6},{6,7},{7,4},{8,9},{9,10},{10,1... | collective-permute-start | bytes 196616 | tf_op jit(solution)/shard_map/ppermute | solution.py:117
  24.8 0.6 copy-start.10
  24.8 0.7 copy-start.6
  24.8 0.8 copy-start.7
  24.8 1.0 copy-start
  25.8 0.8 copy-start.1
  36.1 9.2 %copy-start.12 = (f32[128,128]{1,0:T(8,128)S(1)}, f32[128,128]{1,0:T(8,128)}, u32[]{:S(2)}) copy-start(f32[128,128]{1,0:T(8,128)} %get-tuple-element.5) | copy-start | bytes 196612
  37.4 16.3 %collective-permute-start.7 = (f32[32,2,16,128]{3,2,1,0:T(8,128)S(1)}, f32[32,2,16,128]{3,2,1,0:T(8,128)S(1)}, u32[]{:S(2)}, u32[]{:S(2)}) collective-permute-start(f32[32,2,16,128]{3,2,1,0:T(8,128)S(1)} %get-tuple-element.10), channel_id=1, source_target_pairs={{0,224},{32,0},{64,32},{96,64},{128,96},{160,128},{192,160},{224,1... | collective-permute-start | bytes 1572872 | tf_op jit(solution)/shard_map/ppermute | solution.py:115
  40.5 13.2 %collective-permute-start.6 = (f32[32,2,16,128]{3,2,1,0:T(8,128)S(1)}, f32[32,2,16,128]{3,2,1,0:T(8,128)S(1)}, u32[]{:S(2)}, u32[]{:S(2)}) collective-permute-start(f32[32,2,16,128]{3,2,1,0:T(8,128)S(1)} %get-tuple-element.11), channel_id=1, source_target_pairs={{0,32},{32,64},{64,96},{96,128},{128,160},{160,192},{192,224},{224... | collective-permute-start | bytes 1572872 | tf_op jit(solution)/shard_map/ppermute | solution.py:114
  42.3 11.4 %collective-permute-start.9 = (f32[32,8,2,128]{3,2,1,0:T(2,128)S(1)}, f32[32,8,2,128]{3,2,1,0:T(2,128)S(1)}, u32[]{:S(2)}, u32[]{:S(2)}) collective-permute-start(f32[32,8,2,128]{3,2,1,0:T(2,128)S(1)} %get-tuple-element.8), channel_id=1, source_target_pairs={{0,28},{4,0},{8,4},{12,8},{16,12},{20,16},{24,20},{28,24},{1,29},{... | collective-permute-start | bytes 786440 | tf_op jit(solution)/shard_map/ppermute | solution.py:115
  45.3 8.3 %collective-permute-start.8 = (f32[32,8,2,128]{3,2,1,0:T(2,128)S(1)}, f32[32,8,2,128]{3,2,1,0:T(2,128)S(1)}, u32[]{:S(2)}, u32[]{:S(2)}) collective-permute-start(f32[32,8,2,128]{3,2,1,0:T(2,128)S(1)} %get-tuple-element.9), channel_id=1, source_target_pairs={{0,4},{4,8},{8,12},{12,16},{16,20},{20,24},{24,28},{28,0},{1,5},{5... | collective-permute-start | bytes 786440 | tf_op jit(solution)/shard_map/ppermute | solution.py:114
  45.3 3.4 %collective-permute-start.11 = (f32[128,128]{1,0:T(8,128)S(1)}, f32[128,128]{1,0:T(8,128)S(1)}, u32[]{:S(2)}, u32[]{:S(2)}) collective-permute-start(f32[128,128]{1,0:T(8,128)S(1)} %copy-done.12), channel_id=1, source_target_pairs={{0,3},{1,0},{2,1},{3,2},{4,7},{5,4},{6,5},{7,6},{8,11},{9,8},{10,9... | collective-permute-start | bytes 196616 | tf_op jit(solution)/shard_map/ppermute | solution.py:118
  48.7 5.0 %copy-start.9 = (f32[128,128]{1,0:T(8,128)}, f32[128,128]{1,0:T(8,128)S(1)}, u32[]{:S(2)}) copy-start(f32[128,128]{1,0:T(8,128)S(1)} %collective-permute-done.11.refs_6_) | copy-start | bytes 196612
  48.8 4.9 %collective-permute-start.10 = (f32[128,128]{1,0:T(8,128)S(1)}, f32[128,128]{1,0:T(8,128)S(1)}, u32[]{:S(2)}, u32[]{:S(2)}) collective-permute-start(f32[128,128]{1,0:T(8,128)S(1)} %copy-done.12), channel_id=1, source_target_pairs={{0,1},{1,2},{2,3},{3,0},{4,5},{5,6},{6,7},{7,4},{8,9},{9,10},{10,1... | collective-permute-start | bytes 196616 | tf_op jit(solution)/shard_map/ppermute | solution.py:117
  53.7 0.6 copy-start.11
  53.7 0.7 copy-start.4
  53.7 0.8 copy-start.5
  53.7 1.0 copy-start.2
  54.7 0.8 copy-start.3
  69.2 2.7 %collective-permute-start.12 = (f32[32,32]{0,1:T(8,128)S(1)}, f32[32,32]{0,1:T(8,128)S(1)}, u32[]{:S(2)}, u32[]{:S(2)}) collective-permute-start(f32[32,32]{0,1:T(8,128)S(1)} %fusion.5), channel_id=1, source_target_pairs={{0,1},{1,0},{2,3},{3,2},{4,5},{5,4},{6,7},{7,6},{8,9},{9,8},{10,11... | collective-permute-start | bytes 12296 | tf_op jit(solution)/shard_map/ppermute | solution.py:173
  71.9 4.1 %collective-permute-start.13 = (f32[32,32]{0,1:T(8,128)S(1)}, f32[32,32]{0,1:T(8,128)S(1)}, u32[]{:S(2)}, u32[]{:S(2)}) collective-permute-start(f32[32,32]{0,1:T(8,128)S(1)} %add.33), channel_id=1, source_target_pairs={{0,2},{1,3},{2,0},{3,1},{4,6},{5,7},{6,4},{7,5},{8,10},{9,11},{10,... | collective-permute-start | bytes 12296 | tf_op jit(solution)/shard_map/ppermute | solution.py:173
  76.0 2.6 %collective-permute-start.14 = (f32[32,32]{0,1:T(8,128)S(1)}, f32[32,32]{0,1:T(8,128)S(1)}, u32[]{:S(2)}, u32[]{:S(2)}) collective-permute-start(f32[32,32]{0,1:T(8,128)S(1)} %add.34), channel_id=1, source_target_pairs={{0,4},{4,0},{8,12},{12,8},{16,20},{20,16},{24,28},{28,24},{1,5},{5... | collective-permute-start | bytes 12296 | tf_op jit(solution)/shard_map/ppermute | solution.py:173
  78.6 3.7 %collective-permute-start.15 = (f32[32,32]{0,1:T(8,128)S(1)}, f32[32,32]{0,1:T(8,128)S(1)}, u32[]{:S(2)}, u32[]{:S(2)}) collective-permute-start(f32[32,32]{0,1:T(8,128)S(1)} %add.35), channel_id=1, source_target_pairs={{0,8},{4,12},{8,0},{12,4},{16,24},{20,28},{24,16},{28,20},{1,9},{5... | collective-permute-start | bytes 12296 | tf_op jit(solution)/shard_map/ppermute | solution.py:173
  82.3 6.5 %collective-permute-start.16 = (f32[32,32]{0,1:T(8,128)S(1)}, f32[32,32]{0,1:T(8,128)S(1)}, u32[]{:S(2)}, u32[]{:S(2)}) collective-permute-start(f32[32,32]{0,1:T(8,128)S(1)} %add.36), channel_id=1, source_target_pairs={{0,16},{4,20},{8,24},{12,28},{16,0},{20,4},{24,8},{28,12},{1,17},{... | collective-permute-start | bytes 12296 | tf_op jit(solution)/shard_map/ppermute | solution.py:173
  88.8 9.4 %collective-permute-start.17 = (f32[32,32]{0,1:T(8,128)S(1)}, f32[32,32]{0,1:T(8,128)S(1)}, u32[]{:S(2)}, u32[]{:S(2)}) collective-permute-start(f32[32,32]{0,1:T(8,128)S(1)} %add.37), channel_id=1, source_target_pairs={{0,32},{32,0},{64,96},{96,64},{128,160},{160,128},{192,224},{224,1... | collective-permute-start | bytes 12296 | tf_op jit(solution)/shard_map/ppermute | solution.py:173
  98.1 2.6 %collective-permute-start.18 = (f32[32,32]{0,1:T(8,128)S(1)}, f32[32,32]{0,1:T(8,128)S(1)}, u32[]{:S(2)}, u32[]{:S(2)}) collective-permute-start(f32[32,32]{0,1:T(8,128)S(1)} %add.38), channel_id=1, source_target_pairs={{0,64},{32,96},{64,0},{96,32},{128,192},{160,224},{192,128},{224,1... | collective-permute-start | bytes 12296 | tf_op jit(solution)/shard_map/ppermute | solution.py:173
  100.7 4.1 %collective-permute-start.19 = (f32[32,32]{0,1:T(8,128)S(1)}, f32[32,32]{0,1:T(8,128)S(1)}, u32[]{:S(2)}, u32[]{:S(2)}) collective-permute-start(f32[32,32]{0,1:T(8,128)S(1)} %add.39), channel_id=1, source_target_pairs={{0,128},{32,160},{64,192},{96,224},{128,0},{160,32},{192,64},{224,... | collective-permute-start | bytes 12296 | tf_op jit(solution)/shard_map/ppermute | solution.py:173

commit v8 on v7

--- a/solution.py
+++ b/solution.py
@@ -149,14 +149,21 @@
     n = y_ref.shape[0]
     for j in range(n):
         acc = y_ref[j]
+        other = None
         for k in range(j):
-            acc = acc - l_ref[j, k] * o_ref[k]
+            term = l_ref[j, k] * o_ref[k]
+            if k % 2 == 0:
+                acc = acc - term
+            else:
+                other = term if other is None else other + term
+        if other is not None:
+            acc = acc - other
         o_ref[j] = acc / l_ref[j, j]
 
 
 def solve_lower(lower, y):
     norb, cx, cy, cz = y.shape
-    xb = 2
+    xb = 4
     blk = pl.BlockSpec((norb, xb, cy, cz), lambda i: (0, i, 0, 0))
     return pl.pallas_call(
         solve_kernel, grid=(cx // xb,),

time: 117 us -> 116 us (level)
  no operation moved by 1% of the time
where the time goes in v8:
time: 116 us
  waiting for transfers between devices  35.7 us (31%)
  starting transfers between devices  32.1 us (28%)
  Pallas kernels  25 us (22%)
  local copies, waits for them, and re-layouts  10.4 us (9%)
  matrix products  6.19 us (5%)
  other arithmetic  5.54 us (5%)
    ppermute x8, waiting for transfers between devices, butterfly_sum(): c = c + lax.ppermute(c, axis, [(i, i ^ d) for i in range(n)])  22.9 us
    pallas_call x2, Pallas kernels, stage(): pl.pallas_call(functools.partial(stage_kernel, last=last), grid=(norb //...  17 us
    ppermute x4, starting transfers between devices, exchange(): out.append(lax.ppermute(first, axis, shift_pairs(n, -1)))  14.4 us
    ppermute x8, starting transfers between devices, butterfly_sum(): c = c + lax.ppermute(c, axis, [(i, i ^ d) for i in range(n)])  12.6 us
    ppermute x2, waiting for transfers between devices, exchange(): out.append(lax.ppermute(zface, 'gz', shift_pairs(n, 1)))  9.41 us
    dot_general x1, matrix products, per_device(): jnp.einsum('axyz,bxyz->ab', second, second, precision=HI) / all_cells  6.19 us
    slice x4, local copies, waits for them, and re-layouts, exchange(): first = lax.slice_in_dim(f, 0, 2, axis=dim)  6.12 us
    pallas_call x1, Pallas kernels, solve_lower(): pl.pallas_call(solve_kernel, grid=(cx // xb,), in_specs=[pl.BlockSpec(mem...  4.61 us
  transfers between devices with their start and end apart: 20, of which 12 were waited for; matrix products, arithmetic and copies ran while one was open for 3% of the time, Pallas kernels for 3%

profile of v8, /device:TPU:1, one launch (start us, length us, event | category | flops | bytes accessed | tf_op | source)
XLA Modules:
  0.0 115.7 jit_solution(4664141090684035806)
XLA Ops:
  0.6 1.3 %fusion.12 = (f32[32,2,16,128]{3,2,1,0:T(8,128)S(1)}, f32[32,2,16,128]{3,2,1,0:T(8,128)S(1)}) fusion(f32[32,8,16,128]{3,2,1,0:T(8,128)} %refs_8_.1), kind=kLoop, calls=%fused_computation.14 | loop fusion | bytes 2097152 | tf_op jit(solution)/shard_map/slice | solution.py:113
  1.9 3.2 %collective-permute-start.1 = (f32[32,2,16,128]{3,2,1,0:T(8,128)S(1)}, f32[32,2,16,128]{3,2,1,0:T(8,128)S(1)}, u32[]{:S(2)}, u32[]{:S(2)}) collective-permute-start(f32[32,2,16,128]{3,2,1,0:T(8,128)S(1)} %get-tuple-element.14), channel_id=1, source_target_pairs={{0,224},{32,0},{64,32},{96,64},{128,96},{160,128},{192,160},{224,1... | collective-permute-start | bytes 1572872 | tf_op jit(solution)/shard_map/ppermute | solution.py:115
  5.1 1.8 %fusion.11 = (f32[32,8,2,128]{3,2,1,0:T(2,128)S(1)}, f32[32,8,2,128]{3,2,1,0:T(2,128)S(1)}) fusion(f32[32,8,16,128]{3,2,1,0:T(8,128)} %refs_8_.1), kind=kLoop, calls=%fused_computation.13 | loop fusion | bytes 1048576 | tf_op jit(solution)/shard_map/slice | solution.py:113
  6.9 5.1 %collective-permute-start.3 = (f32[32,8,2,128]{3,2,1,0:T(2,128)S(1)}, f32[32,8,2,128]{3,2,1,0:T(2,128)S(1)}, u32[]{:S(2)}, u32[]{:S(2)}) collective-permute-start(f32[32,8,2,128]{3,2,1,0:T(2,128)S(1)} %get-tuple-element.12), channel_id=1, source_target_pairs={{0,28},{4,0},{8,4},{12,8},{16,12},{20,16},{24,20},{28,24},{1,29},{... | collective-permute-start | bytes 786440 | tf_op jit(solution)/shard_map/ppermute | solution.py:115
  12.0 3.4 %shard_map.41 = f32[128,128]{1,0:T(8,128)} custom-call(f32[32,8,16,128]{3,2,1,0:T(8,128)} %refs_8_.1), custom_call_target="tpu_custom_call" | custom-call | tf_op jit(solution)/shard_map/pallas_call | solution.py:101
  15.4 2.7 %collective-permute-start.5 = (f32[128,128]{1,0:T(8,128)}, f32[128,128]{1,0:T(8,128)S(1)}, u32[]{:S(2)}, u32[]{:S(2)}) collective-permute-start(f32[128,128]{1,0:T(8,128)} %shard_map.41), channel_id=1, source_target_pairs={{0,3},{1,0},{2,1},{3,2},{4,7},{5,4},{6,5},{7,6},{8,11},{9,8},{10,9... | collective-permute-start | bytes 196616 | tf_op jit(solution)/shard_map/ppermute | solution.py:118
  18.1 1.6 %collective-permute-done.5.refs_6_ = f32[128,128]{1,0:T(8,128)S(1)} collective-permute-done((f32[128,128]{1,0:T(8,128)}, f32[128,128]{1,0:T(8,128)S(1)}, u32[]{:S(2)}, u32[]{:S(2)}) %collective-permute-start.5) | collective-permute-done | bytes 65568 | tf_op jit(solution)/shard_map/ppermute | solution.py:118
  19.8 0.5 collective-permute-start.4
  20.3 4.5 %collective-permute-done.4.refs_5_ = f32[128,128]{1,0:T(8,128)S(1)} collective-permute-done((f32[128,128]{1,0:T(8,128)}, f32[128,128]{1,0:T(8,128)S(1)}, u32[]{:S(2)}, u32[]{:S(2)}) %collective-permute-start.4) | collective-permute-done | bytes 65568 | tf_op jit(solution)/shard_map/ppermute | solution.py:117
  24.9 0.6 copy-done.10
  25.4 0.1 copy-done.6
  25.5 0.1 copy-done.7
  25.6 0.2 copy-done
  25.8 0.8 copy-done.1
  26.7 9.5 %shard_map.42 = (f32[32,8,16,128]{3,2,1,0:T(8,128)}, f32[128,128]{1,0:T(8,128)}) custom-call(f32[32,8,16,128]{3,2,1,0:T(8,128)} %refs_8_.1, f32[32,2,16,128]{3,2,1,0:T(8,128)} %copy-done.1, f32[32,2,16,128]{3,2,1,0:T(8,128)} %copy-done, f32[32,8,2,128]{3,2,1,0:T(2,128)} %copy-done.7, f32[32,8,2,128]{3,2,1,0:T(2,128)} %copy-done.6, f32[128,128]{1,0:T(8,128)} %copy-done.10, ...), custom_call_target="tpu_custom_call" | custom-call | tf_op jit(solution)/shard_map/pallas_call | solution.py:141
  36.1 1.3 %fusion.10 = (f32[32,2,16,128]{3,2,1,0:T(8,128)S(1)}, f32[32,2,16,128]{3,2,1,0:T(8,128)S(1)}) fusion(f32[32,8,16,128]{3,2,1,0:T(8,128)} %get-tuple-element.4.refs_0_), kind=kLoop, calls=%fused_computation.12 | loop fusion | bytes 2097152 | tf_op jit(solution)/shard_map/slice | solution.py:113
  37.4 3.1 %collective-permute-start.7 = (f32[32,2,16,128]{3,2,1,0:T(8,128)S(1)}, f32[32,2,16,128]{3,2,1,0:T(8,128)S(1)}, u32[]{:S(2)}, u32[]{:S(2)}) collective-permute-start(f32[32,2,16,128]{3,2,1,0:T(8,128)S(1)} %get-tuple-element.10), channel_id=1, source_target_pairs={{0,224},{32,0},{64,32},{96,64},{128,96},{160,128},{192,160},{224,1... | collective-permute-start | bytes 1572872 | tf_op jit(solution)/shard_map/ppermute | solution.py:115
  40.5 1.8 %fusion.9 = (f32[32,8,2,128]{3,2,1,0:T(2,128)S(1)}, f32[32,8,2,128]{3,2,1,0:T(2,128)S(1)}) fusion(f32[32,8,16,128]{3,2,1,0:T(8,128)} %get-tuple-element.4.refs_0_), kind=kLoop, calls=%fused_computation.11 | loop fusion | bytes 1048576 | tf_op jit(solution)/shard_map/slice | solution.py:113
  42.3 3.0 %collective-permute-start.9 = (f32[32,8,2,128]{3,2,1,0:T(2,128)S(1)}, f32[32,8,2,128]{3,2,1,0:T(2,128)S(1)}, u32[]{:S(2)}, u32[]{:S(2)}) collective-permute-start(f32[32,8,2,128]{3,2,1,0:T(2,128)S(1)} %get-tuple-element.8), channel_id=1, source_target_pairs={{0,28},{4,0},{8,4},{12,8},{16,12},{20,16},{24,20},{28,24},{1,29},{... | collective-permute-start | bytes 786440 | tf_op jit(solution)/shard_map/ppermute | solution.py:115
  45.3 1.7 %collective-permute-start.11 = (f32[128,128]{1,0:T(8,128)S(1)}, f32[128,128]{1,0:T(8,128)S(1)}, u32[]{:S(2)}, u32[]{:S(2)}) collective-permute-start(f32[128,128]{1,0:T(8,128)S(1)} %copy-done.12), channel_id=1, source_target_pairs={{0,3},{1,0},{2,1},{3,2},{4,7},{5,4},{6,5},{7,6},{8,11},{9,8},{10,9... | collective-permute-start | bytes 196616 | tf_op jit(solution)/shard_map/ppermute | solution.py:118
  47.1 1.7 %collective-permute-done.11.refs_6_ = f32[128,128]{1,0:T(8,128)S(1)} collective-permute-done((f32[128,128]{1,0:T(8,128)S(1)}, f32[128,128]{1,0:T(8,128)S(1)}, u32[]{:S(2)}, u32[]{:S(2)}) %collective-permute-start.11) | collective-permute-done | bytes 65568 | tf_op jit(solution)/shard_map/ppermute | solution.py:118
  48.8 4.9 %collective-permute-done.10.refs_5_ = f32[128,128]{1,0:T(8,128)S(1)} collective-permute-done((f32[128,128]{1,0:T(8,128)S(1)}, f32[128,128]{1,0:T(8,128)S(1)}, u32[]{:S(2)}, u32[]{:S(2)}) %collective-permute-start.10) | collective-permute-done | bytes 65568 | tf_op jit(solution)/shard_map/ppermute | solution.py:117
  53.7 0.6 copy-done.11
  54.3 0.1 copy-done.4
  54.4 0.1 copy-done.5
  54.5 0.2 copy-done.2
  54.7 0.8 copy-done.3
  55.5 7.5 %shard_map.43.y_ref = f32[32,8,16,128]{3,2,1,0:T(8,128)} custom-call(f32[32,8,16,128]{3,2,1,0:T(8,128)} %get-tuple-element.4.refs_0_, f32[32,2,16,128]{3,2,1,0:T(8,128)} %copy-done.3, f32[32,2,16,128]{3,2,1,0:T(8,128)} %copy-done.2, f32[32,8,2,128]{3,2,1,0:T(2,128)} %copy-done.5, f32[32,8,2,128]{3,2,1,0:T(2,128)} %copy-done.4, f32[128,128]{1,0:T(8,128)} %copy-done.11, ...), custom_call_target="tpu_custom_call" | custom-call | tf_op jit(solution)/shard_map/pallas_call | solution.py:141
  63.0 6.2 %fusion.5 = f32[32,32]{0,1:T(8,128)S(1)} fusion(f32[32,8,16,128]{3,2,1,0:T(8,128)} %shard_map.43.y_ref), kind=kOutput, calls=%fused_computation.3 | convolution fusion | flops 201327616 | bytes 2101248 | tf_op jit(solution)/shard_map/axyz,bxyz->ab/dot_general | solution.py:190
  69.2 0.1 collective-permute-start.12
  69.3 2.6 %collective-permute-done.12 = f32[32,32]{0,1:T(8,128)S(1)} collective-permute-done((f32[32,32]{0,1:T(8,128)S(1)}, f32[32,32]{0,1:T(8,128)S(1)}, u32[]{:S(2)}, u32[]{:S(2)}) %collective-permute-start.12) | collective-permute-done | bytes 4128 | tf_op jit(solution)/shard_map/ppermute | solution.py:180
  71.9 1.2 %collective-permute-start.13 = (f32[32,32]{0,1:T(8,128)S(1)}, f32[32,32]{0,1:T(8,128)S(1)}, u32[]{:S(2)}, u32[]{:S(2)}) collective-permute-start(f32[32,32]{0,1:T(8,128)S(1)} %add.33), channel_id=1, source_target_pairs={{0,2},{1,3},{2,0},{3,1},{4,6},{5,7},{6,4},{7,5},{8,10},{9,11},{10,... | collective-permute-start | bytes 12296 | tf_op jit(solution)/shard_map/ppermute | solution.py:180
  73.1 2.9 %collective-permute-done.13 = f32[32,32]{0,1:T(8,128)S(1)} collective-permute-done((f32[32,32]{0,1:T(8,128)S(1)}, f32[32,32]{0,1:T(8,128)S(1)}, u32[]{:S(2)}, u32[]{:S(2)}) %collective-permute-start.13) | collective-permute-done | bytes 4128 | tf_op jit(solution)/shard_map/ppermute | solution.py:180
  76.0 2.6 %collective-permute-done.14 = f32[32,32]{0,1:T(8,128)S(1)} collective-permute-done((f32[32,32]{0,1:T(8,128)S(1)}, f32[32,32]{0,1:T(8,128)S(1)}, u32[]{:S(2)}, u32[]{:S(2)}) %collective-permute-start.14) | collective-permute-done | bytes 4128 | tf_op jit(solution)/shard_map/ppermute | solution.py:180
  78.6 3.7 %collective-permute-done.15 = f32[32,32]{0,1:T(8,128)S(1)} collective-permute-done((f32[32,32]{0,1:T(8,128)S(1)}, f32[32,32]{0,1:T(8,128)S(1)}, u32[]{:S(2)}, u32[]{:S(2)}) %collective-permute-start.15) | collective-permute-done | bytes 4128 | tf_op jit(solution)/shard_map/ppermute | solution.py:180
  82.3 1.6 %collective-permute-start.16 = (f32[32,32]{0,1:T(8,128)S(1)}, f32[32,32]{0,1:T(8,128)S(1)}, u32[]{:S(2)}, u32[]{:S(2)}) collective-permute-start(f32[32,32]{0,1:T(8,128)S(1)} %add.36), channel_id=1, source_target_pairs={{0,16},{4,20},{8,24},{12,28},{16,0},{20,4},{24,8},{28,12},{1,17},{... | collective-permute-start | bytes 12296 | tf_op jit(solution)/shard_map/ppermute | solution.py:180
  83.9 4.9 %collective-permute-done.16 = f32[32,32]{0,1:T(8,128)S(1)} collective-permute-done((f32[32,32]{0,1:T(8,128)S(1)}, f32[32,32]{0,1:T(8,128)S(1)}, u32[]{:S(2)}, u32[]{:S(2)}) %collective-permute-start.16) | collective-permute-done | bytes 4128 | tf_op jit(solution)/shard_map/ppermute | solution.py:180
  88.8 8.5 %collective-permute-start.17 = (f32[32,32]{0,1:T(8,128)S(1)}, f32[32,32]{0,1:T(8,128)S(1)}, u32[]{:S(2)}, u32[]{:S(2)}) collective-permute-start(f32[32,32]{0,1:T(8,128)S(1)} %add.37), channel_id=1, source_target_pairs={{0,32},{32,0},{64,96},{96,64},{128,160},{160,128},{192,224},{224,1... | collective-permute-start | bytes 12296 | tf_op jit(solution)/shard_map/ppermute | solution.py:180
  97.3 0.8 collective-permute-done.17
  98.1 2.6 %collective-permute-done.18 = f32[32,32]{0,1:T(8,128)S(1)} collective-permute-done((f32[32,32]{0,1:T(8,128)S(1)}, f32[32,32]{0,1:T(8,128)S(1)}, u32[]{:S(2)}, u32[]{:S(2)}) %collective-permute-start.18) | collective-permute-done | bytes 4128 | tf_op jit(solution)/shard_map/ppermute | solution.py:180
  100.7 1.2 %collective-permute-start.19 = (f32[32,32]{0,1:T(8,128)S(1)}, f32[32,32]{0,1:T(8,128)S(1)}, u32[]{:S(2)}, u32[]{:S(2)}) collective-permute-start(f32[32,32]{0,1:T(8,128)S(1)} %add.39), channel_id=1, source_target_pairs={{0,128},{32,160},{64,192},{96,224},{128,0},{160,32},{192,64},{224,... | collective-permute-start | bytes 12296 | tf_op jit(solution)/shard_map/ppermute | solution.py:180
  101.9 2.9 %collective-permute-done.19 = f32[32,32]{0,1:T(8,128)S(1)} collective-permute-done((f32[32,32]{0,1:T(8,128)S(1)}, f32[32,32]{0,1:T(8,128)S(1)}, u32[]{:S(2)}, u32[]{:S(2)}) %collective-permute-start.19) | collective-permute-done | bytes 4128 | tf_op jit(solution)/shard_map/ppermute | solution.py:180
  104.9 2.9 %cholesky.18 = f32[32,32]{1,0:T(8,128)S(1)} custom-call(f32[32,32]{1,0:T(8,128)S(1)} %fusion.8), custom_call_target="Cholesky" | custom-call | tf_op jit(solution)/shard_map/jit(cholesky)/cholesky | solution.py:191
  107.9 0.6 compare_reduce_fusion
  108.5 0.6 fusion.13
  109.2 1.3 %select_select_fusion.l_ref = f32[32,32]{1,0:T(8,128)} fusion(f32[32,32]{1,0:T(8,128)S(1)} %cholesky.18, pred[]{:T(512)} %compare_reduce_fusion), kind=kLoop, calls=%fused_computation.6 | loop fusion | flops 3072 | bytes 8193 | tf_op jit(solution)/shard_map/jit(cholesky)/select_n | solution.py:191
  110.4 4.6 %shard_map.44 = f32[32,8,16,128]{3,2,1,0:T(8,128)} custom-call(f32[32,32]{1,0:T(8,128)} %select_select_fusion.l_ref, f32[32,8,16,128]{3,2,1,0:T(8,128)} %shard_map.43.y_ref), custom_call_target="tpu_custom_call" | custom-call | tf_op jit(solution)/shard_map/pallas_call | solution.py:168
  115.0 0.7 copy.8
  (43 shorter events, 0.2 us)
Async XLA Ops:
  1.9 22.9 %collective-permute-start.1 = (f32[32,2,16,128]{3,2,1,0:T(8,128)S(1)}, f32[32,2,16,128]{3,2,1,0:T(8,128)S(1)}, u32[]{:S(2)}, u32[]{:S(2)}) collective-permute-start(f32[32,2,16,128]{3,2,1,0:T(8,128)S(1)} %get-tuple-element.14), channel_id=1, source_target_pairs={{0,224},{32,0},{64,32},{96,64},{128,96},{160,128},{192,160},{224,1... | collective-permute-start | bytes 1572872 | tf_op jit(solution)/shard_map/ppermute | solution.py:115
  5.1 19.7 %collective-permute-start = (f32[32,2,16,128]{3,2,1,0:T(8,128)S(1)}, f32[32,2,16,128]{3,2,1,0:T(8,128)S(1)}, u32[]{:S(2)}, u32[]{:S(2)}) collective-permute-start(f32[32,2,16,128]{3,2,1,0:T(8,128)S(1)} %get-tuple-element.15), channel_id=1, source_target_pairs={{0,32},{32,64},{64,96},{96,128},{128,160},{160,192},{192,224},{224... | collective-permute-start | bytes 1572872 | tf_op jit(solution)/shard_map/ppermute | solution.py:114
  6.9 17.9 %collective-permute-start.3 = (f32[32,8,2,128]{3,2,1,0:T(2,128)S(1)}, f32[32,8,2,128]{3,2,1,0:T(2,128)S(1)}, u32[]{:S(2)}, u32[]{:S(2)}) collective-permute-start(f32[32,8,2,128]{3,2,1,0:T(2,128)S(1)} %get-tuple-element.12), channel_id=1, source_target_pairs={{0,28},{4,0},{8,4},{12,8},{16,12},{20,16},{24,20},{28,24},{1,29},{... | collective-permute-start | bytes 786440 | tf_op jit(solution)/shard_map/ppermute | solution.py:115
  12.0 12.9 %collective-permute-start.2 = (f32[32,8,2,128]{3,2,1,0:T(2,128)S(1)}, f32[32,8,2,128]{3,2,1,0:T(2,128)S(1)}, u32[]{:S(2)}, u32[]{:S(2)}) collective-permute-start(f32[32,8,2,128]{3,2,1,0:T(2,128)S(1)} %get-tuple-element.13), channel_id=1, source_target_pairs={{0,4},{4,8},{8,12},{12,16},{16,20},{20,24},{24,28},{28,0},{1,5},{5... | collective-permute-start | bytes 786440 | tf_op jit(solution)/shard_map/ppermute | solution.py:114
  15.4 4.4 %collective-permute-start.5 = (f32[128,128]{1,0:T(8,128)}, f32[128,128]{1,0:T(8,128)S(1)}, u32[]{:S(2)}, u32[]{:S(2)}) collective-permute-start(f32[128,128]{1,0:T(8,128)} %shard_map.41), channel_id=1, source_target_pairs={{0,3},{1,0},{2,1},{3,2},{4,7},{5,4},{6,5},{7,6},{8,11},{9,8},{10,9... | collective-permute-start | bytes 196616 | tf_op jit(solution)/shard_map/ppermute | solution.py:118
  19.8 5.1 %copy-start.8 = (f32[128,128]{1,0:T(8,128)}, f32[128,128]{1,0:T(8,128)S(1)}, u32[]{:S(2)}) copy-start(f32[128,128]{1,0:T(8,128)S(1)} %collective-permute-done.5.refs_6_) | copy-start | bytes 196612
  19.8 5.0 %collective-permute-start.4 = (f32[128,128]{1,0:T(8,128)}, f32[128,128]{1,0:T(8,128)S(1)}, u32[]{:S(2)}, u32[]{:S(2)}) collective-permute-start(f32[128,128]{1,0:T(8,128)} %shard_map.41), channel_id=1, source_target_pairs={{0,1},{1,2},{2,3},{3,0},{4,5},{5,6},{6,7},{7,4},{8,9},{9,10},{10,1... | collective-permute-start | bytes 196616 | tf_op jit(solution)/shard_map/ppermute | solution.py:117
  24.8 0.6 copy-start.10
  24.8 0.7 copy-start.6
  24.8 0.8 copy-start.7
  24.8 1.0 copy-start
  25.8 0.8 copy-start.1
  36.1 9.2 %copy-start.12 = (f32[128,128]{1,0:T(8,128)S(1)}, f32[128,128]{1,0:T(8,128)}, u32[]{:S(2)}) copy-start(f32[128,128]{1,0:T(8,128)} %get-tuple-element.5) | copy-start | bytes 196612
  37.4 16.3 %collective-permute-start.7 = (f32[32,2,16,128]{3,2,1,0:T(8,128)S(1)}, f32[32,2,16,128]{3,2,1,0:T(8,128)S(1)}, u32[]{:S(2)}, u32[]{:S(2)}) collective-permute-start(f32[32,2,16,128]{3,2,1,0:T(8,128)S(1)} %get-tuple-element.10), channel_id=1, source_target_pairs={{0,224},{32,0},{64,32},{96,64},{128,96},{160,128},{192,160},{224,1... | collective-permute-start | bytes 1572872 | tf_op jit(solution)/shard_map/ppermute | solution.py:115
  40.5 13.2 %collective-permute-start.6 = (f32[32,2,16,128]{3,2,1,0:T(8,128)S(1)}, f32[32,2,16,128]{3,2,1,0:T(8,128)S(1)}, u32[]{:S(2)}, u32[]{:S(2)}) collective-permute-start(f32[32,2,16,128]{3,2,1,0:T(8,128)S(1)} %get-tuple-element.11), channel_id=1, source_target_pairs={{0,32},{32,64},{64,96},{96,128},{128,160},{160,192},{192,224},{224... | collective-permute-start | bytes 1572872 | tf_op jit(solution)/shard_map/ppermute | solution.py:114
  42.3 11.4 %collective-permute-start.9 = (f32[32,8,2,128]{3,2,1,0:T(2,128)S(1)}, f32[32,8,2,128]{3,2,1,0:T(2,128)S(1)}, u32[]{:S(2)}, u32[]{:S(2)}) collective-permute-start(f32[32,8,2,128]{3,2,1,0:T(2,128)S(1)} %get-tuple-element.8), channel_id=1, source_target_pairs={{0,28},{4,0},{8,4},{12,8},{16,12},{20,16},{24,20},{28,24},{1,29},{... | collective-permute-start | bytes 786440 | tf_op jit(solution)/shard_map/ppermute | solution.py:115
  45.3 8.3 %collective-permute-start.8 = (f32[32,8,2,128]{3,2,1,0:T(2,128)S(1)}, f32[32,8,2,128]{3,2,1,0:T(2,128)S(1)}, u32[]{:S(2)}, u32[]{:S(2)}) collective-permute-start(f32[32,8,2,128]{3,2,1,0:T(2,128)S(1)} %get-tuple-element.9), channel_id=1, source_target_pairs={{0,4},{4,8},{8,12},{12,16},{16,20},{20,24},{24,28},{28,0},{1,5},{5... | collective-permute-start | bytes 786440 | tf_op jit(solution)/shard_map/ppermute | solution.py:114
  45.3 3.4 %collective-permute-start.11 = (f32[128,128]{1,0:T(8,128)S(1)}, f32[128,128]{1,0:T(8,128)S(1)}, u32[]{:S(2)}, u32[]{:S(2)}) collective-permute-start(f32[128,128]{1,0:T(8,128)S(1)} %copy-done.12), channel_id=1, source_target_pairs={{0,3},{1,0},{2,1},{3,2},{4,7},{5,4},{6,5},{7,6},{8,11},{9,8},{10,9... | collective-permute-start | bytes 196616 | tf_op jit(solution)/shard_map/ppermute | solution.py:118
  48.7 5.0 %copy-start.9 = (f32[128,128]{1,0:T(8,128)}, f32[128,128]{1,0:T(8,128)S(1)}, u32[]{:S(2)}) copy-start(f32[128,128]{1,0:T(8,128)S(1)} %collective-permute-done.11.refs_6_) | copy-start | bytes 196612
  48.8 4.9 %collective-permute-start.10 = (f32[128,128]{1,0:T(8,128)S(1)}, f32[128,128]{1,0:T(8,128)S(1)}, u32[]{:S(2)}, u32[]{:S(2)}) collective-permute-start(f32[128,128]{1,0:T(8,128)S(1)} %copy-done.12), channel_id=1, source_target_pairs={{0,1},{1,2},{2,3},{3,0},{4,5},{5,6},{6,7},{7,4},{8,9},{9,10},{10,1... | collective-permute-start | bytes 196616 | tf_op jit(solution)/shard_map/ppermute | solution.py:117
  53.7 0.6 copy-start.11
  53.7 0.7 copy-start.4
  53.7 0.8 copy-start.5
  53.7 1.0 copy-start.2
  54.7 0.8 copy-start.3
  69.2 2.7 %collective-permute-start.12 = (f32[32,32]{0,1:T(8,128)S(1)}, f32[32,32]{0,1:T(8,128)S(1)}, u32[]{:S(2)}, u32[]{:S(2)}) collective-permute-start(f32[32,32]{0,1:T(8,128)S(1)} %fusion.5), channel_id=1, source_target_pairs={{0,1},{1,0},{2,3},{3,2},{4,5},{5,4},{6,7},{7,6},{8,9},{9,8},{10,11... | collective-permute-start | bytes 12296 | tf_op jit(solution)/shard_map/ppermute | solution.py:180
  71.9 4.1 %collective-permute-start.13 = (f32[32,32]{0,1:T(8,128)S(1)}, f32[32,32]{0,1:T(8,128)S(1)}, u32[]{:S(2)}, u32[]{:S(2)}) collective-permute-start(f32[32,32]{0,1:T(8,128)S(1)} %add.33), channel_id=1, source_target_pairs={{0,2},{1,3},{2,0},{3,1},{4,6},{5,7},{6,4},{7,5},{8,10},{9,11},{10,... | collective-permute-start | bytes 12296 | tf_op jit(solution)/shard_map/ppermute | solution.py:180
  76.0 2.6 %collective-permute-start.14 = (f32[32,32]{0,1:T(8,128)S(1)}, f32[32,32]{0,1:T(8,128)S(1)}, u32[]{:S(2)}, u32[]{:S(2)}) collective-permute-start(f32[32,32]{0,1:T(8,128)S(1)} %add.34), channel_id=1, source_target_pairs={{0,4},{4,0},{8,12},{12,8},{16,20},{20,16},{24,28},{28,24},{1,5},{5... | collective-permute-start | bytes 12296 | tf_op jit(solution)/shard_map/ppermute | solution.py:180
  78.6 3.7 %collective-permute-start.15 = (f32[32,32]{0,1:T(8,128)S(1)}, f32[32,32]{0,1:T(8,128)S(1)}, u32[]{:S(2)}, u32[]{:S(2)}) collective-permute-start(f32[32,32]{0,1:T(8,128)S(1)} %add.35), channel_id=1, source_target_pairs={{0,8},{4,12},{8,0},{12,4},{16,24},{20,28},{24,16},{28,20},{1,9},{5... | collective-permute-start | bytes 12296 | tf_op jit(solution)/shard_map/ppermute | solution.py:180
  82.3 6.5 %collective-permute-start.16 = (f32[32,32]{0,1:T(8,128)S(1)}, f32[32,32]{0,1:T(8,128)S(1)}, u32[]{:S(2)}, u32[]{:S(2)}) collective-permute-start(f32[32,32]{0,1:T(8,128)S(1)} %add.36), channel_id=1, source_target_pairs={{0,16},{4,20},{8,24},{12,28},{16,0},{20,4},{24,8},{28,12},{1,17},{... | collective-permute-start | bytes 12296 | tf_op jit(solution)/shard_map/ppermute | solution.py:180
  88.8 9.4 %collective-permute-start.17 = (f32[32,32]{0,1:T(8,128)S(1)}, f32[32,32]{0,1:T(8,128)S(1)}, u32[]{:S(2)}, u32[]{:S(2)}) collective-permute-start(f32[32,32]{0,1:T(8,128)S(1)} %add.37), channel_id=1, source_target_pairs={{0,32},{32,0},{64,96},{96,64},{128,160},{160,128},{192,224},{224,1... | collective-permute-start | bytes 12296 | tf_op jit(solution)/shard_map/ppermute | solution.py:180
  98.1 2.6 %collective-permute-start.18 = (f32[32,32]{0,1:T(8,128)S(1)}, f32[32,32]{0,1:T(8,128)S(1)}, u32[]{:S(2)}, u32[]{:S(2)}) collective-permute-start(f32[32,32]{0,1:T(8,128)S(1)} %add.38), channel_id=1, source_target_pairs={{0,64},{32,96},{64,0},{96,32},{128,192},{160,224},{192,128},{224,1... | collective-permute-start | bytes 12296 | tf_op jit(solution)/shard_map/ppermute | solution.py:180
  100.7 4.1 %collective-permute-start.19 = (f32[32,32]{0,1:T(8,128)S(1)}, f32[32,32]{0,1:T(8,128)S(1)}, u32[]{:S(2)}, u32[]{:S(2)}) collective-permute-start(f32[32,32]{0,1:T(8,128)S(1)} %add.39), channel_id=1, source_target_pairs={{0,128},{32,160},{64,192},{96,224},{128,0},{160,32},{192,64},{224,... | collective-permute-start | bytes 12296 | tf_op jit(solution)/shard_map/ppermute | solution.py:180

commit v9 on v8

--- a/solution.py
+++ b/solution.py
@@ -172,6 +172,49 @@
     )(lower, y)
 
 
+def gram_kernel(y_ref, o_ref, acc_ref):
+    n, xb, cy, cz = y_ref.shape
+    step = pl.program_id(0)
+
+    @pl.when(step == 0)
+    def _():
+        acc_ref[...] = jnp.zeros(acc_ref.shape, jnp.float32)
+
+    idx = 0
+    for a in range(n):
+        ya = y_ref[a].reshape(xb * cy // 8, 8, cz)
+        for b in range(a, n):
+            yb = y_ref[b].reshape(xb * cy // 8, 8, cz)
+            acc_ref[idx] += (ya * yb).sum(axis=0)
+            idx += 1
+
+    @pl.when(step == pl.num_programs(0) - 1)
+    def _():
+        idx = 0
+        for a in range(n):
+            for b in range(a, n):
+                row = jnp.sum(acc_ref[idx], axis=0, keepdims=True)
+                o_ref[pl.ds(a * n + b, 1), :] = row
+                if b != a:
+                    o_ref[pl.ds(b * n + a, 1), :] = row
+                idx += 1
+
+
+def gram(y):
+    norb, cx, cy, cz = y.shape
+    xb = 4
+    pairs = norb * (norb + 1) // 2
+    lanes = pl.pallas_call(
+        gram_kernel, grid=(cx // xb,),
+        in_specs=[pl.BlockSpec((norb, xb, cy, cz), lambda i: (0, i, 0, 0))],
+        out_specs=pl.BlockSpec((norb * norb, cz), lambda i: (0, 0)),
+        out_shape=jax.ShapeDtypeStruct((norb * norb, cz), jnp.float32),
+        scratch_shapes=[pltpu.VMEM((pairs, 8, cz), jnp.float32)], interpret=INTERPRET,
+        compiler_params=pltpu.CompilerParams(dimension_semantics=("arbitrary",)),
+    )(y)
+    return lanes.sum(axis=1).reshape(norb, norb)
+
+
 def butterfly_sum(c):
     for axis in ("gz", "gy", "gx"):
         n = lax.axis_size(axis)
@@ -187,7 +230,7 @@
     second = stage(first, exchange(first, first_z), potential, orbitals)
     norb_count = orbitals.shape[0]
     all_cells = second[0].size * lax.axis_size("gx") * lax.axis_size("gy") * lax.axis_size("gz")
-    correlation = jnp.einsum("axyz,bxyz->ab", second, second, precision=HI) / all_cells
+    correlation = gram(second) / all_cells
     lower = jnp.linalg.cholesky(butterfly_sum(correlation))
     basis = solve_lower(lower, second)
     return (basis, lower.T)

time: 116 us -> 116 us (level)
  matrix products: 6.19 us -> 0 us
  Pallas kernels: 25 us -> 29.9 us
  other arithmetic: 5.54 us -> 6.79 us
    dot_general x1 -> x0, matrix products: 6.19 us -> none  [per_device(): jnp.einsum('axyz,bxyz->ab', second, second, precision=HI) / all_cells]
    pallas_call x0 -> x1, Pallas kernels: none -> 4.89 us  [gram(): pl.pallas_call(gram_kernel, grid=(cx // xb,), in_specs=[pl.BlockSpec((nor...]
    reduce_sum x0 -> x1, other arithmetic: none -> 1.25 us  [gram(): return lanes.sum(axis=1).reshape(norb, norb)]
where the time goes in v9:
time: 116 us
  waiting for transfers between devices  35.5 us (31%)
  starting transfers between devices  32.3 us (28%)
  Pallas kernels  29.9 us (26%)
  local copies, waits for them, and re-layouts  10.6 us (9%)
  other arithmetic  6.79 us (6%)
    ppermute x8, waiting for transfers between devices, butterfly_sum(): c = c + lax.ppermute(c, axis, [(i, i ^ d) for i in range(n)])  22.8 us
    pallas_call x2, Pallas kernels, stage(): pl.pallas_call(functools.partial(stage_kernel, last=last), grid=(norb //...  17 us
    ppermute x4, starting transfers between devices, exchange(): out.append(lax.ppermute(first, axis, shift_pairs(n, -1)))  14.4 us
    ppermute x8, starting transfers between devices, butterfly_sum(): c = c + lax.ppermute(c, axis, [(i, i ^ d) for i in range(n)])  12.9 us
    ppermute x2, waiting for transfers between devices, exchange(): out.append(lax.ppermute(zface, 'gz', shift_pairs(n, 1)))  9.41 us
    slice x4, local copies, waits for them, and re-layouts, exchange(): first = lax.slice_in_dim(f, 0, 2, axis=dim)  6.12 us
    pallas_call x1, Pallas kernels, gram(): pl.pallas_call(gram_kernel, grid=(cx // xb,), in_specs=[pl.BlockSpec((nor...  4.89 us
    pallas_call x1, Pallas kernels, solve_lower(): pl.pallas_call(solve_kernel, grid=(cx // xb,), in_specs=[pl.BlockSpec(mem...  4.61 us
  transfers between devices with their start and end apart: 20, of which 12 were waited for; matrix products, arithmetic and copies ran while one was open for 3% of the time, Pallas kernels for 3%

profile of v9, /device:TPU:1, one launch (start us, length us, event | category | flops | bytes accessed | tf_op | source)
XLA Modules:
  0.0 115.9 jit_solution(9085845892837261838)
XLA Ops:
  0.6 1.3 %fusion.4 = (f32[32,2,16,128]{3,2,1,0:T(8,128)S(1)}, f32[32,2,16,128]{3,2,1,0:T(8,128)S(1)}) fusion(f32[32,8,16,128]{3,2,1,0:T(8,128)} %refs_8_.1), kind=kLoop, calls=%fused_computation.11 | loop fusion | bytes 2097152 | tf_op jit(solution)/shard_map/slice | solution.py:113
  1.9 3.2 %collective-permute-start.1 = (f32[32,2,16,128]{3,2,1,0:T(8,128)S(1)}, f32[32,2,16,128]{3,2,1,0:T(8,128)S(1)}, u32[]{:S(2)}, u32[]{:S(2)}) collective-permute-start(f32[32,2,16,128]{3,2,1,0:T(8,128)S(1)} %get-tuple-element.16), channel_id=1, source_target_pairs={{0,224},{32,0},{64,32},{96,64},{128,96},{160,128},{192,160},{224,1... | collective-permute-start | bytes 1572872 | tf_op jit(solution)/shard_map/ppermute | solution.py:115
  5.1 1.8 %fusion.3 = (f32[32,8,2,128]{3,2,1,0:T(2,128)S(1)}, f32[32,8,2,128]{3,2,1,0:T(2,128)S(1)}) fusion(f32[32,8,16,128]{3,2,1,0:T(8,128)} %refs_8_.1), kind=kLoop, calls=%fused_computation.10 | loop fusion | bytes 1048576 | tf_op jit(solution)/shard_map/slice | solution.py:113
  6.9 5.1 %collective-permute-start.3 = (f32[32,8,2,128]{3,2,1,0:T(2,128)S(1)}, f32[32,8,2,128]{3,2,1,0:T(2,128)S(1)}, u32[]{:S(2)}, u32[]{:S(2)}) collective-permute-start(f32[32,8,2,128]{3,2,1,0:T(2,128)S(1)} %get-tuple-element.14), channel_id=1, source_target_pairs={{0,28},{4,0},{8,4},{12,8},{16,12},{20,16},{24,20},{28,24},{1,29},{... | collective-permute-start | bytes 786440 | tf_op jit(solution)/shard_map/ppermute | solution.py:115
  12.0 3.4 %shard_map.41 = f32[128,128]{1,0:T(8,128)} custom-call(f32[32,8,16,128]{3,2,1,0:T(8,128)} %refs_8_.1), custom_call_target="tpu_custom_call" | custom-call | tf_op jit(solution)/shard_map/pallas_call | solution.py:101
  15.4 2.7 %collective-permute-start.5 = (f32[128,128]{1,0:T(8,128)}, f32[128,128]{1,0:T(8,128)S(1)}, u32[]{:S(2)}, u32[]{:S(2)}) collective-permute-start(f32[128,128]{1,0:T(8,128)} %shard_map.41), channel_id=1, source_target_pairs={{0,3},{1,0},{2,1},{3,2},{4,7},{5,4},{6,5},{7,6},{8,11},{9,8},{10,9... | collective-permute-start | bytes 196616 | tf_op jit(solution)/shard_map/ppermute | solution.py:118
  18.1 1.6 %collective-permute-done.5.refs_6_ = f32[128,128]{1,0:T(8,128)S(1)} collective-permute-done((f32[128,128]{1,0:T(8,128)}, f32[128,128]{1,0:T(8,128)S(1)}, u32[]{:S(2)}, u32[]{:S(2)}) %collective-permute-start.5) | collective-permute-done | bytes 65568 | tf_op jit(solution)/shard_map/ppermute | solution.py:118
  19.8 0.5 collective-permute-start.4
  20.3 4.5 %collective-permute-done.4.refs_5_ = f32[128,128]{1,0:T(8,128)S(1)} collective-permute-done((f32[128,128]{1,0:T(8,128)}, f32[128,128]{1,0:T(8,128)S(1)}, u32[]{:S(2)}, u32[]{:S(2)}) %collective-permute-start.4) | collective-permute-done | bytes 65568 | tf_op jit(solution)/shard_map/ppermute | solution.py:117
  24.9 0.6 copy-done.10
  25.4 0.1 copy-done.6
  25.5 0.1 copy-done.7
  25.6 0.2 copy-done
  25.8 0.8 copy-done.1
  26.7 9.4 %shard_map.42 = (f32[32,8,16,128]{3,2,1,0:T(8,128)}, f32[128,128]{1,0:T(8,128)}) custom-call(f32[32,8,16,128]{3,2,1,0:T(8,128)} %refs_8_.1, f32[32,2,16,128]{3,2,1,0:T(8,128)} %copy-done.1, f32[32,2,16,128]{3,2,1,0:T(8,128)} %copy-done, f32[32,8,2,128]{3,2,1,0:T(2,128)} %copy-done.7, f32[32,8,2,128]{3,2,1,0:T(2,128)} %copy-done.6, f32[128,128]{1,0:T(8,128)} %copy-done.10, ...), custom_call_target="tpu_custom_call" | custom-call | tf_op jit(solution)/shard_map/pallas_call | solution.py:141
  36.1 1.3 %fusion.2 = (f32[32,2,16,128]{3,2,1,0:T(8,128)S(1)}, f32[32,2,16,128]{3,2,1,0:T(8,128)S(1)}) fusion(f32[32,8,16,128]{3,2,1,0:T(8,128)} %get-tuple-element.4.refs_0_), kind=kLoop, calls=%fused_computation.9 | loop fusion | bytes 2097152 | tf_op jit(solution)/shard_map/slice | solution.py:113
  37.4 3.1 %collective-permute-start.7 = (f32[32,2,16,128]{3,2,1,0:T(8,128)S(1)}, f32[32,2,16,128]{3,2,1,0:T(8,128)S(1)}, u32[]{:S(2)}, u32[]{:S(2)}) collective-permute-start(f32[32,2,16,128]{3,2,1,0:T(8,128)S(1)} %get-tuple-element.12), channel_id=1, source_target_pairs={{0,224},{32,0},{64,32},{96,64},{128,96},{160,128},{192,160},{224,1... | collective-permute-start | bytes 1572872 | tf_op jit(solution)/shard_map/ppermute | solution.py:115
  40.5 1.8 %fusion.1 = (f32[32,8,2,128]{3,2,1,0:T(2,128)S(1)}, f32[32,8,2,128]{3,2,1,0:T(2,128)S(1)}) fusion(f32[32,8,16,128]{3,2,1,0:T(8,128)} %get-tuple-element.4.refs_0_), kind=kLoop, calls=%fused_computation.8 | loop fusion | bytes 1048576 | tf_op jit(solution)/shard_map/slice | solution.py:113
  42.3 3.0 %collective-permute-start.9 = (f32[32,8,2,128]{3,2,1,0:T(2,128)S(1)}, f32[32,8,2,128]{3,2,1,0:T(2,128)S(1)}, u32[]{:S(2)}, u32[]{:S(2)}) collective-permute-start(f32[32,8,2,128]{3,2,1,0:T(2,128)S(1)} %get-tuple-element.10), channel_id=1, source_target_pairs={{0,28},{4,0},{8,4},{12,8},{16,12},{20,16},{24,20},{28,24},{1,29},{... | collective-permute-start | bytes 786440 | tf_op jit(solution)/shard_map/ppermute | solution.py:115
  45.3 1.7 %collective-permute-start.11 = (f32[128,128]{1,0:T(8,128)S(1)}, f32[128,128]{1,0:T(8,128)S(1)}, u32[]{:S(2)}, u32[]{:S(2)}) collective-permute-start(f32[128,128]{1,0:T(8,128)S(1)} %copy-done.12), channel_id=1, source_target_pairs={{0,3},{1,0},{2,1},{3,2},{4,7},{5,4},{6,5},{7,6},{8,11},{9,8},{10,9... | collective-permute-start | bytes 196616 | tf_op jit(solution)/shard_map/ppermute | solution.py:118
  47.1 1.7 %collective-permute-done.11.refs_6_ = f32[128,128]{1,0:T(8,128)S(1)} collective-permute-done((f32[128,128]{1,0:T(8,128)S(1)}, f32[128,128]{1,0:T(8,128)S(1)}, u32[]{:S(2)}, u32[]{:S(2)}) %collective-permute-start.11) | collective-permute-done | bytes 65568 | tf_op jit(solution)/shard_map/ppermute | solution.py:118
  48.7 4.9 %collective-permute-done.10.refs_5_ = f32[128,128]{1,0:T(8,128)S(1)} collective-permute-done((f32[128,128]{1,0:T(8,128)S(1)}, f32[128,128]{1,0:T(8,128)S(1)}, u32[]{:S(2)}, u32[]{:S(2)}) %collective-permute-start.10) | collective-permute-done | bytes 65568 | tf_op jit(solution)/shard_map/ppermute | solution.py:117
  53.7 0.6 copy-done.11
  54.3 0.1 copy-done.4
  54.5 0.2 copy-done.2
  54.7 0.8 copy-done.3
  55.5 7.5 %shard_map.43.y_ref = f32[32,8,16,128]{3,2,1,0:T(8,128)} custom-call(f32[32,8,16,128]{3,2,1,0:T(8,128)} %get-tuple-element.4.refs_0_, f32[32,2,16,128]{3,2,1,0:T(8,128)} %copy-done.3, f32[32,2,16,128]{3,2,1,0:T(8,128)} %copy-done.2, f32[32,8,2,128]{3,2,1,0:T(2,128)} %copy-done.5, f32[32,8,2,128]{3,2,1,0:T(2,128)} %copy-done.4, f32[128,128]{1,0:T(8,128)} %copy-done.11, ...), custom_call_target="tpu_custom_call" | custom-call | tf_op jit(solution)/shard_map/pallas_call | solution.py:141
  63.0 4.9 %shard_map.44 = f32[1024,128]{1,0:T(8,128)} custom-call(f32[32,8,16,128]{3,2,1,0:T(8,128)} %shard_map.43.y_ref), custom_call_target="tpu_custom_call" | custom-call | tf_op jit(solution)/shard_map/pallas_call | solution.py:207
  67.9 1.2 %reduce_sum.9 = f32[1024]{0:T(1024)S(1)} reduce(f32[1024,128]{1,0:T(8,128)} %shard_map.44, f32[]{:T(128)} %constant.36.clone.1), dimensions={1}, to_apply=%region_0.0 | reduce | flops 130048 | bytes 528388 | tf_op jit(solution)/shard_map/reduce_sum | solution.py:215
  69.3 0.2 collective-permute-start.12
  69.5 2.6 %collective-permute-done.12 = f32[32,32]{0,1:T(8,128)S(1)} collective-permute-done((f32[32,32]{0,1:T(8,128)S(1)}, f32[32,32]{0,1:T(8,128)S(1)}, u32[]{:S(2)}, u32[]{:S(2)}) %collective-permute-start.12) | collective-permute-done | bytes 4128 | tf_op jit(solution)/shard_map/ppermute | solution.py:223
  72.1 1.2 %collective-permute-start.13 = (f32[32,32]{0,1:T(8,128)S(1)}, f32[32,32]{0,1:T(8,128)S(1)}, u32[]{:S(2)}, u32[]{:S(2)}) collective-permute-start(f32[32,32]{0,1:T(8,128)S(1)} %add.33), channel_id=1, source_target_pairs={{0,2},{1,3},{2,0},{3,1},{4,6},{5,7},{6,4},{7,5},{8,10},{9,11},{10,... | collective-permute-start | bytes 12296 | tf_op jit(solution)/shard_map/ppermute | solution.py:223
  73.3 2.9 %collective-permute-done.13 = f32[32,32]{0,1:T(8,128)S(1)} collective-permute-done((f32[32,32]{0,1:T(8,128)S(1)}, f32[32,32]{0,1:T(8,128)S(1)}, u32[]{:S(2)}, u32[]{:S(2)}) %collective-permute-start.13) | collective-permute-done | bytes 4128 | tf_op jit(solution)/shard_map/ppermute | solution.py:223
  76.2 2.6 %collective-permute-done.14 = f32[32,32]{0,1:T(8,128)S(1)} collective-permute-done((f32[32,32]{0,1:T(8,128)S(1)}, f32[32,32]{0,1:T(8,128)S(1)}, u32[]{:S(2)}, u32[]{:S(2)}) %collective-permute-start.14) | collective-permute-done | bytes 4128 | tf_op jit(solution)/shard_map/ppermute | solution.py:223
  78.8 3.7 %collective-permute-done.15 = f32[32,32]{0,1:T(8,128)S(1)} collective-permute-done((f32[32,32]{0,1:T(8,128)S(1)}, f32[32,32]{0,1:T(8,128)S(1)}, u32[]{:S(2)}, u32[]{:S(2)}) %collective-permute-start.15) | collective-permute-done | bytes 4128 | tf_op jit(solution)/shard_map/ppermute | solution.py:223
  82.5 1.6 %collective-permute-start.16 = (f32[32,32]{0,1:T(8,128)S(1)}, f32[32,32]{0,1:T(8,128)S(1)}, u32[]{:S(2)}, u32[]{:S(2)}) collective-permute-start(f32[32,32]{0,1:T(8,128)S(1)} %add.36), channel_id=1, source_target_pairs={{0,16},{4,20},{8,24},{12,28},{16,0},{20,4},{24,8},{28,12},{1,17},{... | collective-permute-start | bytes 12296 | tf_op jit(solution)/shard_map/ppermute | solution.py:223
  84.1 4.9 %collective-permute-done.16 = f32[32,32]{0,1:T(8,128)S(1)} collective-permute-done((f32[32,32]{0,1:T(8,128)S(1)}, f32[32,32]{0,1:T(8,128)S(1)}, u32[]{:S(2)}, u32[]{:S(2)}) %collective-permute-start.16) | collective-permute-done | bytes 4128 | tf_op jit(solution)/shard_map/ppermute | solution.py:223
  89.0 8.5 %collective-permute-start.17 = (f32[32,32]{0,1:T(8,128)S(1)}, f32[32,32]{0,1:T(8,128)S(1)}, u32[]{:S(2)}, u32[]{:S(2)}) collective-permute-start(f32[32,32]{0,1:T(8,128)S(1)} %add.37), channel_id=1, source_target_pairs={{0,32},{32,0},{64,96},{96,64},{128,160},{160,128},{192,224},{224,1... | collective-permute-start | bytes 12296 | tf_op jit(solution)/shard_map/ppermute | solution.py:223
  97.5 0.8 collective-permute-done.17
  98.4 2.6 %collective-permute-done.18 = f32[32,32]{0,1:T(8,128)S(1)} collective-permute-done((f32[32,32]{0,1:T(8,128)S(1)}, f32[32,32]{0,1:T(8,128)S(1)}, u32[]{:S(2)}, u32[]{:S(2)}) %collective-permute-start.18) | collective-permute-done | bytes 4128 | tf_op jit(solution)/shard_map/ppermute | solution.py:223
  101.0 1.3 %collective-permute-start.19 = (f32[32,32]{0,1:T(8,128)S(1)}, f32[32,32]{0,1:T(8,128)S(1)}, u32[]{:S(2)}, u32[]{:S(2)}) collective-permute-start(f32[32,32]{0,1:T(8,128)S(1)} %add.39), channel_id=1, source_target_pairs={{0,128},{32,160},{64,192},{96,224},{128,0},{160,32},{192,64},{224,... | collective-permute-start | bytes 12296 | tf_op jit(solution)/shard_map/ppermute | solution.py:223
  102.3 2.7 %collective-permute-done.19 = f32[32,32]{0,1:T(8,128)S(1)} collective-permute-done((f32[32,32]{0,1:T(8,128)S(1)}, f32[32,32]{0,1:T(8,128)S(1)}, u32[]{:S(2)}, u32[]{:S(2)}) %collective-permute-start.19) | collective-permute-done | bytes 4128 | tf_op jit(solution)/shard_map/ppermute | solution.py:223
  105.1 2.9 %cholesky.18 = f32[32,32]{1,0:T(8,128)S(1)} custom-call(f32[32,32]{1,0:T(8,128)S(1)} %fusion), custom_call_target="Cholesky" | custom-call | tf_op jit(solution)/shard_map/jit(cholesky)/cholesky | solution.py:234
  108.1 0.6 compare_reduce_fusion
  108.7 0.6 fusion.5
  109.4 1.3 %select_select_fusion.l_ref = f32[32,32]{1,0:T(8,128)} fusion(f32[32,32]{1,0:T(8,128)S(1)} %cholesky.18, pred[]{:T(512)} %compare_reduce_fusion), kind=kLoop, calls=%fused_computation.2 | loop fusion | flops 3072 | bytes 8193 | tf_op jit(solution)/shard_map/jit(cholesky)/select_n | solution.py:234
  110.6 4.6 %shard_map.45 = f32[32,8,16,128]{3,2,1,0:T(8,128)} custom-call(f32[32,32]{1,0:T(8,128)} %select_select_fusion.l_ref, f32[32,8,16,128]{3,2,1,0:T(8,128)} %shard_map.43.y_ref), custom_call_target="tpu_custom_call" | custom-call | tf_op jit(solution)/shard_map/pallas_call | solution.py:168
  115.3 0.7 copy.9
  (47 shorter events, 0.5 us)
Async XLA Ops:
  1.9 22.9 %collective-permute-start.1 = (f32[32,2,16,128]{3,2,1,0:T(8,128)S(1)}, f32[32,2,16,128]{3,2,1,0:T(8,128)S(1)}, u32[]{:S(2)}, u32[]{:S(2)}) collective-permute-start(f32[32,2,16,128]{3,2,1,0:T(8,128)S(1)} %get-tuple-element.16), channel_id=1, source_target_pairs={{0,224},{32,0},{64,32},{96,64},{128,96},{160,128},{192,160},{224,1... | collective-permute-start | bytes 1572872 | tf_op jit(solution)/shard_map/ppermute | solution.py:115
  5.1 19.7 %collective-permute-start = (f32[32,2,16,128]{3,2,1,0:T(8,128)S(1)}, f32[32,2,16,128]{3,2,1,0:T(8,128)S(1)}, u32[]{:S(2)}, u32[]{:S(2)}) collective-permute-start(f32[32,2,16,128]{3,2,1,0:T(8,128)S(1)} %get-tuple-element.17), channel_id=1, source_target_pairs={{0,32},{32,64},{64,96},{96,128},{128,160},{160,192},{192,224},{224... | collective-permute-start | bytes 1572872 | tf_op jit(solution)/shard_map/ppermute | solution.py:114
  6.9 17.9 %collective-permute-start.3 = (f32[32,8,2,128]{3,2,1,0:T(2,128)S(1)}, f32[32,8,2,128]{3,2,1,0:T(2,128)S(1)}, u32[]{:S(2)}, u32[]{:S(2)}) collective-permute-start(f32[32,8,2,128]{3,2,1,0:T(2,128)S(1)} %get-tuple-element.14), channel_id=1, source_target_pairs={{0,28},{4,0},{8,4},{12,8},{16,12},{20,16},{24,20},{28,24},{1,29},{... | collective-permute-start | bytes 786440 | tf_op jit(solution)/shard_map/ppermute | solution.py:115
  12.0 12.9 %collective-permute-start.2 = (f32[32,8,2,128]{3,2,1,0:T(2,128)S(1)}, f32[32,8,2,128]{3,2,1,0:T(2,128)S(1)}, u32[]{:S(2)}, u32[]{:S(2)}) collective-permute-start(f32[32,8,2,128]{3,2,1,0:T(2,128)S(1)} %get-tuple-element.15), channel_id=1, source_target_pairs={{0,4},{4,8},{8,12},{12,16},{16,20},{20,24},{24,28},{28,0},{1,5},{5... | collective-permute-start | bytes 786440 | tf_op jit(solution)/shard_map/ppermute | solution.py:114
  15.4 4.4 %collective-permute-start.5 = (f32[128,128]{1,0:T(8,128)}, f32[128,128]{1,0:T(8,128)S(1)}, u32[]{:S(2)}, u32[]{:S(2)}) collective-permute-start(f32[128,128]{1,0:T(8,128)} %shard_map.41), channel_id=1, source_target_pairs={{0,3},{1,0},{2,1},{3,2},{4,7},{5,4},{6,5},{7,6},{8,11},{9,8},{10,9... | collective-permute-start | bytes 196616 | tf_op jit(solution)/shard_map/ppermute | solution.py:118
  19.8 5.1 %copy-start.8 = (f32[128,128]{1,0:T(8,128)}, f32[128,128]{1,0:T(8,128)S(1)}, u32[]{:S(2)}) copy-start(f32[128,128]{1,0:T(8,128)S(1)} %collective-permute-done.5.refs_6_) | copy-start | bytes 196612
  19.8 5.0 %collective-permute-start.4 = (f32[128,128]{1,0:T(8,128)}, f32[128,128]{1,0:T(8,128)S(1)}, u32[]{:S(2)}, u32[]{:S(2)}) collective-permute-start(f32[128,128]{1,0:T(8,128)} %shard_map.41), channel_id=1, source_target_pairs={{0,1},{1,2},{2,3},{3,0},{4,5},{5,6},{6,7},{7,4},{8,9},{9,10},{10,1... | collective-permute-start | bytes 196616 | tf_op jit(solution)/shard_map/ppermute | solution.py:117
  24.8 0.6 copy-start.10
  24.8 0.7 copy-start.6
  24.8 0.8 copy-start.7
  24.8 1.0 copy-start
  25.8 0.8 copy-start.1
  36.1 9.2 %copy-start.12 = (f32[128,128]{1,0:T(8,128)S(1)}, f32[128,128]{1,0:T(8,128)}, u32[]{:S(2)}) copy-start(f32[128,128]{1,0:T(8,128)} %get-tuple-element.5) | copy-start | bytes 196612
  37.4 16.3 %collective-permute-start.7 = (f32[32,2,16,128]{3,2,1,0:T(8,128)S(1)}, f32[32,2,16,128]{3,2,1,0:T(8,128)S(1)}, u32[]{:S(2)}, u32[]{:S(2)}) collective-permute-start(f32[32,2,16,128]{3,2,1,0:T(8,128)S(1)} %get-tuple-element.12), channel_id=1, source_target_pairs={{0,224},{32,0},{64,32},{96,64},{128,96},{160,128},{192,160},{224,1... | collective-permute-start | bytes 1572872 | tf_op jit(solution)/shard_map/ppermute | solution.py:115
  40.5 13.2 %collective-permute-start.6 = (f32[32,2,16,128]{3,2,1,0:T(8,128)S(1)}, f32[32,2,16,128]{3,2,1,0:T(8,128)S(1)}, u32[]{:S(2)}, u32[]{:S(2)}) collective-permute-start(f32[32,2,16,128]{3,2,1,0:T(8,128)S(1)} %get-tuple-element.13), channel_id=1, source_target_pairs={{0,32},{32,64},{64,96},{96,128},{128,160},{160,192},{192,224},{224... | collective-permute-start | bytes 1572872 | tf_op jit(solution)/shard_map/ppermute | solution.py:114
  42.3 11.4 %collective-permute-start.9 = (f32[32,8,2,128]{3,2,1,0:T(2,128)S(1)}, f32[32,8,2,128]{3,2,1,0:T(2,128)S(1)}, u32[]{:S(2)}, u32[]{:S(2)}) collective-permute-start(f32[32,8,2,128]{3,2,1,0:T(2,128)S(1)} %get-tuple-element.10), channel_id=1, source_target_pairs={{0,28},{4,0},{8,4},{12,8},{16,12},{20,16},{24,20},{28,24},{1,29},{... | collective-permute-start | bytes 786440 | tf_op jit(solution)/shard_map/ppermute | solution.py:115
  45.3 8.3 %collective-permute-start.8 = (f32[32,8,2,128]{3,2,1,0:T(2,128)S(1)}, f32[32,8,2,128]{3,2,1,0:T(2,128)S(1)}, u32[]{:S(2)}, u32[]{:S(2)}) collective-permute-start(f32[32,8,2,128]{3,2,1,0:T(2,128)S(1)} %get-tuple-element.11), channel_id=1, source_target_pairs={{0,4},{4,8},{8,12},{12,16},{16,20},{20,24},{24,28},{28,0},{1,5},{5... | collective-permute-start | bytes 786440 | tf_op jit(solution)/shard_map/ppermute | solution.py:114
  45.3 3.4 %collective-permute-start.11 = (f32[128,128]{1,0:T(8,128)S(1)}, f32[128,128]{1,0:T(8,128)S(1)}, u32[]{:S(2)}, u32[]{:S(2)}) collective-permute-start(f32[128,128]{1,0:T(8,128)S(1)} %copy-done.12), channel_id=1, source_target_pairs={{0,3},{1,0},{2,1},{3,2},{4,7},{5,4},{6,5},{7,6},{8,11},{9,8},{10,9... | collective-permute-start | bytes 196616 | tf_op jit(solution)/shard_map/ppermute | solution.py:118
  48.7 5.0 %copy-start.9 = (f32[128,128]{1,0:T(8,128)}, f32[128,128]{1,0:T(8,128)S(1)}, u32[]{:S(2)}) copy-start(f32[128,128]{1,0:T(8,128)S(1)} %collective-permute-done.11.refs_6_) | copy-start | bytes 196612
  48.7 4.9 %collective-permute-start.10 = (f32[128,128]{1,0:T(8,128)S(1)}, f32[128,128]{1,0:T(8,128)S(1)}, u32[]{:S(2)}, u32[]{:S(2)}) collective-permute-start(f32[128,128]{1,0:T(8,128)S(1)} %copy-done.12), channel_id=1, source_target_pairs={{0,1},{1,2},{2,3},{3,0},{4,5},{5,6},{6,7},{7,4},{8,9},{9,10},{10,1... | collective-permute-start | bytes 196616 | tf_op jit(solution)/shard_map/ppermute | solution.py:117
  53.6 0.6 copy-start.11
  53.7 0.7 copy-start.4
  53.7 0.8 copy-start.5
  53.7 1.0 copy-start.2
  54.7 0.8 copy-start.3
  69.3 2.8 %collective-permute-start.12 = (f32[32,32]{0,1:T(8,128)S(1)}, f32[32,32]{0,1:T(8,128)S(1)}, u32[]{:S(2)}, u32[]{:S(2)}) collective-permute-start(f32[32,32]{0,1:T(8,128)S(1)} %copy.7), channel_id=1, source_target_pairs={{0,1},{1,0},{2,3},{3,2},{4,5},{5,4},{6,7},{7,6},{8,9},{9,8},{10,11... | collective-permute-start | bytes 12296 | tf_op jit(solution)/shard_map/ppermute | solution.py:223
  72.1 4.1 %collective-permute-start.13 = (f32[32,32]{0,1:T(8,128)S(1)}, f32[32,32]{0,1:T(8,128)S(1)}, u32[]{:S(2)}, u32[]{:S(2)}) collective-permute-start(f32[32,32]{0,1:T(8,128)S(1)} %add.33), channel_id=1, source_target_pairs={{0,2},{1,3},{2,0},{3,1},{4,6},{5,7},{6,4},{7,5},{8,10},{9,11},{10,... | collective-permute-start | bytes 12296 | tf_op jit(solution)/shard_map/ppermute | solution.py:223
  76.2 2.6 %collective-permute-start.14 = (f32[32,32]{0,1:T(8,128)S(1)}, f32[32,32]{0,1:T(8,128)S(1)}, u32[]{:S(2)}, u32[]{:S(2)}) collective-permute-start(f32[32,32]{0,1:T(8,128)S(1)} %add.34), channel_id=1, source_target_pairs={{0,4},{4,0},{8,12},{12,8},{16,20},{20,16},{24,28},{28,24},{1,5},{5... | collective-permute-start | bytes 12296 | tf_op jit(solution)/shard_map/ppermute | solution.py:223
  78.8 3.7 %collective-permute-start.15 = (f32[32,32]{0,1:T(8,128)S(1)}, f32[32,32]{0,1:T(8,128)S(1)}, u32[]{:S(2)}, u32[]{:S(2)}) collective-permute-start(f32[32,32]{0,1:T(8,128)S(1)} %add.35), channel_id=1, source_target_pairs={{0,8},{4,12},{8,0},{12,4},{16,24},{20,28},{24,16},{28,20},{1,9},{5... | collective-permute-start | bytes 12296 | tf_op jit(solution)/shard_map/ppermute | solution.py:223
  82.5 6.5 %collective-permute-start.16 = (f32[32,32]{0,1:T(8,128)S(1)}, f32[32,32]{0,1:T(8,128)S(1)}, u32[]{:S(2)}, u32[]{:S(2)}) collective-permute-start(f32[32,32]{0,1:T(8,128)S(1)} %add.36), channel_id=1, source_target_pairs={{0,16},{4,20},{8,24},{12,28},{16,0},{20,4},{24,8},{28,12},{1,17},{... | collective-permute-start | bytes 12296 | tf_op jit(solution)/shard_map/ppermute | solution.py:223
  89.0 9.4 %collective-permute-start.17 = (f32[32,32]{0,1:T(8,128)S(1)}, f32[32,32]{0,1:T(8,128)S(1)}, u32[]{:S(2)}, u32[]{:S(2)}) collective-permute-start(f32[32,32]{0,1:T(8,128)S(1)} %add.37), channel_id=1, source_target_pairs={{0,32},{32,0},{64,96},{96,64},{128,160},{160,128},{192,224},{224,1... | collective-permute-start | bytes 12296 | tf_op jit(solution)/shard_map/ppermute | solution.py:223
  98.4 2.6 %collective-permute-start.18 = (f32[32,32]{0,1:T(8,128)S(1)}, f32[32,32]{0,1:T(8,128)S(1)}, u32[]{:S(2)}, u32[]{:S(2)}) collective-permute-start(f32[32,32]{0,1:T(8,128)S(1)} %add.38), channel_id=1, source_target_pairs={{0,64},{32,96},{64,0},{96,32},{128,192},{160,224},{192,128},{224,1... | collective-permute-start | bytes 12296 | tf_op jit(solution)/shard_map/ppermute | solution.py:223
  101.0 4.1 %collective-permute-start.19 = (f32[32,32]{0,1:T(8,128)S(1)}, f32[32,32]{0,1:T(8,128)S(1)}, u32[]{:S(2)}, u32[]{:S(2)}) collective-permute-start(f32[32,32]{0,1:T(8,128)S(1)} %add.39), channel_id=1, source_target_pairs={{0,128},{32,160},{64,192},{96,224},{128,0},{160,32},{192,64},{224,... | collective-permute-start | bytes 12296 | tf_op jit(solution)/shard_map/ppermute | solution.py:223

commit v10 on v9

--- a/solution.py
+++ b/solution.py
@@ -29,7 +29,7 @@
          out_ref) = refs
     else:
         (f_ref, xlo_ref, xhi_ref, ylo_ref, yhi_ref, zlo_ref, zhi_ref, pot_ref,
-         out_ref, face_ref) = refs
+         out_ref, face_ref, xl_ref, xf_ref, yl_ref, yf_ref) = refs
     nb, cx, cy, cz = f_ref.shape
     rows = cx * cy
     step = pl.program_id(0)
@@ -74,7 +74,13 @@
         else:
             res = (h - 5.5 * f2) / 3.5
             packed = face_lanes(res, orbital, lane, packed)
-        out_ref[b] = res.reshape(cx, cy, cz)
+        res3 = res.reshape(cx, cy, cz)
+        out_ref[b] = res3
+        if not last:
+            xl_ref[b] = res3[cx - 2:]
+            xf_ref[b] = res3[:2]
+            yl_ref[b] = res3[:, cy - 2:, :]
+            yf_ref[b] = res3[:, :2, :]
     if not last:
         face_ref[...] = packed
 
@@ -105,12 +111,19 @@
     )(f)
 
 
-def exchange(f, zface):
+def own_faces(f):
     out = []
-    for axis, dim in (("gx", 1), ("gy", 2)):
-        n, length = lax.axis_size(axis), f.shape[dim]
-        last = lax.slice_in_dim(f, length - 2, length, axis=dim)
-        first = lax.slice_in_dim(f, 0, 2, axis=dim)
+    for dim in (1, 2):
+        length = f.shape[dim]
+        out.append(lax.slice_in_dim(f, length - 2, length, axis=dim))
+        out.append(lax.slice_in_dim(f, 0, 2, axis=dim))
+    return out
+
+
+def exchange(faces, zface):
+    out = []
+    for axis, (last, first) in (("gx", faces[0:2]), ("gy", faces[2:4])):
+        n = lax.axis_size(axis)
         out.append(lax.ppermute(last, axis, shift_pairs(n, 1)))
         out.append(lax.ppermute(first, axis, shift_pairs(n, -1)))
     n = lax.axis_size("gz")
@@ -135,9 +148,13 @@
         out_specs = blk
         out_shape = jax.ShapeDtypeStruct(f.shape, jnp.float32)
     else:
-        out_specs = (blk, fblk)
+        out_specs = (blk, fblk, xblk, xblk, yblk, yblk)
         out_shape = (jax.ShapeDtypeStruct(f.shape, jnp.float32),
-                     jax.ShapeDtypeStruct((cx * cy, 4 * norb), jnp.float32))
+                     jax.ShapeDtypeStruct((cx * cy, 4 * norb), jnp.float32),
+                     jax.ShapeDtypeStruct((norb, 2, cy, cz), jnp.float32),
+                     jax.ShapeDtypeStruct((norb, 2, cy, cz), jnp.float32),
+                     jax.ShapeDtypeStruct((norb, cx, 2, cz), jnp.float32),
+                     jax.ShapeDtypeStruct((norb, cx, 2, cz), jnp.float32))
     return pl.pallas_call(
         functools.partial(stage_kernel, last=last), grid=(norb // BLOCK,), in_specs=in_specs,
         out_specs=out_specs, out_shape=out_shape, interpret=INTERPRET,
@@ -226,8 +243,8 @@
 
 
 def per_device(orbitals, potential):
-    first, first_z = stage(orbitals, exchange(orbitals, z_faces(orbitals)), potential)
-    second = stage(first, exchange(first, first_z), potential, orbitals)
+    first, first_z, *first_faces = stage(orbitals, exchange(own_faces(orbitals), z_faces(orbitals)), potential)
+    second = stage(first, exchange(first_faces, first_z), potential, orbitals)
     norb_count = orbitals.shape[0]
     all_cells = second[0].size * lax.axis_size("gx") * lax.axis_size("gy") * lax.axis_size("gz")
     correlation = gram(second) / all_cells

time: 116 us -> 115 us (level)
  local copies, waits for them, and re-layouts: 10.6 us -> 6.81 us
  starting transfers between devices: 32.3 us -> 34.3 us
    ppermute x4, starting transfers between devices: 14.4 us -> 11.3 us  [exchange(): out.append(lax.ppermute(first, axis, shift_pairs(n, -1)))]
    slice x4 -> x2, local copies, waits for them, and re-layouts: 6.12 us -> 3.05 us  [own_faces(): out.append(lax.slice_in_dim(f, 0, 2, axis=dim))]
    ppermute x4, starting transfers between devices: 0.01 us -> 3.08 us  [exchange(): out.append(lax.ppermute(last, axis, shift_pairs(n, 1)))]
    ppermute x8, starting transfers between devices: 12.9 us -> 15 us  [butterfly_sum(): c = c + lax.ppermute(c, axis, [(i, i ^ d) for i in range(n)])]
    unnamed x27 -> x25, local copies, waits for them, and re-layouts: 4.24 us -> 3.55 us
  transfers between devices with their start and end apart: 20 -> 20, of which waited for: 12 -> 12; matrix products, arithmetic and copies ran while one was open for 3% -> 2% of each run, Pallas kernels for 3% -> 3%
where the time goes in v10:
time: 115 us
  waiting for transfers between devices  35.7 us (31%)
  starting transfers between devices  34.3 us (30%)
  Pallas kernels  30.1 us (26%)
  local copies, waits for them, and re-layouts  6.81 us (6%)
  other arithmetic  6.79 us (6%)
    ppermute x8, waiting for transfers between devices, butterfly_sum(): c = c + lax.ppermute(c, axis, [(i, i ^ d) for i in range(n)])  22.9 us
    pallas_call x2, Pallas kernels, stage(): pl.pallas_call(functools.partial(stage_kernel, last=last), grid=(norb //...  17.2 us
    ppermute x8, starting transfers between devices, butterfly_sum(): c = c + lax.ppermute(c, axis, [(i, i ^ d) for i in range(n)])  15 us
    ppermute x4, starting transfers between devices, exchange(): out.append(lax.ppermute(first, axis, shift_pairs(n, -1)))  11.3 us
    ppermute x2, waiting for transfers between devices, exchange(): out.append(lax.ppermute(zface, 'gz', shift_pairs(n, 1)))  9.33 us
    pallas_call x1, Pallas kernels, gram(): pl.pallas_call(gram_kernel, grid=(cx // xb,), in_specs=[pl.BlockSpec((nor...  4.89 us
    pallas_call x1, Pallas kernels, solve_lower(): pl.pallas_call(solve_kernel, grid=(cx // xb,), in_specs=[pl.BlockSpec(mem...  4.61 us
    ppermute x2, starting transfers between devices, exchange(): out.append(lax.ppermute(zface, 'gz', shift_pairs(n, -1)))  4.48 us
  transfers between devices with their start and end apart: 20, of which 12 were waited for; matrix products, arithmetic and copies ran while one was open for 2% of the time, Pallas kernels for 3%

profile of v10, /device:TPU:1, one launch (start us, length us, event | category | flops | bytes accessed | tf_op | source)
XLA Modules:
  0.0 114.6 jit_solution(17809621519551979269)
XLA Ops:
  0.6 1.3 %fusion.2 = (f32[32,2,16,128]{3,2,1,0:T(8,128)S(1)}, f32[32,2,16,128]{3,2,1,0:T(8,128)S(1)}) fusion(f32[32,8,16,128]{3,2,1,0:T(8,128)} %refs_8_.1), kind=kLoop, calls=%fused_computation.9 | loop fusion | bytes 2097152 | tf_op jit(solution)/shard_map/slice | solution.py:119
  1.9 3.2 %collective-permute-start.1 = (f32[32,2,16,128]{3,2,1,0:T(8,128)S(1)}, f32[32,2,16,128]{3,2,1,0:T(8,128)S(1)}, u32[]{:S(2)}, u32[]{:S(2)}) collective-permute-start(f32[32,2,16,128]{3,2,1,0:T(8,128)S(1)} %get-tuple-element.20), channel_id=1, source_target_pairs={{0,224},{32,0},{64,32},{96,64},{128,96},{160,128},{192,160},{224,1... | collective-permute-start | bytes 1572872 | tf_op jit(solution)/shard_map/ppermute | solution.py:128
  5.1 1.8 %fusion.1 = (f32[32,8,2,128]{3,2,1,0:T(2,128)S(1)}, f32[32,8,2,128]{3,2,1,0:T(2,128)S(1)}) fusion(f32[32,8,16,128]{3,2,1,0:T(8,128)} %refs_8_.1), kind=kLoop, calls=%fused_computation.8 | loop fusion | bytes 1048576 | tf_op jit(solution)/shard_map/slice | solution.py:119
  6.9 5.1 %collective-permute-start.3 = (f32[32,8,2,128]{3,2,1,0:T(2,128)S(1)}, f32[32,8,2,128]{3,2,1,0:T(2,128)S(1)}, u32[]{:S(2)}, u32[]{:S(2)}) collective-permute-start(f32[32,8,2,128]{3,2,1,0:T(2,128)S(1)} %get-tuple-element.18), channel_id=1, source_target_pairs={{0,28},{4,0},{8,4},{12,8},{16,12},{20,16},{24,20},{28,24},{1,29},{... | collective-permute-start | bytes 786440 | tf_op jit(solution)/shard_map/ppermute | solution.py:128
  12.0 3.4 %shard_map.41 = f32[128,128]{1,0:T(8,128)} custom-call(f32[32,8,16,128]{3,2,1,0:T(8,128)} %refs_8_.1), custom_call_target="tpu_custom_call" | custom-call | tf_op jit(solution)/shard_map/pallas_call | solution.py:107
  15.4 2.7 %collective-permute-start.5 = (f32[128,128]{1,0:T(8,128)}, f32[128,128]{1,0:T(8,128)S(1)}, u32[]{:S(2)}, u32[]{:S(2)}) collective-permute-start(f32[128,128]{1,0:T(8,128)} %shard_map.41), channel_id=1, source_target_pairs={{0,3},{1,0},{2,1},{3,2},{4,7},{5,4},{6,5},{7,6},{8,11},{9,8},{10,9... | collective-permute-start | bytes 196616 | tf_op jit(solution)/shard_map/ppermute | solution.py:131
  18.1 1.6 %collective-permute-done.5.refs_6_ = f32[128,128]{1,0:T(8,128)S(1)} collective-permute-done((f32[128,128]{1,0:T(8,128)}, f32[128,128]{1,0:T(8,128)S(1)}, u32[]{:S(2)}, u32[]{:S(2)}) %collective-permute-start.5) | collective-permute-done | bytes 65568 | tf_op jit(solution)/shard_map/ppermute | solution.py:131
  19.8 0.5 collective-permute-start.4
  20.3 4.5 %collective-permute-done.4.refs_5_ = f32[128,128]{1,0:T(8,128)S(1)} collective-permute-done((f32[128,128]{1,0:T(8,128)}, f32[128,128]{1,0:T(8,128)S(1)}, u32[]{:S(2)}, u32[]{:S(2)}) %collective-permute-start.4) | collective-permute-done | bytes 65568 | tf_op jit(solution)/shard_map/ppermute | solution.py:130
  24.9 0.6 copy-done.10
  25.4 0.1 copy-done.6
  25.5 0.1 copy-done.7
  25.6 0.2 copy-done
  25.8 0.8 copy-done.1
  26.6 9.7 %shard_map.42 = (f32[32,8,16,128]{3,2,1,0:T(8,128)}, f32[128,128]{1,0:T(8,128)}, f32[32,2,16,128]{3,2,1,0:T(8,128)}, f32[32,2,16,128]{3,2,1,0:T(8,128)}, f32[32,...) custom-call(f32[32,8,16,128]{3,2,1,0:T(8,128)} %refs_8_.1, f32[32,2,16,128]{3,2,1,0:T(8,128)} %copy-done.1, ...), custom_call_target="tpu_custom_call" | custom-call | tf_op jit(solution)/shard_map/pallas_call | solution.py:158
  36.3 3.1 %collective-permute-start.6 = (f32[32,2,16,128]{3,2,1,0:T(8,128)}, f32[32,2,16,128]{3,2,1,0:T(8,128)S(1)}, u32[]{:S(2)}, u32[]{:S(2)}) collective-permute-start(f32[32,2,16,128]{3,2,1,0:T(8,128)} %get-tuple-element.9), channel_id=1, source_target_pairs={{0,32},{32,64},{64,96},{96,128},{128,160},{160,192},{192,224},{224... | collective-permute-start | bytes 1572872 | tf_op jit(solution)/shard_map/ppermute | solution.py:127
  39.5 3.0 %collective-permute-start.9 = (f32[32,8,2,128]{3,2,1,0:T(2,128)}, f32[32,8,2,128]{3,2,1,0:T(2,128)S(1)}, u32[]{:S(2)}, u32[]{:S(2)}) collective-permute-start(f32[32,8,2,128]{3,2,1,0:T(2,128)} %get-tuple-element.12), channel_id=1, source_target_pairs={{0,28},{4,0},{8,4},{12,8},{16,12},{20,16},{24,20},{28,24},{1,29},{... | collective-permute-start | bytes 786440 | tf_op jit(solution)/shard_map/ppermute | solution.py:128
  42.4 1.7 %collective-permute-start.11 = (f32[128,128]{1,0:T(8,128)}, f32[128,128]{1,0:T(8,128)S(1)}, u32[]{:S(2)}, u32[]{:S(2)}) collective-permute-start(f32[128,128]{1,0:T(8,128)} %get-tuple-element.13), channel_id=1, source_target_pairs={{0,3},{1,0},{2,1},{3,2},{4,7},{5,4},{6,5},{7,6},{8,11},{9,8},{10,9... | collective-permute-start | bytes 196616 | tf_op jit(solution)/shard_map/ppermute | solution.py:131
  44.2 1.9 %collective-permute-done.11.refs_6_ = f32[128,128]{1,0:T(8,128)S(1)} collective-permute-done((f32[128,128]{1,0:T(8,128)}, f32[128,128]{1,0:T(8,128)S(1)}, u32[]{:S(2)}, u32[]{:S(2)}) %collective-permute-start.11) | collective-permute-done | bytes 65568 | tf_op jit(solution)/shard_map/ppermute | solution.py:131
  46.0 4.8 %collective-permute-done.10.refs_5_ = f32[128,128]{1,0:T(8,128)S(1)} collective-permute-done((f32[128,128]{1,0:T(8,128)}, f32[128,128]{1,0:T(8,128)S(1)}, u32[]{:S(2)}, u32[]{:S(2)}) %collective-permute-start.10) | collective-permute-done | bytes 65568 | tf_op jit(solution)/shard_map/ppermute | solution.py:130
  50.9 0.6 copy-done.11
  51.5 0.1 copy-done.4
  51.6 0.1 copy-done.5
  51.7 0.2 copy-done.2
  51.8 0.2 copy-done.3
  52.0 7.5 %shard_map.43.y_ref = f32[32,8,16,128]{3,2,1,0:T(8,128)} custom-call(f32[32,8,16,128]{3,2,1,0:T(8,128)} %get-tuple-element.8.refs_0_, f32[32,2,16,128]{3,2,1,0:T(8,128)} %copy-done.2, f32[32,2,16,128]{3,2,1,0:T(8,128)} %copy-done.3, f32[32,8,2,128]{3,2,1,0:T(2,128)} %copy-done.4, f32[32,8,2,128]{3,2,1,0:T(2,128)} %copy-done.5, f32[128,128]{1,0:T(8,128)} %copy-done.11, ...), custom_call_target="tpu_custom_call" | custom-call | tf_op jit(solution)/shard_map/pallas_call | solution.py:158
  59.6 4.9 %shard_map.44 = f32[1024,128]{1,0:T(8,128)} custom-call(f32[32,8,16,128]{3,2,1,0:T(8,128)} %shard_map.43.y_ref), custom_call_target="tpu_custom_call" | custom-call | tf_op jit(solution)/shard_map/pallas_call | solution.py:224
  64.5 1.2 %reduce_sum.9 = f32[1024]{0:T(1024)S(1)} reduce(f32[1024,128]{1,0:T(8,128)} %shard_map.44, f32[]{:T(128)} %constant.36.clone.1), dimensions={1}, to_apply=%region_0.0 | reduce | flops 130048 | bytes 528388 | tf_op jit(solution)/shard_map/reduce_sum | solution.py:232
  65.8 0.1 copy.7
  65.9 0.2 collective-permute-start.12
  66.1 2.6 %collective-permute-done.12 = f32[32,32]{0,1:T(8,128)S(1)} collective-permute-done((f32[32,32]{0,1:T(8,128)S(1)}, f32[32,32]{0,1:T(8,128)S(1)}, u32[]{:S(2)}, u32[]{:S(2)}) %collective-permute-start.12) | collective-permute-done | bytes 4128 | tf_op jit(solution)/shard_map/ppermute | solution.py:240
  68.7 1.5 %collective-permute-start.13 = (f32[32,32]{0,1:T(8,128)S(1)}, f32[32,32]{0,1:T(8,128)S(1)}, u32[]{:S(2)}, u32[]{:S(2)}) collective-permute-start(f32[32,32]{0,1:T(8,128)S(1)} %add.33), channel_id=1, source_target_pairs={{0,2},{1,3},{2,0},{3,1},{4,6},{5,7},{6,4},{7,5},{8,10},{9,11},{10,... | collective-permute-start | bytes 12296 | tf_op jit(solution)/shard_map/ppermute | solution.py:240
  70.1 2.6 %collective-permute-done.13 = f32[32,32]{0,1:T(8,128)S(1)} collective-permute-done((f32[32,32]{0,1:T(8,128)S(1)}, f32[32,32]{0,1:T(8,128)S(1)}, u32[]{:S(2)}, u32[]{:S(2)}) %collective-permute-start.13) | collective-permute-done | bytes 4128 | tf_op jit(solution)/shard_map/ppermute | solution.py:240
  72.8 2.6 %collective-permute-done.14 = f32[32,32]{0,1:T(8,128)S(1)} collective-permute-done((f32[32,32]{0,1:T(8,128)S(1)}, f32[32,32]{0,1:T(8,128)S(1)}, u32[]{:S(2)}, u32[]{:S(2)}) %collective-permute-start.14) | collective-permute-done | bytes 4128 | tf_op jit(solution)/shard_map/ppermute | solution.py:240
  75.4 3.8 %collective-permute-done.15 = f32[32,32]{0,1:T(8,128)S(1)} collective-permute-done((f32[32,32]{0,1:T(8,128)S(1)}, f32[32,32]{0,1:T(8,128)S(1)}, u32[]{:S(2)}, u32[]{:S(2)}) %collective-permute-start.15) | collective-permute-done | bytes 4128 | tf_op jit(solution)/shard_map/ppermute | solution.py:240
  79.1 2.5 %collective-permute-start.16 = (f32[32,32]{0,1:T(8,128)S(1)}, f32[32,32]{0,1:T(8,128)S(1)}, u32[]{:S(2)}, u32[]{:S(2)}) collective-permute-start(f32[32,32]{0,1:T(8,128)S(1)} %add.36), channel_id=1, source_target_pairs={{0,16},{4,20},{8,24},{12,28},{16,0},{20,4},{24,8},{28,12},{1,17},{... | collective-permute-start | bytes 12296 | tf_op jit(solution)/shard_map/ppermute | solution.py:240
  81.6 4.0 %collective-permute-done.16 = f32[32,32]{0,1:T(8,128)S(1)} collective-permute-done((f32[32,32]{0,1:T(8,128)S(1)}, f32[32,32]{0,1:T(8,128)S(1)}, u32[]{:S(2)}, u32[]{:S(2)}) %collective-permute-start.16) | collective-permute-done | bytes 4128 | tf_op jit(solution)/shard_map/ppermute | solution.py:240
  85.6 10.5 %collective-permute-start.17 = (f32[32,32]{0,1:T(8,128)S(1)}, f32[32,32]{0,1:T(8,128)S(1)}, u32[]{:S(2)}, u32[]{:S(2)}) collective-permute-start(f32[32,32]{0,1:T(8,128)S(1)} %add.37), channel_id=1, source_target_pairs={{0,32},{32,0},{64,96},{96,64},{128,160},{160,128},{192,224},{224,1... | collective-permute-start | bytes 12296 | tf_op jit(solution)/shard_map/ppermute | solution.py:240
  96.2 0.8 collective-permute-done.17
  97.0 2.6 %collective-permute-done.18 = f32[32,32]{0,1:T(8,128)S(1)} collective-permute-done((f32[32,32]{0,1:T(8,128)S(1)}, f32[32,32]{0,1:T(8,128)S(1)}, u32[]{:S(2)}, u32[]{:S(2)}) %collective-permute-start.18) | collective-permute-done | bytes 4128 | tf_op jit(solution)/shard_map/ppermute | solution.py:240
  99.6 0.2 collective-permute-start.19
  99.8 3.9 %collective-permute-done.19 = f32[32,32]{0,1:T(8,128)S(1)} collective-permute-done((f32[32,32]{0,1:T(8,128)S(1)}, f32[32,32]{0,1:T(8,128)S(1)}, u32[]{:S(2)}, u32[]{:S(2)}) %collective-permute-start.19) | collective-permute-done | bytes 4128 | tf_op jit(solution)/shard_map/ppermute | solution.py:240
  103.8 2.9 %cholesky.18 = f32[32,32]{1,0:T(8,128)S(1)} custom-call(f32[32,32]{1,0:T(8,128)S(1)} %fusion), custom_call_target="Cholesky" | custom-call | tf_op jit(solution)/shard_map/jit(cholesky)/cholesky | solution.py:251
  106.8 0.6 compare_reduce_fusion
  107.4 0.6 fusion.3
  108.1 1.3 %select_select_fusion.l_ref = f32[32,32]{1,0:T(8,128)} fusion(f32[32,32]{1,0:T(8,128)S(1)} %cholesky.18, pred[]{:T(512)} %compare_reduce_fusion), kind=kLoop, calls=%fused_computation.2 | loop fusion | flops 3072 | bytes 8193 | tf_op jit(solution)/shard_map/jit(cholesky)/select_n | solution.py:251
  109.3 4.6 %shard_map.45 = f32[32,8,16,128]{3,2,1,0:T(8,128)} custom-call(f32[32,32]{1,0:T(8,128)} %select_select_fusion.l_ref, f32[32,8,16,128]{3,2,1,0:T(8,128)} %shard_map.43.y_ref), custom_call_target="tpu_custom_call" | custom-call | tf_op jit(solution)/shard_map/pallas_call | solution.py:185
  113.9 0.7 copy.9
  (43 shorter events, 0.3 us)
Async XLA Ops:
  1.9 22.9 %collective-permute-start.1 = (f32[32,2,16,128]{3,2,1,0:T(8,128)S(1)}, f32[32,2,16,128]{3,2,1,0:T(8,128)S(1)}, u32[]{:S(2)}, u32[]{:S(2)}) collective-permute-start(f32[32,2,16,128]{3,2,1,0:T(8,128)S(1)} %get-tuple-element.20), channel_id=1, source_target_pairs={{0,224},{32,0},{64,32},{96,64},{128,96},{160,128},{192,160},{224,1... | collective-permute-start | bytes 1572872 | tf_op jit(solution)/shard_map/ppermute | solution.py:128
  5.1 19.7 %collective-permute-start = (f32[32,2,16,128]{3,2,1,0:T(8,128)S(1)}, f32[32,2,16,128]{3,2,1,0:T(8,128)S(1)}, u32[]{:S(2)}, u32[]{:S(2)}) collective-permute-start(f32[32,2,16,128]{3,2,1,0:T(8,128)S(1)} %get-tuple-element.21), channel_id=1, source_target_pairs={{0,32},{32,64},{64,96},{96,128},{128,160},{160,192},{192,224},{224... | collective-permute-start | bytes 1572872 | tf_op jit(solution)/shard_map/ppermute | solution.py:127
  6.9 17.9 %collective-permute-start.3 = (f32[32,8,2,128]{3,2,1,0:T(2,128)S(1)}, f32[32,8,2,128]{3,2,1,0:T(2,128)S(1)}, u32[]{:S(2)}, u32[]{:S(2)}) collective-permute-start(f32[32,8,2,128]{3,2,1,0:T(2,128)S(1)} %get-tuple-element.18), channel_id=1, source_target_pairs={{0,28},{4,0},{8,4},{12,8},{16,12},{20,16},{24,20},{28,24},{1,29},{... | collective-permute-start | bytes 786440 | tf_op jit(solution)/shard_map/ppermute | solution.py:128
  12.0 12.9 %collective-permute-start.2 = (f32[32,8,2,128]{3,2,1,0:T(2,128)S(1)}, f32[32,8,2,128]{3,2,1,0:T(2,128)S(1)}, u32[]{:S(2)}, u32[]{:S(2)}) collective-permute-start(f32[32,8,2,128]{3,2,1,0:T(2,128)S(1)} %get-tuple-element.19), channel_id=1, source_target_pairs={{0,4},{4,8},{8,12},{12,16},{16,20},{20,24},{24,28},{28,0},{1,5},{5... | collective-permute-start | bytes 786440 | tf_op jit(solution)/shard_map/ppermute | solution.py:127
  15.4 4.4 %collective-permute-start.5 = (f32[128,128]{1,0:T(8,128)}, f32[128,128]{1,0:T(8,128)S(1)}, u32[]{:S(2)}, u32[]{:S(2)}) collective-permute-start(f32[128,128]{1,0:T(8,128)} %shard_map.41), channel_id=1, source_target_pairs={{0,3},{1,0},{2,1},{3,2},{4,7},{5,4},{6,5},{7,6},{8,11},{9,8},{10,9... | collective-permute-start | bytes 196616 | tf_op jit(solution)/shard_map/ppermute | solution.py:131
  19.8 5.1 %copy-start.8 = (f32[128,128]{1,0:T(8,128)}, f32[128,128]{1,0:T(8,128)S(1)}, u32[]{:S(2)}) copy-start(f32[128,128]{1,0:T(8,128)S(1)} %collective-permute-done.5.refs_6_) | copy-start | bytes 196612
  19.8 5.0 %collective-permute-start.4 = (f32[128,128]{1,0:T(8,128)}, f32[128,128]{1,0:T(8,128)S(1)}, u32[]{:S(2)}, u32[]{:S(2)}) collective-permute-start(f32[128,128]{1,0:T(8,128)} %shard_map.41), channel_id=1, source_target_pairs={{0,1},{1,2},{2,3},{3,0},{4,5},{5,6},{6,7},{7,4},{8,9},{9,10},{10,1... | collective-permute-start | bytes 196616 | tf_op jit(solution)/shard_map/ppermute | solution.py:130
  24.8 0.6 copy-start.10
  24.8 0.7 copy-start.6
  24.8 0.8 copy-start.7
  24.8 1.0 copy-start
  25.8 0.8 copy-start.1
  36.3 14.5 %collective-permute-start.6 = (f32[32,2,16,128]{3,2,1,0:T(8,128)}, f32[32,2,16,128]{3,2,1,0:T(8,128)S(1)}, u32[]{:S(2)}, u32[]{:S(2)}) collective-permute-start(f32[32,2,16,128]{3,2,1,0:T(8,128)} %get-tuple-element.9), channel_id=1, source_target_pairs={{0,32},{32,64},{64,96},{96,128},{128,160},{160,192},{192,224},{224... | collective-permute-start | bytes 1572872 | tf_op jit(solution)/shard_map/ppermute | solution.py:127
  39.4 11.5 %collective-permute-start.7 = (f32[32,2,16,128]{3,2,1,0:T(8,128)}, f32[32,2,16,128]{3,2,1,0:T(8,128)S(1)}, u32[]{:S(2)}, u32[]{:S(2)}) collective-permute-start(f32[32,2,16,128]{3,2,1,0:T(8,128)} %get-tuple-element.10), channel_id=1, source_target_pairs={{0,224},{32,0},{64,32},{96,64},{128,96},{160,128},{192,160},{224,1... | collective-permute-start | bytes 1572872 | tf_op jit(solution)/shard_map/ppermute | solution.py:128
  39.5 11.4 %collective-permute-start.8 = (f32[32,8,2,128]{3,2,1,0:T(2,128)}, f32[32,8,2,128]{3,2,1,0:T(2,128)S(1)}, u32[]{:S(2)}, u32[]{:S(2)}) collective-permute-start(f32[32,8,2,128]{3,2,1,0:T(2,128)} %get-tuple-element.11), channel_id=1, source_target_pairs={{0,4},{4,8},{8,12},{12,16},{16,20},{20,24},{24,28},{28,0},{1,5},{5... | collective-permute-start | bytes 786440 | tf_op jit(solution)/shard_map/ppermute | solution.py:127
  39.5 11.4 %collective-permute-start.9 = (f32[32,8,2,128]{3,2,1,0:T(2,128)}, f32[32,8,2,128]{3,2,1,0:T(2,128)S(1)}, u32[]{:S(2)}, u32[]{:S(2)}) collective-permute-start(f32[32,8,2,128]{3,2,1,0:T(2,128)} %get-tuple-element.12), channel_id=1, source_target_pairs={{0,28},{4,0},{8,4},{12,8},{16,12},{20,16},{24,20},{28,24},{1,29},{... | collective-permute-start | bytes 786440 | tf_op jit(solution)/shard_map/ppermute | solution.py:128
  42.4 3.6 %collective-permute-start.11 = (f32[128,128]{1,0:T(8,128)}, f32[128,128]{1,0:T(8,128)S(1)}, u32[]{:S(2)}, u32[]{:S(2)}) collective-permute-start(f32[128,128]{1,0:T(8,128)} %get-tuple-element.13), channel_id=1, source_target_pairs={{0,3},{1,0},{2,1},{3,2},{4,7},{5,4},{6,5},{7,6},{8,11},{9,8},{10,9... | collective-permute-start | bytes 196616 | tf_op jit(solution)/shard_map/ppermute | solution.py:131
  46.0 4.9 %copy-start.9 = (f32[128,128]{1,0:T(8,128)}, f32[128,128]{1,0:T(8,128)S(1)}, u32[]{:S(2)}) copy-start(f32[128,128]{1,0:T(8,128)S(1)} %collective-permute-done.11.refs_6_) | copy-start | bytes 196612
  46.0 4.8 %collective-permute-start.10 = (f32[128,128]{1,0:T(8,128)}, f32[128,128]{1,0:T(8,128)S(1)}, u32[]{:S(2)}, u32[]{:S(2)}) collective-permute-start(f32[128,128]{1,0:T(8,128)} %get-tuple-element.13), channel_id=1, source_target_pairs={{0,1},{1,2},{2,3},{3,0},{4,5},{5,6},{6,7},{7,4},{8,9},{9,10},{10,1... | collective-permute-start | bytes 196616 | tf_op jit(solution)/shard_map/ppermute | solution.py:130
  50.9 0.6 copy-start.11
  50.9 0.7 copy-start.4
  50.9 0.8 copy-start.5
  50.9 1.0 copy-start.2
  50.9 1.1 copy-start.3
  65.9 2.8 %collective-permute-start.12 = (f32[32,32]{0,1:T(8,128)S(1)}, f32[32,32]{0,1:T(8,128)S(1)}, u32[]{:S(2)}, u32[]{:S(2)}) collective-permute-start(f32[32,32]{0,1:T(8,128)S(1)} %copy.7), channel_id=1, source_target_pairs={{0,1},{1,0},{2,3},{3,2},{4,5},{5,4},{6,7},{7,6},{8,9},{9,8},{10,11... | collective-permute-start | bytes 12296 | tf_op jit(solution)/shard_map/ppermute | solution.py:240
  68.7 4.1 %collective-permute-start.13 = (f32[32,32]{0,1:T(8,128)S(1)}, f32[32,32]{0,1:T(8,128)S(1)}, u32[]{:S(2)}, u32[]{:S(2)}) collective-permute-start(f32[32,32]{0,1:T(8,128)S(1)} %add.33), channel_id=1, source_target_pairs={{0,2},{1,3},{2,0},{3,1},{4,6},{5,7},{6,4},{7,5},{8,10},{9,11},{10,... | collective-permute-start | bytes 12296 | tf_op jit(solution)/shard_map/ppermute | solution.py:240
  72.8 2.6 %collective-permute-start.14 = (f32[32,32]{0,1:T(8,128)S(1)}, f32[32,32]{0,1:T(8,128)S(1)}, u32[]{:S(2)}, u32[]{:S(2)}) collective-permute-start(f32[32,32]{0,1:T(8,128)S(1)} %add.34), channel_id=1, source_target_pairs={{0,4},{4,0},{8,12},{12,8},{16,20},{20,16},{24,28},{28,24},{1,5},{5... | collective-permute-start | bytes 12296 | tf_op jit(solution)/shard_map/ppermute | solution.py:240
  75.4 3.8 %collective-permute-start.15 = (f32[32,32]{0,1:T(8,128)S(1)}, f32[32,32]{0,1:T(8,128)S(1)}, u32[]{:S(2)}, u32[]{:S(2)}) collective-permute-start(f32[32,32]{0,1:T(8,128)S(1)} %add.35), channel_id=1, source_target_pairs={{0,8},{4,12},{8,0},{12,4},{16,24},{20,28},{24,16},{28,20},{1,9},{5... | collective-permute-start | bytes 12296 | tf_op jit(solution)/shard_map/ppermute | solution.py:240
  79.1 6.5 %collective-permute-start.16 = (f32[32,32]{0,1:T(8,128)S(1)}, f32[32,32]{0,1:T(8,128)S(1)}, u32[]{:S(2)}, u32[]{:S(2)}) collective-permute-start(f32[32,32]{0,1:T(8,128)S(1)} %add.36), channel_id=1, source_target_pairs={{0,16},{4,20},{8,24},{12,28},{16,0},{20,4},{24,8},{28,12},{1,17},{... | collective-permute-start | bytes 12296 | tf_op jit(solution)/shard_map/ppermute | solution.py:240
  85.6 11.4 %collective-permute-start.17 = (f32[32,32]{0,1:T(8,128)S(1)}, f32[32,32]{0,1:T(8,128)S(1)}, u32[]{:S(2)}, u32[]{:S(2)}) collective-permute-start(f32[32,32]{0,1:T(8,128)S(1)} %add.37), channel_id=1, source_target_pairs={{0,32},{32,0},{64,96},{96,64},{128,160},{160,128},{192,224},{224,1... | collective-permute-start | bytes 12296 | tf_op jit(solution)/shard_map/ppermute | solution.py:240
  97.0 2.6 %collective-permute-start.18 = (f32[32,32]{0,1:T(8,128)S(1)}, f32[32,32]{0,1:T(8,128)S(1)}, u32[]{:S(2)}, u32[]{:S(2)}) collective-permute-start(f32[32,32]{0,1:T(8,128)S(1)} %add.38), channel_id=1, source_target_pairs={{0,64},{32,96},{64,0},{96,32},{128,192},{160,224},{192,128},{224,1... | collective-permute-start | bytes 12296 | tf_op jit(solution)/shard_map/ppermute | solution.py:240
  99.6 4.1 %collective-permute-start.19 = (f32[32,32]{0,1:T(8,128)S(1)}, f32[32,32]{0,1:T(8,128)S(1)}, u32[]{:S(2)}, u32[]{:S(2)}) collective-permute-start(f32[32,32]{0,1:T(8,128)S(1)} %add.39), channel_id=1, source_target_pairs={{0,128},{32,160},{64,192},{96,224},{128,0},{160,32},{192,64},{224,... | collective-permute-start | bytes 12296 | tf_op jit(solution)/shard_map/ppermute | solution.py:240

commit v11 on v10

--- a/solution.py
+++ b/solution.py
@@ -8,7 +8,7 @@
 from jax.sharding import PartitionSpec as P
 
 TAPS = (-1.0 / 12.0, 4.0 / 3.0, -2.5, 4.0 / 3.0, -1.0 / 12.0)
-BLOCK = 8
+BLOCK = 16
 INTERPRET = False
 HI = lax.Precision.HIGHEST
 

time: 115 us -> 114 us (level)
  transfers between devices with their start and end apart: 20 -> 20, of which waited for: 12 -> 12; matrix products, arithmetic and copies ran while one was open for 2% -> 2% of each run, Pallas kernels for 3% -> 2%
where the time goes in v11:
time: 114 us
  waiting for transfers between devices  35.7 us (31%)
  starting transfers between devices  34.1 us (30%)
  Pallas kernels  29.7 us (26%)
  local copies, waits for them, and re-layouts  6.81 us (6%)
  other arithmetic  6.79 us (6%)
    ppermute x8, waiting for transfers between devices, butterfly_sum(): c = c + lax.ppermute(c, axis, [(i, i ^ d) for i in range(n)])  22.9 us
    pallas_call x2, Pallas kernels, stage(): pl.pallas_call(functools.partial(stage_kernel, last=last), grid=(norb //...  17.7 us
    ppermute x8, starting transfers between devices, butterfly_sum(): c = c + lax.ppermute(c, axis, [(i, i ^ d) for i in range(n)])  14.8 us
    ppermute x4, starting transfers between devices, exchange(): out.append(lax.ppermute(first, axis, shift_pairs(n, -1)))  11.3 us
    ppermute x2, waiting for transfers between devices, exchange(): out.append(lax.ppermute(zface, 'gz', shift_pairs(n, 1)))  9.33 us
    pallas_call x1, Pallas kernels, gram(): pl.pallas_call(gram_kernel, grid=(cx // xb,), in_specs=[pl.BlockSpec((nor...  4.89 us
    pallas_call x1, Pallas kernels, solve_lower(): pl.pallas_call(solve_kernel, grid=(cx // xb,), in_specs=[pl.BlockSpec(mem...  4.61 us
    ppermute x2, starting transfers between devices, exchange(): out.append(lax.ppermute(zface, 'gz', shift_pairs(n, -1)))  4.48 us
  transfers between devices with their start and end apart: 20, of which 12 were waited for; matrix products, arithmetic and copies ran while one was open for 2% of the time, Pallas kernels for 2%

profile of v11, /device:TPU:1, one launch (start us, length us, event | category | flops | bytes accessed | tf_op | source)
XLA Modules:
  0.0 114.0 jit_solution(2665567401942182292)
XLA Ops:
  0.6 1.3 %fusion.2 = (f32[32,2,16,128]{3,2,1,0:T(8,128)S(1)}, f32[32,2,16,128]{3,2,1,0:T(8,128)S(1)}) fusion(f32[32,8,16,128]{3,2,1,0:T(8,128)} %refs_8_.1), kind=kLoop, calls=%fused_computation.9 | loop fusion | bytes 2097152 | tf_op jit(solution)/shard_map/slice | solution.py:119
  1.9 3.2 %collective-permute-start.1 = (f32[32,2,16,128]{3,2,1,0:T(8,128)S(1)}, f32[32,2,16,128]{3,2,1,0:T(8,128)S(1)}, u32[]{:S(2)}, u32[]{:S(2)}) collective-permute-start(f32[32,2,16,128]{3,2,1,0:T(8,128)S(1)} %get-tuple-element.20), channel_id=1, source_target_pairs={{0,224},{32,0},{64,32},{96,64},{128,96},{160,128},{192,160},{224,1... | collective-permute-start | bytes 1572872 | tf_op jit(solution)/shard_map/ppermute | solution.py:128
  5.1 1.8 %fusion.1 = (f32[32,8,2,128]{3,2,1,0:T(2,128)S(1)}, f32[32,8,2,128]{3,2,1,0:T(2,128)S(1)}) fusion(f32[32,8,16,128]{3,2,1,0:T(8,128)} %refs_8_.1), kind=kLoop, calls=%fused_computation.8 | loop fusion | bytes 1048576 | tf_op jit(solution)/shard_map/slice | solution.py:119
  6.9 5.1 %collective-permute-start.3 = (f32[32,8,2,128]{3,2,1,0:T(2,128)S(1)}, f32[32,8,2,128]{3,2,1,0:T(2,128)S(1)}, u32[]{:S(2)}, u32[]{:S(2)}) collective-permute-start(f32[32,8,2,128]{3,2,1,0:T(2,128)S(1)} %get-tuple-element.18), channel_id=1, source_target_pairs={{0,28},{4,0},{8,4},{12,8},{16,12},{20,16},{24,20},{28,24},{1,29},{... | collective-permute-start | bytes 786440 | tf_op jit(solution)/shard_map/ppermute | solution.py:128
  12.0 2.6 %shard_map.41 = f32[128,128]{1,0:T(8,128)} custom-call(f32[32,8,16,128]{3,2,1,0:T(8,128)} %refs_8_.1), custom_call_target="tpu_custom_call" | custom-call | tf_op jit(solution)/shard_map/pallas_call | solution.py:107
  14.5 2.7 %collective-permute-start.5 = (f32[128,128]{1,0:T(8,128)}, f32[128,128]{1,0:T(8,128)S(1)}, u32[]{:S(2)}, u32[]{:S(2)}) collective-permute-start(f32[128,128]{1,0:T(8,128)} %shard_map.41), channel_id=1, source_target_pairs={{0,3},{1,0},{2,1},{3,2},{4,7},{5,4},{6,5},{7,6},{8,11},{9,8},{10,9... | collective-permute-start | bytes 196616 | tf_op jit(solution)/shard_map/ppermute | solution.py:131
  17.3 1.6 %collective-permute-done.5.refs_6_ = f32[128,128]{1,0:T(8,128)S(1)} collective-permute-done((f32[128,128]{1,0:T(8,128)}, f32[128,128]{1,0:T(8,128)S(1)}, u32[]{:S(2)}, u32[]{:S(2)}) %collective-permute-start.5) | collective-permute-done | bytes 65568 | tf_op jit(solution)/shard_map/ppermute | solution.py:131
  18.9 0.5 collective-permute-start.4
  19.4 4.5 %collective-permute-done.4.refs_5_ = f32[128,128]{1,0:T(8,128)S(1)} collective-permute-done((f32[128,128]{1,0:T(8,128)}, f32[128,128]{1,0:T(8,128)S(1)}, u32[]{:S(2)}, u32[]{:S(2)}) %collective-permute-start.4) | collective-permute-done | bytes 65568 | tf_op jit(solution)/shard_map/ppermute | solution.py:130
  24.0 0.6 copy-done.10
  24.6 0.1 copy-done.6
  24.7 0.1 copy-done.7
  24.8 0.2 copy-done
  25.0 0.8 copy-done.1
  25.8 10.0 %shard_map.42 = (f32[32,8,16,128]{3,2,1,0:T(8,128)}, f32[128,128]{1,0:T(8,128)}, f32[32,2,16,128]{3,2,1,0:T(8,128)}, f32[32,2,16,128]{3,2,1,0:T(8,128)}, f32[32,...) custom-call(f32[32,8,16,128]{3,2,1,0:T(8,128)} %refs_8_.1, f32[32,2,16,128]{3,2,1,0:T(8,128)} %copy-done.1, ...), custom_call_target="tpu_custom_call" | custom-call | tf_op jit(solution)/shard_map/pallas_call | solution.py:158
  35.8 3.1 %collective-permute-start.6 = (f32[32,2,16,128]{3,2,1,0:T(8,128)}, f32[32,2,16,128]{3,2,1,0:T(8,128)S(1)}, u32[]{:S(2)}, u32[]{:S(2)}) collective-permute-start(f32[32,2,16,128]{3,2,1,0:T(8,128)} %get-tuple-element.9), channel_id=1, source_target_pairs={{0,32},{32,64},{64,96},{96,128},{128,160},{160,192},{192,224},{224... | collective-permute-start | bytes 1572872 | tf_op jit(solution)/shard_map/ppermute | solution.py:127
  38.9 3.0 %collective-permute-start.9 = (f32[32,8,2,128]{3,2,1,0:T(2,128)}, f32[32,8,2,128]{3,2,1,0:T(2,128)S(1)}, u32[]{:S(2)}, u32[]{:S(2)}) collective-permute-start(f32[32,8,2,128]{3,2,1,0:T(2,128)} %get-tuple-element.12), channel_id=1, source_target_pairs={{0,28},{4,0},{8,4},{12,8},{16,12},{20,16},{24,20},{28,24},{1,29},{... | collective-permute-start | bytes 786440 | tf_op jit(solution)/shard_map/ppermute | solution.py:128
  41.8 1.7 %collective-permute-start.11 = (f32[128,128]{1,0:T(8,128)}, f32[128,128]{1,0:T(8,128)S(1)}, u32[]{:S(2)}, u32[]{:S(2)}) collective-permute-start(f32[128,128]{1,0:T(8,128)} %get-tuple-element.13), channel_id=1, source_target_pairs={{0,3},{1,0},{2,1},{3,2},{4,7},{5,4},{6,5},{7,6},{8,11},{9,8},{10,9... | collective-permute-start | bytes 196616 | tf_op jit(solution)/shard_map/ppermute | solution.py:131
  43.6 1.9 %collective-permute-done.11.refs_6_ = f32[128,128]{1,0:T(8,128)S(1)} collective-permute-done((f32[128,128]{1,0:T(8,128)}, f32[128,128]{1,0:T(8,128)S(1)}, u32[]{:S(2)}, u32[]{:S(2)}) %collective-permute-start.11) | collective-permute-done | bytes 65568 | tf_op jit(solution)/shard_map/ppermute | solution.py:131
  45.5 4.8 %collective-permute-done.10.refs_5_ = f32[128,128]{1,0:T(8,128)S(1)} collective-permute-done((f32[128,128]{1,0:T(8,128)}, f32[128,128]{1,0:T(8,128)S(1)}, u32[]{:S(2)}, u32[]{:S(2)}) %collective-permute-start.10) | collective-permute-done | bytes 65568 | tf_op jit(solution)/shard_map/ppermute | solution.py:130
  50.4 0.6 copy-done.11
  50.9 0.1 copy-done.4
  51.0 0.1 copy-done.5
  51.1 0.2 copy-done.2
  51.3 0.2 copy-done.3
  51.4 7.7 %shard_map.43.y_ref = f32[32,8,16,128]{3,2,1,0:T(8,128)} custom-call(f32[32,8,16,128]{3,2,1,0:T(8,128)} %get-tuple-element.8.refs_0_, f32[32,2,16,128]{3,2,1,0:T(8,128)} %copy-done.2, f32[32,2,16,128]{3,2,1,0:T(8,128)} %copy-done.3, f32[32,8,2,128]{3,2,1,0:T(2,128)} %copy-done.4, f32[32,8,2,128]{3,2,1,0:T(2,128)} %copy-done.5, f32[128,128]{1,0:T(8,128)} %copy-done.11, ...), custom_call_target="tpu_custom_call" | custom-call | tf_op jit(solution)/shard_map/pallas_call | solution.py:158
  59.1 4.9 %shard_map.44 = f32[1024,128]{1,0:T(8,128)} custom-call(f32[32,8,16,128]{3,2,1,0:T(8,128)} %shard_map.43.y_ref), custom_call_target="tpu_custom_call" | custom-call | tf_op jit(solution)/shard_map/pallas_call | solution.py:224
  64.0 1.2 %reduce_sum.9 = f32[1024]{0:T(1024)S(1)} reduce(f32[1024,128]{1,0:T(8,128)} %shard_map.44, f32[]{:T(128)} %constant.36.clone.1), dimensions={1}, to_apply=%region_0.0 | reduce | flops 130048 | bytes 528388 | tf_op jit(solution)/shard_map/reduce_sum | solution.py:232
  65.4 0.1 copy.7
  65.5 2.6 %collective-permute-done.12 = f32[32,32]{0,1:T(8,128)S(1)} collective-permute-done((f32[32,32]{0,1:T(8,128)S(1)}, f32[32,32]{0,1:T(8,128)S(1)}, u32[]{:S(2)}, u32[]{:S(2)}) %collective-permute-start.12) | collective-permute-done | bytes 4128 | tf_op jit(solution)/shard_map/ppermute | solution.py:240
  68.1 1.5 %collective-permute-start.13 = (f32[32,32]{0,1:T(8,128)S(1)}, f32[32,32]{0,1:T(8,128)S(1)}, u32[]{:S(2)}, u32[]{:S(2)}) collective-permute-start(f32[32,32]{0,1:T(8,128)S(1)} %add.33), channel_id=1, source_target_pairs={{0,2},{1,3},{2,0},{3,1},{4,6},{5,7},{6,4},{7,5},{8,10},{9,11},{10,... | collective-permute-start | bytes 12296 | tf_op jit(solution)/shard_map/ppermute | solution.py:240
  69.5 2.6 %collective-permute-done.13 = f32[32,32]{0,1:T(8,128)S(1)} collective-permute-done((f32[32,32]{0,1:T(8,128)S(1)}, f32[32,32]{0,1:T(8,128)S(1)}, u32[]{:S(2)}, u32[]{:S(2)}) %collective-permute-start.13) | collective-permute-done | bytes 4128 | tf_op jit(solution)/shard_map/ppermute | solution.py:240
  72.2 2.6 %collective-permute-done.14 = f32[32,32]{0,1:T(8,128)S(1)} collective-permute-done((f32[32,32]{0,1:T(8,128)S(1)}, f32[32,32]{0,1:T(8,128)S(1)}, u32[]{:S(2)}, u32[]{:S(2)}) %collective-permute-start.14) | collective-permute-done | bytes 4128 | tf_op jit(solution)/shard_map/ppermute | solution.py:240
  74.8 3.8 %collective-permute-done.15 = f32[32,32]{0,1:T(8,128)S(1)} collective-permute-done((f32[32,32]{0,1:T(8,128)S(1)}, f32[32,32]{0,1:T(8,128)S(1)}, u32[]{:S(2)}, u32[]{:S(2)}) %collective-permute-start.15) | collective-permute-done | bytes 4128 | tf_op jit(solution)/shard_map/ppermute | solution.py:240
  78.5 2.5 %collective-permute-start.16 = (f32[32,32]{0,1:T(8,128)S(1)}, f32[32,32]{0,1:T(8,128)S(1)}, u32[]{:S(2)}, u32[]{:S(2)}) collective-permute-start(f32[32,32]{0,1:T(8,128)S(1)} %add.36), channel_id=1, source_target_pairs={{0,16},{4,20},{8,24},{12,28},{16,0},{20,4},{24,8},{28,12},{1,17},{... | collective-permute-start | bytes 12296 | tf_op jit(solution)/shard_map/ppermute | solution.py:240
  81.0 4.0 %collective-permute-done.16 = f32[32,32]{0,1:T(8,128)S(1)} collective-permute-done((f32[32,32]{0,1:T(8,128)S(1)}, f32[32,32]{0,1:T(8,128)S(1)}, u32[]{:S(2)}, u32[]{:S(2)}) %collective-permute-start.16) | collective-permute-done | bytes 4128 | tf_op jit(solution)/shard_map/ppermute | solution.py:240
  85.0 10.5 %collective-permute-start.17 = (f32[32,32]{0,1:T(8,128)S(1)}, f32[32,32]{0,1:T(8,128)S(1)}, u32[]{:S(2)}, u32[]{:S(2)}) collective-permute-start(f32[32,32]{0,1:T(8,128)S(1)} %add.37), channel_id=1, source_target_pairs={{0,32},{32,0},{64,96},{96,64},{128,160},{160,128},{192,224},{224,1... | collective-permute-start | bytes 12296 | tf_op jit(solution)/shard_map/ppermute | solution.py:240
  95.6 0.8 collective-permute-done.17
  96.4 2.6 %collective-permute-done.18 = f32[32,32]{0,1:T(8,128)S(1)} collective-permute-done((f32[32,32]{0,1:T(8,128)S(1)}, f32[32,32]{0,1:T(8,128)S(1)}, u32[]{:S(2)}, u32[]{:S(2)}) %collective-permute-start.18) | collective-permute-done | bytes 4128 | tf_op jit(solution)/shard_map/ppermute | solution.py:240
  99.0 0.2 collective-permute-start.19
  99.2 3.9 %collective-permute-done.19 = f32[32,32]{0,1:T(8,128)S(1)} collective-permute-done((f32[32,32]{0,1:T(8,128)S(1)}, f32[32,32]{0,1:T(8,128)S(1)}, u32[]{:S(2)}, u32[]{:S(2)}) %collective-permute-start.19) | collective-permute-done | bytes 4128 | tf_op jit(solution)/shard_map/ppermute | solution.py:240
  103.1 0.1 copy.8
  103.2 2.9 %cholesky.18 = f32[32,32]{1,0:T(8,128)S(1)} custom-call(f32[32,32]{1,0:T(8,128)S(1)} %fusion), custom_call_target="Cholesky" | custom-call | tf_op jit(solution)/shard_map/jit(cholesky)/cholesky | solution.py:251
  106.2 0.6 compare_reduce_fusion
  106.8 0.6 fusion.3
  107.5 1.3 %select_select_fusion.l_ref = f32[32,32]{1,0:T(8,128)} fusion(f32[32,32]{1,0:T(8,128)S(1)} %cholesky.18, pred[]{:T(512)} %compare_reduce_fusion), kind=kLoop, calls=%fused_computation.2 | loop fusion | flops 3072 | bytes 8193 | tf_op jit(solution)/shard_map/jit(cholesky)/select_n | solution.py:251
  108.7 4.6 %shard_map.45 = f32[32,8,16,128]{3,2,1,0:T(8,128)} custom-call(f32[32,32]{1,0:T(8,128)} %select_select_fusion.l_ref, f32[32,8,16,128]{3,2,1,0:T(8,128)} %shard_map.43.y_ref), custom_call_target="tpu_custom_call" | custom-call | tf_op jit(solution)/shard_map/pallas_call | solution.py:185
  113.3 0.7 copy.9
  (43 shorter events, 0.3 us)
Async XLA Ops:
  1.9 22.1 %collective-permute-start.1 = (f32[32,2,16,128]{3,2,1,0:T(8,128)S(1)}, f32[32,2,16,128]{3,2,1,0:T(8,128)S(1)}, u32[]{:S(2)}, u32[]{:S(2)}) collective-permute-start(f32[32,2,16,128]{3,2,1,0:T(8,128)S(1)} %get-tuple-element.20), channel_id=1, source_target_pairs={{0,224},{32,0},{64,32},{96,64},{128,96},{160,128},{192,160},{224,1... | collective-permute-start | bytes 1572872 | tf_op jit(solution)/shard_map/ppermute | solution.py:128
  5.1 18.9 %collective-permute-start = (f32[32,2,16,128]{3,2,1,0:T(8,128)S(1)}, f32[32,2,16,128]{3,2,1,0:T(8,128)S(1)}, u32[]{:S(2)}, u32[]{:S(2)}) collective-permute-start(f32[32,2,16,128]{3,2,1,0:T(8,128)S(1)} %get-tuple-element.21), channel_id=1, source_target_pairs={{0,32},{32,64},{64,96},{96,128},{128,160},{160,192},{192,224},{224... | collective-permute-start | bytes 1572872 | tf_op jit(solution)/shard_map/ppermute | solution.py:127
  6.9 17.1 %collective-permute-start.3 = (f32[32,8,2,128]{3,2,1,0:T(2,128)S(1)}, f32[32,8,2,128]{3,2,1,0:T(2,128)S(1)}, u32[]{:S(2)}, u32[]{:S(2)}) collective-permute-start(f32[32,8,2,128]{3,2,1,0:T(2,128)S(1)} %get-tuple-element.18), channel_id=1, source_target_pairs={{0,28},{4,0},{8,4},{12,8},{16,12},{20,16},{24,20},{28,24},{1,29},{... | collective-permute-start | bytes 786440 | tf_op jit(solution)/shard_map/ppermute | solution.py:128
  12.0 12.0 %collective-permute-start.2 = (f32[32,8,2,128]{3,2,1,0:T(2,128)S(1)}, f32[32,8,2,128]{3,2,1,0:T(2,128)S(1)}, u32[]{:S(2)}, u32[]{:S(2)}) collective-permute-start(f32[32,8,2,128]{3,2,1,0:T(2,128)S(1)} %get-tuple-element.19), channel_id=1, source_target_pairs={{0,4},{4,8},{8,12},{12,16},{16,20},{20,24},{24,28},{28,0},{1,5},{5... | collective-permute-start | bytes 786440 | tf_op jit(solution)/shard_map/ppermute | solution.py:127
  14.5 4.4 %collective-permute-start.5 = (f32[128,128]{1,0:T(8,128)}, f32[128,128]{1,0:T(8,128)S(1)}, u32[]{:S(2)}, u32[]{:S(2)}) collective-permute-start(f32[128,128]{1,0:T(8,128)} %shard_map.41), channel_id=1, source_target_pairs={{0,3},{1,0},{2,1},{3,2},{4,7},{5,4},{6,5},{7,6},{8,11},{9,8},{10,9... | collective-permute-start | bytes 196616 | tf_op jit(solution)/shard_map/ppermute | solution.py:131
  18.9 5.1 %copy-start.8 = (f32[128,128]{1,0:T(8,128)}, f32[128,128]{1,0:T(8,128)S(1)}, u32[]{:S(2)}) copy-start(f32[128,128]{1,0:T(8,128)S(1)} %collective-permute-done.5.refs_6_) | copy-start | bytes 196612
  18.9 5.0 %collective-permute-start.4 = (f32[128,128]{1,0:T(8,128)}, f32[128,128]{1,0:T(8,128)S(1)}, u32[]{:S(2)}, u32[]{:S(2)}) collective-permute-start(f32[128,128]{1,0:T(8,128)} %shard_map.41), channel_id=1, source_target_pairs={{0,1},{1,2},{2,3},{3,0},{4,5},{5,6},{6,7},{7,4},{8,9},{9,10},{10,1... | collective-permute-start | bytes 196616 | tf_op jit(solution)/shard_map/ppermute | solution.py:130
  24.0 0.6 copy-start.10
  24.0 0.7 copy-start.6
  24.0 0.8 copy-start.7
  24.0 1.0 copy-start
  25.0 0.8 copy-start.1
  35.8 14.5 %collective-permute-start.6 = (f32[32,2,16,128]{3,2,1,0:T(8,128)}, f32[32,2,16,128]{3,2,1,0:T(8,128)S(1)}, u32[]{:S(2)}, u32[]{:S(2)}) collective-permute-start(f32[32,2,16,128]{3,2,1,0:T(8,128)} %get-tuple-element.9), channel_id=1, source_target_pairs={{0,32},{32,64},{64,96},{96,128},{128,160},{160,192},{192,224},{224... | collective-permute-start | bytes 1572872 | tf_op jit(solution)/shard_map/ppermute | solution.py:127
  38.8 11.5 %collective-permute-start.7 = (f32[32,2,16,128]{3,2,1,0:T(8,128)}, f32[32,2,16,128]{3,2,1,0:T(8,128)S(1)}, u32[]{:S(2)}, u32[]{:S(2)}) collective-permute-start(f32[32,2,16,128]{3,2,1,0:T(8,128)} %get-tuple-element.10), channel_id=1, source_target_pairs={{0,224},{32,0},{64,32},{96,64},{128,96},{160,128},{192,160},{224,1... | collective-permute-start | bytes 1572872 | tf_op jit(solution)/shard_map/ppermute | solution.py:128
  38.9 11.4 %collective-permute-start.8 = (f32[32,8,2,128]{3,2,1,0:T(2,128)}, f32[32,8,2,128]{3,2,1,0:T(2,128)S(1)}, u32[]{:S(2)}, u32[]{:S(2)}) collective-permute-start(f32[32,8,2,128]{3,2,1,0:T(2,128)} %get-tuple-element.11), channel_id=1, source_target_pairs={{0,4},{4,8},{8,12},{12,16},{16,20},{20,24},{24,28},{28,0},{1,5},{5... | collective-permute-start | bytes 786440 | tf_op jit(solution)/shard_map/ppermute | solution.py:127
  38.9 11.4 %collective-permute-start.9 = (f32[32,8,2,128]{3,2,1,0:T(2,128)}, f32[32,8,2,128]{3,2,1,0:T(2,128)S(1)}, u32[]{:S(2)}, u32[]{:S(2)}) collective-permute-start(f32[32,8,2,128]{3,2,1,0:T(2,128)} %get-tuple-element.12), channel_id=1, source_target_pairs={{0,28},{4,0},{8,4},{12,8},{16,12},{20,16},{24,20},{28,24},{1,29},{... | collective-permute-start | bytes 786440 | tf_op jit(solution)/shard_map/ppermute | solution.py:128
  41.8 3.6 %collective-permute-start.11 = (f32[128,128]{1,0:T(8,128)}, f32[128,128]{1,0:T(8,128)S(1)}, u32[]{:S(2)}, u32[]{:S(2)}) collective-permute-start(f32[128,128]{1,0:T(8,128)} %get-tuple-element.13), channel_id=1, source_target_pairs={{0,3},{1,0},{2,1},{3,2},{4,7},{5,4},{6,5},{7,6},{8,11},{9,8},{10,9... | collective-permute-start | bytes 196616 | tf_op jit(solution)/shard_map/ppermute | solution.py:131
  45.5 4.9 %copy-start.9 = (f32[128,128]{1,0:T(8,128)}, f32[128,128]{1,0:T(8,128)S(1)}, u32[]{:S(2)}) copy-start(f32[128,128]{1,0:T(8,128)S(1)} %collective-permute-done.11.refs_6_) | copy-start | bytes 196612
  45.5 4.8 %collective-permute-start.10 = (f32[128,128]{1,0:T(8,128)}, f32[128,128]{1,0:T(8,128)S(1)}, u32[]{:S(2)}, u32[]{:S(2)}) collective-permute-start(f32[128,128]{1,0:T(8,128)} %get-tuple-element.13), channel_id=1, source_target_pairs={{0,1},{1,2},{2,3},{3,0},{4,5},{5,6},{6,7},{7,4},{8,9},{9,10},{10,1... | collective-permute-start | bytes 196616 | tf_op jit(solution)/shard_map/ppermute | solution.py:130
  50.3 0.6 copy-start.11
  50.3 0.7 copy-start.4
  50.3 0.8 copy-start.5
  50.3 1.0 copy-start.2
  50.3 1.1 copy-start.3
  65.4 2.6 %collective-permute-start.12 = (f32[32,32]{0,1:T(8,128)S(1)}, f32[32,32]{0,1:T(8,128)S(1)}, u32[]{:S(2)}, u32[]{:S(2)}) collective-permute-start(f32[32,32]{0,1:T(8,128)S(1)} %copy.7), channel_id=1, source_target_pairs={{0,1},{1,0},{2,3},{3,2},{4,5},{5,4},{6,7},{7,6},{8,9},{9,8},{10,11... | collective-permute-start | bytes 12296 | tf_op jit(solution)/shard_map/ppermute | solution.py:240
  68.1 4.1 %collective-permute-start.13 = (f32[32,32]{0,1:T(8,128)S(1)}, f32[32,32]{0,1:T(8,128)S(1)}, u32[]{:S(2)}, u32[]{:S(2)}) collective-permute-start(f32[32,32]{0,1:T(8,128)S(1)} %add.33), channel_id=1, source_target_pairs={{0,2},{1,3},{2,0},{3,1},{4,6},{5,7},{6,4},{7,5},{8,10},{9,11},{10,... | collective-permute-start | bytes 12296 | tf_op jit(solution)/shard_map/ppermute | solution.py:240
  72.2 2.6 %collective-permute-start.14 = (f32[32,32]{0,1:T(8,128)S(1)}, f32[32,32]{0,1:T(8,128)S(1)}, u32[]{:S(2)}, u32[]{:S(2)}) collective-permute-start(f32[32,32]{0,1:T(8,128)S(1)} %add.34), channel_id=1, source_target_pairs={{0,4},{4,0},{8,12},{12,8},{16,20},{20,16},{24,28},{28,24},{1,5},{5... | collective-permute-start | bytes 12296 | tf_op jit(solution)/shard_map/ppermute | solution.py:240
  74.7 3.8 %collective-permute-start.15 = (f32[32,32]{0,1:T(8,128)S(1)}, f32[32,32]{0,1:T(8,128)S(1)}, u32[]{:S(2)}, u32[]{:S(2)}) collective-permute-start(f32[32,32]{0,1:T(8,128)S(1)} %add.35), channel_id=1, source_target_pairs={{0,8},{4,12},{8,0},{12,4},{16,24},{20,28},{24,16},{28,20},{1,9},{5... | collective-permute-start | bytes 12296 | tf_op jit(solution)/shard_map/ppermute | solution.py:240
  78.5 6.5 %collective-permute-start.16 = (f32[32,32]{0,1:T(8,128)S(1)}, f32[32,32]{0,1:T(8,128)S(1)}, u32[]{:S(2)}, u32[]{:S(2)}) collective-permute-start(f32[32,32]{0,1:T(8,128)S(1)} %add.36), channel_id=1, source_target_pairs={{0,16},{4,20},{8,24},{12,28},{16,0},{20,4},{24,8},{28,12},{1,17},{... | collective-permute-start | bytes 12296 | tf_op jit(solution)/shard_map/ppermute | solution.py:240
  85.0 11.4 %collective-permute-start.17 = (f32[32,32]{0,1:T(8,128)S(1)}, f32[32,32]{0,1:T(8,128)S(1)}, u32[]{:S(2)}, u32[]{:S(2)}) collective-permute-start(f32[32,32]{0,1:T(8,128)S(1)} %add.37), channel_id=1, source_target_pairs={{0,32},{32,0},{64,96},{96,64},{128,160},{160,128},{192,224},{224,1... | collective-permute-start | bytes 12296 | tf_op jit(solution)/shard_map/ppermute | solution.py:240
  96.4 2.6 %collective-permute-start.18 = (f32[32,32]{0,1:T(8,128)S(1)}, f32[32,32]{0,1:T(8,128)S(1)}, u32[]{:S(2)}, u32[]{:S(2)}) collective-permute-start(f32[32,32]{0,1:T(8,128)S(1)} %add.38), channel_id=1, source_target_pairs={{0,64},{32,96},{64,0},{96,32},{128,192},{160,224},{192,128},{224,1... | collective-permute-start | bytes 12296 | tf_op jit(solution)/shard_map/ppermute | solution.py:240
  99.0 4.1 %collective-permute-start.19 = (f32[32,32]{0,1:T(8,128)S(1)}, f32[32,32]{0,1:T(8,128)S(1)}, u32[]{:S(2)}, u32[]{:S(2)}) collective-permute-start(f32[32,32]{0,1:T(8,128)S(1)} %add.39), channel_id=1, source_target_pairs={{0,128},{32,160},{64,192},{96,224},{128,0},{160,32},{192,64},{224,... | collective-permute-start | bytes 12296 | tf_op jit(solution)/shard_map/ppermute | solution.py:240

commit v12 on v11

--- a/solution.py
+++ b/solution.py
@@ -210,10 +210,10 @@
         idx = 0
         for a in range(n):
             for b in range(a, n):
-                row = jnp.sum(acc_ref[idx], axis=0, keepdims=True)
-                o_ref[pl.ds(a * n + b, 1), :] = row
+                row = jnp.sum(jnp.sum(acc_ref[idx], axis=0, keepdims=True), axis=1, keepdims=True)
+                o_ref[pl.ds(a, 1), pl.ds(b, 1)] = row
                 if b != a:
-                    o_ref[pl.ds(b * n + a, 1), :] = row
+                    o_ref[pl.ds(b, 1), pl.ds(a, 1)] = row
                 idx += 1
 
 
@@ -224,12 +224,12 @@
     lanes = pl.pallas_call(
         gram_kernel, grid=(cx // xb,),
         in_specs=[pl.BlockSpec((norb, xb, cy, cz), lambda i: (0, i, 0, 0))],
-        out_specs=pl.BlockSpec((norb * norb, cz), lambda i: (0, 0)),
-        out_shape=jax.ShapeDtypeStruct((norb * norb, cz), jnp.float32),
+        out_specs=pl.BlockSpec((norb, norb), lambda i: (0, 0)),
+        out_shape=jax.ShapeDtypeStruct((norb, norb), jnp.float32),
         scratch_shapes=[pltpu.VMEM((pairs, 8, cz), jnp.float32)], interpret=INTERPRET,
         compiler_params=pltpu.CompilerParams(dimension_semantics=("arbitrary",)),
     )(y)
-    return lanes.sum(axis=1).reshape(norb, norb)
+    return lanes
 
 
 def butterfly_sum(c):

time: 114 us -> 114 us (level)
  other arithmetic: 6.79 us -> 5.55 us
    reduce_sum x1 -> x0, other arithmetic: 1.25 us -> none  [gram(): return lanes.sum(axis=1).reshape(norb, norb)]
where the time goes in v12:
time: 114 us; the launch traced here: 113 us
  waiting for transfers between devices  35.7 us (31%)
  starting transfers between devices  34.2 us (30%)
  Pallas kernels  29.7 us (26%)
  local copies, waits for them, and re-layouts  7.44 us (7%)
  other arithmetic  5.55 us (5%)
    ppermute x8, waiting for transfers between devices, butterfly_sum(): c = c + lax.ppermute(c, axis, [(i, i ^ d) for i in range(n)])  22.9 us
    pallas_call x2, Pallas kernels, stage(): pl.pallas_call(functools.partial(stage_kernel, last=last), grid=(norb //...  17.6 us
    ppermute x8, starting transfers between devices, butterfly_sum(): c = c + lax.ppermute(c, axis, [(i, i ^ d) for i in range(n)])  14.8 us
    ppermute x4, starting transfers between devices, exchange(): out.append(lax.ppermute(first, axis, shift_pairs(n, -1)))  11.3 us
    ppermute x2, waiting for transfers between devices, exchange(): out.append(lax.ppermute(zface, 'gz', shift_pairs(n, 1)))  9.33 us
    pallas_call x1, Pallas kernels, gram(): pl.pallas_call(gram_kernel, grid=(cx // xb,), in_specs=[pl.BlockSpec((nor...  4.92 us
    pallas_call x1, Pallas kernels, solve_lower(): pl.pallas_call(solve_kernel, grid=(cx // xb,), in_specs=[pl.BlockSpec(mem...  4.61 us
    ppermute x2, starting transfers between devices, exchange(): out.append(lax.ppermute(zface, 'gz', shift_pairs(n, -1)))  4.48 us
  transfers between devices with their start and end apart: 20, of which 12 were waited for; matrix products, arithmetic and copies ran while one was open for 2% of the time, Pallas kernels for 2%

profile of v12, /device:TPU:1, one launch (start us, length us, event | category | flops | bytes accessed | tf_op | source)
XLA Modules:
  0.0 113.4 jit_solution(6709909369874200870)
XLA Ops:
  0.6 1.3 %fusion.3 = (f32[32,2,16,128]{3,2,1,0:T(8,128)S(1)}, f32[32,2,16,128]{3,2,1,0:T(8,128)S(1)}) fusion(f32[32,8,16,128]{3,2,1,0:T(8,128)} %refs_8_.1), kind=kLoop, calls=%fused_computation.10 | loop fusion | bytes 2097152 | tf_op jit(solution)/shard_map/slice | solution.py:119
  1.9 3.2 %collective-permute-start.1 = (f32[32,2,16,128]{3,2,1,0:T(8,128)S(1)}, f32[32,2,16,128]{3,2,1,0:T(8,128)S(1)}, u32[]{:S(2)}, u32[]{:S(2)}) collective-permute-start(f32[32,2,16,128]{3,2,1,0:T(8,128)S(1)} %get-tuple-element.18), channel_id=1, source_target_pairs={{0,224},{32,0},{64,32},{96,64},{128,96},{160,128},{192,160},{224,1... | collective-permute-start | bytes 1572872 | tf_op jit(solution)/shard_map/ppermute | solution.py:128
  5.1 1.8 %fusion.2 = (f32[32,8,2,128]{3,2,1,0:T(2,128)S(1)}, f32[32,8,2,128]{3,2,1,0:T(2,128)S(1)}) fusion(f32[32,8,16,128]{3,2,1,0:T(8,128)} %refs_8_.1), kind=kLoop, calls=%fused_computation.9 | loop fusion | bytes 1048576 | tf_op jit(solution)/shard_map/slice | solution.py:119
  6.9 5.1 %collective-permute-start.3 = (f32[32,8,2,128]{3,2,1,0:T(2,128)S(1)}, f32[32,8,2,128]{3,2,1,0:T(2,128)S(1)}, u32[]{:S(2)}, u32[]{:S(2)}) collective-permute-start(f32[32,8,2,128]{3,2,1,0:T(2,128)S(1)} %get-tuple-element.16), channel_id=1, source_target_pairs={{0,28},{4,0},{8,4},{12,8},{16,12},{20,16},{24,20},{28,24},{1,29},{... | collective-permute-start | bytes 786440 | tf_op jit(solution)/shard_map/ppermute | solution.py:128
  12.0 2.6 %shard_map.41 = f32[128,128]{1,0:T(8,128)} custom-call(f32[32,8,16,128]{3,2,1,0:T(8,128)} %refs_8_.1), custom_call_target="tpu_custom_call" | custom-call | tf_op jit(solution)/shard_map/pallas_call | solution.py:107
  14.5 2.7 %collective-permute-start.5 = (f32[128,128]{1,0:T(8,128)}, f32[128,128]{1,0:T(8,128)S(1)}, u32[]{:S(2)}, u32[]{:S(2)}) collective-permute-start(f32[128,128]{1,0:T(8,128)} %shard_map.41), channel_id=1, source_target_pairs={{0,3},{1,0},{2,1},{3,2},{4,7},{5,4},{6,5},{7,6},{8,11},{9,8},{10,9... | collective-permute-start | bytes 196616 | tf_op jit(solution)/shard_map/ppermute | solution.py:131
  17.3 1.6 %collective-permute-done.5.refs_6_ = f32[128,128]{1,0:T(8,128)S(1)} collective-permute-done((f32[128,128]{1,0:T(8,128)}, f32[128,128]{1,0:T(8,128)S(1)}, u32[]{:S(2)}, u32[]{:S(2)}) %collective-permute-start.5) | collective-permute-done | bytes 65568 | tf_op jit(solution)/shard_map/ppermute | solution.py:131
  18.9 0.5 collective-permute-start.4
  19.4 4.5 %collective-permute-done.4.refs_5_ = f32[128,128]{1,0:T(8,128)S(1)} collective-permute-done((f32[128,128]{1,0:T(8,128)}, f32[128,128]{1,0:T(8,128)S(1)}, u32[]{:S(2)}, u32[]{:S(2)}) %collective-permute-start.4) | collective-permute-done | bytes 65568 | tf_op jit(solution)/shard_map/ppermute | solution.py:130
  24.0 0.6 copy-done.10
  24.6 0.1 copy-done.6
  24.7 0.1 copy-done.7
  24.8 0.2 copy-done
  25.0 0.8 copy-done.1
  25.8 10.0 %shard_map.42 = (f32[32,8,16,128]{3,2,1,0:T(8,128)}, f32[128,128]{1,0:T(8,128)}, f32[32,2,16,128]{3,2,1,0:T(8,128)}, f32[32,2,16,128]{3,2,1,0:T(8,128)}, f32[32,...) custom-call(f32[32,8,16,128]{3,2,1,0:T(8,128)} %refs_8_.1, f32[32,2,16,128]{3,2,1,0:T(8,128)} %copy-done.1, ...), custom_call_target="tpu_custom_call" | custom-call | tf_op jit(solution)/shard_map/pallas_call | solution.py:158
  35.7 3.1 %collective-permute-start.6 = (f32[32,2,16,128]{3,2,1,0:T(8,128)}, f32[32,2,16,128]{3,2,1,0:T(8,128)S(1)}, u32[]{:S(2)}, u32[]{:S(2)}) collective-permute-start(f32[32,2,16,128]{3,2,1,0:T(8,128)} %get-tuple-element.9), channel_id=1, source_target_pairs={{0,32},{32,64},{64,96},{96,128},{128,160},{160,192},{192,224},{224... | collective-permute-start | bytes 1572872 | tf_op jit(solution)/shard_map/ppermute | solution.py:127
  38.9 3.0 %collective-permute-start.9 = (f32[32,8,2,128]{3,2,1,0:T(2,128)}, f32[32,8,2,128]{3,2,1,0:T(2,128)S(1)}, u32[]{:S(2)}, u32[]{:S(2)}) collective-permute-start(f32[32,8,2,128]{3,2,1,0:T(2,128)} %get-tuple-element.12), channel_id=1, source_target_pairs={{0,28},{4,0},{8,4},{12,8},{16,12},{20,16},{24,20},{28,24},{1,29},{... | collective-permute-start | bytes 786440 | tf_op jit(solution)/shard_map/ppermute | solution.py:128
  41.8 1.7 %collective-permute-start.11 = (f32[128,128]{1,0:T(8,128)}, f32[128,128]{1,0:T(8,128)S(1)}, u32[]{:S(2)}, u32[]{:S(2)}) collective-permute-start(f32[128,128]{1,0:T(8,128)} %get-tuple-element.13), channel_id=1, source_target_pairs={{0,3},{1,0},{2,1},{3,2},{4,7},{5,4},{6,5},{7,6},{8,11},{9,8},{10,9... | collective-permute-start | bytes 196616 | tf_op jit(solution)/shard_map/ppermute | solution.py:131
  43.6 1.9 %collective-permute-done.11.refs_6_ = f32[128,128]{1,0:T(8,128)S(1)} collective-permute-done((f32[128,128]{1,0:T(8,128)}, f32[128,128]{1,0:T(8,128)S(1)}, u32[]{:S(2)}, u32[]{:S(2)}) %collective-permute-start.11) | collective-permute-done | bytes 65568 | tf_op jit(solution)/shard_map/ppermute | solution.py:131
  45.5 4.8 %collective-permute-done.10.refs_5_ = f32[128,128]{1,0:T(8,128)S(1)} collective-permute-done((f32[128,128]{1,0:T(8,128)}, f32[128,128]{1,0:T(8,128)S(1)}, u32[]{:S(2)}, u32[]{:S(2)}) %collective-permute-start.10) | collective-permute-done | bytes 65568 | tf_op jit(solution)/shard_map/ppermute | solution.py:130
  50.3 0.6 copy-done.11
  50.9 0.1 copy-done.4
  51.0 0.1 copy-done.5
  51.1 0.2 copy-done.2
  51.3 0.2 copy-done.3
  51.4 7.7 %shard_map.43.y_ref = f32[32,8,16,128]{3,2,1,0:T(8,128)} custom-call(f32[32,8,16,128]{3,2,1,0:T(8,128)} %get-tuple-element.8.refs_0_, f32[32,2,16,128]{3,2,1,0:T(8,128)} %copy-done.2, f32[32,2,16,128]{3,2,1,0:T(8,128)} %copy-done.3, f32[32,8,2,128]{3,2,1,0:T(2,128)} %copy-done.4, f32[32,8,2,128]{3,2,1,0:T(2,128)} %copy-done.5, f32[128,128]{1,0:T(8,128)} %copy-done.11, ...), custom_call_target="tpu_custom_call" | custom-call | tf_op jit(solution)/shard_map/pallas_call | solution.py:158
  59.1 4.9 %shard_map.44 = f32[32,32]{1,0:T(8,128)} custom-call(f32[32,8,16,128]{3,2,1,0:T(8,128)} %shard_map.43.y_ref), custom_call_target="tpu_custom_call" | custom-call | tf_op jit(solution)/shard_map/pallas_call | solution.py:224
  64.0 0.8 copy.4
  64.8 0.1 collective-permute-start.12
  64.9 2.6 %collective-permute-done.12 = f32[32,32]{0,1:T(8,128)S(1)} collective-permute-done((f32[32,32]{0,1:T(8,128)S(1)}, f32[32,32]{0,1:T(8,128)S(1)}, u32[]{:S(2)}, u32[]{:S(2)}) %collective-permute-start.12) | collective-permute-done | bytes 4128 | tf_op jit(solution)/shard_map/ppermute | solution.py:240
  67.5 1.5 %collective-permute-start.13 = (f32[32,32]{0,1:T(8,128)S(1)}, f32[32,32]{0,1:T(8,128)S(1)}, u32[]{:S(2)}, u32[]{:S(2)}) collective-permute-start(f32[32,32]{0,1:T(8,128)S(1)} %fusion.1), channel_id=1, source_target_pairs={{0,2},{1,3},{2,0},{3,1},{4,6},{5,7},{6,4},{7,5},{8,10},{9,11},{10,... | collective-permute-start | bytes 12296 | tf_op jit(solution)/shard_map/ppermute | solution.py:240
  68.9 2.6 %collective-permute-done.13 = f32[32,32]{0,1:T(8,128)S(1)} collective-permute-done((f32[32,32]{0,1:T(8,128)S(1)}, f32[32,32]{0,1:T(8,128)S(1)}, u32[]{:S(2)}, u32[]{:S(2)}) %collective-permute-start.13) | collective-permute-done | bytes 4128 | tf_op jit(solution)/shard_map/ppermute | solution.py:240
  71.6 2.6 %collective-permute-done.14 = f32[32,32]{0,1:T(8,128)S(1)} collective-permute-done((f32[32,32]{0,1:T(8,128)S(1)}, f32[32,32]{0,1:T(8,128)S(1)}, u32[]{:S(2)}, u32[]{:S(2)}) %collective-permute-start.14) | collective-permute-done | bytes 4128 | tf_op jit(solution)/shard_map/ppermute | solution.py:240
  74.2 3.8 %collective-permute-done.15 = f32[32,32]{0,1:T(8,128)S(1)} collective-permute-done((f32[32,32]{0,1:T(8,128)S(1)}, f32[32,32]{0,1:T(8,128)S(1)}, u32[]{:S(2)}, u32[]{:S(2)}) %collective-permute-start.15) | collective-permute-done | bytes 4128 | tf_op jit(solution)/shard_map/ppermute | solution.py:240
  77.9 2.5 %collective-permute-start.16 = (f32[32,32]{0,1:T(8,128)S(1)}, f32[32,32]{0,1:T(8,128)S(1)}, u32[]{:S(2)}, u32[]{:S(2)}) collective-permute-start(f32[32,32]{0,1:T(8,128)S(1)} %add.36), channel_id=1, source_target_pairs={{0,16},{4,20},{8,24},{12,28},{16,0},{20,4},{24,8},{28,12},{1,17},{... | collective-permute-start | bytes 12296 | tf_op jit(solution)/shard_map/ppermute | solution.py:240
  80.4 4.0 %collective-permute-done.16 = f32[32,32]{0,1:T(8,128)S(1)} collective-permute-done((f32[32,32]{0,1:T(8,128)S(1)}, f32[32,32]{0,1:T(8,128)S(1)}, u32[]{:S(2)}, u32[]{:S(2)}) %collective-permute-start.16) | collective-permute-done | bytes 4128 | tf_op jit(solution)/shard_map/ppermute | solution.py:240
  84.4 10.5 %collective-permute-start.17 = (f32[32,32]{0,1:T(8,128)S(1)}, f32[32,32]{0,1:T(8,128)S(1)}, u32[]{:S(2)}, u32[]{:S(2)}) collective-permute-start(f32[32,32]{0,1:T(8,128)S(1)} %add.37), channel_id=1, source_target_pairs={{0,32},{32,0},{64,96},{96,64},{128,160},{160,128},{192,224},{224,1... | collective-permute-start | bytes 12296 | tf_op jit(solution)/shard_map/ppermute | solution.py:240
  95.0 0.8 collective-permute-done.17
  95.8 2.6 %collective-permute-done.18 = f32[32,32]{0,1:T(8,128)S(1)} collective-permute-done((f32[32,32]{0,1:T(8,128)S(1)}, f32[32,32]{0,1:T(8,128)S(1)}, u32[]{:S(2)}, u32[]{:S(2)}) %collective-permute-start.18) | collective-permute-done | bytes 4128 | tf_op jit(solution)/shard_map/ppermute | solution.py:240
  98.4 0.2 collective-permute-start.19
  98.6 3.9 %collective-permute-done.19 = f32[32,32]{0,1:T(8,128)S(1)} collective-permute-done((f32[32,32]{0,1:T(8,128)S(1)}, f32[32,32]{0,1:T(8,128)S(1)}, u32[]{:S(2)}, u32[]{:S(2)}) %collective-permute-start.19) | collective-permute-done | bytes 4128 | tf_op jit(solution)/shard_map/ppermute | solution.py:240
  102.5 0.1 copy.5
  102.6 2.9 %cholesky.18 = f32[32,32]{1,0:T(8,128)S(1)} custom-call(f32[32,32]{1,0:T(8,128)S(1)} %fusion), custom_call_target="Cholesky" | custom-call | tf_op jit(solution)/shard_map/jit(cholesky)/cholesky | solution.py:251
  105.6 0.6 compare_reduce_fusion
  106.2 0.6 fusion.4
  106.9 1.3 %select_select_fusion.l_ref = f32[32,32]{1,0:T(8,128)} fusion(f32[32,32]{1,0:T(8,128)S(1)} %cholesky.18, pred[]{:T(512)} %compare_reduce_fusion), kind=kLoop, calls=%fused_computation.2 | loop fusion | flops 3072 | bytes 8193 | tf_op jit(solution)/shard_map/jit(cholesky)/select_n | solution.py:251
  108.1 4.6 %shard_map.45 = f32[32,8,16,128]{3,2,1,0:T(8,128)} custom-call(f32[32,32]{1,0:T(8,128)} %select_select_fusion.l_ref, f32[32,8,16,128]{3,2,1,0:T(8,128)} %shard_map.43.y_ref), custom_call_target="tpu_custom_call" | custom-call | tf_op jit(solution)/shard_map/pallas_call | solution.py:185
  112.7 0.7 copy.6
  (41 shorter events, 0.2 us)
Async XLA Ops:
  1.9 22.1 %collective-permute-start.1 = (f32[32,2,16,128]{3,2,1,0:T(8,128)S(1)}, f32[32,2,16,128]{3,2,1,0:T(8,128)S(1)}, u32[]{:S(2)}, u32[]{:S(2)}) collective-permute-start(f32[32,2,16,128]{3,2,1,0:T(8,128)S(1)} %get-tuple-element.18), channel_id=1, source_target_pairs={{0,224},{32,0},{64,32},{96,64},{128,96},{160,128},{192,160},{224,1... | collective-permute-start | bytes 1572872 | tf_op jit(solution)/shard_map/ppermute | solution.py:128
  5.1 18.9 %collective-permute-start = (f32[32,2,16,128]{3,2,1,0:T(8,128)S(1)}, f32[32,2,16,128]{3,2,1,0:T(8,128)S(1)}, u32[]{:S(2)}, u32[]{:S(2)}) collective-permute-start(f32[32,2,16,128]{3,2,1,0:T(8,128)S(1)} %get-tuple-element.19), channel_id=1, source_target_pairs={{0,32},{32,64},{64,96},{96,128},{128,160},{160,192},{192,224},{224... | collective-permute-start | bytes 1572872 | tf_op jit(solution)/shard_map/ppermute | solution.py:127
  6.9 17.1 %collective-permute-start.3 = (f32[32,8,2,128]{3,2,1,0:T(2,128)S(1)}, f32[32,8,2,128]{3,2,1,0:T(2,128)S(1)}, u32[]{:S(2)}, u32[]{:S(2)}) collective-permute-start(f32[32,8,2,128]{3,2,1,0:T(2,128)S(1)} %get-tuple-element.16), channel_id=1, source_target_pairs={{0,28},{4,0},{8,4},{12,8},{16,12},{20,16},{24,20},{28,24},{1,29},{... | collective-permute-start | bytes 786440 | tf_op jit(solution)/shard_map/ppermute | solution.py:128
  12.0 12.0 %collective-permute-start.2 = (f32[32,8,2,128]{3,2,1,0:T(2,128)S(1)}, f32[32,8,2,128]{3,2,1,0:T(2,128)S(1)}, u32[]{:S(2)}, u32[]{:S(2)}) collective-permute-start(f32[32,8,2,128]{3,2,1,0:T(2,128)S(1)} %get-tuple-element.17), channel_id=1, source_target_pairs={{0,4},{4,8},{8,12},{12,16},{16,20},{20,24},{24,28},{28,0},{1,5},{5... | collective-permute-start | bytes 786440 | tf_op jit(solution)/shard_map/ppermute | solution.py:127
  14.5 4.4 %collective-permute-start.5 = (f32[128,128]{1,0:T(8,128)}, f32[128,128]{1,0:T(8,128)S(1)}, u32[]{:S(2)}, u32[]{:S(2)}) collective-permute-start(f32[128,128]{1,0:T(8,128)} %shard_map.41), channel_id=1, source_target_pairs={{0,3},{1,0},{2,1},{3,2},{4,7},{5,4},{6,5},{7,6},{8,11},{9,8},{10,9... | collective-permute-start | bytes 196616 | tf_op jit(solution)/shard_map/ppermute | solution.py:131
  18.9 5.1 %copy-start.8 = (f32[128,128]{1,0:T(8,128)}, f32[128,128]{1,0:T(8,128)S(1)}, u32[]{:S(2)}) copy-start(f32[128,128]{1,0:T(8,128)S(1)} %collective-permute-done.5.refs_6_) | copy-start | bytes 196612
  18.9 5.0 %collective-permute-start.4 = (f32[128,128]{1,0:T(8,128)}, f32[128,128]{1,0:T(8,128)S(1)}, u32[]{:S(2)}, u32[]{:S(2)}) collective-permute-start(f32[128,128]{1,0:T(8,128)} %shard_map.41), channel_id=1, source_target_pairs={{0,1},{1,2},{2,3},{3,0},{4,5},{5,6},{6,7},{7,4},{8,9},{9,10},{10,1... | collective-permute-start | bytes 196616 | tf_op jit(solution)/shard_map/ppermute | solution.py:130
  24.0 0.6 copy-start.10
  24.0 0.7 copy-start.6
  24.0 0.8 copy-start.7
  24.0 1.0 copy-start
  25.0 0.8 copy-start.1
  35.7 14.5 %collective-permute-start.6 = (f32[32,2,16,128]{3,2,1,0:T(8,128)}, f32[32,2,16,128]{3,2,1,0:T(8,128)S(1)}, u32[]{:S(2)}, u32[]{:S(2)}) collective-permute-start(f32[32,2,16,128]{3,2,1,0:T(8,128)} %get-tuple-element.9), channel_id=1, source_target_pairs={{0,32},{32,64},{64,96},{96,128},{128,160},{160,192},{192,224},{224... | collective-permute-start | bytes 1572872 | tf_op jit(solution)/shard_map/ppermute | solution.py:127
  38.8 11.5 %collective-permute-start.7 = (f32[32,2,16,128]{3,2,1,0:T(8,128)}, f32[32,2,16,128]{3,2,1,0:T(8,128)S(1)}, u32[]{:S(2)}, u32[]{:S(2)}) collective-permute-start(f32[32,2,16,128]{3,2,1,0:T(8,128)} %get-tuple-element.10), channel_id=1, source_target_pairs={{0,224},{32,0},{64,32},{96,64},{128,96},{160,128},{192,160},{224,1... | collective-permute-start | bytes 1572872 | tf_op jit(solution)/shard_map/ppermute | solution.py:128
  38.9 11.4 %collective-permute-start.8 = (f32[32,8,2,128]{3,2,1,0:T(2,128)}, f32[32,8,2,128]{3,2,1,0:T(2,128)S(1)}, u32[]{:S(2)}, u32[]{:S(2)}) collective-permute-start(f32[32,8,2,128]{3,2,1,0:T(2,128)} %get-tuple-element.11), channel_id=1, source_target_pairs={{0,4},{4,8},{8,12},{12,16},{16,20},{20,24},{24,28},{28,0},{1,5},{5... | collective-permute-start | bytes 786440 | tf_op jit(solution)/shard_map/ppermute | solution.py:127
  38.9 11.4 %collective-permute-start.9 = (f32[32,8,2,128]{3,2,1,0:T(2,128)}, f32[32,8,2,128]{3,2,1,0:T(2,128)S(1)}, u32[]{:S(2)}, u32[]{:S(2)}) collective-permute-start(f32[32,8,2,128]{3,2,1,0:T(2,128)} %get-tuple-element.12), channel_id=1, source_target_pairs={{0,28},{4,0},{8,4},{12,8},{16,12},{20,16},{24,20},{28,24},{1,29},{... | collective-permute-start | bytes 786440 | tf_op jit(solution)/shard_map/ppermute | solution.py:128
  41.8 3.6 %collective-permute-start.11 = (f32[128,128]{1,0:T(8,128)}, f32[128,128]{1,0:T(8,128)S(1)}, u32[]{:S(2)}, u32[]{:S(2)}) collective-permute-start(f32[128,128]{1,0:T(8,128)} %get-tuple-element.13), channel_id=1, source_target_pairs={{0,3},{1,0},{2,1},{3,2},{4,7},{5,4},{6,5},{7,6},{8,11},{9,8},{10,9... | collective-permute-start | bytes 196616 | tf_op jit(solution)/shard_map/ppermute | solution.py:131
  45.4 4.9 %copy-start.9 = (f32[128,128]{1,0:T(8,128)}, f32[128,128]{1,0:T(8,128)S(1)}, u32[]{:S(2)}) copy-start(f32[128,128]{1,0:T(8,128)S(1)} %collective-permute-done.11.refs_6_) | copy-start | bytes 196612
  45.4 4.8 %collective-permute-start.10 = (f32[128,128]{1,0:T(8,128)}, f32[128,128]{1,0:T(8,128)S(1)}, u32[]{:S(2)}, u32[]{:S(2)}) collective-permute-start(f32[128,128]{1,0:T(8,128)} %get-tuple-element.13), channel_id=1, source_target_pairs={{0,1},{1,2},{2,3},{3,0},{4,5},{5,6},{6,7},{7,4},{8,9},{9,10},{10,1... | collective-permute-start | bytes 196616 | tf_op jit(solution)/shard_map/ppermute | solution.py:130
  50.3 0.6 copy-start.11
  50.3 0.7 copy-start.4
  50.3 0.8 copy-start.5
  50.3 1.0 copy-start.2
  50.3 1.1 copy-start.3
  64.8 2.6 %collective-permute-start.12 = (f32[32,32]{0,1:T(8,128)S(1)}, f32[32,32]{0,1:T(8,128)S(1)}, u32[]{:S(2)}, u32[]{:S(2)}) collective-permute-start(f32[32,32]{0,1:T(8,128)S(1)} %broadcast_multiply_fusion), channel_id=1, source_target_pairs={{0,1},{1,0},{2,3},{3,2},{4,5},{5,4},{6,7},{7,6},{8,9},{9,8},{10,11... | collective-permute-start | bytes 12296 | tf_op jit(solution)/shard_map/ppermute | solution.py:240
  67.5 4.1 %collective-permute-start.13 = (f32[32,32]{0,1:T(8,128)S(1)}, f32[32,32]{0,1:T(8,128)S(1)}, u32[]{:S(2)}, u32[]{:S(2)}) collective-permute-start(f32[32,32]{0,1:T(8,128)S(1)} %fusion.1), channel_id=1, source_target_pairs={{0,2},{1,3},{2,0},{3,1},{4,6},{5,7},{6,4},{7,5},{8,10},{9,11},{10,... | collective-permute-start | bytes 12296 | tf_op jit(solution)/shard_map/ppermute | solution.py:240
  71.6 2.6 %collective-permute-start.14 = (f32[32,32]{0,1:T(8,128)S(1)}, f32[32,32]{0,1:T(8,128)S(1)}, u32[]{:S(2)}, u32[]{:S(2)}) collective-permute-start(f32[32,32]{0,1:T(8,128)S(1)} %add.34), channel_id=1, source_target_pairs={{0,4},{4,0},{8,12},{12,8},{16,20},{20,16},{24,28},{28,24},{1,5},{5... | collective-permute-start | bytes 12296 | tf_op jit(solution)/shard_map/ppermute | solution.py:240
  74.2 3.8 %collective-permute-start.15 = (f32[32,32]{0,1:T(8,128)S(1)}, f32[32,32]{0,1:T(8,128)S(1)}, u32[]{:S(2)}, u32[]{:S(2)}) collective-permute-start(f32[32,32]{0,1:T(8,128)S(1)} %add.35), channel_id=1, source_target_pairs={{0,8},{4,12},{8,0},{12,4},{16,24},{20,28},{24,16},{28,20},{1,9},{5... | collective-permute-start | bytes 12296 | tf_op jit(solution)/shard_map/ppermute | solution.py:240
  77.9 6.5 %collective-permute-start.16 = (f32[32,32]{0,1:T(8,128)S(1)}, f32[32,32]{0,1:T(8,128)S(1)}, u32[]{:S(2)}, u32[]{:S(2)}) collective-permute-start(f32[32,32]{0,1:T(8,128)S(1)} %add.36), channel_id=1, source_target_pairs={{0,16},{4,20},{8,24},{12,28},{16,0},{20,4},{24,8},{28,12},{1,17},{... | collective-permute-start | bytes 12296 | tf_op jit(solution)/shard_map/ppermute | solution.py:240
  84.4 11.4 %collective-permute-start.17 = (f32[32,32]{0,1:T(8,128)S(1)}, f32[32,32]{0,1:T(8,128)S(1)}, u32[]{:S(2)}, u32[]{:S(2)}) collective-permute-start(f32[32,32]{0,1:T(8,128)S(1)} %add.37), channel_id=1, source_target_pairs={{0,32},{32,0},{64,96},{96,64},{128,160},{160,128},{192,224},{224,1... | collective-permute-start | bytes 12296 | tf_op jit(solution)/shard_map/ppermute | solution.py:240
  95.8 2.6 %collective-permute-start.18 = (f32[32,32]{0,1:T(8,128)S(1)}, f32[32,32]{0,1:T(8,128)S(1)}, u32[]{:S(2)}, u32[]{:S(2)}) collective-permute-start(f32[32,32]{0,1:T(8,128)S(1)} %add.38), channel_id=1, source_target_pairs={{0,64},{32,96},{64,0},{96,32},{128,192},{160,224},{192,128},{224,1... | collective-permute-start | bytes 12296 | tf_op jit(solution)/shard_map/ppermute | solution.py:240
  98.4 4.1 %collective-permute-start.19 = (f32[32,32]{0,1:T(8,128)S(1)}, f32[32,32]{0,1:T(8,128)S(1)}, u32[]{:S(2)}, u32[]{:S(2)}) collective-permute-start(f32[32,32]{0,1:T(8,128)S(1)} %add.39), channel_id=1, source_target_pairs={{0,128},{32,160},{64,192},{96,224},{128,0},{160,32},{192,64},{224,... | collective-permute-start | bytes 12296 | tf_op jit(solution)/shard_map/ppermute | solution.py:240
